TPU v7x, 32 devices: a whole 2x2x4 slice. The times are simulated.
32 devices in a mesh: dp: 16 (over z, x, core), tensor: 2 (over y).
Axes of the slice: x: 2, y: 2, z: 4, core: 2. Of those that a mesh axis runs over, the one named last changes fastest.
Arguments:
- block_input: bfloat16 [4096, 768], P(('dp', 'tensor')), may hold values from -24 to 24
- cotangent: bfloat16 [4096, 768], P(('dp', 'tensor')), may hold values from -6 to 6
- segments: int32 [16, 256], P('dp'), may hold values from 0 to 3, never falling along the last dimension, each value on 1 to 128 neighbouring positions
- qkv_weight: bfloat16 [2, 768, 3, 768], P(None, 'dp', None, 'tensor'), may hold values from -0.21875 to 0.21875
- proj_weight: bfloat16 [2, 768, 768], P(None, 'tensor', 'dp'), may hold values from -1.75 to 1.75
- up_weight: bfloat16 [2, 768, 3072], P(None, 'dp', 'tensor'), may hold values from -0.21875 to 0.21875
- down_weight: bfloat16 [2, 3072, 768], P(None, 'tensor', 'dp'), may hold values from -0.109375 to 0.109375
- norm_gains: float32 [2, 2, 768], replicated, may hold values from 0.5 to 1.5
- biases: float32 [2, 4, 768], replicated, may hold values from -3 to 3
- qkv_bias: float32 [2, 3, 768], replicated, may hold values from -2.5 to 2.5
- up_bias: float32 [2, 3072], replicated, may hold values from -3 to 3
- qkv_state: float32 [2, 768, 3, 768], P(None, 'dp', None, 'tensor'), may hold values from -40 to 40
- proj_state: float32 [2, 768, 768], P(None, 'tensor', 'dp'), may hold values from -40 to 40
- up_state: float32 [2, 768, 3072], P(None, 'dp', 'tensor'), may hold values from -40 to 40
- down_state: float32 [2, 3072, 768], P(None, 'tensor', 'dp'), may hold values from -40 to 40
Outputs:
- block_output: float32 [4096, 768], P(('dp', 'tensor'))
- input_grad: float32 [4096, 768], P(('dp', 'tensor'))
- qkv_grad: float32 [2, 768, 3, 768], P(None, 'dp', None, 'tensor')
- proj_grad: float32 [2, 768, 768], P(None, 'tensor', 'dp')
- up_grad: float32 [2, 768, 3072], P(None, 'dp', 'tensor')
- down_grad: float32 [2, 3072, 768], P(None, 'tensor', 'dp')
- gains_grad: float32 [2, 2, 768], replicated
- biases_grad: float32 [2, 4, 768], replicated
- qkv_bias_grad: float32 [2, 3, 768], replicated
- up_bias_grad: float32 [2, 3072], replicated
- qkv_new: float32 [2, 768, 3, 768], P(None, 'dp', None, 'tensor')
- proj_new: float32 [2, 768, 768], P(None, 'tensor', 'dp')
- up_new: float32 [2, 768, 3072], P(None, 'dp', 'tensor')
- down_new: float32 [2, 3072, 768], P(None, 'tensor', 'dp')
- gains_new: float32 [2, 2, 768], replicated
- biases_new: float32 [2, 4, 768], replicated
- qkv_bias_new: float32 [2, 3, 768], replicated
- up_bias_new: float32 [2, 3072], replicated
- qkv_state_new: float32 [2, 768, 3, 768], P(None, 'dp', None, 'tensor')
- proj_state_new: float32 [2, 768, 768], P(None, 'tensor', 'dp')
- up_state_new: float32 [2, 768, 3072], P(None, 'dp', 'tensor')
- down_state_new: float32 [2, 3072, 768], P(None, 'tensor', 'dp')
All inputs are finite; a program needn't handle non-finite values.
Results may differ from a plain program's by a relative error of at most 0.02.
Values may be sent and summed in bfloat16 or wider, within the bound.
No kernel may reach another device: no remote copies, remote signals or barrier semaphores. Data moves between devices by JAX's collectives and lax.ppermute only.
A program may use at most 192 MiB of HBM per device.

v0:
```python
import math

import jax
import jax.numpy as jnp
from jax import lax
from jax.sharding import PartitionSpec as P

D = 768
HD = 64
FF = 3072
ROT = 16
LAYERS = 2
NS_ITERS = 5


highest = lax.Precision.HIGHEST
norm_eps = 1e-05
masked_score = -1e30
coef_first = 3.4445
coef_second = -4.775
coef_third = 2.0315
momentum = 0.9
muon_rate = 0.2
match_rms = 0.2
vector_rate = 0.2
vector_eps = 1e-06
frobenius_eps = 1e-07


def rotary_tables(segment_row):
    length = segment_row.shape[0]
    indices = jnp.arange(length, dtype=jnp.int32)
    change = jnp.concatenate([jnp.ones((1,), dtype=bool), segment_row[1:] != segment_row[:-1]])
    starts = lax.cummax(jnp.where(change, indices, jnp.zeros_like(indices)), axis=0)
    positions = (indices - starts).astype(jnp.float32)
    half_rot = ROT // 2
    frequency = 10000.0 ** (-2.0 * jnp.arange(half_rot, dtype=jnp.float32) / ROT)
    angles = positions[:, None] * frequency[None, :]
    return (jnp.cos(angles), jnp.sin(angles))


def rotate(values, cosine_table, sine_table):
    half_rot = ROT // 2
    first_half = values[..., :half_rot]
    second_half = values[..., half_rot:ROT]
    cos_b = cosine_table[:, None, :]
    sin_b = sine_table[:, None, :]
    return jnp.concatenate(
        [
            first_half * cos_b - second_half * sin_b,
            second_half * cos_b + first_half * sin_b,
            values[..., ROT:],
        ],
        axis=-1,
    )


def unrotate(gradient, cosine_table, sine_table):
    half_rot = ROT // 2
    first_half = gradient[..., :half_rot]
    second_half = gradient[..., half_rot:ROT]
    cos_b = cosine_table[:, None, :]
    sin_b = sine_table[:, None, :]
    return jnp.concatenate(
        [
            first_half * cos_b + second_half * sin_b,
            second_half * cos_b - first_half * sin_b,
            gradient[..., ROT:],
        ],
        axis=-1,
    )


def normalize(stream):
    centered = stream - jnp.mean(stream, axis=-1, keepdims=True)
    inverse = lax.rsqrt(jnp.mean(centered * centered, axis=-1, keepdims=True) + norm_eps)
    return (centered * inverse, inverse)


def gelu_exact(values):
    return jax.nn.gelu(values, approximate=False)


def block_mask(segment_row, block_rows):
    query_pos = jnp.arange(block_rows, dtype=jnp.int32)
    key_pos = jnp.arange(segment_row.shape[0], dtype=jnp.int32)
    return (segment_row[:, None] == segment_row[None, :]) & (query_pos[:, None] >= key_pos[None, :])


def block_scores(queries, key_rows, allowed):
    scores = jnp.einsum(
        "qhe,khe->hqk", queries, key_rows, preferred_element_type=jnp.float32
    ) * queries.shape[-1] ** (-0.5)
    return jnp.where(allowed[None], scores, masked_score)


def attend(queries, key_rows, values, segment_row):
    length = queries.shape[0]
    block_rows = min(512, length)
    allowed = block_mask(segment_row, block_rows)
    scores = block_scores(queries, key_rows, allowed)
    row_peak = jnp.max(scores, axis=-1, keepdims=True)
    exponent = jnp.exp(scores - row_peak)
    row_total = jnp.sum(exponent, axis=-1, keepdims=True)
    probs_low = (exponent / row_total).astype(jnp.bfloat16)
    outputs = jnp.einsum(
        "hqk,khe->qhe", probs_low, values, preferred_element_type=jnp.float32
    ).astype(jnp.bfloat16)
    log_sums = row_peak + jnp.log(row_total)
    return (outputs, log_sums)


def attend_back(queries, key_rows, values, heads_grad, log_sums, segment_row):
    length = queries.shape[0]
    block_rows = min(512, length)
    scale_factor = queries.shape[-1] ** (-0.5)
    allowed = block_mask(segment_row, block_rows)
    scores = block_scores(queries, key_rows, allowed)
    probs_full = jnp.exp(scores - log_sums)
    probs_grad = jnp.einsum("qhe,khe->hqk", heads_grad, values, preferred_element_type=jnp.float32)
    row_dot = jnp.sum(probs_full * probs_grad, axis=-1, keepdims=True)
    score_grad = (probs_full * (probs_grad - row_dot)).astype(jnp.bfloat16)
    value_grad = jnp.einsum(
        "hqk,qhe->khe",
        probs_full.astype(jnp.bfloat16),
        heads_grad,
        preferred_element_type=jnp.float32,
    )
    query_grads = (
        jnp.einsum("hqk,khe->qhe", score_grad, key_rows, preferred_element_type=jnp.float32)
        * scale_factor
    )
    key_grad = (
        jnp.einsum("hqk,qhe->khe", score_grad, queries, preferred_element_type=jnp.float32)
        * scale_factor
    )
    return (query_grads, key_grad, value_grad)


def pad_columns(matrix, slot_width):
    return jnp.pad(matrix, ((0, 0), (0, slot_width - matrix.shape[1])))


def gram_matrix(matrix):
    return lax.psum(jnp.dot(matrix, matrix.T, precision=highest), "tensor")


def vector_step(params, gradients):
    return params - vector_rate * gradients * lax.rsqrt(
        jnp.mean(gradients * gradients, axis=-1, keepdims=True) + vector_eps
    )


def local(
    block_input,
    cotangent,
    segments,
    qkv_weight,
    proj_weight,
    up_weight,
    down_weight,
    norm_gains,
    biases,
    qkv_bias,
    up_bias,
    qkv_state,
    proj_state,
    up_state,
    down_state,
):
    tensor_rank = lax.axis_index("tensor")
    local_width = qkv_weight.shape[3]
    local_hidden = up_weight.shape[2]
    head_count = local_width // HD
    model_width = block_input.shape[1]
    segment_row = segments[0]
    cosine_table, sine_table = rotary_tables(segment_row)
    stream = block_input.astype(jnp.float32)
    saved_layers = []
    for layer_id in range(LAYERS):
        layer_weights = (
            lax.all_gather(qkv_weight[layer_id], "dp", axis=0, tiled=True),
            lax.all_gather(proj_weight[layer_id], "dp", axis=1, tiled=True),
            lax.all_gather(up_weight[layer_id], "dp", axis=0, tiled=True),
            lax.all_gather(down_weight[layer_id], "dp", axis=1, tiled=True),
        )
        qkv_full, proj_full, up_full, down_full = layer_weights
        normed, inverse = normalize(stream)
        attn_rows = (normed * norm_gains[layer_id, 0] + biases[layer_id, 0]).astype(jnp.bfloat16)
        mlp_rows = (normed * norm_gains[layer_id, 1] + biases[layer_id, 1]).astype(jnp.bfloat16)
        attn_in, mlp_in = (
            lax.all_gather(attn_rows, "tensor", axis=0, tiled=True),
            lax.all_gather(mlp_rows, "tensor", axis=0, tiled=True),
        )
        length = attn_in.shape[0]
        qkv_local_bias = lax.dynamic_slice_in_dim(
            qkv_bias[layer_id], tensor_rank * local_width, local_width, 1
        )
        qkv_pre = (
            jnp.einsum("ld,dcf->lcf", attn_in, qkv_full, preferred_element_type=jnp.float32)
            + qkv_local_bias
        )
        shaped = qkv_pre.reshape(length, 3, head_count, HD)
        queries = rotate(shaped[:, 0], cosine_table, sine_table).astype(jnp.bfloat16)
        key_rows = rotate(shaped[:, 1], cosine_table, sine_table).astype(jnp.bfloat16)
        values = shaped[:, 2].astype(jnp.bfloat16)
        heads_out, log_sums = attend(queries, key_rows, values, segment_row)
        heads_flat = heads_out.reshape(length, local_width)
        up_local_bias = lax.dynamic_slice_in_dim(
            up_bias[layer_id], tensor_rank * local_hidden, local_hidden, 0
        )
        up_pre = jnp.dot(mlp_in, up_full, preferred_element_type=jnp.float32) + up_local_bias
        act_low = gelu_exact(up_pre).astype(jnp.bfloat16)
        partial_sum = jnp.dot(heads_flat, proj_full, preferred_element_type=jnp.float32) + jnp.dot(
            act_low, down_full, preferred_element_type=jnp.float32
        )
        branch = lax.psum_scatter(partial_sum, "tensor", scatter_dimension=0, tiled=True)
        saved_layers.append(
            (
                normed,
                inverse,
                attn_in,
                mlp_in,
                queries,
                key_rows,
                values,
                log_sums,
                heads_flat,
                up_pre,
                act_low,
                layer_weights,
            )
        )
        stream = stream + branch + biases[layer_id, 2] + biases[layer_id, 3]
    grad_stream = cotangent.astype(jnp.float32)
    gains_list = [None] * LAYERS
    biases_list = [None] * LAYERS
    qkv_bias_list = [None] * LAYERS
    up_bias_list = [None] * LAYERS
    weight_list = [None] * LAYERS
    for layer_id in reversed(range(LAYERS)):
        (
            normed,
            inverse,
            attn_in,
            mlp_in,
            queries,
            key_rows,
            values,
            log_sums,
            heads_flat,
            up_pre,
            act_low,
            layer_weights,
        ) = saved_layers[layer_id]
        layer_weights = (
            lax.all_gather(qkv_weight[layer_id], "dp", axis=0, tiled=True),
            lax.all_gather(proj_weight[layer_id], "dp", axis=1, tiled=True),
            lax.all_gather(up_weight[layer_id], "dp", axis=0, tiled=True),
            lax.all_gather(down_weight[layer_id], "dp", axis=1, tiled=True),
        )
        qkv_full, proj_full, up_full, down_full = layer_weights
        length = attn_in.shape[0]
        out_bias_grad = jnp.sum(grad_stream, axis=0)
        branch_grad = lax.all_gather(grad_stream.astype(jnp.bfloat16), "tensor", axis=0, tiled=True)
        down_part = jnp.einsum(
            "lf,ld->fd", act_low, branch_grad, preferred_element_type=jnp.float32
        )
        act_grad = jnp.einsum(
            "ld,fd->lf", branch_grad, down_full, preferred_element_type=jnp.float32
        )
        gelu_back = jax.vjp(gelu_exact, up_pre)[1]
        up_pre_grad = gelu_back(act_grad)[0].astype(jnp.bfloat16)
        up_bias_part = jnp.sum(up_pre_grad, axis=0, dtype=jnp.float32)
        up_part = jnp.einsum("ld,lf->df", mlp_in, up_pre_grad, preferred_element_type=jnp.float32)
        mlp_in_grad = jnp.einsum(
            "lf,df->ld", up_pre_grad, up_full, preferred_element_type=jnp.float32
        )
        proj_part = jnp.einsum(
            "lf,ld->fd", heads_flat, branch_grad, preferred_element_type=jnp.float32
        )
        heads_grad = (
            jnp.einsum("ld,fd->lf", branch_grad, proj_full, preferred_element_type=jnp.float32)
            .astype(jnp.bfloat16)
            .reshape(length, head_count, HD)
        )
        query_grad, key_grad, value_grad = attend_back(
            queries, key_rows, values, heads_grad, log_sums, segment_row
        )
        qkv_pre_grad = jnp.stack(
            [
                unrotate(query_grad, cosine_table, sine_table),
                unrotate(key_grad, cosine_table, sine_table),
                value_grad,
            ],
            axis=1,
        )
        qkv_pre_grad = qkv_pre_grad.reshape(length, 3, local_width).astype(jnp.bfloat16)
        qkv_bias_part = jnp.sum(qkv_pre_grad, axis=0, dtype=jnp.float32)
        qkv_part = jnp.einsum(
            "ld,lcf->dcf", attn_in, qkv_pre_grad, preferred_element_type=jnp.float32
        )
        attn_in_grad = jnp.einsum(
            "lcf,dcf->ld", qkv_pre_grad, qkv_full, preferred_element_type=jnp.float32
        )
        attn_rows_grad, mlp_rows_grad = (
            lax.psum_scatter(attn_in_grad, "tensor", scatter_dimension=0, tiled=True),
            lax.psum_scatter(mlp_in_grad, "tensor", scatter_dimension=0, tiled=True),
        )
        gains_list[layer_id] = jnp.stack(
            [jnp.sum(attn_rows_grad * normed, axis=0), jnp.sum(mlp_rows_grad * normed, axis=0)]
        )
        biases_list[layer_id] = jnp.stack(
            [
                jnp.sum(attn_rows_grad, axis=0),
                jnp.sum(mlp_rows_grad, axis=0),
                out_bias_grad,
                out_bias_grad,
            ]
        )
        qkv_bias_list[layer_id] = lax.dynamic_update_slice_in_dim(
            jnp.zeros((3, model_width), jnp.float32), qkv_bias_part, tensor_rank * local_width, 1
        )
        up_bias_list[layer_id] = lax.dynamic_update_slice_in_dim(
            jnp.zeros((up_bias.shape[1],), jnp.float32), up_bias_part, tensor_rank * local_hidden, 0
        )
        normed_grad = (
            attn_rows_grad * norm_gains[layer_id, 0] + mlp_rows_grad * norm_gains[layer_id, 1]
        )
        normed_mean = jnp.mean(normed_grad, axis=-1, keepdims=True)
        product_mean = jnp.mean(normed_grad * normed, axis=-1, keepdims=True)
        grad_stream = grad_stream + inverse * (normed_grad - normed_mean - normed * product_mean)
        weight_list[layer_id] = (
            lax.psum_scatter(qkv_part, "dp", scatter_dimension=0, tiled=True),
            lax.psum_scatter(proj_part, "dp", scatter_dimension=1, tiled=True),
            lax.psum_scatter(up_part, "dp", scatter_dimension=0, tiled=True),
            lax.psum_scatter(down_part, "dp", scatter_dimension=1, tiled=True),
        )
    gains_grad, biases_grad, qkv_bias_grad, up_bias_grad = lax.psum(
        (
            jnp.stack(gains_list),
            jnp.stack(biases_list),
            jnp.stack(qkv_bias_list),
            jnp.stack(up_bias_list),
        ),
        ("dp", "tensor"),
    )
    qkv_grad = jnp.stack([weight_list[layer_id][0] for layer_id in range(LAYERS)])
    proj_grad = jnp.stack([weight_list[layer_id][1] for layer_id in range(LAYERS)])
    up_grad = jnp.stack([weight_list[layer_id][2] for layer_id in range(LAYERS)])
    down_grad = jnp.stack([weight_list[layer_id][3] for layer_id in range(LAYERS)])
    qkv_state_new = momentum * qkv_state + qkv_grad
    proj_state_new = momentum * proj_state + proj_grad
    up_state_new = momentum * up_state + up_grad
    down_state_new = momentum * down_state + down_grad
    rows_local = qkv_state.shape[1]
    slot_width = up_state.shape[2]
    slot_list = []
    for layer_id in range(LAYERS):
        slot_list.append(
            pad_columns(qkv_state_new[layer_id].reshape(rows_local, 3 * local_width), slot_width)
        )
        slot_list.append(pad_columns(proj_state_new[layer_id].T, slot_width))
        slot_list.append(up_state_new[layer_id])
        slot_list.append(down_state_new[layer_id].T)
    stacked = jnp.stack(slot_list)
    dp_count = lax.axis_size("dp")
    slot_count = 4 * LAYERS
    groups = dp_count // slot_count
    outgoing = jnp.tile(stacked, (groups, 1, 1))
    owned_slot = lax.all_to_all(outgoing, "dp", split_axis=0, concat_axis=1, tiled=True)[0]
    square_sum = lax.psum(jnp.sum(owned_slot * owned_slot), "tensor")
    current = owned_slot / (jnp.sqrt(square_sum) + frobenius_eps)
    first_gram = gram_matrix(current)
    for iteration in range(NS_ITERS):
        gram_now = first_gram if iteration == 0 else gram_matrix(current)
        polynomial = coef_second * gram_now + coef_third * jnp.dot(
            gram_now, gram_now, precision=highest
        )
        current = coef_first * current + jnp.dot(polynomial, current, precision=highest)
    group_rank = lax.axis_index("dp") // slot_count
    part_width = slot_width // groups
    col_piece = lax.dynamic_slice_in_dim(current, group_rank * part_width, part_width, 1)
    returned = lax.all_to_all(
        col_piece.reshape(dp_count, rows_local, part_width),
        "dp",
        split_axis=0,
        concat_axis=0,
        tiled=True,
    )
    my_rows = (
        returned.reshape(groups, slot_count, rows_local, part_width)
        .transpose(1, 2, 0, 3)
        .reshape(slot_count, rows_local, slot_width)
    )
    muon_step = muon_rate * match_rms
    qkv_list, proj_list, up_list, down_list = ([], [], [], [])
    for layer_id in range(LAYERS):
        base_slot = 4 * layer_id
        qkv_ortho = my_rows[base_slot, :, : 3 * local_width].reshape(rows_local, 3, local_width)
        proj_ortho = my_rows[base_slot + 1, :, :local_width].T
        up_ortho = my_rows[base_slot + 2]
        down_ortho = my_rows[base_slot + 3].T
        qkv_list.append(
            qkv_weight[layer_id].astype(jnp.float32) - muon_step * math.sqrt(3 * D) * qkv_ortho
        )
        proj_list.append(
            proj_weight[layer_id].astype(jnp.float32) - muon_step * math.sqrt(D) * proj_ortho
        )
        up_list.append(
            up_weight[layer_id].astype(jnp.float32) - muon_step * math.sqrt(FF) * up_ortho
        )
        down_list.append(
            down_weight[layer_id].astype(jnp.float32) - muon_step * math.sqrt(FF) * down_ortho
        )
    qkv_new = jnp.stack(qkv_list)
    proj_new = jnp.stack(proj_list)
    up_new = jnp.stack(up_list)
    down_new = jnp.stack(down_list)
    gains_new = vector_step(norm_gains, gains_grad)
    biases_new = vector_step(biases, biases_grad)
    qkv_bias_new = vector_step(qkv_bias, qkv_bias_grad)
    up_bias_new = vector_step(up_bias, up_bias_grad)
    return (
        stream,
        grad_stream,
        qkv_grad,
        proj_grad,
        up_grad,
        down_grad,
        gains_grad,
        biases_grad,
        qkv_bias_grad,
        up_bias_grad,
        qkv_new,
        proj_new,
        up_new,
        down_new,
        gains_new,
        biases_new,
        qkv_bias_new,
        up_bias_new,
        qkv_state_new,
        proj_state_new,
        up_state_new,
        down_state_new,
    )


def solution(mesh):
    return jax.shard_map(
        local,
        mesh=mesh,
        in_specs=(
            P(("dp", "tensor"), None),
            P(("dp", "tensor"), None),
            P("dp", None),
            P(None, "dp", None, "tensor"),
            P(None, "tensor", "dp"),
            P(None, "dp", "tensor"),
            P(None, "tensor", "dp"),
            P(),
            P(),
            P(),
            P(),
            P(None, "dp", None, "tensor"),
            P(None, "tensor", "dp"),
            P(None, "dp", "tensor"),
            P(None, "tensor", "dp"),
        ),
        out_specs=(
            P(("dp", "tensor"), None),
            P(("dp", "tensor"), None),
            P(None, "dp", None, "tensor"),
            P(None, "tensor", "dp"),
            P(None, "dp", "tensor"),
            P(None, "tensor", "dp"),
            P(),
            P(),
            P(),
            P(),
            P(None, "dp", None, "tensor"),
            P(None, "tensor", "dp"),
            P(None, "dp", "tensor"),
            P(None, "tensor", "dp"),
            P(),
            P(),
            P(),
            P(),
            P(None, "dp", None, "tensor"),
            P(None, "tensor", "dp"),
            P(None, "dp", "tensor"),
            P(None, "tensor", "dp"),
        ),
        check_vma=False,
    )
```

profile of v0, /device:TPU:11, one launch (start us, length us, event | category | flops | bytes accessed | tf_op | source)
XLA Modules:
  0.0 1756.7 jit_solution(11827790502097879945)
XLA Ops:
  17.0 6.5 all_gather.50
  23.5 5.7 all_gather.53
  30.9 20.4 %all-gather.1 = bf16[1,384,768]{1,2,0:T(8,128)(2,1)S(1)} all-gather(bf16[1,384,48]{1,2,0:T(8,128)(2,1)S(1)} %get-tuple-element.122), channel_id=3, replica_groups=mesh['dp'=16,'tensor'=2] {'dp'}, dimensions={2}, use_global_device_ids=true | all-gather | bytes 626688 | tf_op jit(solution)/shard_map/all_gather | solution.py:183
  59.5 38.1 %all-gather.17.cloned.1.call-done = bf16[1,768,1536]{2,1,0:T(8,128)(2,1)} async-done(((bf16[1,48,1536]{2,1,0:T(8,128)(2,1)}), bf16[1,768,1536]{2,1,0:T(8,128)(2,1)}) %all-gather.17.cloned.1.call-update) | async-done | bytes 2359312 | tf_op jit(solution)/shard_map/all_gather | solution.py:184
  97.7 7.3 multiply_convert_fusion.3
  105.0 36.6 %all-gather.19.cloned.1.call-done = bf16[1,1536,768]{1,2,0:T(8,128)(2,1)} async-done(((bf16[1,1536,48]{1,2,0:T(8,128)(2,1)}), bf16[1,1536,768]{1,2,0:T(8,128)(2,1)}) %all-gather.19.cloned.1.call-update) | async-done | bytes 2359312 | tf_op jit(solution)/shard_map/all_gather | solution.py:185
  147.6 7.5 all_gather.62
  155.1 22.3 %all-gather.5 = bf16[1,384,768]{1,2,0:T(8,128)(2,1)S(1)} all-gather(bf16[1,384,48]{1,2,0:T(8,128)(2,1)S(1)} %copy-done.73), channel_id=7, replica_groups=mesh['dp'=16,'tensor'=2] {'dp'}, dimensions={2}, use_global_device_ids=true | all-gather | bytes 626688 | tf_op jit(solution)/shard_map/all_gather | solution.py:183
  182.8 7.7 all_gather.56
  190.5 16.1 all-gather.21.cloned.1.call-done
  206.6 3.2 fusion.57
  209.8 2.8 copy.89
  215.2 7.2 all_gather.59
  223.1 27.4 %all-gather.23.cloned.1.call-done = bf16[1,768,1536]{2,1,0:T(8,128)(2,1)} async-done(((bf16[1,48,1536]{2,1,0:T(8,128)(2,1)}), bf16[1,768,1536]{2,1,0:T(8,128)(2,1)}) %all-gather.23.cloned.1.call-update) | async-done | bytes 2359312 | tf_op jit(solution)/shard_map/all_gather | solution.py:184
  250.5 6.9 multiply_convert_fusion.2
  257.4 37.0 %all-gather.25.cloned.1.call-done = bf16[1,1536,768]{1,2,0:T(8,128)(2,1)} async-done(((bf16[1,1536,48]{1,2,0:T(8,128)(2,1)}), bf16[1,1536,768]{1,2,0:T(8,128)(2,1)}) %all-gather.25.cloned.1.call-update) | async-done | bytes 2359312 | tf_op jit(solution)/shard_map/all_gather | solution.py:185
  294.4 4.4 convert_reduce_fusion
  314.3 3.4 fusion.65
  321.4 16.6 reduce-scatter.19.cloned.1.call-done
  341.4 6.3 all_gather.63
  349.3 3.5 fusion.113
  365.4 2.5 fusion.116
  369.2 3.0 fusion.178
  373.6 3.3 convert_reduce_fusion.1
  377.7 3.0 fusion.177
  381.9 3.0 fusion.180
  386.1 2.9 fusion.179
  389.1 8.6 reduce-scatter.33.cloned.1.call-done
  397.7 60.8 %reduce-scatter.31.cloned.1.call-done = f32[384,48]{0,1:T(8,128)} async-done(((f32[384,768]{0,1:T(8,128)}), f32[384,48]{0,1:T(8,128)}) %reduce-scatter.31.cloned.1.call-update) | async-done | bytes 73744 | tf_op jit(solution)/shard_map/reduce_scatter | solution.py:335
  460.8 68.1 %reduce-scatter.29.cloned.1.call-done = f32[48,3,384]{2,0,1:T(8,128)} async-done(((f32[768,3,384]{2,0,1:T(8,128)}), f32[48,3,384]{2,0,1:T(8,128)}) %reduce-scatter.29.cloned.1.call-update) | async-done | bytes 221200 | tf_op jit(solution)/shard_map/reduce_scatter | solution.py:334
  529.0 70.9 %reduce-scatter.27.cloned.1.call-done = f32[48,3,384]{2,0,1:T(8,128)} async-done(((f32[768,3,384]{2,0,1:T(8,128)}), f32[48,3,384]{2,0,1:T(8,128)}) %reduce-scatter.27.cloned.1.call-update) | async-done | bytes 221200 | tf_op jit(solution)/shard_map/reduce_scatter | solution.py:334
  602.5 75.9 %reduce-scatter.37.cloned.1.call-done = f32[48,1536]{1,0:T(8,128)} async-done(((f32[768,1536]{1,0:T(8,128)}), f32[48,1536]{1,0:T(8,128)}) %reduce-scatter.37.cloned.1.call-update) | async-done | bytes 294928 | tf_op jit(solution)/shard_map/reduce_scatter | solution.py:336
  678.4 78.5 %reduce-scatter.35.cloned.1.call-done = f32[48,1536]{1,0:T(8,128)} async-done(((f32[768,1536]{1,0:T(8,128)}), f32[48,1536]{1,0:T(8,128)}) %reduce-scatter.35.cloned.1.call-update) | async-done | bytes 294928 | tf_op jit(solution)/shard_map/reduce_scatter | solution.py:336
  759.0 76.4 %reduce-scatter.41.cloned.1.call-done = f32[1536,48]{0,1:T(8,128)} async-done(((f32[1536,768]{0,1:T(8,128)}), f32[1536,48]{0,1:T(8,128)}) %reduce-scatter.41.cloned.1.call-update) | async-done | bytes 294928 | tf_op jit(solution)/shard_map/reduce_scatter | solution.py:337
  835.5 78.6 %reduce-scatter.39.cloned.1.call-done = f32[1536,48]{0,1:T(8,128)} async-done(((f32[1536,768]{0,1:T(8,128)}), f32[1536,48]{0,1:T(8,128)}) %reduce-scatter.39.cloned.1.call-update) | async-done | bytes 294928 | tf_op jit(solution)/shard_map/reduce_scatter | solution.py:337
  917.6 110.1 %all_to_all.14 = f32[16,48,1536]{2,1,0:T(8,128)S(1)} all-to-all(f32[16,48,1536]{2,1,0:T(8,128)S(1)} %bitcast.318), channel_id=1, replica_groups=mesh['dp'=16,'tensor'=2] {'dp'}, dimensions={0} | all-to-all | bytes 9437184 | tf_op jit(solution)/shard_map/all_to_all | solution.py:371
  1031.8 4.6 psum.74
  1037.0 2.8 broadcast_divide_fusion
  1042.0 13.3 fusion.181
  1055.4 69.6 %all-reduce.12.cloned.1.call-done = f32[768,768]{1,0:T(8,128)} async-done(((f32[768,768]{1,0:T(8,128)}), f32[768,768]{1,0:T(8,128)}) %all-reduce.12.cloned.1.call-update) | async-done | bytes 2359312 | tf_op jit(solution)/shard_map/psum | solution.py:145
  1125.0 8.4 fusion.182
  1133.4 11.7 multiply_add_fusion.3
  1147.3 13.3 fusion.183
  1160.7 68.8 %all-reduce.14.cloned.1.call-done = f32[768,768]{1,0:T(8,128)} async-done(((f32[768,768]{1,0:T(8,128)}), f32[768,768]{1,0:T(8,128)}) %all-reduce.14.cloned.1.call-update) | async-done | bytes 2359312 | tf_op jit(solution)/shard_map/psum | solution.py:145
  1229.5 8.4 fusion.184
  1237.9 11.7 multiply_add_fusion.2
  1251.8 13.3 fusion.185
  1265.2 68.8 %all-reduce.16.cloned.1.call-done = f32[768,768]{1,0:T(8,128)} async-done(((f32[768,768]{1,0:T(8,128)}), f32[768,768]{1,0:T(8,128)}) %all-reduce.16.cloned.1.call-update) | async-done | bytes 2359312 | tf_op jit(solution)/shard_map/psum | solution.py:145
  1334.0 8.4 fusion.186
  1342.4 11.7 multiply_add_fusion.1
  1356.3 13.3 fusion.187
  1369.7 68.8 %all-reduce.18.cloned.1.call-done = f32[768,768]{1,0:T(8,128)} async-done(((f32[768,768]{1,0:T(8,128)}), f32[768,768]{1,0:T(8,128)}) %all-reduce.18.cloned.1.call-update) | async-done | bytes 2359312 | tf_op jit(solution)/shard_map/psum | solution.py:145
  1438.5 8.4 fusion.188
  1446.8 11.7 multiply_add_fusion
  1460.7 13.1 fusion.189
  1479.0 4.0 fusion.11
  1484.9 3.1 fusion.62
  1488.1 54.6 %all-reduce.20.cloned.1.call-done = f32[768,768]{1,0:T(8,128)} async-done(((f32[768,768]{1,0:T(8,128)}), f32[768,768]{1,0:T(8,128)}) %all-reduce.20.cloned.1.call-update) | async-done | bytes 2359312 | tf_op jit(solution)/shard_map/psum | solution.py:145
  1542.7 8.4 fusion.190
  1551.1 14.0 fusion.14
  1567.2 6.6 all-to-all-start.1
  1574.4 7.7 reduce-scatter.25.cloned.1.call-done
  1582.2 19.8 %reduce-scatter.23.cloned.1.call-done = f32[128,768]{1,0:T(8,128)} async-done(((f32[256,768]{1,0:T(8,128)}), f32[128,768]{1,0:T(8,128)}) %reduce-scatter.23.cloned.1.call-update) | async-done | bytes 393232 | tf_op jit(solution)/shard_map/reduce_scatter | solution.py:307
  1607.8 124.8 %all-reduce.22.cloned.1.call-done = (f32[2,2,768]{2,1,0:T(2,128)}, f32[2,4,768]{2,1,0:T(4,128)}, f32[2,3,768]{2,0,1:T(2,128)}, f32[2,3072]{1,0:T(2,128)}) async-done(((f32[2,2,768]{2,1,0:T(2,128)}, f32[2,4,768]{2,1,0:T(4,128)}, f32[2,3,768]{2,0,1:T(2,128)}, f32[2,3072]{1,0:T(2,128)}), (f32[2,2,768]{2,1,0:T(2,128)}, f32[2,4,768]{2,1,0:T(4,128)}, f32[2,3,768]{2,0,1:T(2,128)}, ...) | async-done | bytes 79888 | tf_op jit(solution)/shard_map/psum | solution.py:339
  (530 shorter events, 133.5 us)
Async XLA Ops:
  7.3 46.1 %all-gather.15.cloned.1.call-start = ((), (), s32[]{:S(2)}) async-start(), calls=%async_computation.35 | async-start | bytes 1880064 | tf_op jit(solution)/shard_map/all_gather | solution.py:182
  9.0 88.6 %all-gather.17.cloned.1.call-start = ((), (), s32[]{:S(2)}) async-start(), calls=%async_computation.36 | async-start | bytes 2506752 | tf_op jit(solution)/shard_map/all_gather | solution.py:184
  10.8 19.5 %copy-start.67 = (bf16[2,384,48]{1,2,0:T(8,128)(2,1)S(1)}, bf16[2,384,48]{1,2,0:T(8,128)(2,1)}, u32[]{:S(2)}) copy-start(bf16[2,384,48]{1,2,0:T(8,128)(2,1)} %param.19) | copy-start | bytes 221188
  10.8 130.7 %all-gather.19.cloned.1.call-start = ((), (), s32[]{:S(2)}) async-start(), calls=%async_computation.37 | async-start | bytes 2506752 | tf_op jit(solution)/shard_map/all_gather | solution.py:185
  12.6 166.6 %reduce-scatter.15.cloned.1.call-start = ((), (), s32[]{:S(2)}) async-start(), calls=%async_computation.16 | async-start | bytes 1179648 | tf_op jit(solution)/shard_map/reduce_scatter | solution.py:217
  14.3 39.0 %copy-start.103 = (f32[768]{0:T(1024)}, f32[768]{0:T(1024)S(1)}, u32[]{:S(2)}) copy-start(f32[768]{0:T(1024)S(1)} %get-tuple-element.43) | copy-start | bytes 9220
  14.3 39.0 %copy-start.105 = (f32[768]{0:T(1024)}, f32[768]{0:T(1024)S(1)}, u32[]{:S(2)}) copy-start(f32[768]{0:T(1024)S(1)} %get-tuple-element.44) | copy-start | bytes 9220
  23.5 32.0 %copy-start.42 = (bf16[256,768]{1,0:T(8,128)(2,1)}, bf16[256,768]{1,0:T(8,128)(2,1)S(1)}, u32[]{:S(2)}) copy-start(bf16[256,768]{1,0:T(8,128)(2,1)S(1)} %all_gather.50) | copy-start | bytes 1179652
  51.3 92.8 %copy-start.13 = (bf16[1,384,768]{1,2,0:T(8,128)(2,1)}, bf16[1,384,768]{1,2,0:T(8,128)(2,1)S(1)}, u32[]{:S(2)}) copy-start(bf16[1,384,768]{1,2,0:T(8,128)(2,1)S(1)} %all-gather.1) | copy-start | bytes 1769476
  105.0 39.1 %copy-start.24 = (bf16[256,1536]{1,0:T(8,128)(2,1)}, bf16[256,1536]{1,0:T(8,128)(2,1)S(1)}, u32[]{:S(2)}) copy-start(bf16[256,1536]{1,0:T(8,128)(2,1)S(1)} %get-tuple-element.66) | copy-start | bytes 2359300
  145.5 61.1 %all-gather.21.cloned.1.call-start = ((), (), s32[]{:S(2)}) async-start(), calls=%async_computation.38 | async-start | bytes 1880064 | tf_op jit(solution)/shard_map/all_gather | solution.py:182
  146.1 32.5 %copy-start.117 = (f32[1,3072]{1,0:T(1,128)S(1)}, f32[1,3072]{1,0:T(1,128)}, u32[]{:S(2)}) copy-start(f32[1,3072]{1,0:T(1,128)} %get-tuple-element.123) | copy-start | bytes 36868
  146.1 33.1 %copy-start.78 = (f32[768]{0:T(1024)S(1)}, f32[768]{0:T(1024)}, u32[]{:S(2)}) copy-start(f32[768]{0:T(1024)} %get-tuple-element.37) | copy-start | bytes 9220
  146.1 33.1 %copy-start.80 = (f32[768]{0:T(1024)S(1)}, f32[768]{0:T(1024)}, u32[]{:S(2)}) copy-start(f32[768]{0:T(1024)} %get-tuple-element.38) | copy-start | bytes 9220
  146.1 104.4 %all-gather.23.cloned.1.call-start = ((), (), s32[]{:S(2)}) async-start(), calls=%async_computation.39 | async-start | bytes 2506752 | tf_op jit(solution)/shard_map/all_gather | solution.py:184
  146.7 147.7 %all-gather.25.cloned.1.call-start = ((), (), s32[]{:S(2)}) async-start(), calls=%async_computation.40 | async-start | bytes 2506752 | tf_op jit(solution)/shard_map/all_gather | solution.py:185
  147.5 173.9 %reduce-scatter.21.cloned.1.call-start = ((), (), s32[]{:S(2)}) async-start(), calls=%async_computation.19 | async-start | bytes 1179648 | tf_op jit(solution)/shard_map/reduce_scatter | solution.py:308
  155.1 26.5 %copy-start.107 = (f32[768]{0:T(1024)S(1)}, f32[768]{0:T(1024)}, u32[]{:S(2)}) copy-start(f32[768]{0:T(1024)} %get-tuple-element.42) | copy-start | bytes 9220
  155.1 26.6 %copy-start.122 = (f32[768]{0:T(1024)S(1)}, f32[768]{0:T(1024)}, u32[]{:S(2)}) copy-start(f32[768]{0:T(1024)} %get-tuple-element.36) | copy-start | bytes 9220
  182.8 32.4 %copy-start.9 = (f32[128,768]{1,0:T(8,128)}, f32[128,768]{1,0:T(8,128)S(1)}, u32[]{:S(2)}) copy-start(f32[128,768]{1,0:T(8,128)S(1)} %get-tuple-element.63) | copy-start | bytes 1179652
  190.5 19.3 %copy-start.44 = (bf16[256,768]{1,0:T(8,128)(2,1)}, bf16[256,768]{1,0:T(8,128)(2,1)S(1)}, u32[]{:S(2)}) copy-start(bf16[256,768]{1,0:T(8,128)(2,1)S(1)} %all_gather.56) | copy-start | bytes 1179652
  222.4 35.0 %copy-start.27 = (bf16[256,768]{1,0:T(8,128)(2,1)}, bf16[256,768]{1,0:T(8,128)(2,1)S(1)}, u32[]{:S(2)}) copy-start(bf16[256,768]{1,0:T(8,128)(2,1)S(1)} %all_gather.59) | copy-start | bytes 1179652
  300.7 37.2 %reduce-scatter.19.cloned.1.call-start = ((), (), s32[]{:S(2)}) async-start(), calls=%async_computation.18 | async-start | bytes 1179648 | tf_op jit(solution)/shard_map/reduce_scatter | solution.py:307
  317.7 80.0 %reduce-scatter.33.cloned.1.call-start = ((), (), s32[]{:S(2)}) async-start(), calls=%async_computation.25 | async-start | bytes 1253376 | tf_op jit(solution)/shard_map/reduce_scatter | solution.py:335
  319.2 18.8 %copy-start.10 = (f32[128,768]{1,0:T(8,128)S(1)}, f32[128,768]{1,0:T(8,128)}, u32[]{:S(2)}) copy-start(f32[128,768]{1,0:T(8,128)} %copy-done.9) | copy-start | bytes 1179652
  319.2 18.7 %copy-start.108 = (f32[768]{0:T(1024)S(1)}, f32[768]{0:T(1024)}, u32[]{:S(2)}) copy-start(f32[768]{0:T(1024)} %get-tuple-element.42) | copy-start | bytes 9220
  319.2 18.7 %copy-start.110 = (f32[768]{0:T(1024)S(1)}, f32[768]{0:T(1024)}, u32[]{:S(2)}) copy-start(f32[768]{0:T(1024)} %get-tuple-element.45) | copy-start | bytes 9220
  321.3 137.2 %reduce-scatter.31.cloned.1.call-start = ((), (), s32[]{:S(2)}) async-start(), calls=%async_computation.24 | async-start | bytes 1253376 | tf_op jit(solution)/shard_map/reduce_scatter | solution.py:335
  349.2 179.8 %reduce-scatter.29.cloned.1.call-start = ((), (), s32[]{:S(2)}) async-start(), calls=%async_computation.23 | async-start | bytes 3760128 | tf_op jit(solution)/shard_map/reduce_scatter | solution.py:334
  352.8 247.0 %reduce-scatter.27.cloned.1.call-start = ((), (), s32[]{:S(2)}) async-start(), calls=%async_computation.22 | async-start | bytes 3760128 | tf_op jit(solution)/shard_map/reduce_scatter | solution.py:334
  367.9 310.4 %reduce-scatter.37.cloned.1.call-start = ((), (), s32[]{:S(2)}) async-start(), calls=%async_computation.27 | async-start | bytes 5013504 | tf_op jit(solution)/shard_map/reduce_scatter | solution.py:336
  372.2 384.7 %reduce-scatter.35.cloned.1.call-start = ((), (), s32[]{:S(2)}) async-start(), calls=%async_computation.26 | async-start | bytes 5013504 | tf_op jit(solution)/shard_map/reduce_scatter | solution.py:336
  380.8 454.6 %reduce-scatter.41.cloned.1.call-start = ((), (), s32[]{:S(2)}) async-start(), calls=%async_computation.29 | async-start | bytes 5013504 | tf_op jit(solution)/shard_map/reduce_scatter | solution.py:337
  384.9 529.1 %reduce-scatter.39.cloned.1.call-start = ((), (), s32[]{:S(2)}) async-start(), calls=%async_computation.28 | async-start | bytes 5013504 | tf_op jit(solution)/shard_map/reduce_scatter | solution.py:337
  389.0 69.5 %copy-start.74 = (f32[2,384,48]{1,2,0:T(8,128)S(1)}, f32[2,384,48]{1,2,0:T(8,128)}, u32[]{:S(2)}) copy-start(f32[2,384,48]{1,2,0:T(8,128)} %param.27) | copy-start | bytes 442372
  389.0 210.9 %copy-start.66 = (f32[2,48,3,384]{3,1,2,0:T(8,128)S(1)}, f32[2,48,3,384]{3,1,2,0:T(8,128)}, u32[]{:S(2)}) copy-start(f32[2,48,3,384]{3,1,2,0:T(8,128)} %param.26) | copy-start | bytes 1327108
  389.0 736.0 %all-reduce.12.cloned.1.call-start = ((), (), s32[]{:S(2)}) async-start(), calls=%async_computation.30 | async-start | bytes 4718592 | tf_op jit(solution)/shard_map/psum | solution.py:145
  460.1 141.8 %copy-start.59 = (f32[2,384,48]{1,2,0:T(8,128)}, f32[2,384,48]{1,2,0:T(8,128)S(1)}, u32[]{:S(2)}) copy-start(f32[2,384,48]{1,2,0:T(8,128)S(1)} %get-tuple-element.172) | copy-start | bytes 442372
  759.0 157.3 %copy-start.20 = (f32[2,48,1536]{2,1,0:T(8,128)}, f32[2,48,1536]{2,1,0:T(8,128)S(1)}, u32[]{:S(2)}) copy-start(f32[2,48,1536]{2,1,0:T(8,128)S(1)} %get-tuple-element.173) | copy-start | bytes 1769476
  1055.4 174.1 %all-reduce.14.cloned.1.call-start = ((), (), s32[]{:S(2)}) async-start(), calls=%async_computation.31 | async-start | bytes 4718592 | tf_op jit(solution)/shard_map/psum | solution.py:145
  1160.7 173.3 %all-reduce.16.cloned.1.call-start = ((), (), s32[]{:S(2)}) async-start(), calls=%async_computation.32 | async-start | bytes 4718592 | tf_op jit(solution)/shard_map/psum | solution.py:145
  1265.2 173.3 %all-reduce.18.cloned.1.call-start = ((), (), s32[]{:S(2)}) async-start(), calls=%async_computation.33 | async-start | bytes 4718592 | tf_op jit(solution)/shard_map/psum | solution.py:145
  1369.6 173.1 %all-reduce.20.cloned.1.call-start = ((), (), s32[]{:S(2)}) async-start(), calls=%async_computation.34 | async-start | bytes 4718592 | tf_op jit(solution)/shard_map/psum | solution.py:145
  1473.9 100.5 %reduce-scatter.17.cloned.1.call-start = ((), (), s32[]{:S(2)}) async-start(), calls=%async_computation.17 | async-start | bytes 1179648 | tf_op jit(solution)/shard_map/reduce_scatter | solution.py:217
  1479.0 103.2 %reduce-scatter.25.cloned.1.call-start = ((), (), s32[]{:S(2)}) async-start(), calls=%async_computation.21 | async-start | bytes 1179648 | tf_op jit(solution)/shard_map/reduce_scatter | solution.py:308
  1483.0 118.9 %reduce-scatter.23.cloned.1.call-start = ((), (), s32[]{:S(2)}) async-start(), calls=%async_computation.20 | async-start | bytes 1179648 | tf_op jit(solution)/shard_map/reduce_scatter | solution.py:307
  1542.7 22.4 %slice-start = ((s8[4718592]{0:T(1024)(128)(4,1)}), s8[4194304]{0:T(1024)(128)(4,1)S(1)}, s32[]{:S(2)}) async-start(s8[4718592]{0:T(1024)(128)(4,1)} %bitcast.336), calls=%async_computation.42 | async-start | bytes 8388608
  1567.1 34.9 %copy-start.2 = (bf16[128,768]{1,0:T(8,128)(2,1)S(1)}, bf16[128,768]{1,0:T(8,128)(2,1)}, u32[]{:S(2)}) copy-start(bf16[128,768]{1,0:T(8,128)(2,1)} %param.15) | copy-start | bytes 589828
  1567.1 34.9 %copy-start.8 = (f32[128,768]{1,0:T(8,128)S(1)}, f32[128,768]{1,0:T(8,128)}, u32[]{:S(2)}) copy-start(f32[128,768]{1,0:T(8,128)} %reduce-scatter.15.cloned.1.call-done) | copy-start | bytes 1179652
  1567.1 34.9 %copy-start.79 = (f32[768]{0:T(1024)S(1)}, f32[768]{0:T(1024)}, u32[]{:S(2)}) copy-start(f32[768]{0:T(1024)} %get-tuple-element.37) | copy-start | bytes 9220
  1567.1 34.9 %copy-start.81 = (f32[768]{0:T(1024)S(1)}, f32[768]{0:T(1024)}, u32[]{:S(2)}) copy-start(f32[768]{0:T(1024)} %get-tuple-element.38) | copy-start | bytes 9220
  1567.1 34.9 %copy-start.104 = (f32[768]{0:T(1024)S(1)}, f32[768]{0:T(1024)}, u32[]{:S(2)}) copy-start(f32[768]{0:T(1024)} %copy-done.103) | copy-start | bytes 9220
  1567.1 34.9 %copy-start.106 = (f32[768]{0:T(1024)S(1)}, f32[768]{0:T(1024)}, u32[]{:S(2)}) copy-start(f32[768]{0:T(1024)} %copy-done.105) | copy-start | bytes 9220
  1567.1 34.9 %copy-start.119 = (f32[768]{0:T(1024)S(1)}, f32[768]{0:T(1024)}, u32[]{:S(2)}) copy-start(f32[768]{0:T(1024)} %get-tuple-element.34) | copy-start | bytes 9220
  1567.1 34.9 %copy-start.120 = (f32[768]{0:T(1024)S(1)}, f32[768]{0:T(1024)}, u32[]{:S(2)}) copy-start(f32[768]{0:T(1024)} %get-tuple-element.41) | copy-start | bytes 9220
  1567.2 34.9 %copy-start.131 = (f32[128]{0:T(128)S(1)}, f32[128]{0:T(128)}, u32[]{:S(2)}) copy-start(f32[128]{0:T(128)} %copy-done.130) | copy-start | bytes 1540
  1567.2 34.9 %copy-start.134 = (f32[128]{0:T(128)S(1)}, f32[128]{0:T(128)}, u32[]{:S(2)}) copy-start(f32[128]{0:T(128)} %copy-done.133) | copy-start | bytes 1540
  1567.2 174.4 %all-to-all-start.1 = ((f32[16,48,768]{2,1,0:T(8,128)}), f32[16,48,768]{2,1,0:T(8,128)S(1)}, u32[]{:S(2)}, u32[]{:S(2)}) async-start(f32[16,48,768]{2,1,0:T(8,128)} %bitcast.321), calls=%async_computation.15 | async-start | bytes 4718592 | tf_op jit(solution)/shard_map/all_to_all | solution.py:384
  1573.7 32.1 %copy-start.19 = (f32[128,768]{1,0:T(8,128)S(1)}, f32[128,768]{1,0:T(8,128)}, u32[]{:S(2)}) copy-start(f32[128,768]{1,0:T(8,128)} %copy-done.18) | copy-start | bytes 1179652
  1573.7 158.8 %all-reduce.22.cloned.1.call-start = ((), (), s32[]{:S(2)}) async-start(), calls=%async_computation.41 | async-start | bytes 159744 | tf_op jit(solution)/shard_map/psum | solution.py:339
  1602.0 133.9 %copy-start.102 = (f32[2,2,768]{2,1,0:T(2,128)S(1)}, f32[2,2,768]{2,1,0:T(2,128)}, u32[]{:S(2)}) copy-start(f32[2,2,768]{2,1,0:T(2,128)} %param.22) | copy-start | bytes 36868
  1602.0 135.3 %copy-start.99 = (f32[2,3,768]{2,0,1:T(2,128)S(1)}, f32[2,3,768]{2,0,1:T(2,128)}, u32[]{:S(2)}) copy-start(f32[2,3,768]{2,0,1:T(2,128)} %param.24) | copy-start | bytes 55300
  1602.1 136.7 %copy-start.83 = (f32[2,4,768]{2,1,0:T(4,128)S(1)}, f32[2,4,768]{2,1,0:T(4,128)}, u32[]{:S(2)}) copy-start(f32[2,4,768]{2,1,0:T(4,128)} %param.23) | copy-start | bytes 73732
  1604.5 135.7 %copy-start.85 = (f32[2,3072]{1,0:T(2,128)S(1)}, f32[2,3072]{1,0:T(2,128)}, u32[]{:S(2)}) copy-start(f32[2,3072]{1,0:T(2,128)} %param.25) | copy-start | bytes 73732
  (109 other events, 363.3 us)
Sparse Core Ops, SparseCore 0:
  11.0 42.3 all-gather.14
  56.2 41.4 all-gather.16
  100.5 41.0 all-gather.18
  145.6 18.9 reduce-scatter.14
  167.3 39.2 all-gather.20
  209.3 41.1 all-gather.22
  253.4 41.0 all-gather.24
  300.8 17.2 reduce-scatter.20
  320.4 17.5 reduce-scatter.18
  341.4 56.2 reduce-scatter.32
  401.3 57.1 reduce-scatter.30
  462.3 66.6 reduce-scatter.28
  532.8 66.9 reduce-scatter.26
  603.6 74.7 reduce-scatter.36
  682.1 74.7 reduce-scatter.34
  760.6 74.8 reduce-scatter.40
  839.2 74.8 reduce-scatter.38
  1055.5 69.4 all-reduce.11
  1160.8 68.6 all-reduce.13
  1265.3 68.6 all-reduce.15
  1369.7 68.6 all-reduce.17
  1474.0 68.6 all-reduce.19
  1545.0 17.4 reduce-scatter.16
  1564.6 17.4 reduce-scatter.24
  1584.4 17.4 reduce-scatter.22
  1609.1 123.4 all-reduce.21
where the time goes:
time: 1770 us; the launch traced here: 1760 us
  waiting for transfers between devices  1180 us (67%)
  matrix products  250 us (14%)
  blocking collectives  198 us (11%)
  local copies, waits for them, and re-layouts  57.7 us (3%)
  other arithmetic  48.2 us (3%)
    psum x5, waiting for transfers between devices, gram_matrix(): return lax.psum(jnp.dot(matrix, matrix.T, precision=highest), 'tensor')  331 us
    reduce_scatter x2, waiting for transfers between devices, local(): lax.psum_scatter(down_part, 'dp', scatter_dimension=1, tiled=True)  155 us
    reduce_scatter x2, waiting for transfers between devices, local(): lax.psum_scatter(up_part, 'dp', scatter_dimension=0, tiled=True)  154 us
    reduce_scatter x2, waiting for transfers between devices, local(): lax.psum_scatter(qkv_part, 'dp', scatter_dimension=0, tiled=True)  139 us
    psum x1, waiting for transfers between devices, local(): lax.psum((jnp.stack(gains_list), jnp.stack(biases_list), jnp.stack(qkv_bi...  125 us
    all_to_all x1, blocking collectives, local(): lax.all_to_all(outgoing, 'dp', split_axis=0, concat_axis=1, tiled=True)[0]  110 us
    all_gather x2, waiting for transfers between devices, local(): lax.all_gather(down_weight[layer_id], 'dp', axis=1, tiled=True)  73.6 us
    reduce_scatter x2, waiting for transfers between devices, local(): lax.psum_scatter(proj_part, 'dp', scatter_dimension=1, tiled=True)  69.4 us
  transfers between devices with their start and end apart: 27, of which 23 were waited for; matrix products, arithmetic and copies ran while one was open for 9% of the time, Pallas kernels for 0%

commit v1 on v0

--- a/solution.py
+++ b/solution.py
@@ -14,6 +14,7 @@
 
 
 highest = lax.Precision.HIGHEST
+ns_precision = lax.Precision.HIGH
 norm_eps = 1e-05
 masked_score = -1e30
 coef_first = 3.4445
@@ -137,12 +138,8 @@
     return (query_grads, key_grad, value_grad)
 
 
-def pad_columns(matrix, slot_width):
-    return jnp.pad(matrix, ((0, 0), (0, slot_width - matrix.shape[1])))
-
-
-def gram_matrix(matrix):
-    return lax.psum(jnp.dot(matrix, matrix.T, precision=highest), "tensor")
+def dp_scatter(partial, dimension):
+    return lax.psum_scatter(partial, "dp", scatter_dimension=dimension, tiled=True)
 
 
 def vector_step(params, gradients):
@@ -331,10 +328,10 @@
         product_mean = jnp.mean(normed_grad * normed, axis=-1, keepdims=True)
         grad_stream = grad_stream + inverse * (normed_grad - normed_mean - normed * product_mean)
         weight_list[layer_id] = (
-            lax.psum_scatter(qkv_part, "dp", scatter_dimension=0, tiled=True),
-            lax.psum_scatter(proj_part, "dp", scatter_dimension=1, tiled=True),
-            lax.psum_scatter(up_part, "dp", scatter_dimension=0, tiled=True),
-            lax.psum_scatter(down_part, "dp", scatter_dimension=1, tiled=True),
+            dp_scatter(qkv_part, 0),
+            dp_scatter(proj_part, 1),
+            dp_scatter(up_part, 0),
+            dp_scatter(down_part, 1),
         )
     gains_grad, biases_grad, qkv_bias_grad, up_bias_grad = lax.psum(
         (
@@ -354,51 +351,68 @@
     up_state_new = momentum * up_state + up_grad
     down_state_new = momentum * down_state + down_grad
     rows_local = qkv_state.shape[1]
-    slot_width = up_state.shape[2]
-    slot_list = []
+    dp_count = lax.axis_size("dp")
+    dp_rank = lax.axis_index("dp")
+    slot_count = 4 * LAYERS
+    sub = dp_count // slot_count
+    piece_width = up_state.shape[2] // sub
+    slot_mats = []
     for layer_id in range(LAYERS):
-        slot_list.append(
-            pad_columns(qkv_state_new[layer_id].reshape(rows_local, 3 * local_width), slot_width)
-        )
-        slot_list.append(pad_columns(proj_state_new[layer_id].T, slot_width))
-        slot_list.append(up_state_new[layer_id])
-        slot_list.append(down_state_new[layer_id].T)
-    stacked = jnp.stack(slot_list)
-    dp_count = lax.axis_size("dp")
-    slot_count = 4 * LAYERS
-    groups = dp_count // slot_count
-    outgoing = jnp.tile(stacked, (groups, 1, 1))
-    owned_slot = lax.all_to_all(outgoing, "dp", split_axis=0, concat_axis=1, tiled=True)[0]
-    square_sum = lax.psum(jnp.sum(owned_slot * owned_slot), "tensor")
-    current = owned_slot / (jnp.sqrt(square_sum) + frobenius_eps)
-    first_gram = gram_matrix(current)
+        slot_mats.append(qkv_state_new[layer_id].reshape(rows_local, 3 * local_width))
+        slot_mats.append(proj_state_new[layer_id].T)
+        slot_mats.append(up_state_new[layer_id])
+        slot_mats.append(down_state_new[layer_id].T)
+    pieces = []
+    for mat in slot_mats:
+        width = mat.shape[1] // sub
+        split = mat.reshape(rows_local, sub, width).transpose(1, 0, 2)
+        pieces.append(jnp.pad(split, ((0, 0), (0, 0), (0, piece_width - width))))
+    outgoing = jnp.concatenate(pieces, axis=0)
+    owned = lax.all_to_all(outgoing, "dp", split_axis=0, concat_axis=0, tiled=True)
+    owned = owned.reshape(dp_count * rows_local, piece_width)
+    gram = jnp.dot(owned, owned.T, precision=ns_precision)
+    bit = 1
+    while bit < sub:
+        pairs = [(i, i ^ bit) for i in range(dp_count)]
+        gram = gram + lax.ppermute(gram, "dp", pairs)
+        bit *= 2
+    gram = gram + lax.ppermute(gram, "tensor", [(0, 1), (1, 0)])
+    norm_sq = jnp.trace(gram)
+    scale = 1.0 / (jnp.sqrt(norm_sq) + frobenius_eps)
+    current_gram = gram * (scale * scale)
+    identity = jnp.eye(current_gram.shape[0], dtype=jnp.float32)
+    accumulated = None
     for iteration in range(NS_ITERS):
-        gram_now = first_gram if iteration == 0 else gram_matrix(current)
-        polynomial = coef_second * gram_now + coef_third * jnp.dot(
-            gram_now, gram_now, precision=highest
-        )
-        current = coef_first * current + jnp.dot(polynomial, current, precision=highest)
-    group_rank = lax.axis_index("dp") // slot_count
-    part_width = slot_width // groups
-    col_piece = lax.dynamic_slice_in_dim(current, group_rank * part_width, part_width, 1)
+        squared = jnp.dot(current_gram, current_gram, precision=ns_precision)
+        polynomial = coef_first * identity + coef_second * current_gram + coef_third * squared
+        if accumulated is None:
+            accumulated = polynomial
+        else:
+            accumulated = jnp.dot(polynomial, accumulated, precision=ns_precision)
+        if iteration + 1 < NS_ITERS:
+            current_gram = jnp.dot(
+                polynomial,
+                jnp.dot(current_gram, polynomial, precision=ns_precision),
+                precision=ns_precision,
+            )
+    current = jnp.dot(accumulated, owned * scale, precision=ns_precision)
     returned = lax.all_to_all(
-        col_piece.reshape(dp_count, rows_local, part_width),
+        current.reshape(dp_count, rows_local, piece_width),
         "dp",
         split_axis=0,
         concat_axis=0,
         tiled=True,
-    )
-    my_rows = (
-        returned.reshape(groups, slot_count, rows_local, part_width)
-        .transpose(1, 2, 0, 3)
-        .reshape(slot_count, rows_local, slot_width)
-    )
+    ).reshape(slot_count, sub, rows_local, piece_width)
+    my_rows = []
+    for slot_id, mat in enumerate(slot_mats):
+        width = mat.shape[1] // sub
+        my_rows.append(returned[slot_id, :, :, :width].transpose(1, 0, 2).reshape(rows_local, sub * width))
     muon_step = muon_rate * match_rms
     qkv_list, proj_list, up_list, down_list = ([], [], [], [])
     for layer_id in range(LAYERS):
         base_slot = 4 * layer_id
-        qkv_ortho = my_rows[base_slot, :, : 3 * local_width].reshape(rows_local, 3, local_width)
-        proj_ortho = my_rows[base_slot + 1, :, :local_width].T
+        qkv_ortho = my_rows[base_slot].reshape(rows_local, 3, local_width)
+        proj_ortho = my_rows[base_slot + 1].T
         up_ortho = my_rows[base_slot + 2]
         down_ortho = my_rows[base_slot + 3].T
         qkv_list.append(

time: 1770 us -> 1340 us (0.76)
  waiting for transfers between devices: 1180 us -> 898 us
  matrix products: 250 us -> 145 us
  blocking collectives: 198 us -> 143 us
    psum x5 -> x0, waiting for transfers between devices: 331 us -> none  [gram_matrix(): return lax.psum(jnp.dot(matrix, matrix.T, precision=highest), 'tensor')]
    dot_general x15 -> x19, matrix products: 169 us -> 68.9 us  [the longest x5 19.8 us: local(): squared = jnp.dot(current_gram, current_gram, precision=ns_precision)]
    ppermute x0 -> x2, waiting for transfers between devices: none -> 65.1 us  [the longest x1 65.1 us: local(): gram = gram + lax.ppermute(gram, 'tensor', [(0, 1), (1, 0)])]
    all_to_all x1, blocking collectives: 110 us -> 59.5 us  [local(): lax.all_to_all(outgoing, 'dp', split_axis=0, concat_axis=0, tiled=True)]
    reduce_scatter x2, waiting for transfers between devices: 36.3 us -> 8.64 us  [local(): lax.psum_scatter(attn_in_grad, 'tensor', scatter_dimension=0, tiled=True)]
  transfers between devices with their start and end apart: 27 -> 24, of which waited for: 23 -> 18; matrix products, arithmetic and copies ran while one was open for 9% -> 16% of each run, Pallas kernels for 0% -> 0%
where the time goes in v1:
time: 1340 us; the launch traced here: 1320 us
  waiting for transfers between devices  898 us (67%)
  matrix products  145 us (11%)
  blocking collectives  143 us (11%)
  local copies, waits for them, and re-layouts  58.9 us (4%)
  other arithmetic  52.3 us (4%)
  between operations  17.4 us (1%)
    reduce_scatter x8, waiting for transfers between devices, dp_scatter(): lax.psum_scatter(partial, 'dp', scatter_dimension=dimension, tiled=True)  516 us
    psum x1, waiting for transfers between devices, local(): lax.psum((jnp.stack(gains_list), jnp.stack(biases_list), jnp.stack(qkv_bi...  142 us
    all_gather x2, waiting for transfers between devices, local(): lax.all_gather(down_weight[layer_id], 'dp', axis=1, tiled=True)  73.2 us
    ppermute x1, waiting for transfers between devices, local(): gram = gram + lax.ppermute(gram, 'tensor', [(0, 1), (1, 0)])  65.1 us
    all_to_all x1, blocking collectives, local(): lax.all_to_all(outgoing, 'dp', split_axis=0, concat_axis=0, tiled=True)  59.5 us
    all_gather x2, waiting for transfers between devices, local(): lax.all_gather(up_weight[layer_id], 'dp', axis=0, tiled=True)  53.7 us
    all_gather x2, blocking collectives, local(): lax.all_gather(proj_weight[layer_id], 'dp', axis=1, tiled=True)  42.4 us
  transfers between devices with their start and end apart: 24, of which 18 were waited for; matrix products, arithmetic and copies ran while one was open for 16% of the time, Pallas kernels for 0%

profile of v1, /device:TPU:11, one launch (start us, length us, event | category | flops | bytes accessed | tf_op | source)
XLA Modules:
  0.0 1323.9 jit_solution(189609780770899119)
XLA Ops:
  17.0 6.5 all_gather.50
  23.5 5.7 all_gather.53
  31.0 20.3 %all-gather.1 = bf16[1,384,768]{1,2,0:T(8,128)(2,1)S(1)} all-gather(bf16[1,384,48]{1,2,0:T(8,128)(2,1)S(1)} %get-tuple-element.130), channel_id=3, replica_groups=mesh['dp'=16,'tensor'=2] {'dp'}, dimensions={2}, use_global_device_ids=true | all-gather | bytes 626688 | tf_op jit(solution)/shard_map/all_gather | solution.py:180
  59.5 38.1 %all-gather.17.cloned.1.call-done = bf16[1,768,1536]{2,1,0:T(8,128)(2,1)} async-done(((bf16[1,48,1536]{2,1,0:T(8,128)(2,1)}), bf16[1,768,1536]{2,1,0:T(8,128)(2,1)}) %all-gather.17.cloned.1.call-update) | async-done | bytes 2359312 | tf_op jit(solution)/shard_map/all_gather | solution.py:181
  97.7 7.2 multiply_convert_fusion.3
  104.9 36.7 %all-gather.19.cloned.1.call-done = bf16[1,1536,768]{1,2,0:T(8,128)(2,1)} async-done(((bf16[1,1536,48]{1,2,0:T(8,128)(2,1)}), bf16[1,1536,768]{1,2,0:T(8,128)(2,1)}) %all-gather.19.cloned.1.call-update) | async-done | bytes 2359312 | tf_op jit(solution)/shard_map/all_gather | solution.py:182
  141.6 2.5 fusion.16
  148.2 8.1 all_gather.62
  156.3 22.1 %all-gather.5 = bf16[1,384,768]{1,2,0:T(8,128)(2,1)S(1)} all-gather(bf16[1,384,48]{1,2,0:T(8,128)(2,1)S(1)} %copy-done.67), channel_id=7, replica_groups=mesh['dp'=16,'tensor'=2] {'dp'}, dimensions={2}, use_global_device_ids=true | all-gather | bytes 626688 | tf_op jit(solution)/shard_map/all_gather | solution.py:180
  184.1 7.4 all_gather.56
  191.5 15.6 %all-gather.21.cloned.1.call-done = bf16[1,768,3,384]{3,1,2,0:T(8,128)(2,1)} async-done(((bf16[1,48,3,384]{3,1,2,0:T(8,128)(2,1)}), bf16[1,768,3,384]{3,1,2,0:T(8,128)(2,1)}) %all-gather.21.cloned.1.call-update) | async-done | bytes 1769488 | tf_op jit(solution)/shard_map/all_gather | solution.py:179
  207.1 3.2 fusion.74
  225.1 6.9 all_gather.59
  232.0 3.3 fusion.82
  235.5 15.6 %all-gather.23.cloned.1.call-done = bf16[1,768,1536]{2,1,0:T(8,128)(2,1)} async-done(((bf16[1,48,1536]{2,1,0:T(8,128)(2,1)}), bf16[1,768,1536]{2,1,0:T(8,128)(2,1)}) %all-gather.23.cloned.1.call-update) | async-done | bytes 2359312 | tf_op jit(solution)/shard_map/all_gather | solution.py:181
  251.0 7.5 multiply_convert_fusion.2
  258.5 36.5 %all-gather.25.cloned.1.call-done = bf16[1,1536,768]{1,2,0:T(8,128)(2,1)} async-done(((bf16[1,1536,48]{1,2,0:T(8,128)(2,1)}), bf16[1,1536,768]{1,2,0:T(8,128)(2,1)}) %all-gather.25.cloned.1.call-update) | async-done | bytes 2359312 | tf_op jit(solution)/shard_map/all_gather | solution.py:182
  295.0 4.5 convert_reduce_fusion
  305.9 8.6 reduce-scatter.19.cloned.1.call-done
  314.5 19.8 %reduce-scatter.21.cloned.1.call-done = f32[128,768]{1,0:T(8,128)} async-done(((f32[256,768]{1,0:T(8,128)}), f32[128,768]{1,0:T(8,128)}) %reduce-scatter.21.cloned.1.call-update) | async-done | bytes 393232 | tf_op jit(solution)/shard_map/reduce_scatter | solution.py:305
  337.1 6.4 all_gather.63
  346.5 2.5 fusion.162
  356.6 2.5 fusion.165
  360.4 3.0 fusion.258
  364.6 3.1 fusion.257
  368.9 3.0 fusion.256
  373.3 3.9 convert_reduce_fusion.1
  378.1 2.9 fusion.255
  381.3 12.8 reduce-scatter.33.cloned.1.call-done
  394.1 60.9 %reduce-scatter.31.cloned.1.call-done = f32[384,48]{0,1:T(8,128)} async-done(((f32[384,768]{0,1:T(8,128)}), f32[384,48]{0,1:T(8,128)}) %reduce-scatter.31.cloned.1.call-update) | async-done | bytes 73744 | tf_op jit(solution)/shard_map/reduce_scatter | solution.py:142
  459.1 66.3 %reduce-scatter.29.cloned.1.call-done = f32[48,3,384]{2,0,1:T(8,128)} async-done(((f32[768,3,384]{2,0,1:T(8,128)}), f32[48,3,384]{2,0,1:T(8,128)}) %reduce-scatter.29.cloned.1.call-update) | async-done | bytes 221200 | tf_op jit(solution)/shard_map/reduce_scatter | solution.py:142
  525.4 70.9 %reduce-scatter.27.cloned.1.call-done = f32[48,3,384]{2,0,1:T(8,128)} async-done(((f32[768,3,384]{2,0,1:T(8,128)}), f32[48,3,384]{2,0,1:T(8,128)}) %reduce-scatter.27.cloned.1.call-update) | async-done | bytes 221200 | tf_op jit(solution)/shard_map/reduce_scatter | solution.py:142
  600.7 74.3 %reduce-scatter.41.cloned.1.call-done = f32[1536,48]{0,1:T(8,128)} async-done(((f32[1536,768]{0,1:T(8,128)}), f32[1536,48]{0,1:T(8,128)}) %reduce-scatter.41.cloned.1.call-update) | async-done | bytes 294928 | tf_op jit(solution)/shard_map/reduce_scatter | solution.py:142
  675.0 78.6 %reduce-scatter.39.cloned.1.call-done = f32[1536,48]{0,1:T(8,128)} async-done(((f32[1536,768]{0,1:T(8,128)}), f32[1536,48]{0,1:T(8,128)}) %reduce-scatter.39.cloned.1.call-update) | async-done | bytes 294928 | tf_op jit(solution)/shard_map/reduce_scatter | solution.py:142
  758.2 73.8 %reduce-scatter.37.cloned.1.call-done = f32[48,1536]{1,0:T(8,128)} async-done(((f32[768,1536]{1,0:T(8,128)}), f32[48,1536]{1,0:T(8,128)}) %reduce-scatter.37.cloned.1.call-update) | async-done | bytes 294928 | tf_op jit(solution)/shard_map/reduce_scatter | solution.py:142
  832.0 78.3 %reduce-scatter.35.cloned.1.call-done = f32[48,1536]{1,0:T(8,128)} async-done(((f32[768,1536]{1,0:T(8,128)}), f32[48,1536]{1,0:T(8,128)}) %reduce-scatter.35.cloned.1.call-update) | async-done | bytes 294928 | tf_op jit(solution)/shard_map/reduce_scatter | solution.py:142
  915.0 6.8 concatenate.54
  923.2 59.5 %all_to_all.10 = f32[16,48,768]{2,1,0:T(8,128)S(1)} all-to-all(f32[16,48,768]{2,1,0:T(8,128)S(1)} %copy.124), channel_id=1, replica_groups=mesh['dp'=16,'tensor'=2] {'dp'}, dimensions={0} | all-to-all | bytes 4718592 | tf_op jit(solution)/shard_map/all_to_all | solution.py:371
  982.7 4.5 fusion.259
  989.7 3.6 fusion.18
  993.7 4.4 add.402
  1008.4 65.1 %collective-permute-done.1 = f32[768,768]{1,0:T(8,128)} collective-permute-done((f32[768,768]{1,0:T(8,128)}, f32[768,768]{1,0:T(8,128)}, u32[]{:S(2)}, u32[]{:S(2)}) %collective-permute-start.1) | collective-permute-done | bytes 2359328 | tf_op jit(solution)/shard_map/ppermute | solution.py:379
  1073.5 4.7 select_reduce_fusion
  1079.0 6.6 fusion
  1085.6 3.2 fusion.23
  1088.7 3.2 fusion.260
  1091.9 3.6 fusion.261
  1095.5 3.3 fusion.41
  1098.8 3.2 fusion.45
  1102.1 3.4 fusion.43
  1105.4 3.3 fusion.262
  1108.8 3.2 fusion.39
  1112.0 3.4 fusion.35
  1115.4 3.6 fusion.37
  1118.9 3.1 fusion.263
  1122.1 3.2 fusion.33
  1125.3 3.3 fusion.29
  1128.7 3.8 fusion.31
  1132.5 3.1 fusion.264
  1135.8 3.4 fusion.5
  1139.2 4.5 fusion.265
  1143.8 6.4 all-to-all-start.1
  1151.2 2.4 fusion.236
  1156.9 141.6 %all-reduce.7.cloned.1.call-done = (f32[2,2,768]{2,1,0:T(2,128)}, f32[2,4,768]{2,1,0:T(4,128)}, f32[2,3,768]{2,0,1:T(2,128)}, f32[2,3072]{1,0:T(2,128)}) async-done(((f32[2,2,768]{2,1,0:T(2,128)}, f32[2,4,768]{2,1,0:T(4,128)}, f32[2,3,768]{2,0,1:T(2,128)}, f32[2,3072]{1,0:T(2,128)}), (f32[2,2,768]{2,1,0:T(2,128)}, f32[2,4,768]{2,1,0:T(4,128)}, f32[2,3,768]{2,0,1:T(2,128)}, ...) | async-done | bytes 79888 | tf_op jit(solution)/shard_map/psum | solution.py:336
  (526 shorter events, 123.7 us)
Async XLA Ops:
  7.2 7.7 copy-start.79
  7.2 8.3 copy-start.77
  7.3 46.1 %all-gather.15.cloned.1.call-start = ((), (), s32[]{:S(2)}) async-start(), calls=%async_computation.30 | async-start | bytes 1880064 | tf_op jit(solution)/shard_map/all_gather | solution.py:179
  9.0 88.6 %all-gather.17.cloned.1.call-start = ((), (), s32[]{:S(2)}) async-start(), calls=%async_computation.31 | async-start | bytes 2506752 | tf_op jit(solution)/shard_map/all_gather | solution.py:181
  10.8 19.5 %copy-start.62 = (bf16[2,384,48]{1,2,0:T(8,128)(2,1)S(1)}, bf16[2,384,48]{1,2,0:T(8,128)(2,1)}, u32[]{:S(2)}) copy-start(bf16[2,384,48]{1,2,0:T(8,128)(2,1)} %param.19) | copy-start | bytes 221188
  10.8 130.8 %all-gather.19.cloned.1.call-start = ((), (), s32[]{:S(2)}) async-start(), calls=%async_computation.32 | async-start | bytes 2506752 | tf_op jit(solution)/shard_map/all_gather | solution.py:182
  12.6 167.2 %reduce-scatter.15.cloned.1.call-start = ((), (), s32[]{:S(2)}) async-start(), calls=%async_computation.16 | async-start | bytes 1179648 | tf_op jit(solution)/shard_map/reduce_scatter | solution.py:214
  23.5 32.0 %copy-start.36 = (bf16[256,768]{1,0:T(8,128)(2,1)}, bf16[256,768]{1,0:T(8,128)(2,1)S(1)}, u32[]{:S(2)}) copy-start(bf16[256,768]{1,0:T(8,128)(2,1)S(1)} %all_gather.50) | copy-start | bytes 1179652
  51.2 92.9 %copy-start.9 = (bf16[1,384,768]{1,2,0:T(8,128)(2,1)}, bf16[1,384,768]{1,2,0:T(8,128)(2,1)S(1)}, u32[]{:S(2)}) copy-start(bf16[1,384,768]{1,2,0:T(8,128)(2,1)S(1)} %all-gather.1) | copy-start | bytes 1769476
  104.9 39.2 %copy-start.15 = (bf16[256,1536]{1,0:T(8,128)(2,1)}, bf16[256,1536]{1,0:T(8,128)(2,1)S(1)}, u32[]{:S(2)}) copy-start(bf16[256,1536]{1,0:T(8,128)(2,1)S(1)} %get-tuple-element.68) | copy-start | bytes 2359300
  144.2 12.1 copy-start.67
  145.6 34.3 %copy-start.73 = (f32[768]{0:T(1024)S(1)}, f32[768]{0:T(1024)}, u32[]{:S(2)}) copy-start(f32[768]{0:T(1024)} %get-tuple-element.37) | copy-start | bytes 9220
  145.6 34.3 %copy-start.75 = (f32[768]{0:T(1024)S(1)}, f32[768]{0:T(1024)}, u32[]{:S(2)}) copy-start(f32[768]{0:T(1024)} %get-tuple-element.38) | copy-start | bytes 9220
  145.6 61.5 %all-gather.21.cloned.1.call-start = ((), (), s32[]{:S(2)}) async-start(), calls=%async_computation.33 | async-start | bytes 1880064 | tf_op jit(solution)/shard_map/all_gather | solution.py:179
  146.2 104.9 %all-gather.23.cloned.1.call-start = ((), (), s32[]{:S(2)}) async-start(), calls=%async_computation.34 | async-start | bytes 2506752 | tf_op jit(solution)/shard_map/all_gather | solution.py:181
  146.7 148.2 %all-gather.25.cloned.1.call-start = ((), (), s32[]{:S(2)}) async-start(), calls=%async_computation.35 | async-start | bytes 2506752 | tf_op jit(solution)/shard_map/all_gather | solution.py:182
  147.5 167.0 %reduce-scatter.19.cloned.1.call-start = ((), (), s32[]{:S(2)}) async-start(), calls=%async_computation.18 | async-start | bytes 1179648 | tf_op jit(solution)/shard_map/reduce_scatter | solution.py:304
  156.3 22.1 %copy-start.2 = (bf16[256,768]{1,0:T(8,128)(2,1)}, bf16[256,768]{1,0:T(8,128)(2,1)S(1)}, u32[]{:S(2)}) copy-start(bf16[256,768]{1,0:T(8,128)(2,1)S(1)} %all_gather.62) | copy-start | bytes 1179652
  156.3 25.9 %copy-start.107 = (f32[768]{0:T(1024)S(1)}, f32[768]{0:T(1024)}, u32[]{:S(2)}) copy-start(f32[768]{0:T(1024)} %get-tuple-element.42) | copy-start | bytes 9220
  156.3 25.9 %copy-start.121 = (f32[768]{0:T(1024)S(1)}, f32[768]{0:T(1024)}, u32[]{:S(2)}) copy-start(f32[768]{0:T(1024)} %get-tuple-element.36) | copy-start | bytes 9220
  179.8 34.1 %copy-start.35 = (bf16[256,384]{0,1:T(8,128)(2,1)}, bf16[256,384]{0,1:T(8,128)(2,1)S(1)}, u32[]{:S(2)}) copy-start(bf16[256,384]{0,1:T(8,128)(2,1)S(1)} %copy.104) | copy-start | bytes 589828
  191.5 15.6 %copy-start.38 = (bf16[256,768]{1,0:T(8,128)(2,1)}, bf16[256,768]{1,0:T(8,128)(2,1)S(1)}, u32[]{:S(2)}) copy-start(bf16[256,768]{1,0:T(8,128)(2,1)S(1)} %all_gather.56) | copy-start | bytes 1179652
  235.4 98.9 %reduce-scatter.21.cloned.1.call-start = ((), (), s32[]{:S(2)}) async-start(), calls=%async_computation.19 | async-start | bytes 1179648 | tf_op jit(solution)/shard_map/reduce_scatter | solution.py:305
  302.2 91.9 %reduce-scatter.33.cloned.1.call-start = ((), (), s32[]{:S(2)}) async-start(), calls=%async_computation.25 | async-start | bytes 1253376 | tf_op jit(solution)/shard_map/reduce_scatter | solution.py:142
  303.7 30.6 %copy-start.6 = (f32[128,768]{1,0:T(8,128)S(1)}, f32[128,768]{1,0:T(8,128)}, u32[]{:S(2)}) copy-start(f32[128,768]{1,0:T(8,128)} %get-tuple-element.65) | copy-start | bytes 1179652
  303.7 30.6 %copy-start.108 = (f32[768]{0:T(1024)S(1)}, f32[768]{0:T(1024)}, u32[]{:S(2)}) copy-start(f32[768]{0:T(1024)} %get-tuple-element.42) | copy-start | bytes 9220
  303.7 30.6 %copy-start.109 = (f32[768]{0:T(1024)S(1)}, f32[768]{0:T(1024)}, u32[]{:S(2)}) copy-start(f32[768]{0:T(1024)} %get-tuple-element.45) | copy-start | bytes 9220
  305.8 30.5 %copy-start.49 = (bf16[128,768]{1,0:T(8,128)(2,1)S(1)}, bf16[128,768]{1,0:T(8,128)(2,1)}, u32[]{:S(2)}) copy-start(bf16[128,768]{1,0:T(8,128)(2,1)} %param.16) | copy-start | bytes 589828
  305.8 30.5 %copy-start.137 = (f32[128]{0:T(128)S(1)}, f32[128]{0:T(128)}, u32[]{:S(2)}) copy-start(f32[128]{0:T(128)} %copy-done.136) | copy-start | bytes 1540
  305.8 149.1 %reduce-scatter.31.cloned.1.call-start = ((), (), s32[]{:S(2)}) async-start(), calls=%async_computation.24 | async-start | bytes 1253376 | tf_op jit(solution)/shard_map/reduce_scatter | solution.py:142
  337.1 9.4 copy-start.21
  337.1 9.4 copy-start.23
  337.1 9.4 copy-start.39
  345.9 179.5 %reduce-scatter.29.cloned.1.call-start = ((), (), s32[]{:S(2)}) async-start(), calls=%async_computation.23 | async-start | bytes 3760128 | tf_op jit(solution)/shard_map/reduce_scatter | solution.py:142
  349.1 247.1 %reduce-scatter.27.cloned.1.call-start = ((), (), s32[]{:S(2)}) async-start(), calls=%async_computation.22 | async-start | bytes 3760128 | tf_op jit(solution)/shard_map/reduce_scatter | solution.py:142
  359.2 315.7 %reduce-scatter.41.cloned.1.call-start = ((), (), s32[]{:S(2)}) async-start(), calls=%async_computation.29 | async-start | bytes 5013504 | tf_op jit(solution)/shard_map/reduce_scatter | solution.py:142
  363.5 390.1 %reduce-scatter.39.cloned.1.call-start = ((), (), s32[]{:S(2)}) async-start(), calls=%async_computation.28 | async-start | bytes 5013504 | tf_op jit(solution)/shard_map/reduce_scatter | solution.py:142
  367.7 464.4 %reduce-scatter.37.cloned.1.call-start = ((), (), s32[]{:S(2)}) async-start(), calls=%async_computation.27 | async-start | bytes 5013504 | tf_op jit(solution)/shard_map/reduce_scatter | solution.py:142
  371.9 538.4 %reduce-scatter.35.cloned.1.call-start = ((), (), s32[]{:S(2)}) async-start(), calls=%async_computation.26 | async-start | bytes 5013504 | tf_op jit(solution)/shard_map/reduce_scatter | solution.py:142
  381.1 73.9 %copy-start.68 = (f32[2,384,48]{1,2,0:T(8,128)S(1)}, f32[2,384,48]{1,2,0:T(8,128)}, u32[]{:S(2)}) copy-start(f32[2,384,48]{1,2,0:T(8,128)} %param.27) | copy-start | bytes 442372
  381.1 215.2 %copy-start.61 = (f32[2,48,3,384]{3,1,2,0:T(8,128)S(1)}, f32[2,48,3,384]{3,1,2,0:T(8,128)}, u32[]{:S(2)}) copy-start(f32[2,48,3,384]{3,1,2,0:T(8,128)} %param.26) | copy-start | bytes 1327108
  381.1 769.9 %reduce-scatter.17.cloned.1.call-start = ((), (), s32[]{:S(2)}) async-start(), calls=%async_computation.17 | async-start | bytes 1179648 | tf_op jit(solution)/shard_map/reduce_scatter | solution.py:214
  598.9 154.7 %copy-start.59 = (f32[2,1536,48]{1,2,0:T(8,128)S(1)}, f32[2,1536,48]{1,2,0:T(8,128)}, u32[]{:S(2)}) copy-start(f32[2,1536,48]{1,2,0:T(8,128)} %param.29) | copy-start | bytes 1769476
  755.5 154.8 %copy-start.60 = (f32[2,48,1536]{2,1,0:T(8,128)S(1)}, f32[2,48,1536]{2,1,0:T(8,128)}, u32[]{:S(2)}) copy-start(f32[2,48,1536]{2,1,0:T(8,128)} %param.28) | copy-start | bytes 1769476
  987.2 6.6 collective-permute-start
  989.6 161.4 %reduce-scatter.25.cloned.1.call-start = ((), (), s32[]{:S(2)}) async-start(), calls=%async_computation.21 | async-start | bytes 1179648 | tf_op jit(solution)/shard_map/reduce_scatter | solution.py:305
  993.3 9.1 copy-start.122
  993.4 157.7 %reduce-scatter.23.cloned.1.call-start = ((), (), s32[]{:S(2)}) async-start(), calls=%async_computation.20 | async-start | bytes 1179648 | tf_op jit(solution)/shard_map/reduce_scatter | solution.py:304
  993.7 7.6 copy-start.124
  993.7 8.2 copy-start.123
  993.7 9.3 copy-start.26
  993.7 9.3 copy-start.29
  993.7 9.3 copy-start.32
  993.7 9.3 copy-start.140
  998.1 75.4 %collective-permute-start.1 = (f32[768,768]{1,0:T(8,128)}, f32[768,768]{1,0:T(8,128)}, u32[]{:S(2)}, u32[]{:S(2)}) collective-permute-start(f32[768,768]{1,0:T(8,128)} %add.402), channel_id=1, source_target_pairs={{0,1},{1,0},{2,3},{3,2},{4,5},{5,4},{6,7},{7,6},{8,9},{9,8},{10,11... | collective-permute-start | bytes 7077896 | tf_op jit(solution)/shard_map/ppermute | solution.py:379
  1143.7 7.3 copy-start.106
  1143.7 7.3 copy-start.119
  1143.8 7.3 copy-start.120
  1143.8 163.6 %all-to-all-start.1 = ((f32[16,48,768]{2,1,0:T(8,128)}), f32[16,48,768]{2,1,0:T(8,128)S(1)}, u32[]{:S(2)}, u32[]{:S(2)}) async-start(f32[16,48,768]{2,1,0:T(8,128)} %fusion.265), calls=%async_computation.15 | async-start | bytes 4718592 | tf_op jit(solution)/shard_map/all_to_all | solution.py:399
  1150.2 148.3 %all-reduce.7.cloned.1.call-start = ((), (), s32[]{:S(2)}) async-start(), calls=%async_computation.36 | async-start | bytes 159744 | tf_op jit(solution)/shard_map/psum | solution.py:336
  1151.1 150.7 %copy-start.102 = (f32[2,2,768]{2,1,0:T(2,128)S(1)}, f32[2,2,768]{2,1,0:T(2,128)}, u32[]{:S(2)}) copy-start(f32[2,2,768]{2,1,0:T(2,128)} %param.22) | copy-start | bytes 36868
  1151.1 152.1 %copy-start.98 = (f32[2,3,768]{2,0,1:T(2,128)S(1)}, f32[2,3,768]{2,0,1:T(2,128)}, u32[]{:S(2)}) copy-start(f32[2,3,768]{2,0,1:T(2,128)} %param.24) | copy-start | bytes 55300
  1151.1 153.5 %copy-start.78 = (f32[2,4,768]{2,1,0:T(4,128)S(1)}, f32[2,4,768]{2,1,0:T(4,128)}, u32[]{:S(2)}) copy-start(f32[2,4,768]{2,1,0:T(4,128)} %param.23) | copy-start | bytes 73732
  1151.1 154.9 %copy-start.80 = (f32[2,3072]{1,0:T(2,128)S(1)}, f32[2,3072]{1,0:T(2,128)}, u32[]{:S(2)}) copy-start(f32[2,3072]{1,0:T(2,128)} %param.25) | copy-start | bytes 73732
  (102 other events, 261.7 us)
Sparse Core Ops, SparseCore 0:
  11.0 42.3 all-gather.14
  56.2 41.4 all-gather.16
  100.5 41.0 all-gather.18
  145.7 19.4 reduce-scatter.14
  168.0 39.1 all-gather.20
  209.8 41.1 all-gather.22
  253.9 41.0 all-gather.24
  297.2 17.2 reduce-scatter.18
  316.8 17.4 reduce-scatter.20
  337.8 56.2 reduce-scatter.32
  397.7 57.1 reduce-scatter.30
  458.7 66.6 reduce-scatter.28
  529.3 66.9 reduce-scatter.26
  600.0 74.9 reduce-scatter.40
  678.7 74.8 reduce-scatter.38
  757.3 74.7 reduce-scatter.36
  835.7 74.5 reduce-scatter.34
  989.8 21.5 reduce-scatter.16
  1013.5 27.6 reduce-scatter.24
  1043.4 26.0 reduce-scatter.22
  1158.3 140.0 all-reduce.6

commit v2 on v1

--- a/solution.py
+++ b/solution.py
@@ -140,6 +140,40 @@
 
 def dp_scatter(partial, dimension):
     return lax.psum_scatter(partial, "dp", scatter_dimension=dimension, tiled=True)
+
+
+def dp_gather(block, axis):
+    return lax.all_gather(block, "dp", axis=axis, tiled=True)
+
+
+def a2a_gather(block, axis):
+    count = lax.axis_size("dp")
+    copies = jnp.broadcast_to(block[None], (count,) + block.shape)
+    got = lax.all_to_all(copies, "dp", split_axis=0, concat_axis=0, tiled=True)
+    got = jnp.moveaxis(got, 0, axis)
+    return got.reshape(block.shape[:axis] + (count * block.shape[axis],) + block.shape[axis + 1 :])
+
+
+def a2a_scatter(partial, dimension):
+    count = lax.axis_size("dp")
+    shape = partial.shape
+    chunks = partial.reshape(shape[:dimension] + (count, shape[dimension] // count) + shape[dimension + 1 :])
+    chunks = jnp.moveaxis(chunks, dimension, 0)
+    got = lax.all_to_all(chunks, "dp", split_axis=0, concat_axis=0, tiled=True)
+    return jnp.sum(got, axis=0)
+
+
+def swap_pairs(count, bit):
+    return [(i, i ^ bit) for i in range(count)]
+
+
+def butterfly_sum(flat):
+    count = lax.axis_size("dp")
+    bit = 1
+    while bit < count:
+        flat = flat + lax.ppermute(flat, "dp", swap_pairs(count, bit))
+        bit *= 2
+    return flat + lax.ppermute(flat, "tensor", [(0, 1), (1, 0)])
 
 
 def vector_step(params, gradients):
@@ -176,10 +210,10 @@
     saved_layers = []
     for layer_id in range(LAYERS):
         layer_weights = (
-            lax.all_gather(qkv_weight[layer_id], "dp", axis=0, tiled=True),
-            lax.all_gather(proj_weight[layer_id], "dp", axis=1, tiled=True),
-            lax.all_gather(up_weight[layer_id], "dp", axis=0, tiled=True),
-            lax.all_gather(down_weight[layer_id], "dp", axis=1, tiled=True),
+            a2a_gather(qkv_weight[layer_id], 0),
+            a2a_gather(proj_weight[layer_id], 1),
+            dp_gather(up_weight[layer_id], 0),
+            dp_gather(down_weight[layer_id], 1),
         )
         qkv_full, proj_full, up_full, down_full = layer_weights
         normed, inverse = normalize(stream)
@@ -250,12 +284,6 @@
             act_low,
             layer_weights,
         ) = saved_layers[layer_id]
-        layer_weights = (
-            lax.all_gather(qkv_weight[layer_id], "dp", axis=0, tiled=True),
-            lax.all_gather(proj_weight[layer_id], "dp", axis=1, tiled=True),
-            lax.all_gather(up_weight[layer_id], "dp", axis=0, tiled=True),
-            lax.all_gather(down_weight[layer_id], "dp", axis=1, tiled=True),
-        )
         qkv_full, proj_full, up_full, down_full = layer_weights
         length = attn_in.shape[0]
         out_bias_grad = jnp.sum(grad_stream, axis=0)
@@ -328,20 +356,24 @@
         product_mean = jnp.mean(normed_grad * normed, axis=-1, keepdims=True)
         grad_stream = grad_stream + inverse * (normed_grad - normed_mean - normed * product_mean)
         weight_list[layer_id] = (
-            dp_scatter(qkv_part, 0),
-            dp_scatter(proj_part, 1),
+            a2a_scatter(qkv_part, 0),
+            a2a_scatter(proj_part, 1),
             dp_scatter(up_part, 0),
             dp_scatter(down_part, 1),
         )
-    gains_grad, biases_grad, qkv_bias_grad, up_bias_grad = lax.psum(
-        (
-            jnp.stack(gains_list),
-            jnp.stack(biases_list),
-            jnp.stack(qkv_bias_list),
-            jnp.stack(up_bias_list),
-        ),
-        ("dp", "tensor"),
-    )
+    small_parts = (
+        jnp.stack(gains_list),
+        jnp.stack(biases_list),
+        jnp.stack(qkv_bias_list),
+        jnp.stack(up_bias_list),
+    )
+    flat = butterfly_sum(jnp.concatenate([part.reshape(-1) for part in small_parts]))
+    small_sums = []
+    offset = 0
+    for part in small_parts:
+        small_sums.append(flat[offset : offset + part.size].reshape(part.shape))
+        offset += part.size
+    gains_grad, biases_grad, qkv_bias_grad, up_bias_grad = small_sums
     qkv_grad = jnp.stack([weight_list[layer_id][0] for layer_id in range(LAYERS)])
     proj_grad = jnp.stack([weight_list[layer_id][1] for layer_id in range(LAYERS)])
     up_grad = jnp.stack([weight_list[layer_id][2] for layer_id in range(LAYERS)])
@@ -373,10 +405,18 @@
     gram = jnp.dot(owned, owned.T, precision=ns_precision)
     bit = 1
     while bit < sub:
-        pairs = [(i, i ^ bit) for i in range(dp_count)]
-        gram = gram + lax.ppermute(gram, "dp", pairs)
+        gram = gram + lax.ppermute(gram, "dp", swap_pairs(dp_count, bit))
         bit *= 2
-    gram = gram + lax.ppermute(gram, "tensor", [(0, 1), (1, 0)])
+    core_half = dp_rank % 2
+    half_rows = gram.shape[0] // 2
+    mine = lax.dynamic_slice_in_dim(gram, core_half * half_rows, half_rows, 0)
+    mine = mine + lax.ppermute(mine, "tensor", [(0, 1), (1, 0)])
+    other = lax.ppermute(mine, "dp", swap_pairs(dp_count, 1))
+    gram = jnp.where(
+        core_half == 0,
+        jnp.concatenate([mine, other], axis=0),
+        jnp.concatenate([other, mine], axis=0),
+    )
     norm_sq = jnp.trace(gram)
     scale = 1.0 / (jnp.sqrt(norm_sq) + frobenius_eps)
     current_gram = gram * (scale * scale)

time: 1340 us -> 1010 us (0.75)
  waiting for transfers between devices: 898 us -> 597 us
  blocking collectives: 143 us -> 39.9 us
  starting transfers between devices: 9.62 us -> 62.2 us
  local copies, waits for them, and re-layouts: 58.9 us -> 79.1 us
    reduce_scatter x8 -> x4, waiting for transfers between devices: 516 us -> 69.1 us  [dp_scatter(): lax.psum_scatter(partial, 'dp', scatter_dimension=dimension, tiled=True)]
    all_to_all x0 -> x9, waiting for transfers between devices: none -> 388 us  [the longest x4 251 us: a2a_scatter(): got = lax.all_to_all(chunks, 'dp', split_axis=0, concat_axis=0, tiled=True)]
    psum x1 -> x0, waiting for transfers between devices: 142 us -> none  [local(): lax.psum((jnp.stack(gains_list), jnp.stack(biases_list), jnp.stack(qkv_bi...]
    all_gather x6 -> x4, waiting for transfers between devices: 145 us -> 25.3 us  [dp_gather(): return lax.all_gather(block, 'dp', axis=axis, tiled=True)]
    all_to_all x1 -> x0, blocking collectives: 59.5 us -> none  [local(): lax.all_to_all(outgoing, 'dp', split_axis=0, concat_axis=0, tiled=True)]
    all_to_all x0 -> x9, starting transfers between devices: none -> 50.2 us  [the longest x4 21.9 us: a2a_scatter(): got = lax.all_to_all(chunks, 'dp', split_axis=0, concat_axis=0, tiled=True)]
    all_gather x2 -> x0, blocking collectives: 42.4 us -> none  [local(): lax.all_gather(proj_weight[layer_id], 'dp', axis=1, tiled=True)]
    ppermute x2 -> x8, waiting for transfers between devices: 65.1 us -> 93.7 us  [the longest x4 51.6 us: butterfly_sum(): flat = flat + lax.ppermute(flat, 'dp', swap_pairs(count, bit))]
  transfers between devices with their start and end apart: 24 -> 32, of which waited for: 18 -> 18; matrix products, arithmetic and copies ran while one was open for 16% -> 17% of each run, Pallas kernels for 0% -> 0%
where the time goes in v2:
time: 1010 us; the launch traced here: 998 us
  waiting for transfers between devices  597 us (59%)
  matrix products  152 us (15%)
  local copies, waits for them, and re-layouts  79.1 us (8%)
  starting transfers between devices  62.2 us (6%)
  other arithmetic  50.3 us (5%)
  blocking collectives  39.9 us (4%)
  between operations  17.2 us (2%)
    all_to_all x4, waiting for transfers between devices, a2a_scatter(): got = lax.all_to_all(chunks, 'dp', split_axis=0, concat_axis=0, tiled=True)  251 us
    all_to_all x4, waiting for transfers between devices, a2a_gather(): got = lax.all_to_all(copies, 'dp', split_axis=0, concat_axis=0, tiled=True)  89 us
    reduce_scatter x4, waiting for transfers between devices, dp_scatter(): lax.psum_scatter(partial, 'dp', scatter_dimension=dimension, tiled=True)  69.1 us
    ppermute x4, waiting for transfers between devices, butterfly_sum(): flat = flat + lax.ppermute(flat, 'dp', swap_pairs(count, bit))  51.6 us
    all_to_all x1, waiting for transfers between devices, local(): lax.all_to_all(outgoing, 'dp', split_axis=0, concat_axis=0, tiled=True)  48.8 us
    ppermute x1, waiting for transfers between devices, local(): mine = mine + lax.ppermute(mine, 'tensor', [(0, 1), (1, 0)])  37.8 us
    all_gather x4, waiting for transfers between devices, dp_gather(): return lax.all_gather(block, 'dp', axis=axis, tiled=True)  25.3 us
    dot_general x5, matrix products, local(): squared = jnp.dot(current_gram, current_gram, precision=ns_precision)  22.4 us
  transfers between devices with their start and end apart: 32, of which 18 were waited for; matrix products, arithmetic and copies ran while one was open for 17% of the time, Pallas kernels for 0%

profile of v2, /device:TPU:11, one launch (start us, length us, event | category | flops | bytes accessed | tf_op | source)
XLA Modules:
  0.0 997.7 jit_solution(1273829635157876620)
XLA Ops:
  12.8 6.7 all-to-all-start
  25.2 6.7 all_gather.30
  32.0 6.0 all_gather.31
  39.6 34.4 %all-to-all-done = bf16[16,48,3,384]{3,1,2,0:T(8,128)(2,1)S(1)} async-done(((bf16[16,48,3,384]{3,1,2,0:T(8,128)(2,1)}), bf16[16,48,3,384]{3,1,2,0:T(8,128)(2,1)S(1)}, u32[]{:S(2)}, u32[]{:S(2)}) %all-to-all-start) | async-done | bytes 1769504 | tf_op jit(solution)/shard_map/all_to_all | solution.py:152
  74.9 4.8 all-to-all-start.1
  85.8 6.8 multiply_convert_fusion.3
  92.6 25.2 %all-gather.11.cloned.1.call-done = bf16[1,1536,768]{1,2,0:T(8,128)(2,1)} async-done(((bf16[1,1536,48]{1,2,0:T(8,128)(2,1)}), bf16[1,1536,768]{1,2,0:T(8,128)(2,1)}) %all-gather.11.cloned.1.call-update) | async-done | bytes 2359312 | tf_op jit(solution)/shard_map/all_gather | solution.py:146
  124.2 5.4 all-to-all-start.3
  129.7 15.0 %all-to-all-done.3 = bf16[16,384,48]{1,2,0:T(8,128)(2,1)S(1)} async-done(((bf16[16,384,48]{1,2,0:T(8,128)(2,1)}), bf16[16,384,48]{1,2,0:T(8,128)(2,1)S(1)}, u32[]{:S(2)}, u32[]{:S(2)}) %all-to-all-start.3) | async-done | bytes 589856 | tf_op jit(solution)/shard_map/all_to_all | solution.py:152
  146.1 4.8 all-to-all-start.2
  154.1 7.0 all_gather.38
  165.8 39.7 %all-to-all-done.2 = bf16[16,48,3,384]{3,1,2,0:T(8,128)(2,1)S(1)} async-done(((bf16[16,48,3,384]{3,1,2,0:T(8,128)(2,1)}), bf16[16,48,3,384]{3,1,2,0:T(8,128)(2,1)S(1)}, u32[]{:S(2)}, u32[]{:S(2)}) %all-to-all-start.2) | async-done | bytes 1769504 | tf_op jit(solution)/shard_map/all_to_all | solution.py:152
  210.6 7.2 all_gather.34
  237.7 6.2 all_gather.35
  243.9 3.4 convolution_bitcast_fusion.3
  247.4 7.5 multiply_convert_fusion.2
  254.9 4.4 convert_reduce_fusion
  262.1 4.1 fusion.234
  266.3 19.4 %reduce-scatter.17.cloned.1.call-done = f32[128,768]{1,0:T(8,128)} async-done(((f32[256,768]{1,0:T(8,128)}), f32[128,768]{1,0:T(8,128)}) %reduce-scatter.17.cloned.1.call-update) | async-done | bytes 393232 | tf_op jit(solution)/shard_map/reduce_scatter | solution.py:333
  290.3 6.8 all_gather.39
  297.9 3.0 fusion.233
  305.4 7.4 all-to-all-start.7
  315.3 44.2 %all-to-all-done.7 = f32[16,384,48]{1,2,0:T(8,128)S(1)} async-done(((f32[16,384,48]{1,2,0:T(8,128)}), f32[16,384,48]{1,2,0:T(8,128)S(1)}, u32[]{:S(2)}, u32[]{:S(2)}) %all-to-all-start.7) | async-done | bytes 1179680 | tf_op jit(solution)/shard_map/all_to_all | solution.py:162
  359.5 4.7 all-to-all-start.6
  366.2 3.5 fusion.117
  369.6 31.1 %all-to-all-done.6 = f32[16,384,48]{1,2,0:T(8,128)} async-done(((f32[16,384,48]{1,2,0:T(8,128)}), f32[16,384,48]{1,2,0:T(8,128)}, u32[]{:S(2)}, u32[]{:S(2)}) %all-to-all-start.6) | async-done | bytes 1179680 | tf_op jit(solution)/shard_map/all_to_all | solution.py:162
  400.8 5.0 all-to-all-start.5
  405.9 3.0 fusion.232
  419.0 93.7 %all-to-all-done.5 = f32[16,48,3,384]{3,1,2,0:T(8,128)} async-done(((f32[16,48,3,384]{3,1,2,0:T(8,128)}), f32[16,48,3,384]{3,1,2,0:T(8,128)}, u32[]{:S(2)}, u32[]{:S(2)}) %all-to-all-start.5) | async-done | bytes 3538976 | tf_op jit(solution)/shard_map/all_to_all | solution.py:162
  512.7 4.8 all-to-all-start.4
  517.7 4.5 convert_reduce_fusion.1
  523.0 2.9 fusion.231
  539.7 2.9 reduce_sum.329
  542.6 81.6 %all-to-all-done.4 = f32[16,48,3,384]{3,1,2,0:T(8,128)S(1)} async-done(((f32[16,48,3,384]{3,1,2,0:T(8,128)}), f32[16,48,3,384]{3,1,2,0:T(8,128)S(1)}, u32[]{:S(2)}, u32[]{:S(2)}) %all-to-all-start.4) | async-done | bytes 3538976 | tf_op jit(solution)/shard_map/all_to_all | solution.py:162
  632.8 69.0 %reduce-scatter.23.cloned.1.call-done = f32[48,1536]{1,0:T(8,128)} async-done(((f32[768,1536]{1,0:T(8,128)}), f32[48,1536]{1,0:T(8,128)}) %reduce-scatter.23.cloned.1.call-update) | async-done | bytes 294928 | tf_op jit(solution)/shard_map/reduce_scatter | solution.py:142
  706.5 7.1 concatenate.64
  716.3 6.6 all-to-all-start.8
  727.2 48.8 %all-to-all-done.8 = f32[16,48,768]{2,1,0:T(8,128)S(1)} async-done(((f32[16,48,768]{2,1,0:T(8,128)}), f32[16,48,768]{2,1,0:T(8,128)S(1)}, u32[]{:S(2)}, u32[]{:S(2)}) %all-to-all-start.8) | async-done | bytes 2359328 | tf_op jit(solution)/shard_map/all_to_all | solution.py:403
  776.0 4.4 fusion.235
  785.3 2.8 dynamic-slice_add_fusion
  791.3 37.8 %collective-permute-done.6 = f32[384,768]{1,0:T(8,128)} collective-permute-done((f32[384,768]{1,0:T(8,128)}, f32[384,768]{1,0:T(8,128)}, u32[]{:S(2)}, u32[]{:S(2)}) %collective-permute-start.6) | collective-permute-done | bytes 1179680 | tf_op jit(solution)/shard_map/ppermute | solution.py:413
  840.0 3.1 select_reduce_fusion
  843.9 9.4 fusion
  853.3 5.6 fusion.23
  858.9 3.2 fusion.236
  862.1 3.5 fusion.237
  865.7 3.3 fusion.41
  869.0 3.2 fusion.45
  872.3 3.5 fusion.43
  875.8 3.1 fusion.238
  879.0 3.2 fusion.39
  882.2 3.3 fusion.35
  885.6 3.6 fusion.37
  889.1 3.1 fusion.239
  892.3 3.2 fusion.33
  895.5 3.3 fusion.29
  898.9 3.8 fusion.31
  902.6 3.1 fusion.240
  905.8 3.4 fusion.5
  909.4 4.5 fusion.241
  913.9 5.5 all-to-all-start.9
  921.4 10.4 %collective-permute-done.1 = f32[19968]{0:T(1024)S(1)} collective-permute-done((f32[19968]{0:T(1024)S(1)}, f32[19968]{0:T(1024)S(1)}, u32[]{:S(2)}, u32[]{:S(2)}) %collective-permute-start.1) | collective-permute-done | bytes 79904 | tf_op jit(solution)/shard_map/ppermute | solution.py:174
  932.5 28.3 %collective-permute-done.2 = f32[19968]{0:T(1024)S(1)} collective-permute-done((f32[19968]{0:T(1024)S(1)}, f32[19968]{0:T(1024)S(1)}, u32[]{:S(2)}, u32[]{:S(2)}) %collective-permute-start.2) | collective-permute-done | bytes 79904 | tf_op jit(solution)/shard_map/ppermute | solution.py:174
  961.7 11.9 %collective-permute-done.3 = f32[19968]{0:T(1024)S(1)} collective-permute-done((f32[19968]{0:T(1024)S(1)}, f32[19968]{0:T(1024)S(1)}, u32[]{:S(2)}, u32[]{:S(2)}) %collective-permute-start.3) | collective-permute-done | bytes 79904 | tf_op jit(solution)/shard_map/ppermute | solution.py:174
  (564 shorter events, 161.4 us)
Async XLA Ops:
  7.2 78.0 %all-gather.9.cloned.1.call-start = ((), (), s32[]{:S(2)}) async-start(), calls=%async_computation.30 | async-start | bytes 2506752 | tf_op jit(solution)/shard_map/all_gather | solution.py:146
  12.8 61.2 %all-to-all-start = ((bf16[16,48,3,384]{3,1,2,0:T(8,128)(2,1)}), bf16[16,48,3,384]{3,1,2,0:T(8,128)(2,1)S(1)}, u32[]{:S(2)}, u32[]{:S(2)}) async-start(bf16[16,48,3,384]{3,1,2,0:T(8,128)(2,1)} %broadcast_in_dim.44), calls=%async_computation | async-start | bytes 3538944 | tf_op jit(solution)/shard_map/all_to_all | solution.py:152
  19.5 19.5 %copy-start.70 = (bf16[2,384,48]{1,2,0:T(8,128)(2,1)S(1)}, bf16[2,384,48]{1,2,0:T(8,128)(2,1)}, u32[]{:S(2)}) copy-start(bf16[2,384,48]{1,2,0:T(8,128)(2,1)} %param.19) | copy-start | bytes 221188
  19.5 98.3 %all-gather.11.cloned.1.call-start = ((), (), s32[]{:S(2)}) async-start(), calls=%async_computation.31 | async-start | bytes 2506752 | tf_op jit(solution)/shard_map/all_gather | solution.py:146
  32.0 47.9 %copy-start.39 = (bf16[256,768]{1,0:T(8,128)(2,1)}, bf16[256,768]{1,0:T(8,128)(2,1)S(1)}, u32[]{:S(2)}) copy-start(bf16[256,768]{1,0:T(8,128)(2,1)S(1)} %all_gather.30) | copy-start | bytes 1179652
  74.9 45.4 %all-to-all-start.1 = ((bf16[16,384,48]{1,2,0:T(8,128)(2,1)}), bf16[16,384,48]{1,2,0:T(8,128)(2,1)}, u32[]{:S(2)}, u32[]{:S(2)}) async-start(bf16[16,384,48]{1,2,0:T(8,128)(2,1)} %broadcast_in_dim.49), calls=%async_computation.1 | async-start | bytes 1179648 | tf_op jit(solution)/shard_map/all_to_all | solution.py:152
  79.6 127.3 %reduce-scatter.11.cloned.1.call-start = ((), (), s32[]{:S(2)}) async-start(), calls=%async_computation.20 | async-start | bytes 1179648 | tf_op jit(solution)/shard_map/reduce_scatter | solution.py:248
  85.2 35.1 %copy-start.56 = (bf16[6,64,256]{2,1,0:T(8,128)(2,1)}, bf16[6,64,256]{2,1,0:T(8,128)(2,1)S(1)}, u32[]{:S(2)}) copy-start(bf16[6,64,256]{2,1,0:T(8,128)(2,1)S(1)} %convolution_convert_fusion.5) | copy-start | bytes 589828
  92.6 27.7 %copy-start.18 = (bf16[256,1536]{1,0:T(8,128)(2,1)}, bf16[256,1536]{1,0:T(8,128)(2,1)S(1)}, u32[]{:S(2)}) copy-start(bf16[256,1536]{1,0:T(8,128)(2,1)S(1)} %get-tuple-element.106) | copy-start | bytes 2359300
  122.7 124.7 %all-gather.13.cloned.1.call-start = ((), (), s32[]{:S(2)}) async-start(), calls=%async_computation.32 | async-start | bytes 2506752 | tf_op jit(solution)/shard_map/all_gather | solution.py:146
  124.2 20.5 %all-to-all-start.3 = ((bf16[16,384,48]{1,2,0:T(8,128)(2,1)}), bf16[16,384,48]{1,2,0:T(8,128)(2,1)S(1)}, u32[]{:S(2)}, u32[]{:S(2)}) async-start(bf16[16,384,48]{1,2,0:T(8,128)(2,1)} %broadcast_in_dim.53), calls=%async_computation.4 | async-start | bytes 1179648 | tf_op jit(solution)/shard_map/all_to_all | solution.py:152
  146.1 59.4 %all-to-all-start.2 = ((bf16[16,48,3,384]{3,1,2,0:T(8,128)(2,1)}), bf16[16,48,3,384]{3,1,2,0:T(8,128)(2,1)S(1)}, u32[]{:S(2)}, u32[]{:S(2)}) async-start(bf16[16,48,3,384]{3,1,2,0:T(8,128)(2,1)} %broadcast_in_dim.51), calls=%async_computation.3 | async-start | bytes 3538944 | tf_op jit(solution)/shard_map/all_to_all | solution.py:152
  150.9 104.0 %all-gather.15.cloned.1.call-start = ((), (), s32[]{:S(2)}) async-start(), calls=%async_computation.33 | async-start | bytes 2506752 | tf_op jit(solution)/shard_map/all_gather | solution.py:146
  151.5 114.8 %reduce-scatter.15.cloned.1.call-start = ((), (), s32[]{:S(2)}) async-start(), calls=%async_computation.22 | async-start | bytes 1179648 | tf_op jit(solution)/shard_map/reduce_scatter | solution.py:332
  206.9 11.7 %copy-start.134 = (f32[1,3,384]{2,1,0:T(4,128)S(1)}, f32[1,3,384]{2,1,0:T(4,128)}, u32[]{:S(2)}) copy-start(f32[1,3,384]{2,1,0:T(4,128)} %copy.197) | copy-start | bytes 13828
  206.9 11.7 %copy-start.38 = (bf16[16,48,3,384]{3,1,0,2:T(8,128)(2,1)S(1)}, bf16[16,48,3,384]{3,1,0,2:T(8,128)(2,1)}, u32[]{:S(2)}) copy-start(bf16[16,48,3,384]{3,1,0,2:T(8,128)(2,1)} %copy.121) | copy-start | bytes 5308420
  210.6 26.4 %copy-start.7 = (f32[128,768]{1,0:T(8,128)}, f32[128,768]{1,0:T(8,128)S(1)}, u32[]{:S(2)}) copy-start(f32[128,768]{1,0:T(8,128)S(1)} %get-tuple-element.103) | copy-start | bytes 1179652
  247.3 38.3 %reduce-scatter.17.cloned.1.call-start = ((), (), s32[]{:S(2)}) async-start(), calls=%async_computation.23 | async-start | bytes 1179648 | tf_op jit(solution)/shard_map/reduce_scatter | solution.py:333
  262.0 366.9 %reduce-scatter.29.cloned.1.call-start = ((), (), s32[]{:S(2)}) async-start(), calls=%async_computation.29 | async-start | bytes 5013504 | tf_op jit(solution)/shard_map/reduce_scatter | solution.py:142
  266.2 362.7 %reduce-scatter.27.cloned.1.call-start = ((), (), s32[]{:S(2)}) async-start(), calls=%async_computation.28 | async-start | bytes 5013504 | tf_op jit(solution)/shard_map/reduce_scatter | solution.py:142
  285.7 12.2 %copy-start.19 = (bf16[256,1536]{1,0:T(8,128)(2,1)S(1)}, bf16[256,1536]{1,0:T(8,128)(2,1)}, u32[]{:S(2)}) copy-start(bf16[256,1536]{1,0:T(8,128)(2,1)} %copy-done.18) | copy-start | bytes 2359300
  305.4 54.0 %all-to-all-start.7 = ((f32[16,384,48]{1,2,0:T(8,128)}), f32[16,384,48]{1,2,0:T(8,128)S(1)}, u32[]{:S(2)}, u32[]{:S(2)}) async-start(f32[16,384,48]{1,2,0:T(8,128)} %convolution_bitcast_fusion), calls=%async_computation.13 | async-start | bytes 2359296 | tf_op jit(solution)/shard_map/all_to_all | solution.py:162
  315.3 50.8 %copy-start.23 = (bf16[256,1,384]{2,0,1:T(8,128)(2,1)S(1)}, bf16[256,1,384]{2,0,1:T(8,128)(2,1)}, u32[]{:S(2)}) copy-start(bf16[256,1,384]{2,0,1:T(8,128)(2,1)} %copy.130) | copy-start | bytes 589828
  315.3 50.8 %copy-start.25 = (bf16[256,1,384]{2,0,1:T(8,128)(2,1)S(1)}, bf16[256,1,384]{2,0,1:T(8,128)(2,1)}, u32[]{:S(2)}) copy-start(bf16[256,1,384]{2,0,1:T(8,128)(2,1)} %copy.128) | copy-start | bytes 589828
  359.5 41.3 %all-to-all-start.6 = ((f32[16,384,48]{1,2,0:T(8,128)}), f32[16,384,48]{1,2,0:T(8,128)}, u32[]{:S(2)}, u32[]{:S(2)}) async-start(f32[16,384,48]{1,2,0:T(8,128)} %convolution_bitcast_fusion.1), calls=%async_computation.12 | async-start | bytes 2359296 | tf_op jit(solution)/shard_map/all_to_all | solution.py:162
  369.6 36.2 %copy-start.22 = (bf16[256,768]{1,0:T(8,128)(2,1)S(1)}, bf16[256,768]{1,0:T(8,128)(2,1)}, u32[]{:S(2)}) copy-start(bf16[256,768]{1,0:T(8,128)(2,1)} %all_gather.35) | copy-start | bytes 1179652
  400.8 111.9 %all-to-all-start.5 = ((f32[16,48,3,384]{3,1,2,0:T(8,128)}), f32[16,48,3,384]{3,1,2,0:T(8,128)}, u32[]{:S(2)}, u32[]{:S(2)}) async-start(f32[16,48,3,384]{3,1,2,0:T(8,128)} %fusion.117), calls=%async_computation.11 | async-start | bytes 7077888 | tf_op jit(solution)/shard_map/all_to_all | solution.py:162
  405.8 227.0 %reduce-scatter.25.cloned.1.call-start = ((), (), s32[]{:S(2)}) async-start(), calls=%async_computation.27 | async-start | bytes 5013504 | tf_op jit(solution)/shard_map/reduce_scatter | solution.py:142
  512.7 111.5 %all-to-all-start.4 = ((f32[16,48,3,384]{3,1,2,0:T(8,128)}), f32[16,48,3,384]{3,1,2,0:T(8,128)S(1)}, u32[]{:S(2)}, u32[]{:S(2)}) async-start(f32[16,48,3,384]{3,1,2,0:T(8,128)} %fusion.119), calls=%async_computation.10 | async-start | bytes 7077888 | tf_op jit(solution)/shard_map/all_to_all | solution.py:162
  517.4 184.4 %reduce-scatter.23.cloned.1.call-start = ((), (), s32[]{:S(2)}) async-start(), calls=%async_computation.26 | async-start | bytes 5013504 | tf_op jit(solution)/shard_map/reduce_scatter | solution.py:142
  630.9 72.9 %copy-start.16 = (f32[2,1536,48]{1,2,0:T(8,128)}, f32[2,1536,48]{1,2,0:T(8,128)S(1)}, u32[]{:S(2)}) copy-start(f32[2,1536,48]{1,2,0:T(8,128)S(1)} %get-tuple-element.90) | copy-start | bytes 1769476
  630.9 70.9 %copy-start.69 = (f32[2,48,1536]{2,1,0:T(8,128)S(1)}, f32[2,48,1536]{2,1,0:T(8,128)}, u32[]{:S(2)}) copy-start(f32[2,48,1536]{2,1,0:T(8,128)} %param.28) | copy-start | bytes 1769476
  716.3 59.6 %all-to-all-start.8 = ((f32[16,48,768]{2,1,0:T(8,128)}), f32[16,48,768]{2,1,0:T(8,128)S(1)}, u32[]{:S(2)}, u32[]{:S(2)}) async-start(f32[16,48,768]{2,1,0:T(8,128)} %copy.146), calls=%async_computation.18 | async-start | bytes 4718592 | tf_op jit(solution)/shard_map/all_to_all | solution.py:403
  722.9 114.5 %reduce-scatter.13.cloned.1.call-start = ((), (), s32[]{:S(2)}) async-start(), calls=%async_computation.21 | async-start | bytes 1179648 | tf_op jit(solution)/shard_map/reduce_scatter | solution.py:248
  727.1 110.4 %reduce-scatter.21.cloned.1.call-start = ((), (), s32[]{:S(2)}) async-start(), calls=%async_computation.25 | async-start | bytes 1179648 | tf_op jit(solution)/shard_map/reduce_scatter | solution.py:333
  780.4 4.9 collective-permute-start.5
  782.3 55.3 %reduce-scatter.19.cloned.1.call-start = ((), (), s32[]{:S(2)}) async-start(), calls=%async_computation.24 | async-start | bytes 1179648 | tf_op jit(solution)/shard_map/reduce_scatter | solution.py:332
  788.1 41.0 %collective-permute-start.6 = (f32[384,768]{1,0:T(8,128)}, f32[384,768]{1,0:T(8,128)}, u32[]{:S(2)}, u32[]{:S(2)}) collective-permute-start(f32[384,768]{1,0:T(8,128)} %dynamic-slice_add_fusion), channel_id=1, source_target_pairs={{0,1},{1,0},{2,3},{3,2},{4,5},{5,4},{6,7},{7,6},{8,9},{9,8},{10,11... | collective-permute-start | bytes 3538952 | tf_op jit(solution)/shard_map/ppermute | solution.py:413
  791.1 41.9 %copy-start.131 = (f32[1536]{0:T(1024)S(1)}, f32[1536]{0:T(1024)}, u32[]{:S(2)}) copy-start(f32[1536]{0:T(1024)} %get-tuple-element.193) | copy-start | bytes 18436
  791.2 41.9 %copy-start.119 = (f32[768]{0:T(1024)S(1)}, f32[768]{0:T(1024)}, u32[]{:S(2)}) copy-start(f32[768]{0:T(1024)} %get-tuple-element.70) | copy-start | bytes 9220
  791.2 42.5 %copy-start.121 = (f32[768]{0:T(1024)S(1)}, f32[768]{0:T(1024)}, u32[]{:S(2)}) copy-start(f32[768]{0:T(1024)} %get-tuple-element.98) | copy-start | bytes 9220
  791.2 43.1 %copy-start.120 = (f32[768]{0:T(1024)S(1)}, f32[768]{0:T(1024)}, u32[]{:S(2)}) copy-start(f32[768]{0:T(1024)} %get-tuple-element.159) | copy-start | bytes 9220
  791.2 43.7 %copy-start.118 = (f32[768]{0:T(1024)S(1)}, f32[768]{0:T(1024)}, u32[]{:S(2)}) copy-start(f32[768]{0:T(1024)} %get-tuple-element.71) | copy-start | bytes 9220
  791.2 44.2 %copy-start.117 = (f32[768]{0:T(1024)S(1)}, f32[768]{0:T(1024)}, u32[]{:S(2)}) copy-start(f32[768]{0:T(1024)} %get-tuple-element.72) | copy-start | bytes 9220
  791.2 44.8 %copy-start.116 = (f32[768]{0:T(1024)S(1)}, f32[768]{0:T(1024)}, u32[]{:S(2)}) copy-start(f32[768]{0:T(1024)} %get-tuple-element.73) | copy-start | bytes 9220
  791.2 45.4 %copy-start.132 = (f32[1536]{0:T(1024)S(1)}, f32[1536]{0:T(1024)}, u32[]{:S(2)}) copy-start(f32[1536]{0:T(1024)} %get-tuple-element.195) | copy-start | bytes 18436
  791.2 46.3 %copy-start.1 = (bf16[128,768]{1,0:T(8,128)(2,1)S(1)}, bf16[128,768]{1,0:T(8,128)(2,1)}, u32[]{:S(2)}) copy-start(bf16[128,768]{1,0:T(8,128)(2,1)} %param.15) | copy-start | bytes 589828
  791.3 46.3 %copy-start.6 = (f32[128,768]{1,0:T(8,128)S(1)}, f32[128,768]{1,0:T(8,128)}, u32[]{:S(2)}) copy-start(f32[128,768]{1,0:T(8,128)} %reduce-scatter.11.cloned.1.call-done) | copy-start | bytes 1179652
  791.3 46.3 %copy-start.79 = (f32[768]{0:T(1024)S(1)}, f32[768]{0:T(1024)}, u32[]{:S(2)}) copy-start(f32[768]{0:T(1024)} %get-tuple-element.81) | copy-start | bytes 9220
  791.3 46.3 %copy-start.80 = (f32[768]{0:T(1024)S(1)}, f32[768]{0:T(1024)}, u32[]{:S(2)}) copy-start(f32[768]{0:T(1024)} %get-tuple-element.82) | copy-start | bytes 9220
  791.3 46.3 %copy-start.107 = (f32[768]{0:T(1024)S(1)}, f32[768]{0:T(1024)}, u32[]{:S(2)}) copy-start(f32[768]{0:T(1024)} %copy-done.106) | copy-start | bytes 9220
  791.3 46.3 %copy-start.109 = (f32[768]{0:T(1024)S(1)}, f32[768]{0:T(1024)}, u32[]{:S(2)}) copy-start(f32[768]{0:T(1024)} %copy-done.108) | copy-start | bytes 9220
  831.9 8.1 collective-permute-start.7
  913.9 60.6 %copy-start.15 = (f32[128,768]{1,0:T(8,128)S(1)}, f32[128,768]{1,0:T(8,128)}, u32[]{:S(2)}) copy-start(f32[128,768]{1,0:T(8,128)} %copy-done.14) | copy-start | bytes 1179652
  913.9 60.6 %copy-start.130 = (f32[128]{0:T(128)S(1)}, f32[128]{0:T(128)}, u32[]{:S(2)}) copy-start(f32[128]{0:T(128)} %copy-done.129) | copy-start | bytes 1540
  913.9 60.5 %copy-start.136 = (f32[128]{0:T(128)S(1)}, f32[128]{0:T(128)}, u32[]{:S(2)}) copy-start(f32[128]{0:T(128)} %copy-done.135) | copy-start | bytes 1540
  913.9 68.5 %all-to-all-start.9 = ((f32[16,48,768]{2,1,0:T(8,128)}), f32[16,48,768]{2,1,0:T(8,128)S(1)}, u32[]{:S(2)}, u32[]{:S(2)}) async-start(f32[16,48,768]{2,1,0:T(8,128)} %fusion.241), calls=%async_computation.19 | async-start | bytes 4718592 | tf_op jit(solution)/shard_map/all_to_all | solution.py:439
  919.5 61.6 %copy-start.82 = (f32[2,4,768]{2,1,0:T(4,128)S(1)}, f32[2,4,768]{2,1,0:T(4,128)}, u32[]{:S(2)}) copy-start(f32[2,4,768]{2,1,0:T(4,128)} %param.23) | copy-start | bytes 73732
  919.6 62.2 %copy-start.85 = (f32[2,3072]{1,0:T(2,128)S(1)}, f32[2,3072]{1,0:T(2,128)}, u32[]{:S(2)}) copy-start(f32[2,3072]{1,0:T(2,128)} %param.25) | copy-start | bytes 73732
  919.7 1.4 collective-permute-start
  921.1 10.8 %collective-permute-start.1 = (f32[19968]{0:T(1024)S(1)}, f32[19968]{0:T(1024)S(1)}, u32[]{:S(2)}, u32[]{:S(2)}) collective-permute-start(f32[19968]{0:T(1024)S(1)} %add.404), channel_id=1, source_target_pairs={{0,4},{2,6},{4,0},{6,2},{8,12},{10,14},{12,8},{14,10},{16,20},{18,... | collective-permute-start | bytes 239624 | tf_op jit(solution)/shard_map/ppermute | solution.py:174
  931.8 29.0 %collective-permute-start.2 = (f32[19968]{0:T(1024)S(1)}, f32[19968]{0:T(1024)S(1)}, u32[]{:S(2)}, u32[]{:S(2)}) collective-permute-start(f32[19968]{0:T(1024)S(1)} %add.405), channel_id=1, source_target_pairs={{0,8},{2,10},{4,12},{6,14},{8,0},{10,2},{12,4},{14,6},{16,24},{18,... | collective-permute-start | bytes 239624 | tf_op jit(solution)/shard_map/ppermute | solution.py:174
  960.8 12.9 %collective-permute-start.3 = (f32[19968]{0:T(1024)S(1)}, f32[19968]{0:T(1024)S(1)}, u32[]{:S(2)}, u32[]{:S(2)}) collective-permute-start(f32[19968]{0:T(1024)S(1)} %add.406), channel_id=1, source_target_pairs={{0,16},{2,18},{4,20},{6,22},{8,24},{10,26},{12,28},{14,30},{16,0},... | collective-permute-start | bytes 239624 | tf_op jit(solution)/shard_map/ppermute | solution.py:174
  973.7 3.4 collective-permute-start.4
  (108 other events, 321.9 us)
Sparse Core Ops, SparseCore 0:
  10.9 57.8 all-gather.8
  71.6 46.1 all-gather.10
  122.8 17.2 reduce-scatter.10
  142.9 56.0 all-gather.12
  201.7 43.3 all-gather.14
  247.4 18.3 reduce-scatter.14
  268.1 17.4 reduce-scatter.16
  289.5 96.9 reduce-scatter.28
  390.4 118.1 reduce-scatter.26
  512.3 109.1 reduce-scatter.24
  625.4 76.4 reduce-scatter.22
  727.2 17.9 reduce-scatter.12
  782.4 24.3 reduce-scatter.20
  808.8 24.5 reduce-scatter.18

commit v3 on v2

--- a/solution.py
+++ b/solution.py
@@ -174,6 +174,45 @@
         flat = flat + lax.ppermute(flat, "dp", swap_pairs(count, bit))
         bit *= 2
     return flat + lax.ppermute(flat, "tensor", [(0, 1), (1, 0)])
+
+
+def chip_gather(block, gather_axis, split_axis):
+    count = lax.axis_size("dp")
+    parity = lax.axis_index("dp") % 2
+    width = block.shape[split_axis] // 2
+    halves = jnp.stack(
+        [lax.slice_in_dim(block, 0, width, axis=split_axis), lax.slice_in_dim(block, width, 2 * width, axis=split_axis)]
+    )
+    outgoing = jnp.tile(halves, (count // 2,) + (1,) * block.ndim)
+    got = lax.all_to_all(outgoing, "dp", split_axis=0, concat_axis=0, tiled=True)
+    got = jnp.moveaxis(got, 0, gather_axis)
+    shape = got.shape
+    mine = got.reshape(shape[:gather_axis] + (shape[gather_axis] * shape[gather_axis + 1],) + shape[gather_axis + 2 :])
+    theirs = lax.ppermute(mine, "dp", swap_pairs(count, 1))
+    return jnp.where(
+        parity == 0,
+        jnp.concatenate([mine, theirs], axis=split_axis),
+        jnp.concatenate([theirs, mine], axis=split_axis),
+    )
+
+
+def chip_scatter(partial, scatter_axis, split_axis):
+    count = lax.axis_size("dp")
+    parity = lax.axis_index("dp") % 2
+    width = partial.shape[split_axis] // 2
+    keep = lax.dynamic_slice_in_dim(partial, parity * width, width, split_axis)
+    send = lax.dynamic_slice_in_dim(partial, (1 - parity) * width, width, split_axis)
+    chip_sum = keep + lax.ppermute(send, "dp", swap_pairs(count, 1))
+    shape = chip_sum.shape
+    chunks = chip_sum.reshape(
+        shape[:scatter_axis] + (count, shape[scatter_axis] // count) + shape[scatter_axis + 1 :]
+    )
+    chunks = jnp.moveaxis(chunks, scatter_axis, 0)
+    got = lax.all_to_all(chunks, "dp", split_axis=0, concat_axis=0, tiled=True)
+    got = got.reshape((count // 2, 2) + got.shape[1:])
+    even = jnp.sum(got[:, 0], axis=0)
+    odd = jnp.sum(got[:, 1], axis=0)
+    return jnp.concatenate([even, odd], axis=split_axis)
 
 
 def vector_step(params, gradients):
@@ -210,10 +249,10 @@
     saved_layers = []
     for layer_id in range(LAYERS):
         layer_weights = (
-            a2a_gather(qkv_weight[layer_id], 0),
-            a2a_gather(proj_weight[layer_id], 1),
-            dp_gather(up_weight[layer_id], 0),
-            dp_gather(down_weight[layer_id], 1),
+            chip_gather(qkv_weight[layer_id], 0, 2),
+            chip_gather(proj_weight[layer_id], 1, 0),
+            chip_gather(up_weight[layer_id], 0, 1),
+            chip_gather(down_weight[layer_id], 1, 0),
         )
         qkv_full, proj_full, up_full, down_full = layer_weights
         normed, inverse = normalize(stream)
@@ -356,10 +395,10 @@
         product_mean = jnp.mean(normed_grad * normed, axis=-1, keepdims=True)
         grad_stream = grad_stream + inverse * (normed_grad - normed_mean - normed * product_mean)
         weight_list[layer_id] = (
-            a2a_scatter(qkv_part, 0),
-            a2a_scatter(proj_part, 1),
-            dp_scatter(up_part, 0),
-            dp_scatter(down_part, 1),
+            chip_scatter(qkv_part, 0, 2),
+            chip_scatter(proj_part, 1, 0),
+            chip_scatter(up_part, 0, 1),
+            chip_scatter(down_part, 1, 0),
         )
     small_parts = (
         jnp.stack(gains_list),

time: 1010 us -> 1030 us (1.020)
  waiting for transfers between devices: 597 us -> 525 us
  starting transfers between devices: 62.2 us -> 110 us
  other arithmetic: 50.3 us -> 67.5 us
    reduce_scatter x4 -> x0, waiting for transfers between devices: 69.1 us -> none  [dp_scatter(): lax.psum_scatter(partial, 'dp', scatter_dimension=dimension, tiled=True)]
    all_to_all x8 -> x16, starting transfers between devices: 43.6 us -> 81.6 us  [the longest x8 41.1 us: chip_gather(): lax.all_to_all(outgoing, 'dp', split_axis=0, concat_axis=0, tiled=True)]
    all_to_all x8 -> x16, waiting for transfers between devices: 340 us -> 370 us  [the longest x8 251 us: chip_scatter(): got = lax.all_to_all(chunks, 'dp', split_axis=0, concat_axis=0, tiled=True)]
    all_gather x4 -> x0, waiting for transfers between devices: 25.3 us -> none  [dp_gather(): return lax.all_gather(block, 'dp', axis=axis, tiled=True)]
    ppermute x0 -> x16, waiting for transfers between devices: none -> 20.3 us  [the longest x8 20.3 us: chip_scatter(): chip_sum = keep + lax.ppermute(send, 'dp', swap_pairs(count, 1))]
    reduce_scatter x2, waiting for transfers between devices: 19.4 us -> 0.04 us  [local(): lax.psum_scatter(mlp_in_grad, 'tensor', scatter_dimension=0, tiled=True)]
    add x0 -> x8, other arithmetic: none -> 16.3 us  [chip_scatter(): chip_sum = keep + lax.ppermute(send, 'dp', swap_pairs(count, 1))]
    ppermute x0 -> x16, starting transfers between devices: none -> 10.6 us  [the longest x8 5.64 us: chip_scatter(): chip_sum = keep + lax.ppermute(send, 'dp', swap_pairs(count, 1))]
  transfers between devices with their start and end apart: 32 -> 48, of which waited for: 18 -> 30; matrix products, arithmetic and copies ran while one was open for 17% -> 19% of each run, Pallas kernels for 0% -> 0%
where the time goes in v3:
time: 1030 us; the launch traced here: 1010 us
  waiting for transfers between devices  525 us (51%)
  matrix products  160 us (16%)
  starting transfers between devices  110 us (11%)
  local copies, waits for them, and re-layouts  85.9 us (8%)
  other arithmetic  67.5 us (7%)
  blocking collectives  43.9 us (4%)
  between operations  18 us (2%)
    all_to_all x8, waiting for transfers between devices, chip_scatter(): got = lax.all_to_all(chunks, 'dp', split_axis=0, concat_axis=0, tiled=True)  251 us
    all_to_all x8, waiting for transfers between devices, chip_gather(): lax.all_to_all(outgoing, 'dp', split_axis=0, concat_axis=0, tiled=True)  118 us
    ppermute x4, waiting for transfers between devices, butterfly_sum(): flat = flat + lax.ppermute(flat, 'dp', swap_pairs(count, bit))  51.6 us
    all_to_all x1, waiting for transfers between devices, local(): lax.all_to_all(outgoing, 'dp', split_axis=0, concat_axis=0, tiled=True)  46.8 us
    all_to_all x8, starting transfers between devices, chip_gather(): lax.all_to_all(outgoing, 'dp', split_axis=0, concat_axis=0, tiled=True)  41.1 us
    all_to_all x8, starting transfers between devices, chip_scatter(): got = lax.all_to_all(chunks, 'dp', split_axis=0, concat_axis=0, tiled=True)  40.6 us
    ppermute x1, waiting for transfers between devices, local(): mine = mine + lax.ppermute(mine, 'tensor', [(0, 1), (1, 0)])  34.3 us
    dot_general x5, matrix products, local(): squared = jnp.dot(current_gram, current_gram, precision=ns_precision)  22.1 us
  transfers between devices with their start and end apart: 48, of which 30 were waited for; matrix products, arithmetic and copies ran while one was open for 19% of the time, Pallas kernels for 0%

profile of v3, /device:TPU:11, one launch (start us, length us, event | category | flops | bytes accessed | tf_op | source)
XLA Modules:
  0.0 1010.5 jit_solution(3190275466920038746)
XLA Ops:
  8.9 6.5 all-to-all-start.1
  15.4 10.7 %all-to-all-done.1 = bf16[16,192,48]{1,2,0:T(8,128)(2,1)S(1)} async-done(((bf16[16,192,48]{1,2,0:T(8,128)(2,1)}), bf16[16,192,48]{1,2,0:T(8,128)(2,1)S(1)}, u32[]{:S(2)}, u32[]{:S(2)}) %all-to-all-start.1) | async-done | bytes 294944 | tf_op jit(solution)/shard_map/all_to_all | solution.py:187
  27.0 5.5 all-to-all-start.5
  33.5 9.9 all-to-all-done.5
  44.6 5.0 all-to-all-start
  49.7 27.7 %all-to-all-done = bf16[16,48,3,192]{3,1,2,0:T(8,128)(2,1)S(1)} async-done(((bf16[16,48,3,192]{3,1,2,0:T(8,128)(2,1)}), bf16[16,48,3,192]{3,1,2,0:T(8,128)(2,1)S(1)}, u32[]{:S(2)}, u32[]{:S(2)}) %all-to-all-start) | async-done | bytes 884768 | tf_op jit(solution)/shard_map/all_to_all | solution.py:187
  78.5 4.7 all-to-all-start.2
  86.2 24.9 %all-to-all-done.2 = bf16[16,48,768]{2,1,0:T(8,128)(2,1)} async-done(((bf16[16,48,768]{2,1,0:T(8,128)(2,1)}), bf16[16,48,768]{2,1,0:T(8,128)(2,1)}, u32[]{:S(2)}, u32[]{:S(2)}) %all-to-all-start.2) | async-done | bytes 1179680 | tf_op jit(solution)/shard_map/all_to_all | solution.py:187
  112.2 4.7 all-to-all-start.3
  120.7 24.1 %all-to-all-done.3 = bf16[16,768,48]{1,2,0:T(8,128)(2,1)} async-done(((bf16[16,768,48]{1,2,0:T(8,128)(2,1)}), bf16[16,768,48]{1,2,0:T(8,128)(2,1)}, u32[]{:S(2)}, u32[]{:S(2)}) %all-to-all-start.3) | async-done | bytes 1179680 | tf_op jit(solution)/shard_map/all_to_all | solution.py:187
  145.9 4.7 all-to-all-start.4
  150.6 6.7 all_gather.18
  160.9 7.2 all_gather.19
  179.7 5.1 all-to-all-start.6
  187.3 8.2 multiply_convert_fusion.3
  195.4 17.1 %all-to-all-done.6 = bf16[16,48,768]{2,1,0:T(8,128)(2,1)} async-done(((bf16[16,48,768]{2,1,0:T(8,128)(2,1)}), bf16[16,48,768]{2,1,0:T(8,128)(2,1)}, u32[]{:S(2)}, u32[]{:S(2)}) %all-to-all-start.6) | async-done | bytes 1179680 | tf_op jit(solution)/shard_map/all_to_all | solution.py:187
  213.7 4.7 all-to-all-start.7
  229.2 10.3 %all_gather.22 = bf16[256,768]{1,0:T(8,128)(2,1)S(1)} all-gather(bf16[128,768]{1,0:T(8,128)(2,1)S(1)} %copy-done.63), channel_id=1, replica_groups=mesh['dp'=16,'tensor'=2] {'tensor'}, dimensions={0}, use_global_device_ids=true | all-gather | bytes 589824 | tf_op jit(solution)/shard_map/all_gather | solution.py:329
  252.4 6.7 all_gather.20
  266.4 6.3 all_gather.21
  273.4 7.5 multiply_convert_fusion.2
  280.9 4.6 convert_reduce_fusion
  286.5 4.1 fusion.108
  306.0 4.9 convolution_bitcast_fusion.2
  325.1 5.1 all-to-all-start.11
  333.8 6.7 all_gather.23
  349.6 5.5 all-to-all-start.10
  366.1 8.3 all-to-all-done.10
  374.4 5.2 all-to-all-start.9
  390.7 41.9 %all-to-all-done.9 = f32[16,48,3,192]{3,1,2,0:T(8,128)} async-done(((f32[16,48,3,192]{3,1,2,0:T(8,128)}), f32[16,48,3,192]{3,1,2,0:T(8,128)}, u32[]{:S(2)}, u32[]{:S(2)}) %all-to-all-start.9) | async-done | bytes 1769504 | tf_op jit(solution)/shard_map/all_to_all | solution.py:211
  432.6 4.8 all-to-all-start.8
  442.6 4.5 collective-permute-done.15
  447.1 4.1 dynamic-slice_add_fusion
  451.2 39.2 %all-to-all-done.8 = f32[16,48,3,192]{3,1,2,0:T(8,128)S(1)} async-done(((f32[16,48,3,192]{3,1,2,0:T(8,128)}), f32[16,48,3,192]{3,1,2,0:T(8,128)S(1)}, u32[]{:S(2)}, u32[]{:S(2)}) %all-to-all-start.8) | async-done | bytes 1769504 | tf_op jit(solution)/shard_map/all_to_all | solution.py:211
  490.4 4.9 all-to-all-start.15
  497.9 4.2 collective-permute-done.13
  504.0 44.4 %all-to-all-done.15 = f32[16,768,48]{1,2,0:T(8,128)} async-done(((f32[16,768,48]{1,2,0:T(8,128)}), f32[16,768,48]{1,2,0:T(8,128)}, u32[]{:S(2)}, u32[]{:S(2)}) %all-to-all-start.15) | async-done | bytes 2359328 | tf_op jit(solution)/shard_map/all_to_all | solution.py:211
  548.4 4.9 all-to-all-start.13
  556.0 4.2 collective-permute-done.14
  562.1 44.4 %all-to-all-done.13 = f32[16,48,768]{2,1,0:T(8,128)} async-done(((f32[16,48,768]{2,1,0:T(8,128)}), f32[16,48,768]{2,1,0:T(8,128)}, u32[]{:S(2)}, u32[]{:S(2)}) %all-to-all-start.13) | async-done | bytes 2359328 | tf_op jit(solution)/shard_map/all_to_all | solution.py:211
  606.5 4.8 all-to-all-start.14
  611.3 5.5 convert_reduce_fusion.1
  618.3 4.2 collective-permute-done.12
  624.4 40.0 %all-to-all-done.14 = f32[16,768,48]{1,2,0:T(8,128)} async-done(((f32[16,768,48]{1,2,0:T(8,128)}), f32[16,768,48]{1,2,0:T(8,128)}, u32[]{:S(2)}, u32[]{:S(2)}) %all-to-all-start.14) | async-done | bytes 2359328 | tf_op jit(solution)/shard_map/all_to_all | solution.py:211
  664.4 5.5 all-to-all-start.12
  690.3 32.6 %all-to-all-done.12 = f32[16,48,768]{2,1,0:T(8,128)} async-done(((f32[16,48,768]{2,1,0:T(8,128)}), f32[16,48,768]{2,1,0:T(8,128)}, u32[]{:S(2)}, u32[]{:S(2)}) %all-to-all-start.12) | async-done | bytes 2359328 | tf_op jit(solution)/shard_map/all_to_all | solution.py:211
  727.5 6.8 concatenate.160
  737.1 4.9 all-to-all-start.16
  748.2 46.8 %all-to-all-done.16 = f32[16,48,768]{2,1,0:T(8,128)S(1)} async-done(((f32[16,48,768]{2,1,0:T(8,128)}), f32[16,48,768]{2,1,0:T(8,128)S(1)}, u32[]{:S(2)}, u32[]{:S(2)}) %all-to-all-start.16) | async-done | bytes 2359328 | tf_op jit(solution)/shard_map/all_to_all | solution.py:442
  795.0 4.4 fusion.242
  799.5 4.2 fusion.109
  808.5 3.4 convolution_bitcast_fusion.1
  812.2 34.3 %collective-permute-done.22 = f32[384,768]{1,0:T(8,128)} collective-permute-done((f32[384,768]{1,0:T(8,128)}, f32[384,768]{1,0:T(8,128)}, u32[]{:S(2)}, u32[]{:S(2)}) %collective-permute-start.22) | collective-permute-done | bytes 1179680 | tf_op jit(solution)/shard_map/ppermute | solution.py:452
  860.1 9.3 fusion
  869.4 5.6 fusion.9
  875.0 3.4 fusion.243
  888.1 3.8 fusion.29
  914.7 3.6 fusion.21
  921.7 3.4 fusion.5
  925.2 4.8 fusion.248
  930.0 5.3 all-to-all-start.17
  937.4 10.4 %collective-permute-done.17 = f32[19968]{0:T(1024)S(1)} collective-permute-done((f32[19968]{0:T(1024)S(1)}, f32[19968]{0:T(1024)S(1)}, u32[]{:S(2)}, u32[]{:S(2)}) %collective-permute-start.17) | collective-permute-done | bytes 79904 | tf_op jit(solution)/shard_map/ppermute | solution.py:174
  948.4 28.3 %collective-permute-done.18 = f32[19968]{0:T(1024)S(1)} collective-permute-done((f32[19968]{0:T(1024)S(1)}, f32[19968]{0:T(1024)S(1)}, u32[]{:S(2)}, u32[]{:S(2)}) %collective-permute-start.18) | collective-permute-done | bytes 79904 | tf_op jit(solution)/shard_map/ppermute | solution.py:174
  977.7 11.9 %collective-permute-done.19 = f32[19968]{0:T(1024)S(1)} collective-permute-done((f32[19968]{0:T(1024)S(1)}, f32[19968]{0:T(1024)S(1)}, u32[]{:S(2)}, u32[]{:S(2)}) %collective-permute-start.19) | collective-permute-done | bytes 79904 | tf_op jit(solution)/shard_map/ppermute | solution.py:174
  (667 shorter events, 251.3 us)
Async XLA Ops:
  8.9 17.3 %all-to-all-start.1 = ((bf16[16,192,48]{1,2,0:T(8,128)(2,1)}), bf16[16,192,48]{1,2,0:T(8,128)(2,1)S(1)}, u32[]{:S(2)}, u32[]{:S(2)}) async-start(bf16[16,192,48]{1,2,0:T(8,128)(2,1)} %bitcast.15), calls=%async_computation.1 | async-start | bytes 786432 | tf_op jit(solution)/shard_map/all_to_all | solution.py:187
  27.0 16.4 %all-to-all-start.5 = ((bf16[16,192,48]{1,2,0:T(8,128)(2,1)}), bf16[16,192,48]{1,2,0:T(8,128)(2,1)}, u32[]{:S(2)}, u32[]{:S(2)}) async-start(bf16[16,192,48]{1,2,0:T(8,128)(2,1)} %bitcast.40), calls=%async_computation.6 | async-start | bytes 786432 | tf_op jit(solution)/shard_map/all_to_all | solution.py:187
  32.5 52.5 %copy-start.55 = (bf16[1,48,3,384]{3,1,2,0:T(8,128)(2,1)}, bf16[1,48,3,384]{3,1,2,0:T(8,128)(2,1)S(1)}, u32[]{:S(2)}) copy-start(bf16[1,48,3,384]{3,1,2,0:T(8,128)(2,1)S(1)} %get-tuple-element.217) | copy-start | bytes 331780
  44.6 32.8 %all-to-all-start = ((bf16[16,48,3,192]{3,1,2,0:T(8,128)(2,1)}), bf16[16,48,3,192]{3,1,2,0:T(8,128)(2,1)S(1)}, u32[]{:S(2)}, u32[]{:S(2)}) async-start(bf16[16,48,3,192]{3,1,2,0:T(8,128)(2,1)} %bitcast.4), calls=%async_computation | async-start | bytes 2359296 | tf_op jit(solution)/shard_map/all_to_all | solution.py:187
  78.5 32.6 %all-to-all-start.2 = ((bf16[16,48,768]{2,1,0:T(8,128)(2,1)}), bf16[16,48,768]{2,1,0:T(8,128)(2,1)}, u32[]{:S(2)}, u32[]{:S(2)}) async-start(bf16[16,48,768]{2,1,0:T(8,128)(2,1)} %bitcast.22), calls=%async_computation.2 | async-start | bytes 2359296 | tf_op jit(solution)/shard_map/all_to_all | solution.py:187
  112.2 32.6 %all-to-all-start.3 = ((bf16[16,768,48]{1,2,0:T(8,128)(2,1)}), bf16[16,768,48]{1,2,0:T(8,128)(2,1)}, u32[]{:S(2)}, u32[]{:S(2)}) async-start(bf16[16,768,48]{1,2,0:T(8,128)(2,1)} %bitcast.24), calls=%async_computation.3 | async-start | bytes 2359296 | tf_op jit(solution)/shard_map/all_to_all | solution.py:187
  145.9 32.6 %all-to-all-start.4 = ((bf16[16,48,3,192]{3,1,2,0:T(8,128)(2,1)}), bf16[16,48,3,192]{3,1,2,0:T(8,128)(2,1)}, u32[]{:S(2)}, u32[]{:S(2)}) async-start(bf16[16,48,3,192]{3,1,2,0:T(8,128)(2,1)} %bitcast.32), calls=%async_computation.5 | async-start | bytes 2359296 | tf_op jit(solution)/shard_map/all_to_all | solution.py:187
  159.6 11.4 %collective-permute-start = (bf16[768,3,192]{0,2,1:T(8,128)(2,1)}, bf16[768,3,192]{0,2,1:T(8,128)(2,1)S(1)}, u32[]{:S(2)}, u32[]{:S(2)}) collective-permute-start(bf16[768,3,192]{0,2,1:T(8,128)(2,1)} %copy.210), channel_id=1, source_target_pairs={{0,2},{2,0},{4,6},{6,4},{8,10},{10,8},{12,14},{14,12},{16,18},{18,... | collective-permute-start | bytes 2654216 | tf_op jit(solution)/shard_map/ppermute | solution.py:191
  169.8 52.0 %collective-permute-start.1 = (bf16[192,768]{0,1:T(8,128)(2,1)}, bf16[192,768]{0,1:T(8,128)(2,1)}, u32[]{:S(2)}, u32[]{:S(2)}) collective-permute-start(bf16[192,768]{0,1:T(8,128)(2,1)} %bitcast.375), channel_id=1, source_target_pairs={{0,2},{2,0},{4,6},{6,4},{8,10},{10,8},{12,14},{14,12},{16,18},{18,... | collective-permute-start | bytes 884744 | tf_op jit(solution)/shard_map/ppermute | solution.py:191
  170.5 16.6 %collective-permute-start.2 = (bf16[768,768]{1,0:T(8,128)(2,1)}, bf16[768,768]{1,0:T(8,128)(2,1)}, u32[]{:S(2)}, u32[]{:S(2)}) collective-permute-start(bf16[768,768]{1,0:T(8,128)(2,1)} %bitcast.23), channel_id=1, source_target_pairs={{0,2},{2,0},{4,6},{6,4},{8,10},{10,8},{12,14},{14,12},{16,18},{18,... | collective-permute-start | bytes 3538952 | tf_op jit(solution)/shard_map/ppermute | solution.py:191
  170.5 47.9 %collective-permute-start.3 = (bf16[768,768]{0,1:T(8,128)(2,1)}, bf16[768,768]{0,1:T(8,128)(2,1)}, u32[]{:S(2)}, u32[]{:S(2)}) collective-permute-start(bf16[768,768]{0,1:T(8,128)(2,1)} %bitcast.26), channel_id=1, source_target_pairs={{0,2},{2,0},{4,6},{6,4},{8,10},{10,8},{12,14},{14,12},{16,18},{18,... | collective-permute-start | bytes 3538952 | tf_op jit(solution)/shard_map/ppermute | solution.py:191
  179.7 32.8 %all-to-all-start.6 = ((bf16[16,48,768]{2,1,0:T(8,128)(2,1)}), bf16[16,48,768]{2,1,0:T(8,128)(2,1)}, u32[]{:S(2)}, u32[]{:S(2)}) async-start(bf16[16,48,768]{2,1,0:T(8,128)(2,1)} %bitcast.47), calls=%async_computation.7 | async-start | bytes 2359296 | tf_op jit(solution)/shard_map/all_to_all | solution.py:187
  213.7 32.6 %all-to-all-start.7 = ((bf16[16,768,48]{1,2,0:T(8,128)(2,1)}), bf16[16,768,48]{1,2,0:T(8,128)(2,1)}, u32[]{:S(2)}, u32[]{:S(2)}) async-start(bf16[16,768,48]{1,2,0:T(8,128)(2,1)} %bitcast.49), calls=%async_computation.8 | async-start | bytes 2359296 | tf_op jit(solution)/shard_map/all_to_all | solution.py:187
  218.4 30.3 %reduce-scatter.7.cloned.1.call-start = ((), (), s32[]{:S(2)}) async-start(), calls=%async_computation.24 | async-start | bytes 1179648 | tf_op jit(solution)/shard_map/reduce_scatter | solution.py:287
  224.6 105.7 %reduce-scatter.13.cloned.1.call-start = ((), (), s32[]{:S(2)}) async-start(), calls=%async_computation.27 | async-start | bytes 1179648 | tf_op jit(solution)/shard_map/reduce_scatter | solution.py:372
  227.5 18.9 %collective-permute-start.4 = (bf16[768,3,192]{0,2,1:T(8,128)(2,1)}, bf16[768,3,192]{0,2,1:T(8,128)(2,1)}, u32[]{:S(2)}, u32[]{:S(2)}) collective-permute-start(bf16[768,3,192]{0,2,1:T(8,128)(2,1)} %copy.218), channel_id=1, source_target_pairs={{0,2},{2,0},{4,6},{6,4},{8,10},{10,8},{12,14},{14,12},{16,18},{18,... | collective-permute-start | bytes 2654216 | tf_op jit(solution)/shard_map/ppermute | solution.py:191
  227.8 11.6 %collective-permute-start.5 = (bf16[192,768]{0,1:T(8,128)(2,1)}, bf16[192,768]{0,1:T(8,128)(2,1)S(1)}, u32[]{:S(2)}, u32[]{:S(2)}) collective-permute-start(bf16[192,768]{0,1:T(8,128)(2,1)} %bitcast.42), channel_id=1, source_target_pairs={{0,2},{2,0},{4,6},{6,4},{8,10},{10,8},{12,14},{14,12},{16,18},{18,... | collective-permute-start | bytes 884744 | tf_op jit(solution)/shard_map/ppermute | solution.py:191
  242.0 50.6 %copy-start.62 = (bf16[384,256]{1,0:T(8,128)(2,1)}, bf16[384,256]{1,0:T(8,128)(2,1)S(1)}, u32[]{:S(2)}) copy-start(bf16[384,256]{1,0:T(8,128)(2,1)S(1)} %convolution_convert_fusion.3) | copy-start | bytes 589828
  242.0 31.4 %collective-permute-start.6 = (bf16[768,768]{1,0:T(8,128)(2,1)}, bf16[768,768]{1,0:T(8,128)(2,1)}, u32[]{:S(2)}, u32[]{:S(2)}) collective-permute-start(bf16[768,768]{1,0:T(8,128)(2,1)} %bitcast.48), channel_id=1, source_target_pairs={{0,2},{2,0},{4,6},{6,4},{8,10},{10,8},{12,14},{14,12},{16,18},{18,... | collective-permute-start | bytes 3538952 | tf_op jit(solution)/shard_map/ppermute | solution.py:191
  246.2 34.6 %collective-permute-start.7 = (bf16[768,768]{0,1:T(8,128)(2,1)}, bf16[768,768]{0,1:T(8,128)(2,1)}, u32[]{:S(2)}, u32[]{:S(2)}) collective-permute-start(bf16[768,768]{0,1:T(8,128)(2,1)} %bitcast.51), channel_id=1, source_target_pairs={{0,2},{2,0},{4,6},{6,4},{8,10},{10,8},{12,14},{14,12},{16,18},{18,... | collective-permute-start | bytes 3538952 | tf_op jit(solution)/shard_map/ppermute | solution.py:191
  290.6 39.7 %reduce-scatter.11.cloned.1.call-start = ((), (), s32[]{:S(2)}) async-start(), calls=%async_computation.26 | async-start | bytes 1179648 | tf_op jit(solution)/shard_map/reduce_scatter | solution.py:371
  313.9 6.9 collective-permute-start.11
  320.8 37.7 %collective-permute-start.9 = (f32[768,3,192]{0,2,1:T(8,128)}, f32[768,3,192]{0,2,1:T(8,128)}, u32[]{:S(2)}, u32[]{:S(2)}) collective-permute-start(f32[768,3,192]{0,2,1:T(8,128)} %constant_dynamic-slice_fusion.6), channel_id=1, source_target_pairs={{0,2},{2,0},{4,6},{6,4},{8,10},{10,8},{12,14},{14,12},{16,18},{18,... | collective-permute-start | bytes 5308424 | tf_op jit(solution)/shard_map/ppermute | solution.py:205
  325.1 24.5 %all-to-all-start.11 = ((f32[16,192,48]{1,2,0:T(8,128)}), f32[16,192,48]{1,2,0:T(8,128)}, u32[]{:S(2)}, u32[]{:S(2)}) async-start(f32[16,192,48]{1,2,0:T(8,128)} %bitcast.85), calls=%async_computation.17 | async-start | bytes 1572864 | tf_op jit(solution)/shard_map/all_to_all | solution.py:211
  340.9 6.1 collective-permute-start.10
  349.6 24.8 %all-to-all-start.10 = ((f32[16,192,48]{1,2,0:T(8,128)}), f32[16,192,48]{1,2,0:T(8,128)}, u32[]{:S(2)}, u32[]{:S(2)}) async-start(f32[16,192,48]{1,2,0:T(8,128)} %bitcast.80), calls=%async_computation.16 | async-start | bytes 1572864 | tf_op jit(solution)/shard_map/all_to_all | solution.py:211
  374.4 58.2 %all-to-all-start.9 = ((f32[16,48,3,192]{3,1,2,0:T(8,128)}), f32[16,48,3,192]{3,1,2,0:T(8,128)}, u32[]{:S(2)}, u32[]{:S(2)}) async-start(f32[16,48,3,192]{3,1,2,0:T(8,128)} %copy.241), calls=%async_computation.15 | async-start | bytes 4718592 | tf_op jit(solution)/shard_map/all_to_all | solution.py:211
  382.0 3.8 collective-permute-start.8
  390.7 46.6 %copy-start.17 = (bf16[256,768]{1,0:T(8,128)(2,1)S(1)}, bf16[256,768]{1,0:T(8,128)(2,1)}, u32[]{:S(2)}) copy-start(bf16[256,768]{1,0:T(8,128)(2,1)} %copy-done.14) | copy-start | bytes 1179652
  432.6 57.8 %all-to-all-start.8 = ((f32[16,48,3,192]{3,1,2,0:T(8,128)}), f32[16,48,3,192]{3,1,2,0:T(8,128)S(1)}, u32[]{:S(2)}, u32[]{:S(2)}) async-start(f32[16,48,3,192]{3,1,2,0:T(8,128)} %copy.238), calls=%async_computation.14 | async-start | bytes 4718592 | tf_op jit(solution)/shard_map/all_to_all | solution.py:211
  442.2 4.9 collective-permute-start.15
  490.4 58.1 %all-to-all-start.15 = ((f32[16,768,48]{1,2,0:T(8,128)}), f32[16,768,48]{1,2,0:T(8,128)}, u32[]{:S(2)}, u32[]{:S(2)}) async-start(f32[16,768,48]{1,2,0:T(8,128)} %bitcast.99), calls=%async_computation.21 | async-start | bytes 4718592 | tf_op jit(solution)/shard_map/all_to_all | solution.py:211
  497.4 4.6 collective-permute-start.13
  548.4 58.1 %all-to-all-start.13 = ((f32[16,48,768]{2,1,0:T(8,128)}), f32[16,48,768]{2,1,0:T(8,128)}, u32[]{:S(2)}, u32[]{:S(2)}) async-start(f32[16,48,768]{2,1,0:T(8,128)} %bitcast.91), calls=%async_computation.19 | async-start | bytes 4718592 | tf_op jit(solution)/shard_map/all_to_all | solution.py:211
  555.5 4.6 collective-permute-start.14
  606.5 57.9 %all-to-all-start.14 = ((f32[16,768,48]{1,2,0:T(8,128)}), f32[16,768,48]{1,2,0:T(8,128)}, u32[]{:S(2)}, u32[]{:S(2)}) async-start(f32[16,768,48]{1,2,0:T(8,128)} %bitcast.95), calls=%async_computation.20 | async-start | bytes 4718592 | tf_op jit(solution)/shard_map/all_to_all | solution.py:211
  617.8 4.6 collective-permute-start.12
  664.4 58.5 %all-to-all-start.12 = ((f32[16,48,768]{2,1,0:T(8,128)}), f32[16,48,768]{2,1,0:T(8,128)}, u32[]{:S(2)}, u32[]{:S(2)}) async-start(f32[16,48,768]{2,1,0:T(8,128)} %bitcast.88), calls=%async_computation.18 | async-start | bytes 4718592 | tf_op jit(solution)/shard_map/all_to_all | solution.py:211
  737.1 57.9 %all-to-all-start.16 = ((f32[16,48,768]{2,1,0:T(8,128)}), f32[16,48,768]{2,1,0:T(8,128)S(1)}, u32[]{:S(2)}, u32[]{:S(2)}) async-start(f32[16,48,768]{2,1,0:T(8,128)} %copy.246), calls=%async_computation.22 | async-start | bytes 4718592 | tf_op jit(solution)/shard_map/all_to_all | solution.py:442
  742.0 110.7 %reduce-scatter.9.cloned.1.call-start = ((), (), s32[]{:S(2)}) async-start(), calls=%async_computation.25 | async-start | bytes 1179648 | tf_op jit(solution)/shard_map/reduce_scatter | solution.py:287
  748.1 104.5 %reduce-scatter.17.cloned.1.call-start = ((), (), s32[]{:S(2)}) async-start(), calls=%async_computation.29 | async-start | bytes 1179648 | tf_op jit(solution)/shard_map/reduce_scatter | solution.py:372
  799.4 4.9 collective-permute-start.21
  803.8 49.5 %reduce-scatter.15.cloned.1.call-start = ((), (), s32[]{:S(2)}) async-start(), calls=%async_computation.28 | async-start | bytes 1179648 | tf_op jit(solution)/shard_map/reduce_scatter | solution.py:371
  807.2 39.3 %collective-permute-start.22 = (f32[384,768]{1,0:T(8,128)}, f32[384,768]{1,0:T(8,128)}, u32[]{:S(2)}, u32[]{:S(2)}) collective-permute-start(f32[384,768]{1,0:T(8,128)} %dynamic-slice_add_fusion.6), channel_id=1, source_target_pairs={{0,1},{1,0},{2,3},{3,2},{4,5},{5,4},{6,7},{7,6},{8,9},{9,8},{10,11... | collective-permute-start | bytes 3538952 | tf_op jit(solution)/shard_map/ppermute | solution.py:452
  812.1 41.2 %copy-start.6 = (f32[128,768]{1,0:T(8,128)S(1)}, f32[128,768]{1,0:T(8,128)}, u32[]{:S(2)}) copy-start(f32[128,768]{1,0:T(8,128)} %reduce-scatter.7.cloned.1.call-done) | copy-start | bytes 1179652
  812.1 41.2 %copy-start.94 = (f32[768]{0:T(1024)S(1)}, f32[768]{0:T(1024)}, u32[]{:S(2)}) copy-start(f32[768]{0:T(1024)} %get-tuple-element.141) | copy-start | bytes 9220
  812.1 41.2 %copy-start.95 = (f32[768]{0:T(1024)S(1)}, f32[768]{0:T(1024)}, u32[]{:S(2)}) copy-start(f32[768]{0:T(1024)} %get-tuple-element.142) | copy-start | bytes 9220
  812.1 41.2 %copy-start.117 = (f32[768]{0:T(1024)S(1)}, f32[768]{0:T(1024)}, u32[]{:S(2)}) copy-start(f32[768]{0:T(1024)} %copy-done.116) | copy-start | bytes 9220
  849.3 6.9 collective-permute-start.23
  930.0 47.7 %copy-start.150 = (f32[128]{0:T(128)S(1)}, f32[128]{0:T(128)}, u32[]{:S(2)}) copy-start(f32[128]{0:T(128)} %get-tuple-element.180) | copy-start | bytes 1540
  930.0 47.7 %copy-start.151 = (f32[128]{0:T(128)S(1)}, f32[128]{0:T(128)}, u32[]{:S(2)}) copy-start(f32[128]{0:T(128)} %get-tuple-element.181) | copy-start | bytes 1540
  930.0 60.9 %copy-start.21 = (f32[128,768]{1,0:T(8,128)S(1)}, f32[128,768]{1,0:T(8,128)}, u32[]{:S(2)}) copy-start(f32[128,768]{1,0:T(8,128)} %copy-done.20) | copy-start | bytes 1179652
  930.0 60.9 %copy-start.140 = (f32[128]{0:T(128)S(1)}, f32[128]{0:T(128)}, u32[]{:S(2)}) copy-start(f32[128]{0:T(128)} %copy-done.139) | copy-start | bytes 1540
  930.0 60.9 %copy-start.147 = (f32[128]{0:T(128)S(1)}, f32[128]{0:T(128)}, u32[]{:S(2)}) copy-start(f32[128]{0:T(128)} %copy-done.146) | copy-start | bytes 1540
  930.0 67.0 %all-to-all-start.17 = ((f32[16,48,768]{2,1,0:T(8,128)}), f32[16,48,768]{2,1,0:T(8,128)S(1)}, u32[]{:S(2)}, u32[]{:S(2)}) async-start(f32[16,48,768]{2,1,0:T(8,128)} %fusion.248), calls=%async_computation.23 | async-start | bytes 4718592 | tf_op jit(solution)/shard_map/all_to_all | solution.py:478
  935.4 58.4 %copy-start.113 = (f32[2,3,768]{2,0,1:T(2,128)S(1)}, f32[2,3,768]{2,0,1:T(2,128)}, u32[]{:S(2)}) copy-start(f32[2,3,768]{2,0,1:T(2,128)} %param.24) | copy-start | bytes 55300
  935.4 59.6 %copy-start.115 = (f32[2,2,768]{2,1,0:T(2,128)S(1)}, f32[2,2,768]{2,1,0:T(2,128)}, u32[]{:S(2)}) copy-start(f32[2,2,768]{2,1,0:T(2,128)} %param.22) | copy-start | bytes 36868
  935.4 60.2 %copy-start.97 = (f32[2,4,768]{2,1,0:T(4,128)S(1)}, f32[2,4,768]{2,1,0:T(4,128)}, u32[]{:S(2)}) copy-start(f32[2,4,768]{2,1,0:T(4,128)} %param.23) | copy-start | bytes 73732
  935.4 60.9 %copy-start.99 = (f32[2,3072]{1,0:T(2,128)S(1)}, f32[2,3072]{1,0:T(2,128)}, u32[]{:S(2)}) copy-start(f32[2,3072]{1,0:T(2,128)} %param.25) | copy-start | bytes 73732
  935.6 1.4 collective-permute-start.16
  937.0 10.8 %collective-permute-start.17 = (f32[19968]{0:T(1024)S(1)}, f32[19968]{0:T(1024)S(1)}, u32[]{:S(2)}, u32[]{:S(2)}) collective-permute-start(f32[19968]{0:T(1024)S(1)} %add.473), channel_id=1, source_target_pairs={{0,4},{2,6},{4,0},{6,2},{8,12},{10,14},{12,8},{14,10},{16,20},{18,... | collective-permute-start | bytes 239624 | tf_op jit(solution)/shard_map/ppermute | solution.py:174
  947.8 29.0 %collective-permute-start.18 = (f32[19968]{0:T(1024)S(1)}, f32[19968]{0:T(1024)S(1)}, u32[]{:S(2)}, u32[]{:S(2)}) collective-permute-start(f32[19968]{0:T(1024)S(1)} %add.474), channel_id=1, source_target_pairs={{0,8},{2,10},{4,12},{6,14},{8,0},{10,2},{12,4},{14,6},{16,24},{18,... | collective-permute-start | bytes 239624 | tf_op jit(solution)/shard_map/ppermute | solution.py:174
  976.8 12.9 %collective-permute-start.19 = (f32[19968]{0:T(1024)S(1)}, f32[19968]{0:T(1024)S(1)}, u32[]{:S(2)}, u32[]{:S(2)}) collective-permute-start(f32[19968]{0:T(1024)S(1)} %add.475), channel_id=1, source_target_pairs={{0,16},{2,18},{4,20},{6,22},{8,24},{10,26},{12,28},{14,30},{16,0},... | collective-permute-start | bytes 239624 | tf_op jit(solution)/shard_map/ppermute | solution.py:174
  989.6 3.4 collective-permute-start.20
  (139 other events, 1564.5 us)
Sparse Core Ops, SparseCore 0:
  224.7 21.4 reduce-scatter.6
  290.7 18.7 reduce-scatter.12
  311.8 18.0 reduce-scatter.10
  748.3 17.9 reduce-scatter.8
  803.9 25.7 reduce-scatter.16
  831.8 21.4 reduce-scatter.14

commit v4 on v3

--- a/solution.py
+++ b/solution.py
@@ -251,7 +251,7 @@
         layer_weights = (
             chip_gather(qkv_weight[layer_id], 0, 2),
             chip_gather(proj_weight[layer_id], 1, 0),
-            chip_gather(up_weight[layer_id], 0, 1),
+            dp_gather(up_weight[layer_id], 0),
             chip_gather(down_weight[layer_id], 1, 0),
         )
         qkv_full, proj_full, up_full, down_full = layer_weights
@@ -397,7 +397,7 @@
         weight_list[layer_id] = (
             chip_scatter(qkv_part, 0, 2),
             chip_scatter(proj_part, 1, 0),
-            chip_scatter(up_part, 0, 1),
+            dp_scatter(up_part, 0),
             chip_scatter(down_part, 1, 0),
         )
     small_parts = (
@@ -441,6 +441,7 @@
     outgoing = jnp.concatenate(pieces, axis=0)
     owned = lax.all_to_all(outgoing, "dp", split_axis=0, concat_axis=0, tiled=True)
     owned = owned.reshape(dp_count * rows_local, piece_width)
+    owned, flat, grad_stream = lax.optimization_barrier((owned, flat, grad_stream))
     gram = jnp.dot(owned, owned.T, precision=ns_precision)
     bit = 1
     while bit < sub:

time: 1030 us -> 896 us (0.87)
  waiting for transfers between devices: 525 us -> 425 us
  starting transfers between devices: 110 us -> 91.3 us
    all_to_all x1, waiting for transfers between devices: 0.01 us -> 49.1 us  [local(): lax.all_to_all(current.reshape(dp_count, rows_local, piece_width), 'dp',...]
    all_to_all x1, waiting for transfers between devices: 46.8 us -> 0.01 us  [local(): lax.all_to_all(outgoing, 'dp', split_axis=0, concat_axis=0, tiled=True)]
    all_to_all x8 -> x6, waiting for transfers between devices: 251 us -> 212 us  [chip_scatter(): got = lax.all_to_all(chunks, 'dp', split_axis=0, concat_axis=0, tiled=True)]
    all_to_all x8 -> x6, waiting for transfers between devices: 118 us -> 93.2 us  [chip_gather(): lax.all_to_all(outgoing, 'dp', split_axis=0, concat_axis=0, tiled=True)]
    ppermute x4, waiting for transfers between devices: 51.6 us -> 33 us  [butterfly_sum(): flat = flat + lax.ppermute(flat, 'dp', swap_pairs(count, bit))]
    ppermute x8 -> x6, waiting for transfers between devices: 20.3 us -> 4.17 us  [chip_scatter(): chip_sum = keep + lax.ppermute(send, 'dp', swap_pairs(count, 1))]
    all_to_all x8 -> x6, starting transfers between devices: 40.6 us -> 28.8 us  [chip_scatter(): got = lax.all_to_all(chunks, 'dp', split_axis=0, concat_axis=0, tiled=True)]
    all_to_all x8 -> x6, starting transfers between devices: 41.1 us -> 31.1 us  [chip_gather(): lax.all_to_all(outgoing, 'dp', split_axis=0, concat_axis=0, tiled=True)]
  transfers between devices with their start and end apart: 48 -> 44, of which waited for: 30 -> 20; matrix products, arithmetic and copies ran while one was open for 19% -> 23% of each run, Pallas kernels for 0% -> 0%
where the time goes in v4:
time: 896 us; the launch traced here: 884 us
  waiting for transfers between devices  425 us (47%)
  matrix products  157 us (18%)
  local copies, waits for them, and re-layouts  94.8 us (11%)
  starting transfers between devices  91.3 us (10%)
  other arithmetic  58 us (6%)
  blocking collectives  40.8 us (5%)
  between operations  17.5 us (2%)
    all_to_all x6, waiting for transfers between devices, chip_scatter(): got = lax.all_to_all(chunks, 'dp', split_axis=0, concat_axis=0, tiled=True)  212 us
    all_to_all x6, waiting for transfers between devices, chip_gather(): lax.all_to_all(outgoing, 'dp', split_axis=0, concat_axis=0, tiled=True)  93.2 us
    all_to_all x1, waiting for transfers between devices, local(): lax.all_to_all(current.reshape(dp_count, rows_local, piece_width), 'dp',...  49.1 us
    ppermute x4, waiting for transfers between devices, butterfly_sum(): flat = flat + lax.ppermute(flat, 'dp', swap_pairs(count, bit))  33 us
    all_to_all x6, starting transfers between devices, chip_gather(): lax.all_to_all(outgoing, 'dp', split_axis=0, concat_axis=0, tiled=True)  31.1 us
    all_to_all x6, starting transfers between devices, chip_scatter(): got = lax.all_to_all(chunks, 'dp', split_axis=0, concat_axis=0, tiled=True)  28.8 us
    ppermute x1, waiting for transfers between devices, local(): mine = mine + lax.ppermute(mine, 'tensor', [(0, 1), (1, 0)])  26 us
    dot_general x5, matrix products, local(): squared = jnp.dot(current_gram, current_gram, precision=ns_precision)  20.1 us
  transfers between devices with their start and end apart: 44, of which 20 were waited for; matrix products, arithmetic and copies ran while one was open for 23% of the time, Pallas kernels for 0%

profile of v4, /device:TPU:11, one launch (start us, length us, event | category | flops | bytes accessed | tf_op | source)
XLA Modules:
  0.0 884.4 jit_solution(13853002234501904340)
XLA Ops:
  11.4 6.5 all-to-all-start.1
  19.6 14.0 %all-to-all-done.1 = bf16[16,192,48]{1,2,0:T(8,128)(2,1)S(1)} async-done(((bf16[16,192,48]{1,2,0:T(8,128)(2,1)}), bf16[16,192,48]{1,2,0:T(8,128)(2,1)S(1)}, u32[]{:S(2)}, u32[]{:S(2)}) %all-to-all-start.1) | async-done | bytes 294944 | tf_op jit(solution)/shard_map/all_to_all | solution.py:187
  34.8 4.4 all-to-all-start
  43.4 33.0 %all-to-all-done = bf16[16,48,3,192]{3,1,2,0:T(8,128)(2,1)S(1)} async-done(((bf16[16,48,3,192]{3,1,2,0:T(8,128)(2,1)}), bf16[16,48,3,192]{3,1,2,0:T(8,128)(2,1)S(1)}, u32[]{:S(2)}, u32[]{:S(2)}) %all-to-all-start) | async-done | bytes 884768 | tf_op jit(solution)/shard_map/all_to_all | solution.py:187
  77.4 5.0 all-to-all-start.2
  84.6 6.8 all_gather.24
  94.7 7.2 all_gather.25
  103.1 7.1 all-to-all-done.2
  111.0 4.7 all-to-all-start.4
  123.9 6.8 multiply_convert_fusion.3
  131.6 4.3 fusion.118
  137.0 5.7 all-to-all-start.3
  146.0 24.5 %all-to-all-done.3 = bf16[16,48,3,192]{3,1,2,0:T(8,128)(2,1)S(1)} async-done(((bf16[16,48,3,192]{3,1,2,0:T(8,128)(2,1)}), bf16[16,48,3,192]{3,1,2,0:T(8,128)(2,1)S(1)}, u32[]{:S(2)}, u32[]{:S(2)}) %all-to-all-start.3) | async-done | bytes 884768 | tf_op jit(solution)/shard_map/all_to_all | solution.py:187
  171.6 4.7 all-to-all-start.5
  183.3 7.0 all_gather.30
  194.3 14.7 %all-to-all-done.5 = bf16[16,768,48]{1,2,0:T(8,128)(2,1)} async-done(((bf16[16,768,48]{1,2,0:T(8,128)(2,1)}), bf16[16,768,48]{1,2,0:T(8,128)(2,1)}, u32[]{:S(2)}, u32[]{:S(2)}) %all-to-all-start.5) | async-done | bytes 1179680 | tf_op jit(solution)/shard_map/all_to_all | solution.py:187
  214.2 6.8 all_gather.27
  227.0 6.1 all_gather.28
  234.5 6.5 multiply_convert_fusion.2
  241.0 4.6 convert_reduce_fusion
  264.1 5.0 convolution_bitcast_fusion.2
  284.4 5.0 all-to-all-start.9
  293.0 6.8 all_gather.31
  308.8 5.0 all-to-all-start.8
  321.6 3.7 copy.251
  325.3 21.6 %all-to-all-done.8 = f32[16,192,48]{1,2,0:T(8,128)} async-done(((f32[16,192,48]{1,2,0:T(8,128)}), f32[16,192,48]{1,2,0:T(8,128)}, u32[]{:S(2)}, u32[]{:S(2)}) %all-to-all-start.8) | async-done | bytes 589856 | tf_op jit(solution)/shard_map/all_to_all | solution.py:211
  346.9 4.5 all-to-all-start.7
  356.1 4.3 fusion.245
  366.8 47.0 %all-to-all-done.7 = f32[16,48,3,192]{3,1,2,0:T(8,128)} async-done(((f32[16,48,3,192]{3,1,2,0:T(8,128)}), f32[16,48,3,192]{3,1,2,0:T(8,128)}, u32[]{:S(2)}, u32[]{:S(2)}) %all-to-all-start.7) | async-done | bytes 1769504 | tf_op jit(solution)/shard_map/all_to_all | solution.py:211
  413.8 4.7 all-to-all-start.6
  418.6 3.5 constant_dynamic-slice_fusion
  422.5 4.6 convert_reduce_fusion.1
  431.0 4.2 dynamic-slice_add_fusion
  435.1 54.5 %all-to-all-done.6 = f32[16,48,3,192]{3,1,2,0:T(8,128)S(1)} async-done(((f32[16,48,3,192]{3,1,2,0:T(8,128)}), f32[16,48,3,192]{3,1,2,0:T(8,128)S(1)}, u32[]{:S(2)}, u32[]{:S(2)}) %all-to-all-start.6) | async-done | bytes 1769504 | tf_op jit(solution)/shard_map/all_to_all | solution.py:211
  489.6 4.7 all-to-all-start.11
  495.8 4.2 collective-permute-done.10
  501.9 55.0 %all-to-all-done.11 = f32[16,768,48]{1,2,0:T(8,128)} async-done(((f32[16,768,48]{1,2,0:T(8,128)}), f32[16,768,48]{1,2,0:T(8,128)}, u32[]{:S(2)}, u32[]{:S(2)}) %all-to-all-start.11) | async-done | bytes 2359328 | tf_op jit(solution)/shard_map/all_to_all | solution.py:211
  556.9 4.9 all-to-all-start.10
  561.9 4.4 convolution_bitcast_fusion.1
  566.3 3.6 fusion.10
  581.8 33.2 %all-to-all-done.10 = f32[16,768,48]{1,2,0:T(8,128)} async-done(((f32[16,768,48]{1,2,0:T(8,128)}), f32[16,768,48]{1,2,0:T(8,128)}, u32[]{:S(2)}, u32[]{:S(2)}) %all-to-all-start.10) | async-done | bytes 2359328 | tf_op jit(solution)/shard_map/all_to_all | solution.py:211
  625.0 7.0 concatenate.135
  634.9 4.9 all-to-all-start.12
  659.1 3.5 collective-permute-done.13
  664.5 16.6 %collective-permute-done.14 = f32[19968]{0:T(1024)S(1)} collective-permute-done((f32[19968]{0:T(1024)S(1)}, f32[19968]{0:T(1024)S(1)}, u32[]{:S(2)}, u32[]{:S(2)}) %collective-permute-start.14) | collective-permute-done | bytes 79904 | tf_op jit(solution)/shard_map/ppermute | solution.py:174
  682.0 12.0 %collective-permute-done.15 = f32[19968]{0:T(1024)S(1)} collective-permute-done((f32[19968]{0:T(1024)S(1)}, f32[19968]{0:T(1024)S(1)}, u32[]{:S(2)}, u32[]{:S(2)}) %collective-permute-start.15) | collective-permute-done | bytes 79904 | tf_op jit(solution)/shard_map/ppermute | solution.py:174
  699.2 4.4 fusion.246
  705.1 4.5 collective-permute-done.17
  713.2 26.0 %collective-permute-done.18 = f32[384,768]{1,0:T(8,128)S(1)} collective-permute-done((f32[384,768]{1,0:T(8,128)S(1)}, f32[384,768]{1,0:T(8,128)S(1)}, u32[]{:S(2)}, u32[]{:S(2)}) %collective-permute-start.18) | collective-permute-done | bytes 1179680 | tf_op jit(solution)/shard_map/ppermute | solution.py:453
  745.3 7.5 fusion
  752.9 3.4 fusion.17
  762.6 3.2 fusion.39
  765.9 3.6 fusion.35
  769.4 3.4 fusion.37
  776.0 3.2 fusion.33
  779.2 3.8 fusion.31
  786.1 3.2 fusion.27
  789.3 3.5 fusion.25
  796.0 3.4 fusion.29
  799.4 3.3 fusion.23
  802.8 3.6 fusion.5
  806.3 4.5 fusion.13
  810.9 7.2 all-to-all-start.13
  822.0 49.1 %all-to-all-done.13 = f32[16,48,768]{2,1,0:T(8,128)S(1)} async-done(((f32[16,48,768]{2,1,0:T(8,128)}), f32[16,48,768]{2,1,0:T(8,128)S(1)}, u32[]{:S(2)}, u32[]{:S(2)}) %all-to-all-start.13) | async-done | bytes 2359328 | tf_op jit(solution)/shard_map/all_to_all | solution.py:479
  (624 shorter events, 217.3 us)
Async XLA Ops:
  7.2 116.7 %all-gather.5.cloned.1.call-start = ((), (), s32[]{:S(2)}) async-start(), calls=%async_computation.30 | async-start | bytes 2506752 | tf_op jit(solution)/shard_map/all_gather | solution.py:146
  11.4 22.2 %all-to-all-start.1 = ((bf16[16,192,48]{1,2,0:T(8,128)(2,1)}), bf16[16,192,48]{1,2,0:T(8,128)(2,1)S(1)}, u32[]{:S(2)}, u32[]{:S(2)}) async-start(bf16[16,192,48]{1,2,0:T(8,128)(2,1)} %bitcast.15), calls=%async_computation.1 | async-start | bytes 786432 | tf_op jit(solution)/shard_map/all_to_all | solution.py:187
  19.6 20.2 %copy-start.128 = (s32[1,256]{1,0:T(1,128)S(1)}, s32[1,256]{1,0:T(1,128)}, u32[]{:S(2)}) copy-start(s32[1,256]{1,0:T(1,128)} %param.17) | copy-start | bytes 3076
  19.6 20.4 %copy-start.93 = (f32[2,3072]{1,0:T(2,128)S(1)}, f32[2,3072]{1,0:T(2,128)}, u32[]{:S(2)}) copy-start(f32[2,3072]{1,0:T(2,128)} %param.25) | copy-start | bytes 73732
  34.8 41.5 %all-to-all-start = ((bf16[16,48,3,192]{3,1,2,0:T(8,128)(2,1)}), bf16[16,48,3,192]{3,1,2,0:T(8,128)(2,1)S(1)}, u32[]{:S(2)}, u32[]{:S(2)}) async-start(bf16[16,48,3,192]{3,1,2,0:T(8,128)(2,1)} %bitcast.4), calls=%async_computation | async-start | bytes 2359296 | tf_op jit(solution)/shard_map/all_to_all | solution.py:187
  77.4 32.8 %all-to-all-start.2 = ((bf16[16,768,48]{1,2,0:T(8,128)(2,1)}), bf16[16,768,48]{1,2,0:T(8,128)(2,1)}, u32[]{:S(2)}, u32[]{:S(2)}) async-start(bf16[16,768,48]{1,2,0:T(8,128)(2,1)} %bitcast.20), calls=%async_computation.2 | async-start | bytes 2359296 | tf_op jit(solution)/shard_map/all_to_all | solution.py:187
  91.4 26.2 %copy-start.38 = (bf16[256,768]{1,0:T(8,128)(2,1)}, bf16[256,768]{1,0:T(8,128)(2,1)S(1)}, u32[]{:S(2)}) copy-start(bf16[256,768]{1,0:T(8,128)(2,1)S(1)} %all_gather.24) | copy-start | bytes 1179652
  92.1 25.5 %copy-start.9 = (bf16[16,48,3,192]{3,1,0,2:T(8,128)(2,1)}, bf16[16,48,3,192]{3,1,0,2:T(8,128)(2,1)S(1)}, u32[]{:S(2)}) copy-start(bf16[16,48,3,192]{3,1,0,2:T(8,128)(2,1)S(1)} %copy.223) | copy-start | bytes 2654212
  93.5 22.7 %collective-permute-start = (bf16[768,3,192]{0,2,1:T(8,128)(2,1)}, bf16[768,3,192]{0,2,1:T(8,128)(2,1)S(1)}, u32[]{:S(2)}, u32[]{:S(2)}) collective-permute-start(bf16[768,3,192]{0,2,1:T(8,128)(2,1)} %copy.224), channel_id=1, source_target_pairs={{0,2},{2,0},{4,6},{6,4},{8,10},{10,8},{12,14},{14,12},{16,18},{18,... | collective-permute-start | bytes 2654216 | tf_op jit(solution)/shard_map/ppermute | solution.py:191
  101.9 22.0 %copy-start.24 = (bf16[256,768]{1,0:T(8,128)(2,1)}, bf16[256,768]{1,0:T(8,128)(2,1)S(1)}, u32[]{:S(2)}) copy-start(bf16[256,768]{1,0:T(8,128)(2,1)S(1)} %all_gather.25) | copy-start | bytes 1179652
  102.3 40.5 %collective-permute-start.1 = (bf16[192,768]{0,1:T(8,128)(2,1)}, bf16[192,768]{0,1:T(8,128)(2,1)}, u32[]{:S(2)}, u32[]{:S(2)}) collective-permute-start(bf16[192,768]{0,1:T(8,128)(2,1)} %bitcast.363), channel_id=1, source_target_pairs={{0,2},{2,0},{4,6},{6,4},{8,10},{10,8},{12,14},{14,12},{16,18},{18,... | collective-permute-start | bytes 884744 | tf_op jit(solution)/shard_map/ppermute | solution.py:191
  111.0 24.9 %all-to-all-start.4 = ((bf16[16,192,48]{1,2,0:T(8,128)(2,1)}), bf16[16,192,48]{1,2,0:T(8,128)(2,1)}, u32[]{:S(2)}, u32[]{:S(2)}) async-start(bf16[16,192,48]{1,2,0:T(8,128)(2,1)} %bitcast.36), calls=%async_computation.5 | async-start | bytes 786432 | tf_op jit(solution)/shard_map/all_to_all | solution.py:187
  115.8 14.9 %collective-permute-start.2 = (bf16[768,768]{0,1:T(8,128)(2,1)}, bf16[768,768]{0,1:T(8,128)(2,1)}, u32[]{:S(2)}, u32[]{:S(2)}) collective-permute-start(bf16[768,768]{0,1:T(8,128)(2,1)} %bitcast.22), channel_id=1, source_target_pairs={{0,2},{2,0},{4,6},{6,4},{8,10},{10,8},{12,14},{14,12},{16,18},{18,... | collective-permute-start | bytes 3538952 | tf_op jit(solution)/shard_map/ppermute | solution.py:191
  137.0 33.5 %all-to-all-start.3 = ((bf16[16,48,3,192]{3,1,2,0:T(8,128)(2,1)}), bf16[16,48,3,192]{3,1,2,0:T(8,128)(2,1)S(1)}, u32[]{:S(2)}, u32[]{:S(2)}) async-start(bf16[16,48,3,192]{3,1,2,0:T(8,128)(2,1)} %bitcast.332), calls=%async_computation.4 | async-start | bytes 2359296 | tf_op jit(solution)/shard_map/all_to_all | solution.py:187
  142.8 67.7 %reduce-scatter.9.cloned.1.call-start = ((), (), s32[]{:S(2)}) async-start(), calls=%async_computation.22 | async-start | bytes 1179648 | tf_op jit(solution)/shard_map/reduce_scatter | solution.py:287
  142.8 27.7 %copy-start.67 = (bf16[2,768,48]{1,2,0:T(8,128)(2,1)S(1)}, bf16[2,768,48]{1,2,0:T(8,128)(2,1)}, u32[]{:S(2)}) copy-start(bf16[2,768,48]{1,2,0:T(8,128)(2,1)} %get-tuple-element.288) | copy-start | bytes 442372
  171.6 37.3 %all-to-all-start.5 = ((bf16[16,768,48]{1,2,0:T(8,128)(2,1)}), bf16[16,768,48]{1,2,0:T(8,128)(2,1)}, u32[]{:S(2)}, u32[]{:S(2)}) async-start(bf16[16,768,48]{1,2,0:T(8,128)(2,1)} %bitcast.331), calls=%async_computation.6 | async-start | bytes 2359296 | tf_op jit(solution)/shard_map/all_to_all | solution.py:187
  176.3 58.1 %all-gather.7.cloned.1.call-start = ((), (), s32[]{:S(2)}) async-start(), calls=%async_computation.31 | async-start | bytes 2506752 | tf_op jit(solution)/shard_map/all_gather | solution.py:146
  177.1 112.4 %reduce-scatter.15.cloned.1.call-start = ((), (), s32[]{:S(2)}) async-start(), calls=%async_computation.25 | async-start | bytes 1179648 | tf_op jit(solution)/shard_map/reduce_scatter | solution.py:372
  180.1 29.0 %collective-permute-start.3 = (bf16[768,3,192]{0,2,1:T(8,128)(2,1)S(1)}, bf16[768,3,192]{0,2,1:T(8,128)(2,1)S(1)}, u32[]{:S(2)}, u32[]{:S(2)}) collective-permute-start(bf16[768,3,192]{0,2,1:T(8,128)(2,1)S(1)} %copy.232), channel_id=1, source_target_pairs={{0,2},{2,0},{4,6},{6,4},{8,10},{10,8},{12,14},{14,12},{16,18},{18,... | collective-permute-start | bytes 2654216 | tf_op jit(solution)/shard_map/ppermute | solution.py:191
  180.5 9.7 %collective-permute-start.4 = (bf16[192,768]{0,1:T(8,128)(2,1)}, bf16[192,768]{0,1:T(8,128)(2,1)S(1)}, u32[]{:S(2)}, u32[]{:S(2)}) collective-permute-start(bf16[192,768]{0,1:T(8,128)(2,1)} %bitcast.38), channel_id=1, source_target_pairs={{0,2},{2,0},{4,6},{6,4},{8,10},{10,8},{12,14},{14,12},{16,18},{18,... | collective-permute-start | bytes 884744 | tf_op jit(solution)/shard_map/ppermute | solution.py:191
  209.0 32.1 %collective-permute-start.5 = (bf16[768,768]{0,1:T(8,128)(2,1)}, bf16[768,768]{0,1:T(8,128)(2,1)}, u32[]{:S(2)}, u32[]{:S(2)}) collective-permute-start(bf16[768,768]{0,1:T(8,128)(2,1)} %bitcast.43), channel_id=1, source_target_pairs={{0,2},{2,0},{4,6},{6,4},{8,10},{10,8},{12,14},{14,12},{16,18},{18,... | collective-permute-start | bytes 3538952 | tf_op jit(solution)/shard_map/ppermute | solution.py:191
  247.3 42.2 %reduce-scatter.13.cloned.1.call-start = ((), (), s32[]{:S(2)}) async-start(), calls=%async_computation.24 | async-start | bytes 1179648 | tf_op jit(solution)/shard_map/reduce_scatter | solution.py:371
  269.2 351.2 %reduce-scatter.19.cloned.1.call-start = ((), (), s32[]{:S(2)}) async-start(), calls=%async_computation.27 | async-start | bytes 5013504 | tf_op jit(solution)/shard_map/reduce_scatter | solution.py:142
  272.0 8.3 collective-permute-start.9
  277.1 40.1 %collective-permute-start.7 = (f32[768,3,192]{0,2,1:T(8,128)}, f32[768,3,192]{0,2,1:T(8,128)}, u32[]{:S(2)}, u32[]{:S(2)}) collective-permute-start(f32[768,3,192]{0,2,1:T(8,128)} %constant_dynamic-slice_fusion.4), channel_id=1, source_target_pairs={{0,2},{2,0},{4,6},{6,4},{8,10},{10,8},{12,14},{14,12},{16,18},{18,... | collective-permute-start | bytes 5308424 | tf_op jit(solution)/shard_map/ppermute | solution.py:205
  284.4 24.3 %all-to-all-start.9 = ((f32[16,192,48]{1,2,0:T(8,128)}), f32[16,192,48]{1,2,0:T(8,128)}, u32[]{:S(2)}, u32[]{:S(2)}) async-start(f32[16,192,48]{1,2,0:T(8,128)} %bitcast.77), calls=%async_computation.13 | async-start | bytes 1572864 | tf_op jit(solution)/shard_map/all_to_all | solution.py:211
  300.3 5.5 collective-permute-start.8
  308.8 38.1 %all-to-all-start.8 = ((f32[16,192,48]{1,2,0:T(8,128)}), f32[16,192,48]{1,2,0:T(8,128)}, u32[]{:S(2)}, u32[]{:S(2)}) async-start(f32[16,192,48]{1,2,0:T(8,128)} %bitcast.72), calls=%async_computation.12 | async-start | bytes 1572864 | tf_op jit(solution)/shard_map/all_to_all | solution.py:211
  325.3 26.2 %copy-start.5 = (bf16[6,256,256]{1,2,0:T(8,128)(2,1)S(1)}, bf16[6,256,256]{1,2,0:T(8,128)(2,1)}, u32[]{:S(2)}) copy-start(bf16[6,256,256]{1,2,0:T(8,128)(2,1)} %copy-done.4) | copy-start | bytes 2359300
  325.3 26.2 %copy-start.60 = (bf16[256,6,48]{0,2,1:T(8,128)(2,1)S(1)}, bf16[256,6,48]{0,2,1:T(8,128)(2,1)}, u32[]{:S(2)}) copy-start(bf16[256,6,48]{0,2,1:T(8,128)(2,1)} %copy-done.59) | copy-start | bytes 442372
  325.3 26.2 %copy-start.96 = (bf16[256,6,8]{0,2,1:T(8,128)(2,1)S(1)}, bf16[256,6,8]{0,2,1:T(8,128)(2,1)}, u32[]{:S(2)}) copy-start(bf16[256,6,8]{0,2,1:T(8,128)(2,1)} %copy-done.95) | copy-start | bytes 73732
  325.3 27.3 %copy-start.48 = (f32[256,6,64]{0,2,1:T(8,128)S(1)}, f32[256,6,64]{0,2,1:T(8,128)}, u32[]{:S(2)}) copy-start(f32[256,6,64]{0,2,1:T(8,128)} %fusion.56) | copy-start | bytes 1179652
  346.9 66.9 %all-to-all-start.7 = ((f32[16,48,3,192]{3,1,2,0:T(8,128)}), f32[16,48,3,192]{3,1,2,0:T(8,128)}, u32[]{:S(2)}, u32[]{:S(2)}) async-start(f32[16,48,3,192]{3,1,2,0:T(8,128)} %copy.251), calls=%async_computation.11 | async-start | bytes 4718592 | tf_op jit(solution)/shard_map/all_to_all | solution.py:211
  355.8 4.6 collective-permute-start.6
  413.8 75.8 %all-to-all-start.6 = ((f32[16,48,3,192]{3,1,2,0:T(8,128)}), f32[16,48,3,192]{3,1,2,0:T(8,128)S(1)}, u32[]{:S(2)}, u32[]{:S(2)}) async-start(f32[16,48,3,192]{3,1,2,0:T(8,128)} %copy.248), calls=%async_computation.10 | async-start | bytes 4718592 | tf_op jit(solution)/shard_map/all_to_all | solution.py:211
  418.6 201.8 %reduce-scatter.17.cloned.1.call-start = ((), (), s32[]{:S(2)}) async-start(), calls=%async_computation.26 | async-start | bytes 5013504 | tf_op jit(solution)/shard_map/reduce_scatter | solution.py:142
  422.1 8.9 %collective-permute-start.11 = (f32[768,768]{0,1:T(8,128)}, f32[768,768]{0,1:T(8,128)}, u32[]{:S(2)}, u32[]{:S(2)}) collective-permute-start(f32[768,768]{0,1:T(8,128)} %constant_dynamic-slice_fusion), channel_id=1, source_target_pairs={{0,2},{2,0},{4,6},{6,4},{8,10},{10,8},{12,14},{14,12},{16,18},{18,... | collective-permute-start | bytes 7077896 | tf_op jit(solution)/shard_map/ppermute | solution.py:205
  489.6 67.3 %all-to-all-start.11 = ((f32[16,768,48]{1,2,0:T(8,128)}), f32[16,768,48]{1,2,0:T(8,128)}, u32[]{:S(2)}, u32[]{:S(2)}) async-start(f32[16,768,48]{1,2,0:T(8,128)} %bitcast.91), calls=%async_computation.17 | async-start | bytes 4718592 | tf_op jit(solution)/shard_map/all_to_all | solution.py:211
  495.3 4.6 collective-permute-start.10
  556.9 58.1 %all-to-all-start.10 = ((f32[16,768,48]{1,2,0:T(8,128)}), f32[16,768,48]{1,2,0:T(8,128)}, u32[]{:S(2)}, u32[]{:S(2)}) async-start(f32[16,768,48]{1,2,0:T(8,128)} %bitcast.87), calls=%async_computation.16 | async-start | bytes 4718592 | tf_op jit(solution)/shard_map/all_to_all | solution.py:211
  561.8 93.2 %reduce-scatter.21.cloned.1.call-start = ((), (), s32[]{:S(2)}) async-start(), calls=%async_computation.28 | async-start | bytes 1179648 | tf_op jit(solution)/shard_map/reduce_scatter | solution.py:371
  566.3 88.8 %reduce-scatter.23.cloned.1.call-start = ((), (), s32[]{:S(2)}) async-start(), calls=%async_computation.29 | async-start | bytes 1179648 | tf_op jit(solution)/shard_map/reduce_scatter | solution.py:372
  581.8 35.0 %copy-start.65 = (f32[2,1536,48]{1,2,0:T(8,128)S(1)}, f32[2,1536,48]{1,2,0:T(8,128)}, u32[]{:S(2)}) copy-start(f32[2,1536,48]{1,2,0:T(8,128)} %param.29) | copy-start | bytes 1769476
  634.9 64.4 %all-to-all-start.12 = ((f32[16,48,768]{2,1,0:T(8,128)}), f32[16,48,768]{2,1,0:T(8,128)S(1)}, u32[]{:S(2)}, u32[]{:S(2)}) async-start(f32[16,48,768]{2,1,0:T(8,128)} %copy.256), calls=%async_computation.18 | async-start | bytes 4718592 | tf_op jit(solution)/shard_map/all_to_all | solution.py:442
  639.8 56.6 %reduce-scatter.11.cloned.1.call-start = ((), (), s32[]{:S(2)}) async-start(), calls=%async_computation.23 | async-start | bytes 1179648 | tf_op jit(solution)/shard_map/reduce_scatter | solution.py:287
  647.9 48.5 %copy-start.6 = (f32[128,768]{1,0:T(8,128)S(1)}, f32[128,768]{1,0:T(8,128)}, u32[]{:S(2)}) copy-start(f32[128,768]{1,0:T(8,128)} %reduce-scatter.9.cloned.1.call-done) | copy-start | bytes 1179652
  647.9 48.5 %copy-start.18 = (f32[128,768]{1,0:T(8,128)S(1)}, f32[128,768]{1,0:T(8,128)}, u32[]{:S(2)}) copy-start(f32[128,768]{1,0:T(8,128)} %copy-done.17) | copy-start | bytes 1179652
  647.9 48.5 %copy-start.88 = (f32[768]{0:T(1024)S(1)}, f32[768]{0:T(1024)}, u32[]{:S(2)}) copy-start(f32[768]{0:T(1024)} %get-tuple-element.163) | copy-start | bytes 9220
  647.9 48.5 %copy-start.90 = (f32[768]{0:T(1024)S(1)}, f32[768]{0:T(1024)}, u32[]{:S(2)}) copy-start(f32[768]{0:T(1024)} %get-tuple-element.164) | copy-start | bytes 9220
  649.2 47.2 %copy-start.125 = (f32[768]{0:T(1024)S(1)}, f32[768]{0:T(1024)}, u32[]{:S(2)}) copy-start(f32[768]{0:T(1024)} %get-tuple-element.160) | copy-start | bytes 9220
  649.3 47.2 %copy-start.126 = (f32[768]{0:T(1024)S(1)}, f32[768]{0:T(1024)}, u32[]{:S(2)}) copy-start(f32[768]{0:T(1024)} %get-tuple-element.167) | copy-start | bytes 9220
  657.4 1.4 collective-permute-start.12
  658.8 3.8 collective-permute-start.13
  662.6 18.5 %collective-permute-start.14 = (f32[19968]{0:T(1024)S(1)}, f32[19968]{0:T(1024)S(1)}, u32[]{:S(2)}, u32[]{:S(2)}) collective-permute-start(f32[19968]{0:T(1024)S(1)} %add.464), channel_id=1, source_target_pairs={{0,8},{2,10},{4,12},{6,14},{8,0},{10,2},{12,4},{14,6},{16,24},{18,... | collective-permute-start | bytes 239624 | tf_op jit(solution)/shard_map/ppermute | solution.py:174
  681.1 12.9 %collective-permute-start.15 = (f32[19968]{0:T(1024)S(1)}, f32[19968]{0:T(1024)S(1)}, u32[]{:S(2)}, u32[]{:S(2)}) collective-permute-start(f32[19968]{0:T(1024)S(1)} %add.465), channel_id=1, source_target_pairs={{0,16},{2,18},{4,20},{6,22},{8,24},{10,26},{12,28},{14,30},{16,0},... | collective-permute-start | bytes 239624 | tf_op jit(solution)/shard_map/ppermute | solution.py:174
  694.0 4.6 collective-permute-start.16
  703.7 6.0 collective-permute-start.17
  711.4 27.8 %collective-permute-start.18 = (f32[384,768]{1,0:T(8,128)S(1)}, f32[384,768]{1,0:T(8,128)S(1)}, u32[]{:S(2)}, u32[]{:S(2)}) collective-permute-start(f32[384,768]{1,0:T(8,128)S(1)} %dynamic-slice_add_fusion.4), channel_id=1, source_target_pairs={{0,1},{1,0},{2,3},{3,2},{4,5},{5,4},{6,7},{7,6},{8,9},{9,8},{10,11... | collective-permute-start | bytes 3538952 | tf_op jit(solution)/shard_map/ppermute | solution.py:453
  739.3 3.5 collective-permute-start.19
  810.9 60.2 %all-to-all-start.13 = ((f32[16,48,768]{2,1,0:T(8,128)}), f32[16,48,768]{2,1,0:T(8,128)S(1)}, u32[]{:S(2)}, u32[]{:S(2)}) async-start(f32[16,48,768]{2,1,0:T(8,128)} %bitcast.319), calls=%async_computation.21 | async-start | bytes 4718592 | tf_op jit(solution)/shard_map/all_to_all | solution.py:479
  818.1 53.2 %copy-start.76 = (f32[2,3072]{1,0:T(2,128)}, f32[2,3072]{1,0:T(2,128)S(1)}, u32[]{:S(2)}) copy-start(f32[2,3072]{1,0:T(2,128)S(1)} %reshape.600) | copy-start | bytes 73732
  819.5 51.7 %copy-start.77 = (f32[2,4,768]{2,1,0:T(4,128)}, f32[2,4,768]{2,1,0:T(4,128)S(1)}, u32[]{:S(2)}) copy-start(f32[2,4,768]{2,1,0:T(4,128)S(1)} %reshape.598) | copy-start | bytes 73732
  819.6 51.7 %copy-start.86 = (f32[2,2,768]{2,1,0:T(2,128)}, f32[2,2,768]{2,1,0:T(2,128)S(1)}, u32[]{:S(2)}) copy-start(f32[2,2,768]{2,1,0:T(2,128)S(1)} %slice.448) | copy-start | bytes 36868
  (125 other events, 510.8 us)
Sparse Core Ops, SparseCore 0:
  10.9 54.1 all-gather.4
  146.1 18.1 reduce-scatter.8
  180.0 48.5 all-gather.6
  247.5 18.6 reduce-scatter.14
  269.3 18.6 reduce-scatter.12
  291.8 94.5 reduce-scatter.18
  431.1 97.4 reduce-scatter.16
  566.4 18.9 reduce-scatter.20
  587.7 17.5 reduce-scatter.22
  646.5 19.0 reduce-scatter.10

commit v5 on v2

--- a/solution.py
+++ b/solution.py
@@ -146,23 +146,6 @@
     return lax.all_gather(block, "dp", axis=axis, tiled=True)
 
 
-def a2a_gather(block, axis):
-    count = lax.axis_size("dp")
-    copies = jnp.broadcast_to(block[None], (count,) + block.shape)
-    got = lax.all_to_all(copies, "dp", split_axis=0, concat_axis=0, tiled=True)
-    got = jnp.moveaxis(got, 0, axis)
-    return got.reshape(block.shape[:axis] + (count * block.shape[axis],) + block.shape[axis + 1 :])
-
-
-def a2a_scatter(partial, dimension):
-    count = lax.axis_size("dp")
-    shape = partial.shape
-    chunks = partial.reshape(shape[:dimension] + (count, shape[dimension] // count) + shape[dimension + 1 :])
-    chunks = jnp.moveaxis(chunks, dimension, 0)
-    got = lax.all_to_all(chunks, "dp", split_axis=0, concat_axis=0, tiled=True)
-    return jnp.sum(got, axis=0)
-
-
 def swap_pairs(count, bit):
     return [(i, i ^ bit) for i in range(count)]
 
@@ -174,6 +157,105 @@
         flat = flat + lax.ppermute(flat, "dp", swap_pairs(count, bit))
         bit *= 2
     return flat + lax.ppermute(flat, "tensor", [(0, 1), (1, 0)])
+
+
+def tensor_swap(block):
+    return lax.ppermute(block, "tensor", [(0, 1), (1, 0)])
+
+
+def tensor_gather(block):
+    other = tensor_swap(block)
+    first = lax.axis_index("tensor") == 0
+    return jnp.where(
+        first, jnp.concatenate([block, other], axis=0), jnp.concatenate([other, block], axis=0)
+    )
+
+
+def tensor_scatter(partial):
+    rank = lax.axis_index("tensor")
+    half = partial.shape[0] // 2
+    mine = lax.dynamic_slice_in_dim(partial, rank * half, half, 0)
+    theirs = lax.dynamic_slice_in_dim(partial, (1 - rank) * half, half, 0)
+    return mine + tensor_swap(theirs)
+
+
+def unpack(flat_rows, shapes):
+    pieces = []
+    offset = 0
+    for shape in shapes:
+        size = math.prod(shape)
+        pieces.append(flat_rows[..., offset : offset + size].reshape(flat_rows.shape[:-1] + shape))
+        offset += size
+    return pieces
+
+
+def merge_axis(array, axis):
+    shape = array.shape
+    return array.reshape(shape[:axis] + (shape[axis] * shape[axis + 1],) + shape[axis + 2 :])
+
+
+def chip_gather_many(blocks, gather_axes, split_axes):
+    count = lax.axis_size("dp")
+    parity = lax.axis_index("dp") % 2
+    packed, shapes = [], []
+    for block, split_axis in zip(blocks, split_axes):
+        width = block.shape[split_axis] // 2
+        halves = jnp.stack(
+            [
+                lax.slice_in_dim(block, 0, width, axis=split_axis),
+                lax.slice_in_dim(block, width, 2 * width, axis=split_axis),
+            ]
+        )
+        shapes.append(halves.shape[1:])
+        packed.append(halves.reshape(2, -1))
+    packed = jnp.concatenate(packed, axis=1)
+    outgoing = jnp.tile(packed, (count // 2, 1))
+    got = lax.all_to_all(outgoing, "dp", split_axis=0, concat_axis=0, tiled=True)
+    mines = []
+    for piece, gather_axis in zip(unpack(got, shapes), gather_axes):
+        mines.append(merge_axis(jnp.moveaxis(piece, 0, gather_axis), gather_axis))
+    flat_mine = jnp.concatenate([mine.reshape(-1) for mine in mines])
+    flat_theirs = lax.ppermute(flat_mine, "dp", swap_pairs(count, 1))
+    results = []
+    for mine, theirs, split_axis in zip(mines, unpack(flat_theirs, [m.shape for m in mines]), split_axes):
+        results.append(
+            jnp.where(
+                parity == 0,
+                jnp.concatenate([mine, theirs], axis=split_axis),
+                jnp.concatenate([theirs, mine], axis=split_axis),
+            )
+        )
+    return results
+
+
+def chip_scatter_many(partials, scatter_axes, split_axes):
+    count = lax.axis_size("dp")
+    parity = lax.axis_index("dp") % 2
+    keeps, sends = [], []
+    for partial, split_axis in zip(partials, split_axes):
+        width = partial.shape[split_axis] // 2
+        keeps.append(lax.dynamic_slice_in_dim(partial, parity * width, width, split_axis))
+        sends.append(lax.dynamic_slice_in_dim(partial, (1 - parity) * width, width, split_axis))
+    flat_send = jnp.concatenate([send.reshape(-1) for send in sends])
+    flat_recv = lax.ppermute(flat_send, "dp", swap_pairs(count, 1))
+    packed, shapes = [], []
+    for keep, received, scatter_axis in zip(keeps, unpack(flat_recv, [k.shape for k in keeps]), scatter_axes):
+        chip_sum = keep + received
+        shape = chip_sum.shape
+        chunks = chip_sum.reshape(
+            shape[:scatter_axis] + (count, shape[scatter_axis] // count) + shape[scatter_axis + 1 :]
+        )
+        chunks = jnp.moveaxis(chunks, scatter_axis, 0)
+        shapes.append(chunks.shape[1:])
+        packed.append(chunks.reshape(count, -1))
+    got = lax.all_to_all(jnp.concatenate(packed, axis=1), "dp", split_axis=0, concat_axis=0, tiled=True)
+    results = []
+    for piece, split_axis in zip(unpack(got, shapes), split_axes):
+        piece = piece.reshape((count // 2, 2) + piece.shape[1:])
+        even = jnp.sum(piece[:, 0], axis=0)
+        odd = jnp.sum(piece[:, 1], axis=0)
+        results.append(jnp.concatenate([even, odd], axis=split_axis))
+    return results
 
 
 def vector_step(params, gradients):
@@ -209,20 +291,16 @@
     stream = block_input.astype(jnp.float32)
     saved_layers = []
     for layer_id in range(LAYERS):
-        layer_weights = (
-            a2a_gather(qkv_weight[layer_id], 0),
-            a2a_gather(proj_weight[layer_id], 1),
-            dp_gather(up_weight[layer_id], 0),
-            dp_gather(down_weight[layer_id], 1),
-        )
-        qkv_full, proj_full, up_full, down_full = layer_weights
+        up_full = dp_gather(up_weight[layer_id], 0)
+        qkv_full, proj_full, down_full = chip_gather_many(
+            (qkv_weight[layer_id], proj_weight[layer_id], down_weight[layer_id]), (0, 1, 1), (2, 0, 0)
+        )
+        layer_weights = (qkv_full, proj_full, up_full, down_full)
         normed, inverse = normalize(stream)
         attn_rows = (normed * norm_gains[layer_id, 0] + biases[layer_id, 0]).astype(jnp.bfloat16)
         mlp_rows = (normed * norm_gains[layer_id, 1] + biases[layer_id, 1]).astype(jnp.bfloat16)
-        attn_in, mlp_in = (
-            lax.all_gather(attn_rows, "tensor", axis=0, tiled=True),
-            lax.all_gather(mlp_rows, "tensor", axis=0, tiled=True),
-        )
+        both_in = tensor_gather(jnp.concatenate([attn_rows, mlp_rows], axis=1))
+        attn_in, mlp_in = both_in[:, :model_width], both_in[:, model_width:]
         length = attn_in.shape[0]
         qkv_local_bias = lax.dynamic_slice_in_dim(
             qkv_bias[layer_id], tensor_rank * local_width, local_width, 1
@@ -245,7 +323,7 @@
         partial_sum = jnp.dot(heads_flat, proj_full, preferred_element_type=jnp.float32) + jnp.dot(
             act_low, down_full, preferred_element_type=jnp.float32
         )
-        branch = lax.psum_scatter(partial_sum, "tensor", scatter_dimension=0, tiled=True)
+        branch = tensor_scatter(partial_sum)
         saved_layers.append(
             (
                 normed,
@@ -287,7 +365,7 @@
         qkv_full, proj_full, up_full, down_full = layer_weights
         length = attn_in.shape[0]
         out_bias_grad = jnp.sum(grad_stream, axis=0)
-        branch_grad = lax.all_gather(grad_stream.astype(jnp.bfloat16), "tensor", axis=0, tiled=True)
+        branch_grad = tensor_gather(grad_stream.astype(jnp.bfloat16))
         down_part = jnp.einsum(
             "lf,ld->fd", act_low, branch_grad, preferred_element_type=jnp.float32
         )
@@ -328,10 +406,8 @@
         attn_in_grad = jnp.einsum(
             "lcf,dcf->ld", qkv_pre_grad, qkv_full, preferred_element_type=jnp.float32
         )
-        attn_rows_grad, mlp_rows_grad = (
-            lax.psum_scatter(attn_in_grad, "tensor", scatter_dimension=0, tiled=True),
-            lax.psum_scatter(mlp_in_grad, "tensor", scatter_dimension=0, tiled=True),
-        )
+        both_grad = tensor_scatter(jnp.concatenate([attn_in_grad, mlp_in_grad], axis=1))
+        attn_rows_grad, mlp_rows_grad = both_grad[:, :model_width], both_grad[:, model_width:]
         gains_list[layer_id] = jnp.stack(
             [jnp.sum(attn_rows_grad * normed, axis=0), jnp.sum(mlp_rows_grad * normed, axis=0)]
         )
@@ -355,12 +431,8 @@
         normed_mean = jnp.mean(normed_grad, axis=-1, keepdims=True)
         product_mean = jnp.mean(normed_grad * normed, axis=-1, keepdims=True)
         grad_stream = grad_stream + inverse * (normed_grad - normed_mean - normed * product_mean)
-        weight_list[layer_id] = (
-            a2a_scatter(qkv_part, 0),
-            a2a_scatter(proj_part, 1),
-            dp_scatter(up_part, 0),
-            dp_scatter(down_part, 1),
-        )
+        qkv_sum, proj_sum, down_sum = chip_scatter_many((qkv_part, proj_part, down_part), (0, 1, 1), (2, 0, 0))
+        weight_list[layer_id] = (qkv_sum, proj_sum, dp_scatter(up_part, 0), down_sum)
     small_parts = (
         jnp.stack(gains_list),
         jnp.stack(biases_list),
@@ -402,6 +474,7 @@
     outgoing = jnp.concatenate(pieces, axis=0)
     owned = lax.all_to_all(outgoing, "dp", split_axis=0, concat_axis=0, tiled=True)
     owned = owned.reshape(dp_count * rows_local, piece_width)
+    owned, flat, grad_stream = lax.optimization_barrier((owned, flat, grad_stream))
     gram = jnp.dot(owned, owned.T, precision=ns_precision)
     bit = 1
     while bit < sub:
@@ -437,7 +510,7 @@
             )
     current = jnp.dot(accumulated, owned * scale, precision=ns_precision)
     returned = lax.all_to_all(
-        current.reshape(dp_count, rows_local, piece_width),
+        current.astype(jnp.bfloat16).reshape(dp_count, rows_local, piece_width),
         "dp",
         split_axis=0,
         concat_axis=0,
@@ -446,7 +519,12 @@
     my_rows = []
     for slot_id, mat in enumerate(slot_mats):
         width = mat.shape[1] // sub
-        my_rows.append(returned[slot_id, :, :, :width].transpose(1, 0, 2).reshape(rows_local, sub * width))
+        my_rows.append(
+            returned[slot_id, :, :, :width]
+            .astype(jnp.float32)
+            .transpose(1, 0, 2)
+            .reshape(rows_local, sub * width)
+        )
     muon_step = muon_rate * match_rms
     qkv_list, proj_list, up_list, down_list = ([], [], [], [])
     for layer_id in range(LAYERS):

time: 1010 us -> 1050 us (1.040)
  local copies, waits for them, and re-layouts: 79.1 us -> 392 us
  waiting for transfers between devices: 597 us -> 289 us
  other arithmetic: 50.3 us -> 155 us
  blocking collectives: 39.9 us -> 0 us
  matrix products: 152 us -> 133 us
    all_to_all x9 -> x5, waiting for transfers between devices: 340 us -> 219 us  [the longest x2 133 us: chip_scatter_many(): lax.all_to_all(jnp.concatenate(packed, axis=1), 'dp', split_axis=0, conca...]
    slice x3 -> x58, local copies, waits for them, and re-layouts: 2.52 us -> 80.6 us  [the longest x44 77.4 us: unpack(): flat_rows[..., offset:offset + size].reshape(flat_rows.shape[:-1] + shape)]
    reduce_scatter x4 -> x2, waiting for transfers between devices: 69.1 us -> 0.04 us  [dp_scatter(): lax.psum_scatter(partial, 'dp', scatter_dimension=dimension, tiled=True)]
    unnamed x293 -> x395, local copies, waits for them, and re-layouts: 20.9 us -> 77.8 us
    another operation x1 -> x29, local copies, waits for them, and re-layouts: 0.11 us -> 53.7 us  [the longest x6 18.3 us: chip_scatter_many(): piece = piece.reshape((count // 2, 2) + piece.shape[1:])]
    reshape x0 -> x16, local copies, waits for them, and re-layouts: none -> 52.5 us  [the longest x4 19.5 us: chip_scatter_many(): packed.append(chunks.reshape(count, -1))]
    all_to_all x1, waiting for transfers between devices: 48.8 us -> 0.01 us  [local(): lax.all_to_all(outgoing, 'dp', split_axis=0, concat_axis=0, tiled=True)]
    ppermute x4, waiting for transfers between devices: 51.6 us -> 7.42 us  [butterfly_sum(): flat = flat + lax.ppermute(flat, 'dp', swap_pairs(count, bit))]
  transfers between devices with their start and end apart: 32 -> 30, of which waited for: 18 -> 16; matrix products, arithmetic and copies ran while one was open for 17% -> 49% of each run, Pallas kernels for 0% -> 0%
where the time goes in v5:
time: 1050 us; the launch traced here: 1040 us
  local copies, waits for them, and re-layouts  392 us (37%)
  waiting for transfers between devices  289 us (28%)
  other arithmetic  155 us (15%)
  matrix products  133 us (13%)
  starting transfers between devices  57.1 us (5%)
  between operations  18.3 us (2%)
    all_to_all x2, waiting for transfers between devices, chip_scatter_many(): lax.all_to_all(jnp.concatenate(packed, axis=1), 'dp', split_axis=0, conca...  133 us
    unnamed x395, local copies, waits for them, and re-layouts  77.8 us
    slice x44, local copies, waits for them, and re-layouts, unpack(): flat_rows[..., offset:offset + size].reshape(flat_rows.shape[:-1] + shape)  77.4 us
    all_to_all x2, waiting for transfers between devices, chip_gather_many(): lax.all_to_all(outgoing, 'dp', split_axis=0, concat_axis=0, tiled=True)  64.3 us
    all_to_all x2, other arithmetic, chip_gather_many(): lax.all_to_all(outgoing, 'dp', split_axis=0, concat_axis=0, tiled=True)  32.3 us
    ppermute x8, waiting for transfers between devices, tensor_swap(): return lax.ppermute(block, 'tensor', [(0, 1), (1, 0)])  27.6 us
    ppermute x1, waiting for transfers between devices, local(): mine = mine + lax.ppermute(mine, 'tensor', [(0, 1), (1, 0)])  25.9 us
    transpose x8, local copies, waits for them, and re-layouts, chip_gather_many(): mines.append(merge_axis(jnp.moveaxis(piece, 0, gather_axis), gather_axis))  22.6 us
  transfers between devices with their start and end apart: 30, of which 16 were waited for; matrix products, arithmetic and copies ran while one was open for 49% of the time, Pallas kernels for 0%

profile of v5, /device:TPU:11, one launch (start us, length us, event | category | flops | bytes accessed | tf_op | source)
XLA Modules:
  0.0 1043.4 jit_solution(16417210675242903444)
XLA Ops:
  21.6 4.7 all_to_all.53
  26.8 15.4 %reduce.44 = bf16[16,73728]{1,0:T(8,128)(2,1)S(1)} reduce(bf16[16,1,73728]{2,1,0:T(2,128)(2,1)} %all_to_all.53, bf16[]{:T(256)} %broadcast.833), dimensions={1}, to_apply=%all_to_all.53.reduce_sub_computation | reduce | bytes 4718594 | tf_op jit(solution)/shard_map/all_to_all | solution.py:213
  45.3 7.1 all-to-all-start.1
  61.6 7.0 all_to_all.52
  68.6 16.8 %reduce.45 = bf16[16,73728]{1,0:T(8,128)(2,1)} reduce(bf16[16,1,73728]{2,1,0:T(2,128)(2,1)} %all_to_all.52, bf16[]{:T(256)} %broadcast.833), dimensions={1}, to_apply=%all_to_all.52.reduce_sub_computation | reduce | bytes 4718594 | tf_op jit(solution)/shard_map/all_to_all | solution.py:213
  85.5 4.4 reshape.773
  93.8 25.8 %all-to-all-done.1 = bf16[16,2,36864]{2,1,0:T(2,128)(2,1)S(1)} async-done(((bf16[16,2,36864]{2,1,0:T(2,128)(2,1)}), bf16[16,2,36864]{2,1,0:T(2,128)(2,1)S(1)}, u32[]{:S(2)}, u32[]{:S(2)}) %all-to-all-start.1) | async-done | bytes 2359328 | tf_op jit(solution)/shard_map/all_to_all | solution.py:213
  119.7 4.7 all-to-all-start
  124.8 7.0 reshape.776
  131.8 4.9 copy.602
  139.1 38.4 %all-to-all-done = bf16[16,2,36864]{2,1,0:T(2,128)(2,1)} async-done(((bf16[16,2,36864]{2,1,0:T(2,128)(2,1)}), bf16[16,2,36864]{2,1,0:T(2,128)(2,1)}, u32[]{:S(2)}, u32[]{:S(2)}) %all-to-all-start) | async-done | bytes 2359328 | tf_op jit(solution)/shard_map/all_to_all | solution.py:213
  177.5 10.7 %reshape.774 = bf16[16,1,73728]{2,1,0:T(2,128)(2,1)} reshape(bf16[16,2,36864]{2,1,0:T(2,128)(2,1)} %all-to-all-done) | data formatting | bytes 4718592
  188.2 4.9 copy.603
  199.8 4.4 reshape.712
  204.2 3.8 copy.488
  208.0 6.2 reshape_reshape.49
  224.5 5.4 reshape.705
  229.9 5.6 copy.471
  235.4 6.2 reshape_reshape.46
  241.7 4.5 pad_maximum_fusion.2
  246.3 13.2 %pad_maximum_fusion.3 = bf16[1179648]{0:T(1024)(128)(2,1)} fusion(bf16[589824]{0:T(1024)(128)(2,1)S(1)} %copy-done.16, bf16[147456]{0:T(1024)(128)(2,1)S(1)} %reshape_reshape.48, bf16[442368]{0:T(1024)(128)(2,1)S(1)} %bitcast.326), kind=kLoop, calls=%fused_computation.28 | loop fusion | flops 7077888 | bytes 4718592 | tf_op jit(solution)/shard_map/concatenate | solution.py:217
  261.7 4.2 copy.478
  265.9 4.0 reshape_reshape.44
  270.3 7.6 multiply_convert_fusion.3
  291.5 4.3 slice.593
  295.8 6.6 maximum_select_fusion
  343.1 4.5 maximum_select_fusion.2
  347.7 5.5 collective-permute-done.3
  384.2 5.6 multiply_convert_fusion.2
  408.1 4.0 fusion.145
  412.3 6.5 collective-permute-done.7
  425.4 6.1 pad_maximum_fusion.1
  460.2 6.8 pad_maximum_fusion
  490.4 4.5 copy.523
  506.6 4.0 copy.528
  510.5 7.9 reshape.732
  518.5 3.9 maximum_bitcast_fusion.1
  522.4 9.4 copy.529
  531.8 5.1 all-to-all-start.3
  553.6 4.5 copy.513
  569.4 4.0 copy.518
  573.4 7.6 reshape.725
  581.0 3.9 maximum_bitcast_fusion
  584.9 9.4 copy.519
  594.3 62.5 %all-to-all-done.3 = f32[16,1,73728]{2,1,0:T(1,128)} async-done(((f32[16,1,73728]{2,1,0:T(1,128)}), f32[16,1,73728]{2,1,0:T(1,128)}, u32[]{:S(2)}, u32[]{:S(2)}) %all-to-all-start.3) | async-done | bytes 4718624 | tf_op jit(solution)/shard_map/all_to_all | solution.py:251
  656.8 4.8 all-to-all-start.2
  666.4 5.1 copy.600
  680.1 5.9 reshape_reshape.57
  686.0 4.1 slice_reduce_fusion.1
  695.1 70.2 %all-to-all-done.2 = f32[16,1,73728]{2,1,0:T(1,128)} async-done(((f32[16,1,73728]{2,1,0:T(1,128)}), f32[16,1,73728]{2,1,0:T(1,128)}, u32[]{:S(2)}, u32[]{:S(2)}) %all-to-all-start.2) | async-done | bytes 4718624 | tf_op jit(solution)/shard_map/all_to_all | solution.py:251
  765.2 5.1 copy.601
  787.2 4.3 reshape_reshape.56
  801.3 6.8 concatenate.220
  810.9 5.1 all-to-all-start.4
  829.5 15.6 %collective-permute-done.11 = f32[128,1536]{1,0:T(8,128)} collective-permute-done((f32[128,1536]{1,0:T(8,128)}, f32[128,1536]{1,0:T(8,128)}, u32[]{:S(2)}, u32[]{:S(2)}) %collective-permute-start.11) | collective-permute-done | bytes 786464 | tf_op jit(solution)/shard_map/ppermute | solution.py:163
  875.7 4.4 fusion.253
  880.1 5.1 collective-permute-start.17
  885.3 4.5 collective-permute-done.17
  892.8 25.9 %collective-permute-done.18 = f32[384,768]{1,0:T(8,128)S(1)} collective-permute-done((f32[384,768]{1,0:T(8,128)S(1)}, f32[384,768]{1,0:T(8,128)S(1)}, u32[]{:S(2)}, u32[]{:S(2)}) %collective-permute-start.18) | collective-permute-done | bytes 1179680 | tf_op jit(solution)/shard_map/ppermute | solution.py:486
  927.8 9.1 fusion
  936.8 5.8 fusion.17
  992.7 4.1 fusion.53
  996.7 5.7 all-to-all-start.5
  1007.8 22.4 %all-to-all-done.5 = bf16[16,48,768]{2,1,0:T(8,128)(2,1)S(1)} async-done(((bf16[16,48,768]{2,1,0:T(8,128)(2,1)}), bf16[16,48,768]{2,1,0:T(8,128)(2,1)S(1)}, u32[]{:S(2)}, u32[]{:S(2)}) %all-to-all-start.5) | async-done | bytes 1179680 | tf_op jit(solution)/shard_map/all_to_all | solution.py:512
  (803 shorter events, 417.9 us)
Async XLA Ops:
  7.2 10.5 %copy-start.101 = (bf16[2,384,48]{1,2,0:T(8,128)(2,1)S(1)}, bf16[2,384,48]{1,2,0:T(8,128)(2,1)}, u32[]{:S(2)}) copy-start(bf16[2,384,48]{1,2,0:T(8,128)(2,1)} %param.19) | copy-start | bytes 221188
  7.2 11.1 %copy-start.110 = (bf16[2,48,3,384]{3,1,2,0:T(8,128)(2,1)S(1)}, bf16[2,48,3,384]{3,1,2,0:T(8,128)(2,1)}, u32[]{:S(2)}) copy-start(bf16[2,48,3,384]{3,1,2,0:T(8,128)(2,1)} %param.18) | copy-start | bytes 663556
  7.2 11.6 %copy-start.65 = (bf16[2,1536,48]{1,2,0:T(8,128)(2,1)S(1)}, bf16[2,1536,48]{1,2,0:T(8,128)(2,1)}, u32[]{:S(2)}) copy-start(bf16[2,1536,48]{1,2,0:T(8,128)(2,1)} %param.21) | copy-start | bytes 884740
  7.2 263.1 %all-gather.5.cloned.1.call-start = ((), (), s32[]{:S(2)}) async-start(), calls=%async_computation.10 | async-start | bytes 2506752 | tf_op jit(solution)/shard_map/all_gather | solution.py:146
  7.3 320.8 %collective-permute-start.6 = (bf16[128,768]{1,0:T(8,128)(2,1)}, bf16[128,768]{1,0:T(8,128)(2,1)}, u32[]{:S(2)}, u32[]{:S(2)}) collective-permute-start(bf16[128,768]{1,0:T(8,128)(2,1)} %param.16), channel_id=1, source_target_pairs={{0,1},{1,0},{2,3},{3,2},{4,5},{5,4},{6,7},{7,6},{8,9},{9,8},{10,11... | collective-permute-start | bytes 589832 | tf_op jit(solution)/shard_map/ppermute | solution.py:163
  17.4 74.1 %collective-permute-start = (bf16[128,1536]{1,0:T(8,128)(2,1)}, bf16[128,1536]{1,0:T(8,128)(2,1)}, u32[]{:S(2)}, u32[]{:S(2)}) collective-permute-start(bf16[128,1536]{1,0:T(8,128)(2,1)} %pad_maximum_fusion.12), channel_id=1, source_target_pairs={{0,1},{1,0},{2,3},{3,2},{4,5},{5,4},{6,7},{7,6},{8,9},{9,8},{10,11... | collective-permute-start | bytes 1179656 | tf_op jit(solution)/shard_map/ppermute | solution.py:163
  18.3 35.3 %copy-start.73 = (bf16[1,48,3,384]{3,1,2,0:T(8,128)(2,1)}, bf16[1,48,3,384]{3,1,2,0:T(8,128)(2,1)S(1)}, u32[]{:S(2)}) copy-start(bf16[1,48,3,384]{3,1,2,0:T(8,128)(2,1)S(1)} %get-tuple-element.272) | copy-start | bytes 331780
  45.3 74.4 %all-to-all-start.1 = ((bf16[16,2,36864]{2,1,0:T(2,128)(2,1)}), bf16[16,2,36864]{2,1,0:T(2,128)(2,1)S(1)}, u32[]{:S(2)}, u32[]{:S(2)}) async-start(bf16[16,2,36864]{2,1,0:T(2,128)(2,1)} %reshape.775), calls=%async_computation.1 | async-start | bytes 4718592 | tf_op jit(solution)/shard_map/all_to_all | solution.py:213
  52.4 331.8 %all-gather.7.cloned.1.call-start = ((), (), s32[]{:S(2)}) async-start(), calls=%async_computation.11 | async-start | bytes 2506752 | tf_op jit(solution)/shard_map/all_gather | solution.py:146
  119.7 57.8 %all-to-all-start = ((bf16[16,2,36864]{2,1,0:T(2,128)(2,1)}), bf16[16,2,36864]{2,1,0:T(2,128)(2,1)}, u32[]{:S(2)}, u32[]{:S(2)}) async-start(bf16[16,2,36864]{2,1,0:T(2,128)(2,1)} %reshape.773), calls=%async_computation | async-start | bytes 4718592 | tf_op jit(solution)/shard_map/all_to_all | solution.py:213
  124.4 537.3 %reduce-scatter.5.cloned.1.call-start = ((), (), s32[]{:S(2)}) async-start(), calls=%async_computation.9 | async-start | bytes 5013504 | tf_op jit(solution)/shard_map/reduce_scatter | solution.py:142
  246.2 31.7 %collective-permute-start.1 = (bf16[1179648]{0:T(1024)(128)(2,1)}, bf16[1179648]{0:T(1024)(128)(2,1)}, u32[]{:S(2)}, u32[]{:S(2)}) collective-permute-start(bf16[1179648]{0:T(1024)(128)(2,1)} %pad_maximum_fusion.2), channel_id=1, source_target_pairs={{0,2},{2,0},{4,6},{6,4},{8,10},{10,8},{12,14},{14,12},{16,18},{18,... | collective-permute-start | bytes 7077896 | tf_op jit(solution)/shard_map/ppermute | solution.py:218
  269.9 56.7 %collective-permute-start.4 = (bf16[1179648]{0:T(1024)(128)(2,1)}, bf16[1179648]{0:T(1024)(128)(2,1)}, u32[]{:S(2)}, u32[]{:S(2)}) collective-permute-start(bf16[1179648]{0:T(1024)(128)(2,1)} %pad_maximum_fusion.3), channel_id=1, source_target_pairs={{0,2},{2,0},{4,6},{6,4},{8,10},{10,8},{12,14},{14,12},{16,18},{18,... | collective-permute-start | bytes 7077896 | tf_op jit(solution)/shard_map/ppermute | solution.py:218
  281.0 31.7 %copy-start.105 = (bf16[192,768]{0,1:T(8,128)(2,1)}, bf16[192,768]{0,1:T(8,128)(2,1)S(1)}, u32[]{:S(2)}) copy-start(bf16[192,768]{0,1:T(8,128)(2,1)S(1)} %copy.476) | copy-start | bytes 884740
  317.3 23.4 %collective-permute-start.2 = (f32[128,768]{1,0:T(8,128)}, f32[128,768]{1,0:T(8,128)}, u32[]{:S(2)}, u32[]{:S(2)}) collective-permute-start(f32[128,768]{1,0:T(8,128)} %constant_dynamic-slice_fusion.9), channel_id=1, source_target_pairs={{0,1},{1,0},{2,3},{3,2},{4,5},{5,4},{6,7},{7,6},{8,9},{9,8},{10,11... | collective-permute-start | bytes 1179656 | tf_op jit(solution)/shard_map/ppermute | solution.py:163
  342.8 11.4 %copy-start.174 = (f32[1,3,384]{2,1,0:T(4,128)S(1)}, f32[1,3,384]{2,1,0:T(4,128)}, u32[]{:S(2)}) copy-start(f32[1,3,384]{2,1,0:T(4,128)} %copy.606) | copy-start | bytes 13828
  342.8 10.4 collective-permute-start.3
  359.2 9.9 copy-start.46
  384.1 12.4 %copy-start.26 = (f32[256,768]{1,0:T(8,128)}, f32[256,768]{1,0:T(8,128)S(1)}, u32[]{:S(2)}) copy-start(f32[256,768]{1,0:T(8,128)S(1)} %convolution_bitcast_fusion.1) | copy-start | bytes 2359300
  392.1 28.8 %collective-permute-start.5 = (f32[128,768]{1,0:T(8,128)}, f32[128,768]{1,0:T(8,128)}, u32[]{:S(2)}, u32[]{:S(2)}) collective-permute-start(f32[128,768]{1,0:T(8,128)} %constant_dynamic-slice_fusion.6), channel_id=1, source_target_pairs={{0,1},{1,0},{2,3},{3,2},{4,5},{5,4},{6,7},{7,6},{8,9},{9,8},{10,11... | collective-permute-start | bytes 1179656 | tf_op jit(solution)/shard_map/ppermute | solution.py:163
  397.6 21.1 %collective-permute-start.7 = (f32[128,1536]{1,0:T(8,128)}, f32[128,1536]{1,0:T(8,128)}, u32[]{:S(2)}, u32[]{:S(2)}) collective-permute-start(f32[128,1536]{1,0:T(8,128)} %fusion.116), channel_id=1, source_target_pairs={{0,1},{1,0},{2,3},{3,2},{4,5},{5,4},{6,7},{7,6},{8,9},{9,8},{10,11... | collective-permute-start | bytes 2359304 | tf_op jit(solution)/shard_map/ppermute | solution.py:163
  412.1 8.8 copy-start.86
  412.1 249.6 %reduce-scatter.3.cloned.1.call-start = ((), (), s32[]{:S(2)}) async-start(), calls=%async_computation.8 | async-start | bytes 5013504 | tf_op jit(solution)/shard_map/reduce_scatter | solution.py:142
  412.2 8.7 copy-start.81
  412.2 8.7 copy-start.159
  412.3 8.7 copy-start.160
  425.0 8.8 copy-start.104
  425.0 8.8 copy-start.106
  425.0 8.8 collective-permute-start.8
  431.5 42.3 %collective-permute-start.10 = (f32[1179648]{0:T(1024)}, f32[1179648]{0:T(1024)}, u32[]{:S(2)}, u32[]{:S(2)}) collective-permute-start(f32[1179648]{0:T(1024)} %pad_maximum_fusion.1), channel_id=1, source_target_pairs={{0,2},{2,0},{4,6},{6,4},{8,10},{10,8},{12,14},{14,12},{16,18},{18,... | collective-permute-start | bytes 14155784 | tf_op jit(solution)/shard_map/ppermute | solution.py:240
  467.0 70.0 %collective-permute-start.9 = (f32[1179648]{0:T(1024)}, f32[1179648]{0:T(1024)}, u32[]{:S(2)}, u32[]{:S(2)}) collective-permute-start(f32[1179648]{0:T(1024)} %pad_maximum_fusion), channel_id=1, source_target_pairs={{0,2},{2,0},{4,6},{6,4},{8,10},{10,8},{12,14},{14,12},{16,18},{18,... | collective-permute-start | bytes 14155784 | tf_op jit(solution)/shard_map/ppermute | solution.py:240
  531.8 124.9 %all-to-all-start.3 = ((f32[16,1,73728]{2,1,0:T(1,128)}), f32[16,1,73728]{2,1,0:T(1,128)}, u32[]{:S(2)}, u32[]{:S(2)}) async-start(f32[16,1,73728]{2,1,0:T(1,128)} %copy.529), calls=%async_computation.3 | async-start | bytes 9437184 | tf_op jit(solution)/shard_map/all_to_all | solution.py:251
  594.3 67.3 %copy-start.48 = (bf16[256,1,384]{2,0,1:T(8,128)(2,1)S(1)}, bf16[256,1,384]{2,0,1:T(8,128)(2,1)}, u32[]{:S(2)}) copy-start(bf16[256,1,384]{2,0,1:T(8,128)(2,1)} %copy-done.46) | copy-start | bytes 589828
  594.3 67.3 %copy-start.50 = (bf16[256,1,384]{2,0,1:T(8,128)(2,1)S(1)}, bf16[256,1,384]{2,0,1:T(8,128)(2,1)}, u32[]{:S(2)}) copy-start(bf16[256,1,384]{2,0,1:T(8,128)(2,1)} %copy-done.49) | copy-start | bytes 589828
  594.3 67.3 %copy-start.52 = (bf16[256,1,384]{2,0,1:T(8,128)(2,1)S(1)}, bf16[256,1,384]{2,0,1:T(8,128)(2,1)}, u32[]{:S(2)}) copy-start(bf16[256,1,384]{2,0,1:T(8,128)(2,1)} %copy-done.51) | copy-start | bytes 589828
  594.3 67.5 %copy-start.96 = (f32[2,48,1536]{2,1,0:T(8,128)S(1)}, f32[2,48,1536]{2,1,0:T(8,128)}, u32[]{:S(2)}) copy-start(f32[2,48,1536]{2,1,0:T(8,128)} %param.28) | copy-start | bytes 1769476
  656.8 108.5 %all-to-all-start.2 = ((f32[16,1,73728]{2,1,0:T(1,128)}), f32[16,1,73728]{2,1,0:T(1,128)}, u32[]{:S(2)}, u32[]{:S(2)}) async-start(f32[16,1,73728]{2,1,0:T(1,128)} %copy.519), calls=%async_computation.2 | async-start | bytes 9437184 | tf_op jit(solution)/shard_map/all_to_all | solution.py:251
  810.9 9.8 copy-start.165
  810.9 10.5 %copy-start.43 = (bf16[256,6,64]{0,2,1:T(8,128)(2,1)S(1)}, bf16[256,6,64]{0,2,1:T(8,128)(2,1)}, u32[]{:S(2)}) copy-start(bf16[256,6,64]{0,2,1:T(8,128)(2,1)} %copy-done.42) | copy-start | bytes 589828
  810.9 10.5 %copy-start.45 = (bf16[256,6,64]{0,2,1:T(8,128)(2,1)S(1)}, bf16[256,6,64]{0,2,1:T(8,128)(2,1)}, u32[]{:S(2)}) copy-start(bf16[256,6,64]{0,2,1:T(8,128)(2,1)} %copy-done.44) | copy-start | bytes 589828
  810.9 10.5 %copy-start.54 = (bf16[6,64,256]{2,1,0:T(8,128)(2,1)S(1)}, bf16[6,64,256]{2,1,0:T(8,128)(2,1)}, u32[]{:S(2)}) copy-start(bf16[6,64,256]{2,1,0:T(8,128)(2,1)} %copy-done.53) | copy-start | bytes 589828
  810.9 64.8 %all-to-all-start.4 = ((f32[16,48,768]{2,1,0:T(8,128)}), f32[16,48,768]{2,1,0:T(8,128)S(1)}, u32[]{:S(2)}, u32[]{:S(2)}) async-start(f32[16,48,768]{2,1,0:T(8,128)} %copy.538), calls=%async_computation.6 | async-start | bytes 4718592 | tf_op jit(solution)/shard_map/all_to_all | solution.py:475
  826.1 20.5 %copy-start.13 = (bf16[128,768]{1,0:T(8,128)(2,1)S(1)}, bf16[128,768]{1,0:T(8,128)(2,1)}, u32[]{:S(2)}) copy-start(bf16[128,768]{1,0:T(8,128)(2,1)} %param.15) | copy-start | bytes 589828
  826.1 20.5 %copy-start.145 = (f32[768]{0:T(1024)S(1)}, f32[768]{0:T(1024)}, u32[]{:S(2)}) copy-start(f32[768]{0:T(1024)} %copy-done.144) | copy-start | bytes 9220
  826.1 19.0 %collective-permute-start.11 = (f32[128,1536]{1,0:T(8,128)}, f32[128,1536]{1,0:T(8,128)}, u32[]{:S(2)}, u32[]{:S(2)}) collective-permute-start(f32[128,1536]{1,0:T(8,128)} %fusion.113), channel_id=1, source_target_pairs={{0,1},{1,0},{2,3},{3,2},{4,5},{5,4},{6,7},{7,6},{8,9},{9,8},{10,11... | collective-permute-start | bytes 2359304 | tf_op jit(solution)/shard_map/ppermute | solution.py:163
  829.5 43.8 %copy-start.25 = (f32[128,768]{1,0:T(8,128)S(1)}, f32[128,768]{1,0:T(8,128)}, u32[]{:S(2)}) copy-start(f32[128,768]{1,0:T(8,128)} %copy-done.24) | copy-start | bytes 1179652
  858.0 2.2 collective-permute-start.12
  860.2 3.7 collective-permute-start.13
  863.9 3.8 collective-permute-start.14
  867.7 4.4 collective-permute-start.15
  872.0 3.7 collective-permute-start.16
  880.1 9.6 collective-permute-start.17
  891.5 29.7 %copy-start.140 = (f32[2,3,768]{2,0,1:T(2,128)S(1)}, f32[2,3,768]{2,0,1:T(2,128)}, u32[]{:S(2)}) copy-start(f32[2,3,768]{2,0,1:T(2,128)} %param.24) | copy-start | bytes 55300
  891.5 27.2 %collective-permute-start.18 = (f32[384,768]{1,0:T(8,128)S(1)}, f32[384,768]{1,0:T(8,128)S(1)}, u32[]{:S(2)}, u32[]{:S(2)}) collective-permute-start(f32[384,768]{1,0:T(8,128)S(1)} %dynamic-slice_add_fusion.4), channel_id=1, source_target_pairs={{0,1},{1,0},{2,3},{3,2},{4,5},{5,4},{6,7},{7,6},{8,9},{9,8},{10,11... | collective-permute-start | bytes 3538952 | tf_op jit(solution)/shard_map/ppermute | solution.py:486
  919.9 4.0 collective-permute-start.19
  996.7 8.1 copy-start.120
  996.7 8.8 copy-start.122
  996.7 10.3 copy-start.41
  996.7 33.5 %all-to-all-start.5 = ((bf16[16,48,768]{2,1,0:T(8,128)(2,1)}), bf16[16,48,768]{2,1,0:T(8,128)(2,1)S(1)}, u32[]{:S(2)}, u32[]{:S(2)}) async-start(bf16[16,48,768]{2,1,0:T(8,128)(2,1)} %bitcast.323), calls=%async_computation.7 | async-start | bytes 2359296 | tf_op jit(solution)/shard_map/all_to_all | solution.py:512
  1003.1 27.7 %copy-start.119 = (f32[2,2,768]{2,1,0:T(2,128)}, f32[2,2,768]{2,1,0:T(2,128)S(1)}, u32[]{:S(2)}) copy-start(f32[2,2,768]{2,1,0:T(2,128)S(1)} %slice.708) | copy-start | bytes 36868
  1003.8 27.4 %copy-start.111 = (f32[2,3072]{1,0:T(2,128)}, f32[2,3072]{1,0:T(2,128)S(1)}, u32[]{:S(2)}) copy-start(f32[2,3072]{1,0:T(2,128)S(1)} %reshape.744) | copy-start | bytes 73732
  1003.8 27.4 %copy-start.112 = (f32[2,4,768]{2,1,0:T(4,128)}, f32[2,4,768]{2,1,0:T(4,128)S(1)}, u32[]{:S(2)}) copy-start(f32[2,4,768]{2,1,0:T(4,128)S(1)} %reshape.742) | copy-start | bytes 73732
  1007.0 24.6 %copy-start.72 = (bf16[1,48,3,384]{3,1,2,0:T(8,128)(2,1)S(1)}, bf16[1,48,3,384]{3,1,2,0:T(8,128)(2,1)}, u32[]{:S(2)}) copy-start(bf16[1,48,3,384]{3,1,2,0:T(8,128)(2,1)} %copy-done.71) | copy-start | bytes 331780
  1007.0 24.6 %copy-start.74 = (bf16[1,48,3,384]{3,1,2,0:T(8,128)(2,1)S(1)}, bf16[1,48,3,384]{3,1,2,0:T(8,128)(2,1)}, u32[]{:S(2)}) copy-start(bf16[1,48,3,384]{3,1,2,0:T(8,128)(2,1)} %copy-done.73) | copy-start | bytes 331780
  (152 other events, 483.3 us)
Sparse Core Ops, SparseCore 0:
  10.9 42.0 all-gather.4
  56.1 58.8 all-gather.6
  412.3 73.6 reduce-scatter.4
  489.7 134.6 reduce-scatter.2

commit v6 on v4

--- a/solution.py
+++ b/solution.py
@@ -146,23 +146,6 @@
     return lax.all_gather(block, "dp", axis=axis, tiled=True)
 
 
-def a2a_gather(block, axis):
-    count = lax.axis_size("dp")
-    copies = jnp.broadcast_to(block[None], (count,) + block.shape)
-    got = lax.all_to_all(copies, "dp", split_axis=0, concat_axis=0, tiled=True)
-    got = jnp.moveaxis(got, 0, axis)
-    return got.reshape(block.shape[:axis] + (count * block.shape[axis],) + block.shape[axis + 1 :])
-
-
-def a2a_scatter(partial, dimension):
-    count = lax.axis_size("dp")
-    shape = partial.shape
-    chunks = partial.reshape(shape[:dimension] + (count, shape[dimension] // count) + shape[dimension + 1 :])
-    chunks = jnp.moveaxis(chunks, dimension, 0)
-    got = lax.all_to_all(chunks, "dp", split_axis=0, concat_axis=0, tiled=True)
-    return jnp.sum(got, axis=0)
-
-
 def swap_pairs(count, bit):
     return [(i, i ^ bit) for i in range(count)]
 
@@ -174,6 +157,26 @@
         flat = flat + lax.ppermute(flat, "dp", swap_pairs(count, bit))
         bit *= 2
     return flat + lax.ppermute(flat, "tensor", [(0, 1), (1, 0)])
+
+
+def tensor_swap(block):
+    return lax.ppermute(block, "tensor", [(0, 1), (1, 0)])
+
+
+def tensor_gather(block):
+    other = tensor_swap(block)
+    first = lax.axis_index("tensor") == 0
+    return jnp.where(
+        first, jnp.concatenate([block, other], axis=0), jnp.concatenate([other, block], axis=0)
+    )
+
+
+def tensor_scatter(partial):
+    rank = lax.axis_index("tensor")
+    half = partial.shape[0] // 2
+    mine = lax.dynamic_slice_in_dim(partial, rank * half, half, 0)
+    theirs = lax.dynamic_slice_in_dim(partial, (1 - rank) * half, half, 0)
+    return mine + tensor_swap(theirs)
 
 
 def chip_gather(block, gather_axis, split_axis):
@@ -258,10 +261,8 @@
         normed, inverse = normalize(stream)
         attn_rows = (normed * norm_gains[layer_id, 0] + biases[layer_id, 0]).astype(jnp.bfloat16)
         mlp_rows = (normed * norm_gains[layer_id, 1] + biases[layer_id, 1]).astype(jnp.bfloat16)
-        attn_in, mlp_in = (
-            lax.all_gather(attn_rows, "tensor", axis=0, tiled=True),
-            lax.all_gather(mlp_rows, "tensor", axis=0, tiled=True),
-        )
+        both_in = tensor_gather(jnp.concatenate([attn_rows, mlp_rows], axis=1))
+        attn_in, mlp_in = both_in[:, :model_width], both_in[:, model_width:]
         length = attn_in.shape[0]
         qkv_local_bias = lax.dynamic_slice_in_dim(
             qkv_bias[layer_id], tensor_rank * local_width, local_width, 1
@@ -284,7 +285,7 @@
         partial_sum = jnp.dot(heads_flat, proj_full, preferred_element_type=jnp.float32) + jnp.dot(
             act_low, down_full, preferred_element_type=jnp.float32
         )
-        branch = lax.psum_scatter(partial_sum, "tensor", scatter_dimension=0, tiled=True)
+        branch = tensor_scatter(partial_sum)
         saved_layers.append(
             (
                 normed,
@@ -326,7 +327,7 @@
         qkv_full, proj_full, up_full, down_full = layer_weights
         length = attn_in.shape[0]
         out_bias_grad = jnp.sum(grad_stream, axis=0)
-        branch_grad = lax.all_gather(grad_stream.astype(jnp.bfloat16), "tensor", axis=0, tiled=True)
+        branch_grad = tensor_gather(grad_stream.astype(jnp.bfloat16))
         down_part = jnp.einsum(
             "lf,ld->fd", act_low, branch_grad, preferred_element_type=jnp.float32
         )
@@ -367,10 +368,8 @@
         attn_in_grad = jnp.einsum(
             "lcf,dcf->ld", qkv_pre_grad, qkv_full, preferred_element_type=jnp.float32
         )
-        attn_rows_grad, mlp_rows_grad = (
-            lax.psum_scatter(attn_in_grad, "tensor", scatter_dimension=0, tiled=True),
-            lax.psum_scatter(mlp_in_grad, "tensor", scatter_dimension=0, tiled=True),
-        )
+        both_grad = tensor_scatter(jnp.concatenate([attn_in_grad, mlp_in_grad], axis=1))
+        attn_rows_grad, mlp_rows_grad = both_grad[:, :model_width], both_grad[:, model_width:]
         gains_list[layer_id] = jnp.stack(
             [jnp.sum(attn_rows_grad * normed, axis=0), jnp.sum(mlp_rows_grad * normed, axis=0)]
         )
@@ -477,7 +476,7 @@
             )
     current = jnp.dot(accumulated, owned * scale, precision=ns_precision)
     returned = lax.all_to_all(
-        current.reshape(dp_count, rows_local, piece_width),
+        current.astype(jnp.bfloat16).reshape(dp_count, rows_local, piece_width),
         "dp",
         split_axis=0,
         concat_axis=0,
@@ -486,7 +485,12 @@
     my_rows = []
     for slot_id, mat in enumerate(slot_mats):
         width = mat.shape[1] // sub
-        my_rows.append(returned[slot_id, :, :, :width].transpose(1, 0, 2).reshape(rows_local, sub * width))
+        my_rows.append(
+            returned[slot_id, :, :, :width]
+            .astype(jnp.float32)
+            .transpose(1, 0, 2)
+            .reshape(rows_local, sub * width)
+        )
     muon_step = muon_rate * match_rms
     qkv_list, proj_list, up_list, down_list = ([], [], [], [])
     for layer_id in range(LAYERS):

time: 896 us -> 873 us (0.974)
  blocking collectives: 40.8 us -> 0 us
  waiting for transfers between devices: 425 us -> 440 us
  matrix products: 157 us -> 143 us
  starting transfers between devices: 91.3 us -> 101 us
    ppermute x0 -> x8, waiting for transfers between devices: none -> 52.8 us  [tensor_swap(): return lax.ppermute(block, 'tensor', [(0, 1), (1, 0)])]
    all_gather x6 -> x0, blocking collectives: 40.8 us -> none  [the longest x2 13.9 us: local(): lax.all_gather(grad_stream.astype(jnp.bfloat16), 'tensor', axis=0, tiled=...]
    all_to_all x1, waiting for transfers between devices: 49.1 us -> 24 us  [local(): lax.all_to_all(current.astype(jnp.bfloat16).reshape(dp_count, rows_local,...]
    ppermute x4, waiting for transfers between devices: 33 us -> 16.6 us  [butterfly_sum(): flat = flat + lax.ppermute(flat, 'dp', swap_pairs(count, bit))]
    all_to_all x6, waiting for transfers between devices: 212 us -> 228 us  [chip_scatter(): got = lax.all_to_all(chunks, 'dp', split_axis=0, concat_axis=0, tiled=True)]
    all_to_all x6, waiting for transfers between devices: 93.2 us -> 81.6 us  [chip_gather(): lax.all_to_all(outgoing, 'dp', split_axis=0, concat_axis=0, tiled=True)]
    unnamed x295 -> x351, local copies, waits for them, and re-layouts: 19.3 us -> 23 us
  transfers between devices with their start and end apart: 44 -> 46, of which waited for: 20 -> 26; matrix products, arithmetic and copies ran while one was open for 23% -> 22% of each run, Pallas kernels for 0% -> 0%
where the time goes in v6:
time: 873 us; the launch traced here: 863 us
  waiting for transfers between devices  440 us (50%)
  matrix products  143 us (16%)
  local copies, waits for them, and re-layouts  101 us (12%)
  starting transfers between devices  101 us (12%)
  other arithmetic  60.9 us (7%)
  between operations  17.6 us (2%)
    all_to_all x6, waiting for transfers between devices, chip_scatter(): got = lax.all_to_all(chunks, 'dp', split_axis=0, concat_axis=0, tiled=True)  228 us
    all_to_all x6, waiting for transfers between devices, chip_gather(): lax.all_to_all(outgoing, 'dp', split_axis=0, concat_axis=0, tiled=True)  81.6 us
    ppermute x8, waiting for transfers between devices, tensor_swap(): return lax.ppermute(block, 'tensor', [(0, 1), (1, 0)])  52.8 us
    all_to_all x6, starting transfers between devices, chip_scatter(): got = lax.all_to_all(chunks, 'dp', split_axis=0, concat_axis=0, tiled=True)  30.7 us
    all_to_all x6, starting transfers between devices, chip_gather(): lax.all_to_all(outgoing, 'dp', split_axis=0, concat_axis=0, tiled=True)  30.6 us
    ppermute x1, waiting for transfers between devices, local(): mine = mine + lax.ppermute(mine, 'tensor', [(0, 1), (1, 0)])  25.9 us
    all_to_all x1, waiting for transfers between devices, local(): lax.all_to_all(current.astype(jnp.bfloat16).reshape(dp_count, rows_local,...  24 us
    unnamed x351, local copies, waits for them, and re-layouts  23 us
  transfers between devices with their start and end apart: 46, of which 26 were waited for; matrix products, arithmetic and copies ran while one was open for 22% of the time, Pallas kernels for 0%

profile of v6, /device:TPU:11, one launch (start us, length us, event | category | flops | bytes accessed | tf_op | source)
XLA Modules:
  0.0 863.5 jit_solution(16799371407399414163)
XLA Ops:
  10.8 6.5 all-to-all-start.1
  18.8 14.0 %all-to-all-done.1 = bf16[16,192,48]{1,2,0:T(8,128)(2,1)} async-done(((bf16[16,192,48]{1,2,0:T(8,128)(2,1)}), bf16[16,192,48]{1,2,0:T(8,128)(2,1)}, u32[]{:S(2)}, u32[]{:S(2)}) %all-to-all-start.1) | async-done | bytes 294944 | tf_op jit(solution)/shard_map/all_to_all | solution.py:190
  33.8 4.3 all-to-all-start
  43.4 31.9 %all-to-all-done = bf16[16,48,3,192]{3,1,2,0:T(8,128)(2,1)S(1)} async-done(((bf16[16,48,3,192]{3,1,2,0:T(8,128)(2,1)}), bf16[16,48,3,192]{3,1,2,0:T(8,128)(2,1)S(1)}, u32[]{:S(2)}, u32[]{:S(2)}) %all-to-all-start) | async-done | bytes 884768 | tf_op jit(solution)/shard_map/all_to_all | solution.py:190
  76.4 5.0 all-to-all-start.2
  89.2 20.1 %all-to-all-done.2 = bf16[16,768,48]{1,2,0:T(8,128)(2,1)} async-done(((bf16[16,768,48]{1,2,0:T(8,128)(2,1)}), bf16[16,768,48]{1,2,0:T(8,128)(2,1)}, u32[]{:S(2)}, u32[]{:S(2)}) %all-to-all-start.2) | async-done | bytes 1179680 | tf_op jit(solution)/shard_map/all_to_all | solution.py:190
  110.1 4.7 all-to-all-start.4
  117.6 3.2 convolution_add_fusion.3
  127.7 5.3 all-to-all-start.3
  133.1 7.3 multiply_convert_fusion.3
  140.4 3.5 fusion.128
  146.9 13.8 %all-to-all-done.3 = bf16[16,48,3,192]{3,1,2,0:T(8,128)(2,1)S(1)} async-done(((bf16[16,48,3,192]{3,1,2,0:T(8,128)(2,1)}), bf16[16,48,3,192]{3,1,2,0:T(8,128)(2,1)S(1)}, u32[]{:S(2)}, u32[]{:S(2)}) %all-to-all-start.3) | async-done | bytes 884768 | tf_op jit(solution)/shard_map/all_to_all | solution.py:190
  161.8 4.7 all-to-all-start.5
  174.1 4.9 collective-permute-done.4
  185.1 11.1 %collective-permute-done.10 = bf16[128,768]{1,0:T(8,128)(2,1)S(1)} collective-permute-done((bf16[128,768]{1,0:T(8,128)(2,1)S(1)}, bf16[128,768]{1,0:T(8,128)(2,1)S(1)}, u32[]{:S(2)}, u32[]{:S(2)}) %collective-permute-start.10) | collective-permute-done | bytes 196640 | tf_op jit(solution)/shard_map/ppermute | solution.py:163
  205.8 4.1 convolution_add_fusion.2
  236.6 5.8 multiply_convert_fusion.2
  242.4 4.8 convert_reduce_fusion
  249.5 3.2 fusion.126
  255.1 12.1 %collective-permute-done.11 = f32[128,1536]{1,0:T(8,128)S(1)} collective-permute-done((f32[128,1536]{1,0:T(8,128)S(1)}, f32[128,1536]{1,0:T(8,128)S(1)}, u32[]{:S(2)}, u32[]{:S(2)}) %collective-permute-start.11) | collective-permute-done | bytes 786464 | tf_op jit(solution)/shard_map/ppermute | solution.py:163
  268.2 7.4 collective-permute-done.9
  281.7 6.9 all-to-all-start.9
  295.8 12.0 %all-to-all-done.9 = f32[16,192,48]{1,2,0:T(8,128)S(1)} async-done(((f32[16,192,48]{1,2,0:T(8,128)}), f32[16,192,48]{1,2,0:T(8,128)S(1)}, u32[]{:S(2)}, u32[]{:S(2)}) %all-to-all-start.9) | async-done | bytes 589856 | tf_op jit(solution)/shard_map/all_to_all | solution.py:214
  307.9 4.8 all-to-all-start.8
  320.4 3.2 copy.258
  323.7 8.3 all-to-all-done.8
  332.0 4.8 all-to-all-start.7
  351.8 57.2 %all-to-all-done.7 = f32[16,48,3,192]{3,1,2,0:T(8,128)} async-done(((f32[16,48,3,192]{3,1,2,0:T(8,128)}), f32[16,48,3,192]{3,1,2,0:T(8,128)}, u32[]{:S(2)}, u32[]{:S(2)}) %all-to-all-start.7) | async-done | bytes 1769504 | tf_op jit(solution)/shard_map/all_to_all | solution.py:214
  409.0 4.7 all-to-all-start.6
  417.9 4.5 collective-permute-done.18
  422.4 4.2 dynamic-slice_add_fusion
  426.6 47.8 %all-to-all-done.6 = f32[16,48,3,192]{3,1,2,0:T(8,128)S(1)} async-done(((f32[16,48,3,192]{3,1,2,0:T(8,128)}), f32[16,48,3,192]{3,1,2,0:T(8,128)S(1)}, u32[]{:S(2)}, u32[]{:S(2)}) %all-to-all-start.6) | async-done | bytes 1769504 | tf_op jit(solution)/shard_map/all_to_all | solution.py:214
  474.4 4.9 all-to-all-start.11
  484.5 4.6 convert_reduce_fusion.1
  493.0 4.1 dynamic-slice_add_fusion.1
  497.0 52.6 %all-to-all-done.11 = f32[16,768,48]{1,2,0:T(8,128)} async-done(((f32[16,768,48]{1,2,0:T(8,128)}), f32[16,768,48]{1,2,0:T(8,128)}, u32[]{:S(2)}, u32[]{:S(2)}) %all-to-all-start.11) | async-done | bytes 2359328 | tf_op jit(solution)/shard_map/all_to_all | solution.py:214
  549.6 4.5 all-to-all-start.10
  565.8 50.5 %all-to-all-done.10 = f32[16,768,48]{1,2,0:T(8,128)} async-done(((f32[16,768,48]{1,2,0:T(8,128)}), f32[16,768,48]{1,2,0:T(8,128)}, u32[]{:S(2)}, u32[]{:S(2)}) %all-to-all-start.10) | async-done | bytes 2359328 | tf_op jit(solution)/shard_map/all_to_all | solution.py:214
  626.3 7.0 concatenate.182
  636.3 5.2 all-to-all-start.12
  646.9 3.6 convolution_bitcast_fusion
  654.1 17.2 %collective-permute-done.19 = f32[128,1536]{1,0:T(8,128)} collective-permute-done((f32[128,1536]{1,0:T(8,128)}, f32[128,1536]{1,0:T(8,128)}, u32[]{:S(2)}, u32[]{:S(2)}) %collective-permute-start.19) | collective-permute-done | bytes 786464 | tf_op jit(solution)/shard_map/ppermute | solution.py:163
  675.9 6.8 collective-permute-done.21
  682.8 5.9 collective-permute-done.22
  688.8 5.4 collective-permute-start.23
  701.1 4.4 fusion.248
  707.2 4.5 collective-permute-done.25
  714.8 25.9 %collective-permute-done.26 = f32[384,768]{1,0:T(8,128)S(1)} collective-permute-done((f32[384,768]{1,0:T(8,128)S(1)}, f32[384,768]{1,0:T(8,128)S(1)}, u32[]{:S(2)}, u32[]{:S(2)}) %collective-permute-start.26) | collective-permute-done | bytes 1179680 | tf_op jit(solution)/shard_map/ppermute | solution.py:452
  749.5 7.1 fusion
  756.6 5.0 fusion.17
  761.6 3.2 fusion.249
  768.0 3.3 fusion.35
  771.3 3.4 fusion.39
  774.8 3.4 fusion.37
  781.3 3.6 fusion.33
  785.0 3.3 fusion.29
  788.3 3.4 fusion.31
  794.8 3.4 fusion.27
  798.2 3.3 fusion.23
  801.6 3.3 fusion.25
  808.1 3.6 fusion.5
  811.7 4.1 fusion.53
  815.8 6.9 all-to-all-start.13
  826.4 24.0 %all-to-all-done.13 = bf16[16,48,768]{2,1,0:T(8,128)(2,1)S(1)} async-done(((bf16[16,48,768]{2,1,0:T(8,128)(2,1)}), bf16[16,48,768]{2,1,0:T(8,128)(2,1)S(1)}, u32[]{:S(2)}, u32[]{:S(2)}) %all-to-all-start.13) | async-done | bytes 1179680 | tf_op jit(solution)/shard_map/all_to_all | solution.py:478
  (681 shorter events, 217.9 us)
Async XLA Ops:
  7.2 125.9 %all-gather.5.cloned.1.call-start = ((), (), s32[]{:S(2)}) async-start(), calls=%async_computation.18 | async-start | bytes 2506752 | tf_op jit(solution)/shard_map/all_gather | solution.py:146
  10.8 21.9 %all-to-all-start.1 = ((bf16[16,192,48]{1,2,0:T(8,128)(2,1)}), bf16[16,192,48]{1,2,0:T(8,128)(2,1)}, u32[]{:S(2)}, u32[]{:S(2)}) async-start(bf16[16,192,48]{1,2,0:T(8,128)(2,1)} %bitcast.15), calls=%async_computation.1 | async-start | bytes 786432 | tf_op jit(solution)/shard_map/all_to_all | solution.py:190
  17.5 24.8 %copy-start.52 = (bf16[1,48,3,384]{3,1,2,0:T(8,128)(2,1)}, bf16[1,48,3,384]{3,1,2,0:T(8,128)(2,1)S(1)}, u32[]{:S(2)}) copy-start(bf16[1,48,3,384]{3,1,2,0:T(8,128)(2,1)S(1)} %get-tuple-element.245) | copy-start | bytes 331780
  18.5 20.9 %copy-start.152 = (f32[128]{0:T(128)}, f32[128]{0:T(128)S(1)}, u32[]{:S(2)}) copy-start(f32[128]{0:T(128)S(1)} %broadcast_multiply_fusion.5) | copy-start | bytes 1540
  18.7 20.7 %copy-start.158 = (f32[128]{0:T(128)}, f32[128]{0:T(128)S(1)}, u32[]{:S(2)}) copy-start(f32[128]{0:T(128)S(1)} %add_rsqrt_fusion.1) | copy-start | bytes 1540
  33.8 41.5 %all-to-all-start = ((bf16[16,48,3,192]{3,1,2,0:T(8,128)(2,1)}), bf16[16,48,3,192]{3,1,2,0:T(8,128)(2,1)S(1)}, u32[]{:S(2)}, u32[]{:S(2)}) async-start(bf16[16,48,3,192]{3,1,2,0:T(8,128)(2,1)} %bitcast.4), calls=%async_computation | async-start | bytes 2359296 | tf_op jit(solution)/shard_map/all_to_all | solution.py:190
  40.4 47.3 %collective-permute-start = (bf16[128,1536]{1,0:T(8,128)(2,1)}, bf16[128,1536]{1,0:T(8,128)(2,1)}, u32[]{:S(2)}, u32[]{:S(2)}) collective-permute-start(bf16[128,1536]{1,0:T(8,128)(2,1)} %pad_maximum_fusion.8), channel_id=1, source_target_pairs={{0,1},{1,0},{2,3},{3,2},{4,5},{5,4},{6,7},{7,6},{8,9},{9,8},{10,11... | collective-permute-start | bytes 1179656 | tf_op jit(solution)/shard_map/ppermute | solution.py:163
  43.4 38.3 %copy-start.120 = (f32[2,3,768]{2,0,1:T(2,128)S(1)}, f32[2,3,768]{2,0,1:T(2,128)}, u32[]{:S(2)}) copy-start(f32[2,3,768]{2,0,1:T(2,128)} %param.24) | copy-start | bytes 55300
  43.4 38.9 %copy-start.102 = (f32[2,3072]{1,0:T(2,128)S(1)}, f32[2,3072]{1,0:T(2,128)}, u32[]{:S(2)}) copy-start(f32[2,3072]{1,0:T(2,128)} %param.25) | copy-start | bytes 73732
  76.4 32.9 %all-to-all-start.2 = ((bf16[16,768,48]{1,2,0:T(8,128)(2,1)}), bf16[16,768,48]{1,2,0:T(8,128)(2,1)}, u32[]{:S(2)}, u32[]{:S(2)}) async-start(bf16[16,768,48]{1,2,0:T(8,128)(2,1)} %bitcast.20), calls=%async_computation.2 | async-start | bytes 2359296 | tf_op jit(solution)/shard_map/all_to_all | solution.py:190
  83.0 34.5 %copy-start.10 = (bf16[16,48,3,192]{3,1,0,2:T(8,128)(2,1)}, bf16[16,48,3,192]{3,1,0,2:T(8,128)(2,1)S(1)}, u32[]{:S(2)}) copy-start(bf16[16,48,3,192]{3,1,0,2:T(8,128)(2,1)S(1)} %copy.229) | copy-start | bytes 2654212
  84.5 30.7 %collective-permute-start.1 = (bf16[768,3,192]{0,2,1:T(8,128)(2,1)}, bf16[768,3,192]{0,2,1:T(8,128)(2,1)}, u32[]{:S(2)}, u32[]{:S(2)}) collective-permute-start(bf16[768,3,192]{0,2,1:T(8,128)(2,1)} %copy.230), channel_id=1, source_target_pairs={{0,2},{2,0},{4,6},{6,4},{8,10},{10,8},{12,14},{14,12},{16,18},{18,... | collective-permute-start | bytes 2654216 | tf_op jit(solution)/shard_map/ppermute | solution.py:194
  89.0 31.7 %copy-start.14 = (bf16[256,1536]{1,0:T(8,128)(2,1)}, bf16[256,1536]{1,0:T(8,128)(2,1)S(1)}, u32[]{:S(2)}) copy-start(bf16[256,1536]{1,0:T(8,128)(2,1)S(1)} %maximum_select_fusion.5) | copy-start | bytes 2359300
  89.0 54.9 %collective-permute-start.2 = (bf16[192,768]{0,1:T(8,128)(2,1)}, bf16[192,768]{0,1:T(8,128)(2,1)}, u32[]{:S(2)}, u32[]{:S(2)}) collective-permute-start(bf16[192,768]{0,1:T(8,128)(2,1)} %bitcast.17), channel_id=1, source_target_pairs={{0,2},{2,0},{4,6},{6,4},{8,10},{10,8},{12,14},{14,12},{16,18},{18,... | collective-permute-start | bytes 884744 | tf_op jit(solution)/shard_map/ppermute | solution.py:194
  110.1 15.6 %all-to-all-start.4 = ((bf16[16,192,48]{1,2,0:T(8,128)(2,1)}), bf16[16,192,48]{1,2,0:T(8,128)(2,1)}, u32[]{:S(2)}, u32[]{:S(2)}) async-start(bf16[16,192,48]{1,2,0:T(8,128)(2,1)} %bitcast.36), calls=%async_computation.4 | async-start | bytes 786432 | tf_op jit(solution)/shard_map/all_to_all | solution.py:190
  114.8 25.6 %collective-permute-start.3 = (bf16[768,768]{0,1:T(8,128)(2,1)}, bf16[768,768]{0,1:T(8,128)(2,1)}, u32[]{:S(2)}, u32[]{:S(2)}) collective-permute-start(bf16[768,768]{0,1:T(8,128)(2,1)} %bitcast.22), channel_id=1, source_target_pairs={{0,2},{2,0},{4,6},{6,4},{8,10},{10,8},{12,14},{14,12},{16,18},{18,... | collective-permute-start | bytes 3538952 | tf_op jit(solution)/shard_map/ppermute | solution.py:194
  127.7 33.0 %all-to-all-start.3 = ((bf16[16,48,3,192]{3,1,2,0:T(8,128)(2,1)}), bf16[16,48,3,192]{3,1,2,0:T(8,128)(2,1)S(1)}, u32[]{:S(2)}, u32[]{:S(2)}) async-start(bf16[16,48,3,192]{3,1,2,0:T(8,128)(2,1)} %bitcast.310), calls=%async_computation.3 | async-start | bytes 2359296 | tf_op jit(solution)/shard_map/all_to_all | solution.py:190
  161.8 37.3 %all-to-all-start.5 = ((bf16[16,768,48]{1,2,0:T(8,128)(2,1)}), bf16[16,768,48]{1,2,0:T(8,128)(2,1)}, u32[]{:S(2)}, u32[]{:S(2)}) async-start(bf16[16,768,48]{1,2,0:T(8,128)(2,1)} %bitcast.41), calls=%async_computation.5 | async-start | bytes 2359296 | tf_op jit(solution)/shard_map/all_to_all | solution.py:190
  166.5 70.0 %all-gather.7.cloned.1.call-start = ((), (), s32[]{:S(2)}) async-start(), calls=%async_computation.19 | async-start | bytes 2506752 | tf_op jit(solution)/shard_map/all_gather | solution.py:146
  168.6 10.5 %collective-permute-start.4 = (f32[128,768]{1,0:T(8,128)}, f32[128,768]{1,0:T(8,128)S(1)}, u32[]{:S(2)}, u32[]{:S(2)}) collective-permute-start(f32[128,768]{1,0:T(8,128)} %constant_dynamic-slice_fusion.9), channel_id=1, source_target_pairs={{0,1},{1,0},{2,3},{3,2},{4,5},{5,4},{6,7},{7,6},{8,9},{9,8},{10,11... | collective-permute-start | bytes 1179656 | tf_op jit(solution)/shard_map/ppermute | solution.py:163
  169.9 26.3 %collective-permute-start.7 = (bf16[192,768]{0,1:T(8,128)(2,1)}, bf16[192,768]{0,1:T(8,128)(2,1)}, u32[]{:S(2)}, u32[]{:S(2)}) collective-permute-start(bf16[192,768]{0,1:T(8,128)(2,1)} %bitcast.38), channel_id=1, source_target_pairs={{0,2},{2,0},{4,6},{6,4},{8,10},{10,8},{12,14},{14,12},{16,18},{18,... | collective-permute-start | bytes 884744 | tf_op jit(solution)/shard_map/ppermute | solution.py:194
  174.1 27.1 %collective-permute-start.6 = (bf16[768,3,192]{0,2,1:T(8,128)(2,1)}, bf16[768,3,192]{0,2,1:T(8,128)(2,1)}, u32[]{:S(2)}, u32[]{:S(2)}) collective-permute-start(bf16[768,3,192]{0,2,1:T(8,128)(2,1)} %copy.238), channel_id=1, source_target_pairs={{0,2},{2,0},{4,6},{6,4},{8,10},{10,8},{12,14},{14,12},{16,18},{18,... | collective-permute-start | bytes 2654216 | tf_op jit(solution)/shard_map/ppermute | solution.py:194
  182.4 21.2 %collective-permute-start.5 = (bf16[128,1536]{1,0:T(8,128)(2,1)}, bf16[128,1536]{1,0:T(8,128)(2,1)}, u32[]{:S(2)}, u32[]{:S(2)}) collective-permute-start(bf16[128,1536]{1,0:T(8,128)(2,1)} %pad_maximum_fusion.9), channel_id=1, source_target_pairs={{0,1},{1,0},{2,3},{3,2},{4,5},{5,4},{6,7},{7,6},{8,9},{9,8},{10,11... | collective-permute-start | bytes 1179656 | tf_op jit(solution)/shard_map/ppermute | solution.py:163
  183.7 12.5 %collective-permute-start.10 = (bf16[128,768]{1,0:T(8,128)(2,1)S(1)}, bf16[128,768]{1,0:T(8,128)(2,1)S(1)}, u32[]{:S(2)}, u32[]{:S(2)}) collective-permute-start(bf16[128,768]{1,0:T(8,128)(2,1)S(1)} %copy-done.60), channel_id=1, source_target_pairs={{0,1},{1,0},{2,3},{3,2},{4,5},{5,4},{6,7},{7,6},{8,9},{9,8},{10,11... | collective-permute-start | bytes 589832 | tf_op jit(solution)/shard_map/ppermute | solution.py:163
  199.1 43.2 %collective-permute-start.8 = (bf16[768,768]{0,1:T(8,128)(2,1)}, bf16[768,768]{0,1:T(8,128)(2,1)}, u32[]{:S(2)}, u32[]{:S(2)}) collective-permute-start(bf16[768,768]{0,1:T(8,128)(2,1)} %bitcast.43), channel_id=1, source_target_pairs={{0,2},{2,0},{4,6},{6,4},{8,10},{10,8},{12,14},{14,12},{16,18},{18,... | collective-permute-start | bytes 3538952 | tf_op jit(solution)/shard_map/ppermute | solution.py:194
  229.7 49.7 %collective-permute-start.16 = (f32[192,768]{1,0:T(8,128)}, f32[192,768]{1,0:T(8,128)}, u32[]{:S(2)}, u32[]{:S(2)}) collective-permute-start(f32[192,768]{1,0:T(8,128)} %constant_dynamic-slice_fusion.2), channel_id=1, source_target_pairs={{0,2},{2,0},{4,6},{6,4},{8,10},{10,8},{12,14},{14,12},{16,18},{18,... | collective-permute-start | bytes 1769480 | tf_op jit(solution)/shard_map/ppermute | solution.py:208
  236.1 80.1 %collective-permute-start.14 = (f32[768,3,192]{0,2,1:T(8,128)}, f32[768,3,192]{0,2,1:T(8,128)}, u32[]{:S(2)}, u32[]{:S(2)}) collective-permute-start(f32[768,3,192]{0,2,1:T(8,128)} %constant_dynamic-slice_fusion.4), channel_id=1, source_target_pairs={{0,2},{2,0},{4,6},{6,4},{8,10},{10,8},{12,14},{14,12},{16,18},{18,... | collective-permute-start | bytes 5308424 | tf_op jit(solution)/shard_map/ppermute | solution.py:208
  248.1 19.1 %collective-permute-start.11 = (f32[128,1536]{1,0:T(8,128)S(1)}, f32[128,1536]{1,0:T(8,128)S(1)}, u32[]{:S(2)}, u32[]{:S(2)}) collective-permute-start(f32[128,1536]{1,0:T(8,128)S(1)} %fusion.112), channel_id=1, source_target_pairs={{0,1},{1,0},{2,3},{3,2},{4,5},{5,4},{6,7},{7,6},{8,9},{9,8},{10,11... | collective-permute-start | bytes 2359304 | tf_op jit(solution)/shard_map/ppermute | solution.py:163
  254.9 20.8 %copy-start.142 = (f32[768]{0:T(1024)S(1)}, f32[768]{0:T(1024)}, u32[]{:S(2)}) copy-start(f32[768]{0:T(1024)} %get-tuple-element.164) | copy-start | bytes 9220
  254.9 20.8 %copy-start.143 = (f32[768]{0:T(1024)S(1)}, f32[768]{0:T(1024)}, u32[]{:S(2)}) copy-start(f32[768]{0:T(1024)} %get-tuple-element.171) | copy-start | bytes 9220
  254.9 20.7 %collective-permute-start.9 = (f32[128,768]{1,0:T(8,128)S(1)}, f32[128,768]{1,0:T(8,128)S(1)}, u32[]{:S(2)}, u32[]{:S(2)}) collective-permute-start(f32[128,768]{1,0:T(8,128)S(1)} %constant_dynamic-slice_fusion.6), channel_id=1, source_target_pairs={{0,1},{1,0},{2,3},{3,2},{4,5},{5,4},{6,7},{7,6},{8,9},{9,8},{10,11... | collective-permute-start | bytes 1179656 | tf_op jit(solution)/shard_map/ppermute | solution.py:163
  278.0 10.6 %collective-permute-start.12 = (bf16[128,768]{1,0:T(8,128)(2,1)S(1)}, bf16[128,768]{1,0:T(8,128)(2,1)S(1)}, u32[]{:S(2)}, u32[]{:S(2)}) collective-permute-start(bf16[128,768]{1,0:T(8,128)(2,1)S(1)} %convert_element_type.202), channel_id=1, source_target_pairs={{0,1},{1,0},{2,3},{3,2},{4,5},{5,4},{6,7},{7,6},{8,9},{9,8},{10,11... | collective-permute-start | bytes 589832 | tf_op jit(solution)/shard_map/ppermute | solution.py:163
  281.7 26.2 %all-to-all-start.9 = ((f32[16,192,48]{1,2,0:T(8,128)}), f32[16,192,48]{1,2,0:T(8,128)S(1)}, u32[]{:S(2)}, u32[]{:S(2)}) async-start(f32[16,192,48]{1,2,0:T(8,128)} %bitcast.74), calls=%async_computation.9 | async-start | bytes 1572864 | tf_op jit(solution)/shard_map/all_to_all | solution.py:214
  290.1 3.3 collective-permute-start.15
  307.9 24.2 %all-to-all-start.8 = ((f32[16,192,48]{1,2,0:T(8,128)}), f32[16,192,48]{1,2,0:T(8,128)}, u32[]{:S(2)}, u32[]{:S(2)}) async-start(f32[16,192,48]{1,2,0:T(8,128)} %bitcast.69), calls=%async_computation.8 | async-start | bytes 1572864 | tf_op jit(solution)/shard_map/all_to_all | solution.py:214
  332.0 77.0 %all-to-all-start.7 = ((f32[16,48,3,192]{3,1,2,0:T(8,128)}), f32[16,48,3,192]{3,1,2,0:T(8,128)}, u32[]{:S(2)}, u32[]{:S(2)}) async-start(f32[16,48,3,192]{3,1,2,0:T(8,128)} %copy.258), calls=%async_computation.7 | async-start | bytes 4718592 | tf_op jit(solution)/shard_map/all_to_all | solution.py:214
  336.9 284.9 %reduce-scatter.5.cloned.1.call-start = ((), (), s32[]{:S(2)}) async-start(), calls=%async_computation.17 | async-start | bytes 5013504 | tf_op jit(solution)/shard_map/reduce_scatter | solution.py:142
  341.4 4.1 collective-permute-start.13
  351.8 61.9 %copy-start.43 = (bf16[256,1536]{1,0:T(8,128)(2,1)S(1)}, bf16[256,1536]{1,0:T(8,128)(2,1)}, u32[]{:S(2)}) copy-start(bf16[256,1536]{1,0:T(8,128)(2,1)} %copy-done.42) | copy-start | bytes 2359300
  351.8 61.9 %copy-start.63 = (bf16[128,768]{1,0:T(8,128)(2,1)S(1)}, bf16[128,768]{1,0:T(8,128)(2,1)}, u32[]{:S(2)}) copy-start(bf16[128,768]{1,0:T(8,128)(2,1)} %param.16) | copy-start | bytes 589828
  351.8 61.9 %copy-start.91 = (bf16[128,768]{1,0:T(8,128)(2,1)S(1)}, bf16[128,768]{1,0:T(8,128)(2,1)}, u32[]{:S(2)}) copy-start(bf16[128,768]{1,0:T(8,128)(2,1)} %copy-done.88) | copy-start | bytes 589828
  409.0 65.4 %all-to-all-start.6 = ((f32[16,48,3,192]{3,1,2,0:T(8,128)}), f32[16,48,3,192]{3,1,2,0:T(8,128)S(1)}, u32[]{:S(2)}, u32[]{:S(2)}) async-start(f32[16,48,3,192]{3,1,2,0:T(8,128)} %copy.255), calls=%async_computation.6 | async-start | bytes 4718592 | tf_op jit(solution)/shard_map/all_to_all | solution.py:214
  417.5 4.9 collective-permute-start.18
  474.4 75.2 %all-to-all-start.11 = ((f32[16,768,48]{1,2,0:T(8,128)}), f32[16,768,48]{1,2,0:T(8,128)}, u32[]{:S(2)}, u32[]{:S(2)}) async-start(f32[16,768,48]{1,2,0:T(8,128)} %bitcast.88), calls=%async_computation.13 | async-start | bytes 4718592 | tf_op jit(solution)/shard_map/all_to_all | solution.py:214
  479.4 142.3 %reduce-scatter.3.cloned.1.call-start = ((), (), s32[]{:S(2)}) async-start(), calls=%async_computation.16 | async-start | bytes 5013504 | tf_op jit(solution)/shard_map/reduce_scatter | solution.py:142
  483.7 9.3 %collective-permute-start.17 = (f32[768,768]{0,1:T(8,128)}, f32[768,768]{0,1:T(8,128)}, u32[]{:S(2)}, u32[]{:S(2)}) collective-permute-start(f32[768,768]{0,1:T(8,128)} %constant_dynamic-slice_fusion.1), channel_id=1, source_target_pairs={{0,2},{2,0},{4,6},{6,4},{8,10},{10,8},{12,14},{14,12},{16,18},{18,... | collective-permute-start | bytes 7077896 | tf_op jit(solution)/shard_map/ppermute | solution.py:208
  549.6 66.7 %all-to-all-start.10 = ((f32[16,768,48]{1,2,0:T(8,128)}), f32[16,768,48]{1,2,0:T(8,128)}, u32[]{:S(2)}, u32[]{:S(2)}) async-start(f32[16,768,48]{1,2,0:T(8,128)} %bitcast.84), calls=%async_computation.12 | async-start | bytes 4718592 | tf_op jit(solution)/shard_map/all_to_all | solution.py:214
  565.8 52.3 %copy-start.75 = (f32[2,1536,48]{1,2,0:T(8,128)S(1)}, f32[2,1536,48]{1,2,0:T(8,128)}, u32[]{:S(2)}) copy-start(f32[2,1536,48]{1,2,0:T(8,128)} %param.29) | copy-start | bytes 1769476
  636.3 64.8 %all-to-all-start.12 = ((f32[16,48,768]{2,1,0:T(8,128)}), f32[16,48,768]{2,1,0:T(8,128)S(1)}, u32[]{:S(2)}, u32[]{:S(2)}) async-start(f32[16,48,768]{2,1,0:T(8,128)} %copy.263), calls=%async_computation.14 | async-start | bytes 4718592 | tf_op jit(solution)/shard_map/all_to_all | solution.py:441
  652.4 19.0 %collective-permute-start.19 = (f32[128,1536]{1,0:T(8,128)}, f32[128,1536]{1,0:T(8,128)}, u32[]{:S(2)}, u32[]{:S(2)}) collective-permute-start(f32[128,1536]{1,0:T(8,128)} %fusion.109), channel_id=1, source_target_pairs={{0,1},{1,0},{2,3},{3,2},{4,5},{5,4},{6,7},{7,6},{8,9},{9,8},{10,11... | collective-permute-start | bytes 2359304 | tf_op jit(solution)/shard_map/ppermute | solution.py:163
  672.8 25.6 %copy-start.21 = (f32[128,768]{1,0:T(8,128)S(1)}, f32[128,768]{1,0:T(8,128)}, u32[]{:S(2)}) copy-start(f32[128,768]{1,0:T(8,128)} %copy-done.20) | copy-start | bytes 1179652
  673.3 2.2 collective-permute-start.20
  675.6 7.1 collective-permute-start.21
  682.7 6.0 collective-permute-start.22
  688.8 8.3 collective-permute-start.23
  697.1 3.4 collective-permute-start.24
  705.5 6.2 collective-permute-start.25
  713.5 28.7 %copy-start.81 = (f32[19968]{0:T(1024)S(1)}, f32[19968]{0:T(1024)}, u32[]{:S(2)}) copy-start(f32[19968]{0:T(1024)} %add.485) | copy-start | bytes 239620
  713.5 27.2 %collective-permute-start.26 = (f32[384,768]{1,0:T(8,128)S(1)}, f32[384,768]{1,0:T(8,128)S(1)}, u32[]{:S(2)}, u32[]{:S(2)}) collective-permute-start(f32[384,768]{1,0:T(8,128)S(1)} %dynamic-slice_add_fusion.4), channel_id=1, source_target_pairs={{0,1},{1,0},{2,3},{3,2},{4,5},{5,4},{6,7},{7,6},{8,9},{9,8},{10,11... | collective-permute-start | bytes 3538952 | tf_op jit(solution)/shard_map/ppermute | solution.py:452
  740.9 5.5 collective-permute-start.27
  815.8 34.6 %all-to-all-start.13 = ((bf16[16,48,768]{2,1,0:T(8,128)(2,1)}), bf16[16,48,768]{2,1,0:T(8,128)(2,1)S(1)}, u32[]{:S(2)}, u32[]{:S(2)}) async-start(bf16[16,48,768]{2,1,0:T(8,128)(2,1)} %bitcast.110), calls=%async_computation.15 | async-start | bytes 2359296 | tf_op jit(solution)/shard_map/all_to_all | solution.py:478
  823.3 28.2 %copy-start.99 = (f32[2,2,768]{2,1,0:T(2,128)}, f32[2,2,768]{2,1,0:T(2,128)S(1)}, u32[]{:S(2)}) copy-start(f32[2,2,768]{2,1,0:T(2,128)S(1)} %slice.480) | copy-start | bytes 36868
  824.0 27.5 %copy-start.86 = (f32[2,3072]{1,0:T(2,128)}, f32[2,3072]{1,0:T(2,128)S(1)}, u32[]{:S(2)}) copy-start(f32[2,3072]{1,0:T(2,128)S(1)} %reshape.604) | copy-start | bytes 73732
  824.0 27.5 %copy-start.87 = (f32[2,4,768]{2,1,0:T(4,128)}, f32[2,4,768]{2,1,0:T(4,128)S(1)}, u32[]{:S(2)}) copy-start(f32[2,4,768]{2,1,0:T(4,128)S(1)} %reshape.602) | copy-start | bytes 73732
  (153 other events, 764.5 us)
Sparse Core Ops, SparseCore 0:
  10.9 55.7 all-gather.4
  184.0 43.1 all-gather.6
  345.2 90.5 reduce-scatter.4
  493.1 95.3 reduce-scatter.2

commit v7 on v6

--- a/solution.py
+++ b/solution.py
@@ -179,43 +179,41 @@
     return mine + tensor_swap(theirs)
 
 
-def chip_gather(block, gather_axis, split_axis):
+def chip_gather_rows(block):
     count = lax.axis_size("dp")
     parity = lax.axis_index("dp") % 2
-    width = block.shape[split_axis] // 2
-    halves = jnp.stack(
-        [lax.slice_in_dim(block, 0, width, axis=split_axis), lax.slice_in_dim(block, width, 2 * width, axis=split_axis)]
-    )
+    half = block.shape[0] // 2
+    halves = block.reshape((2, half) + block.shape[1:])
     outgoing = jnp.tile(halves, (count // 2,) + (1,) * block.ndim)
     got = lax.all_to_all(outgoing, "dp", split_axis=0, concat_axis=0, tiled=True)
-    got = jnp.moveaxis(got, 0, gather_axis)
-    shape = got.shape
-    mine = got.reshape(shape[:gather_axis] + (shape[gather_axis] * shape[gather_axis + 1],) + shape[gather_axis + 2 :])
-    theirs = lax.ppermute(mine, "dp", swap_pairs(count, 1))
-    return jnp.where(
-        parity == 0,
-        jnp.concatenate([mine, theirs], axis=split_axis),
-        jnp.concatenate([theirs, mine], axis=split_axis),
-    )
-
-
-def chip_scatter(partial, scatter_axis, split_axis):
+    theirs = lax.ppermute(got, "dp", swap_pairs(count, 1))
+    pair = jnp.where(parity == 0, jnp.stack([got, theirs], axis=1), jnp.stack([theirs, got], axis=1))
+    return pair.reshape((count * 2 * half,) + block.shape[1:])
+
+
+def chip_scatter_rows(partial):
     count = lax.axis_size("dp")
     parity = lax.axis_index("dp") % 2
-    width = partial.shape[split_axis] // 2
-    keep = lax.dynamic_slice_in_dim(partial, parity * width, width, split_axis)
-    send = lax.dynamic_slice_in_dim(partial, (1 - parity) * width, width, split_axis)
+    half = partial.shape[0] // count // 2
+    blocks = partial.reshape((count, 2, half) + partial.shape[1:])
+    keep = lax.dynamic_index_in_dim(blocks, parity, axis=1, keepdims=False)
+    send = lax.dynamic_index_in_dim(blocks, 1 - parity, axis=1, keepdims=False)
     chip_sum = keep + lax.ppermute(send, "dp", swap_pairs(count, 1))
-    shape = chip_sum.shape
-    chunks = chip_sum.reshape(
-        shape[:scatter_axis] + (count, shape[scatter_axis] // count) + shape[scatter_axis + 1 :]
-    )
-    chunks = jnp.moveaxis(chunks, scatter_axis, 0)
-    got = lax.all_to_all(chunks, "dp", split_axis=0, concat_axis=0, tiled=True)
+    got = lax.all_to_all(chip_sum, "dp", split_axis=0, concat_axis=0, tiled=True)
     got = got.reshape((count // 2, 2) + got.shape[1:])
     even = jnp.sum(got[:, 0], axis=0)
     odd = jnp.sum(got[:, 1], axis=0)
-    return jnp.concatenate([even, odd], axis=split_axis)
+    return jnp.concatenate([even, odd], axis=0)
+
+
+def scatter_layer(parts):
+    qkv_part, proj_part, up_part, down_part = parts
+    return (
+        chip_scatter_rows(qkv_part),
+        chip_scatter_rows(proj_part).T,
+        dp_scatter(up_part, 0),
+        chip_scatter_rows(down_part).T,
+    )
 
 
 def vector_step(params, gradients):
@@ -252,10 +250,10 @@
     saved_layers = []
     for layer_id in range(LAYERS):
         layer_weights = (
-            chip_gather(qkv_weight[layer_id], 0, 2),
-            chip_gather(proj_weight[layer_id], 1, 0),
+            chip_gather_rows(qkv_weight[layer_id]),
+            chip_gather_rows(proj_weight[layer_id].T),
             dp_gather(up_weight[layer_id], 0),
-            chip_gather(down_weight[layer_id], 1, 0),
+            chip_gather_rows(down_weight[layer_id].T),
         )
         qkv_full, proj_full, up_full, down_full = layer_weights
         normed, inverse = normalize(stream)
@@ -282,9 +280,9 @@
         )
         up_pre = jnp.dot(mlp_in, up_full, preferred_element_type=jnp.float32) + up_local_bias
         act_low = gelu_exact(up_pre).astype(jnp.bfloat16)
-        partial_sum = jnp.dot(heads_flat, proj_full, preferred_element_type=jnp.float32) + jnp.dot(
-            act_low, down_full, preferred_element_type=jnp.float32
-        )
+        partial_sum = jnp.einsum(
+            "lf,df->ld", heads_flat, proj_full, preferred_element_type=jnp.float32
+        ) + jnp.einsum("lf,df->ld", act_low, down_full, preferred_element_type=jnp.float32)
         branch = tensor_scatter(partial_sum)
         saved_layers.append(
             (
@@ -329,10 +327,10 @@
         out_bias_grad = jnp.sum(grad_stream, axis=0)
         branch_grad = tensor_gather(grad_stream.astype(jnp.bfloat16))
         down_part = jnp.einsum(
-            "lf,ld->fd", act_low, branch_grad, preferred_element_type=jnp.float32
+            "lf,ld->df", act_low, branch_grad, preferred_element_type=jnp.float32
         )
         act_grad = jnp.einsum(
-            "ld,fd->lf", branch_grad, down_full, preferred_element_type=jnp.float32
+            "ld,df->lf", branch_grad, down_full, preferred_element_type=jnp.float32
         )
         gelu_back = jax.vjp(gelu_exact, up_pre)[1]
         up_pre_grad = gelu_back(act_grad)[0].astype(jnp.bfloat16)
@@ -342,10 +340,10 @@
             "lf,df->ld", up_pre_grad, up_full, preferred_element_type=jnp.float32
         )
         proj_part = jnp.einsum(
-            "lf,ld->fd", heads_flat, branch_grad, preferred_element_type=jnp.float32
+            "lf,ld->df", heads_flat, branch_grad, preferred_element_type=jnp.float32
         )
         heads_grad = (
-            jnp.einsum("ld,fd->lf", branch_grad, proj_full, preferred_element_type=jnp.float32)
+            jnp.einsum("ld,df->lf", branch_grad, proj_full, preferred_element_type=jnp.float32)
             .astype(jnp.bfloat16)
             .reshape(length, head_count, HD)
         )
@@ -393,12 +391,9 @@
         normed_mean = jnp.mean(normed_grad, axis=-1, keepdims=True)
         product_mean = jnp.mean(normed_grad * normed, axis=-1, keepdims=True)
         grad_stream = grad_stream + inverse * (normed_grad - normed_mean - normed * product_mean)
-        weight_list[layer_id] = (
-            chip_scatter(qkv_part, 0, 2),
-            chip_scatter(proj_part, 1, 0),
-            dp_scatter(up_part, 0),
-            chip_scatter(down_part, 1, 0),
-        )
+        weight_list[layer_id] = (qkv_part, proj_part, up_part, down_part)
+        if layer_id > 0:
+            weight_list[layer_id] = scatter_layer(weight_list[layer_id])
     small_parts = (
         jnp.stack(gains_list),
         jnp.stack(biases_list),
@@ -412,6 +407,8 @@
         small_sums.append(flat[offset : offset + part.size].reshape(part.shape))
         offset += part.size
     gains_grad, biases_grad, qkv_bias_grad, up_bias_grad = small_sums
+    flat, first_parts = lax.optimization_barrier((flat, weight_list[0]))
+    weight_list[0] = scatter_layer(first_parts)
     qkv_grad = jnp.stack([weight_list[layer_id][0] for layer_id in range(LAYERS)])
     proj_grad = jnp.stack([weight_list[layer_id][1] for layer_id in range(LAYERS)])
     up_grad = jnp.stack([weight_list[layer_id][2] for layer_id in range(LAYERS)])
@@ -440,7 +437,7 @@
     outgoing = jnp.concatenate(pieces, axis=0)
     owned = lax.all_to_all(outgoing, "dp", split_axis=0, concat_axis=0, tiled=True)
     owned = owned.reshape(dp_count * rows_local, piece_width)
-    owned, flat, grad_stream = lax.optimization_barrier((owned, flat, grad_stream))
+    owned, grad_stream = lax.optimization_barrier((owned, grad_stream))
     gram = jnp.dot(owned, owned.T, precision=ns_precision)
     bit = 1
     while bit < sub:

time: 873 us -> 866 us (level)
  local copies, waits for them, and re-layouts: 101 us -> 83.2 us
  matrix products: 143 us -> 129 us
  other arithmetic: 60.9 us -> 73.2 us
  waiting for transfers between devices: 440 us -> 452 us
    all_to_all x1, waiting for transfers between devices: 0.01 us -> 51.6 us  [local(): lax.all_to_all(outgoing, 'dp', split_axis=0, concat_axis=0, tiled=True)]
    all_to_all x12, waiting for transfers between devices: 310 us -> 290 us  [the longest x6 199 us: chip_scatter_rows(): lax.all_to_all(chip_sum, 'dp', split_axis=0, concat_axis=0, tiled=True)]
    select_n x0 -> x6, other arithmetic: none -> 13.8 us  [chip_gather_rows(): jnp.where(parity == 0, jnp.stack([got, theirs], axis=1), jnp.stack([their...]
    ppermute x8, waiting for transfers between devices: 52.8 us -> 39.1 us  [tensor_swap(): return lax.ppermute(block, 'tensor', [(0, 1), (1, 0)])]
    ppermute x4, waiting for transfers between devices: 16.6 us -> 3.95 us  [butterfly_sum(): flat = flat + lax.ppermute(flat, 'dp', swap_pairs(count, bit))]
    dot_general x12, matrix products: 27.5 us -> 15.1 us  [the longest x2 4.33 us: local(): jnp.einsum('ld,df->lf', branch_grad, down_full, preferred_element_type=jn...]
    unnamed x351 -> x339, local copies, waits for them, and re-layouts: 23 us -> 18.9 us
  transfers between devices with their start and end apart: 46 -> 46, of which waited for: 26 -> 28; matrix products, arithmetic and copies ran while one was open for 22% -> 20% of each run, Pallas kernels for 0% -> 0%
where the time goes in v7:
time: 866 us; the launch traced here: 858 us
  waiting for transfers between devices  452 us (52%)
  matrix products  129 us (15%)
  starting transfers between devices  102 us (12%)
  local copies, waits for them, and re-layouts  83.2 us (10%)
  other arithmetic  73.2 us (8%)
  between operations  17.5 us (2%)
    all_to_all x6, waiting for transfers between devices, chip_scatter_rows(): lax.all_to_all(chip_sum, 'dp', split_axis=0, concat_axis=0, tiled=True)  199 us
    all_to_all x6, waiting for transfers between devices, chip_gather_rows(): lax.all_to_all(outgoing, 'dp', split_axis=0, concat_axis=0, tiled=True)  91.4 us
    all_to_all x1, waiting for transfers between devices, local(): lax.all_to_all(outgoing, 'dp', split_axis=0, concat_axis=0, tiled=True)  51.6 us
    ppermute x8, waiting for transfers between devices, tensor_swap(): return lax.ppermute(block, 'tensor', [(0, 1), (1, 0)])  39.1 us
    all_to_all x6, starting transfers between devices, chip_scatter_rows(): lax.all_to_all(chip_sum, 'dp', split_axis=0, concat_axis=0, tiled=True)  32.1 us
    all_to_all x6, starting transfers between devices, chip_gather_rows(): lax.all_to_all(outgoing, 'dp', split_axis=0, concat_axis=0, tiled=True)  29.9 us
    ppermute x1, waiting for transfers between devices, local(): mine = mine + lax.ppermute(mine, 'tensor', [(0, 1), (1, 0)])  26.3 us
    all_to_all x1, waiting for transfers between devices, local(): lax.all_to_all(current.astype(jnp.bfloat16).reshape(dp_count, rows_local,...  24 us
  transfers between devices with their start and end apart: 46, of which 28 were waited for; matrix products, arithmetic and copies ran while one was open for 20% of the time, Pallas kernels for 0%

profile of v7, /device:TPU:11, one launch (start us, length us, event | category | flops | bytes accessed | tf_op | source)
XLA Modules:
  0.0 857.5 jit_solution(7427489635113655619)
XLA Ops:
  10.7 6.5 all-to-all-start.1
  18.8 10.3 %all-to-all-done.1 = bf16[16,24,384]{2,1,0:T(8,128)(2,1)S(1)} async-done(((bf16[16,24,384]{2,1,0:T(8,128)(2,1)}), bf16[16,24,384]{2,1,0:T(8,128)(2,1)S(1)}, u32[]{:S(2)}, u32[]{:S(2)}) %all-to-all-start.1) | async-done | bytes 294944 | tf_op jit(solution)/shard_map/all_to_all | solution.py:188
  29.8 4.2 all-to-all-start.4
  34.2 12.9 %all-to-all-done.4 = bf16[16,24,384]{2,1,0:T(8,128)(2,1)S(1)} async-done(((bf16[16,24,384]{2,1,0:T(8,128)(2,1)}), bf16[16,24,384]{2,1,0:T(8,128)(2,1)S(1)}, u32[]{:S(2)}, u32[]{:S(2)}) %all-to-all-start.4) | async-done | bytes 294944 | tf_op jit(solution)/shard_map/all_to_all | solution.py:188
  48.1 4.9 all-to-all-start
  58.1 21.3 %all-to-all-done = bf16[16,24,3,384]{3,1,2,0:T(8,128)(2,1)S(1)} async-done(((bf16[16,24,3,384]{3,1,2,0:T(8,128)(2,1)}), bf16[16,24,3,384]{3,1,2,0:T(8,128)(2,1)S(1)}, u32[]{:S(2)}, u32[]{:S(2)}) %all-to-all-start) | async-done | bytes 884768 | tf_op jit(solution)/shard_map/all_to_all | solution.py:188
  80.6 4.3 all-to-all-start.2
  94.6 27.6 %all-to-all-done.2 = bf16[16,24,1536]{2,1,0:T(8,128)(2,1)} async-done(((bf16[16,24,1536]{2,1,0:T(8,128)(2,1)}), bf16[16,24,1536]{2,1,0:T(8,128)(2,1)}, u32[]{:S(2)}, u32[]{:S(2)}) %all-to-all-start.2) | async-done | bytes 1179680 | tf_op jit(solution)/shard_map/all_to_all | solution.py:188
  123.2 5.1 all-to-all-start.3
  136.5 13.3 %all-to-all-done.3 = bf16[16,24,3,384]{3,1,2,0:T(8,128)(2,1)} async-done(((bf16[16,24,3,384]{3,1,2,0:T(8,128)(2,1)}), bf16[16,24,3,384]{3,1,2,0:T(8,128)(2,1)}, u32[]{:S(2)}, u32[]{:S(2)}) %all-to-all-start.3) | async-done | bytes 884768 | tf_op jit(solution)/shard_map/all_to_all | solution.py:188
  151.8 5.0 all-to-all-start.5
  159.2 4.4 maximum_select_fusion
  163.6 7.5 multiply_convert_fusion.3
  178.6 6.0 all-to-all-done.5
  192.7 4.5 collective-permute-done.5
  232.3 5.6 multiply_convert_fusion.2
  246.3 13.0 %collective-permute-done.11 = f32[128,1536]{1,0:T(8,128)S(1)} collective-permute-done((f32[128,1536]{1,0:T(8,128)S(1)}, f32[128,1536]{1,0:T(8,128)S(1)}, u32[]{:S(2)}, u32[]{:S(2)}) %collective-permute-start.11) | collective-permute-done | bytes 786464 | tf_op jit(solution)/shard_map/ppermute | solution.py:163
  259.8 7.9 collective-permute-done.9
  281.7 3.2 convert_reduce_fusion.1
  291.4 12.4 %collective-permute-done.13 = f32[128,1536]{1,0:T(8,128)} collective-permute-done((f32[128,1536]{1,0:T(8,128)}, f32[128,1536]{1,0:T(8,128)}, u32[]{:S(2)}, u32[]{:S(2)}) %collective-permute-start.13) | collective-permute-done | bytes 786464 | tf_op jit(solution)/shard_map/ppermute | solution.py:163
  308.9 3.2 collective-permute-start.14
  314.1 5.0 all-to-all-start.9
  319.5 4.1 fusion.145
  339.9 4.0 collective-permute-start.21
  346.4 7.0 all-to-all-start.8
  356.3 12.2 %all-to-all-done.8 = f32[16,24,384]{2,1,0:T(8,128)} async-done(((f32[16,24,384]{2,1,0:T(8,128)}), f32[16,24,384]{2,1,0:T(8,128)}, u32[]{:S(2)}, u32[]{:S(2)}) %all-to-all-start.8) | async-done | bytes 589856 | tf_op jit(solution)/shard_map/all_to_all | solution.py:202
  368.5 4.8 all-to-all-start.7
  381.8 3.5 bitcast_add_fusion
  385.3 32.7 %all-to-all-done.7 = f32[16,24,3,384]{3,1,2,0:T(8,128)} async-done(((f32[16,24,3,384]{3,1,2,0:T(8,128)}), f32[16,24,3,384]{3,1,2,0:T(8,128)}, u32[]{:S(2)}, u32[]{:S(2)}) %all-to-all-start.7) | async-done | bytes 1769504 | tf_op jit(solution)/shard_map/all_to_all | solution.py:202
  418.0 5.7 all-to-all-start.11
  424.5 3.3 collective-permute-done.19
  429.3 66.0 %all-to-all-done.11 = f32[16,24,1536]{2,1,0:T(8,128)} async-done(((f32[16,24,1536]{2,1,0:T(8,128)}), f32[16,24,1536]{2,1,0:T(8,128)}, u32[]{:S(2)}, u32[]{:S(2)}) %all-to-all-start.11) | async-done | bytes 2359328 | tf_op jit(solution)/shard_map/all_to_all | solution.py:202
  495.4 4.7 all-to-all-start.6
  500.2 3.2 dynamic-slice_bitcast_fusion.1
  503.8 4.5 collective-permute-done.23
  508.3 4.1 bitcast_add_fusion.1
  512.4 38.2 %all-to-all-done.6 = f32[16,24,3,384]{3,1,2,0:T(8,128)S(1)} async-done(((f32[16,24,3,384]{3,1,2,0:T(8,128)}), f32[16,24,3,384]{3,1,2,0:T(8,128)S(1)}, u32[]{:S(2)}, u32[]{:S(2)}) %all-to-all-start.6) | async-done | bytes 1769504 | tf_op jit(solution)/shard_map/all_to_all | solution.py:202
  551.9 4.9 all-to-all-start.10
  571.4 49.7 %all-to-all-done.10 = f32[16,24,1536]{2,1,0:T(8,128)S(1)} async-done(((f32[16,24,1536]{2,1,0:T(8,128)}), f32[16,24,1536]{2,1,0:T(8,128)S(1)}, u32[]{:S(2)}, u32[]{:S(2)}) %all-to-all-start.10) | async-done | bytes 2359328 | tf_op jit(solution)/shard_map/all_to_all | solution.py:202
  630.5 7.0 concatenate.136
  640.4 5.5 all-to-all-start.12
  646.9 51.6 %all-to-all-done.12 = f32[16,48,768]{2,1,0:T(8,128)S(1)} async-done(((f32[16,48,768]{2,1,0:T(8,128)}), f32[16,48,768]{2,1,0:T(8,128)S(1)}, u32[]{:S(2)}, u32[]{:S(2)}) %all-to-all-start.12) | async-done | bytes 2359328 | tf_op jit(solution)/shard_map/all_to_all | solution.py:438
  698.5 4.4 fusion.240
  703.1 4.8 collective-permute-done.25
  710.8 26.3 %collective-permute-done.26 = f32[384,768]{1,0:T(8,128)S(1)} collective-permute-done((f32[384,768]{1,0:T(8,128)S(1)}, f32[384,768]{1,0:T(8,128)S(1)}, u32[]{:S(2)}, u32[]{:S(2)}) %collective-permute-start.26) | collective-permute-done | bytes 1179680 | tf_op jit(solution)/shard_map/ppermute | solution.py:449
  745.6 7.0 fusion
  752.6 4.8 fusion.17
  757.5 3.4 fusion.241
  760.8 3.1 fusion.242
  764.0 3.4 fusion.35
  767.3 3.2 fusion.39
  770.6 3.6 fusion.37
  774.2 3.1 fusion.243
  777.3 3.2 fusion.33
  780.5 3.3 fusion.29
  783.9 3.8 fusion.31
  787.7 3.1 fusion.244
  790.8 3.2 fusion.27
  794.1 3.5 fusion.23
  797.6 3.4 fusion.25
  804.1 3.4 fusion.5
  807.5 4.3 fusion.53
  811.8 4.9 all-to-all-start.13
  820.5 24.0 %all-to-all-done.13 = bf16[16,48,768]{2,1,0:T(8,128)(2,1)S(1)} async-done(((bf16[16,48,768]{2,1,0:T(8,128)(2,1)}), bf16[16,48,768]{2,1,0:T(8,128)(2,1)S(1)}, u32[]{:S(2)}, u32[]{:S(2)}) %all-to-all-start.13) | async-done | bytes 1179680 | tf_op jit(solution)/shard_map/all_to_all | solution.py:475
  (665 shorter events, 208.0 us)
Async XLA Ops:
  7.2 156.4 %all-gather.5.cloned.1.call-start = ((), (), s32[]{:S(2)}) async-start(), calls=%async_computation.18 | async-start | bytes 2506752 | tf_op jit(solution)/shard_map/all_gather | solution.py:146
  10.7 18.4 %all-to-all-start.1 = ((bf16[16,24,384]{2,1,0:T(8,128)(2,1)}), bf16[16,24,384]{2,1,0:T(8,128)(2,1)S(1)}, u32[]{:S(2)}, u32[]{:S(2)}) async-start(bf16[16,24,384]{2,1,0:T(8,128)(2,1)} %bitcast.18), calls=%async_computation.1 | async-start | bytes 589824 | tf_op jit(solution)/shard_map/all_to_all | solution.py:188
  17.2 71.5 %collective-permute-start.10 = (bf16[128,768]{1,0:T(8,128)(2,1)S(1)}, bf16[128,768]{1,0:T(8,128)(2,1)S(1)}, u32[]{:S(2)}, u32[]{:S(2)}) collective-permute-start(bf16[128,768]{1,0:T(8,128)(2,1)S(1)} %copy-done.43), channel_id=1, source_target_pairs={{0,1},{1,0},{2,3},{3,2},{4,5},{5,4},{6,7},{7,6},{8,9},{9,8},{10,11... | collective-permute-start | bytes 589832 | tf_op jit(solution)/shard_map/ppermute | solution.py:163
  18.5 29.6 %copy-start.55 = (bf16[1,48,3,384]{3,1,2,0:T(8,128)(2,1)}, bf16[1,48,3,384]{3,1,2,0:T(8,128)(2,1)S(1)}, u32[]{:S(2)}) copy-start(bf16[1,48,3,384]{3,1,2,0:T(8,128)(2,1)S(1)} %get-tuple-element.258) | copy-start | bytes 331780
  18.5 68.4 %copy-start.53 = (bf16[1,48,3,384]{3,1,2,0:T(8,128)(2,1)}, bf16[1,48,3,384]{3,1,2,0:T(8,128)(2,1)S(1)}, u32[]{:S(2)}) copy-start(bf16[1,48,3,384]{3,1,2,0:T(8,128)(2,1)S(1)} %get-tuple-element.257) | copy-start | bytes 331780
  29.8 23.2 %copy-start.119 = (f32[2,2,768]{2,1,0:T(2,128)S(1)}, f32[2,2,768]{2,1,0:T(2,128)}, u32[]{:S(2)}) copy-start(f32[2,2,768]{2,1,0:T(2,128)} %param.22) | copy-start | bytes 36868
  29.8 23.9 %copy-start.96 = (f32[2,4,768]{2,1,0:T(4,128)S(1)}, f32[2,4,768]{2,1,0:T(4,128)}, u32[]{:S(2)}) copy-start(f32[2,4,768]{2,1,0:T(4,128)} %param.23) | copy-start | bytes 73732
  29.8 17.3 %all-to-all-start.4 = ((bf16[16,24,384]{2,1,0:T(8,128)(2,1)}), bf16[16,24,384]{2,1,0:T(8,128)(2,1)S(1)}, u32[]{:S(2)}, u32[]{:S(2)}) async-start(bf16[16,24,384]{2,1,0:T(8,128)(2,1)} %bitcast.45), calls=%async_computation.4 | async-start | bytes 589824 | tf_op jit(solution)/shard_map/all_to_all | solution.py:188
  34.0 20.5 %copy-start.150 = (f32[128]{0:T(128)}, f32[128]{0:T(128)S(1)}, u32[]{:S(2)}) copy-start(f32[128]{0:T(128)S(1)} %broadcast_multiply_fusion.5) | copy-start | bytes 1540
  34.2 21.1 %copy-start.156 = (f32[128]{0:T(128)}, f32[128]{0:T(128)S(1)}, u32[]{:S(2)}) copy-start(f32[128]{0:T(128)S(1)} %add_rsqrt_fusion.1) | copy-start | bytes 1540
  48.1 31.4 %all-to-all-start = ((bf16[16,24,3,384]{3,1,2,0:T(8,128)(2,1)}), bf16[16,24,3,384]{3,1,2,0:T(8,128)(2,1)S(1)}, u32[]{:S(2)}, u32[]{:S(2)}) async-start(bf16[16,24,3,384]{3,1,2,0:T(8,128)(2,1)} %bitcast.2), calls=%async_computation | async-start | bytes 1769472 | tf_op jit(solution)/shard_map/all_to_all | solution.py:188
  53.0 179.4 %all-gather.7.cloned.1.call-start = ((), (), s32[]{:S(2)}) async-start(), calls=%async_computation.19 | async-start | bytes 2506752 | tf_op jit(solution)/shard_map/all_gather | solution.py:146
  53.6 25.8 %copy-start.126 = (f32[768]{0:T(1024)}, f32[768]{0:T(1024)S(1)}, u32[]{:S(2)}) copy-start(f32[768]{0:T(1024)S(1)} %get-tuple-element.181) | copy-start | bytes 9220
  53.6 26.9 %copy-start.128 = (f32[768]{0:T(1024)}, f32[768]{0:T(1024)S(1)}, u32[]{:S(2)}) copy-start(f32[768]{0:T(1024)S(1)} %get-tuple-element.182) | copy-start | bytes 9220
  55.3 34.7 %collective-permute-start = (bf16[128,1536]{1,0:T(8,128)(2,1)}, bf16[128,1536]{1,0:T(8,128)(2,1)}, u32[]{:S(2)}, u32[]{:S(2)}) collective-permute-start(bf16[128,1536]{1,0:T(8,128)(2,1)} %pad_maximum_fusion.8), channel_id=1, source_target_pairs={{0,1},{1,0},{2,3},{3,2},{4,5},{5,4},{6,7},{7,6},{8,9},{9,8},{10,11... | collective-permute-start | bytes 1179656 | tf_op jit(solution)/shard_map/ppermute | solution.py:163
  80.6 41.6 %all-to-all-start.2 = ((bf16[16,24,1536]{2,1,0:T(8,128)(2,1)}), bf16[16,24,1536]{2,1,0:T(8,128)(2,1)}, u32[]{:S(2)}, u32[]{:S(2)}) async-start(bf16[16,24,1536]{2,1,0:T(8,128)(2,1)} %bitcast.26), calls=%async_computation.2 | async-start | bytes 2359296 | tf_op jit(solution)/shard_map/all_to_all | solution.py:188
  85.9 42.7 %collective-permute-start.1 = (bf16[16,24,3,384]{3,1,0,2:T(8,128)(2,1)S(1)}, bf16[16,24,3,384]{3,1,0,2:T(8,128)(2,1)}, u32[]{:S(2)}, u32[]{:S(2)}) collective-permute-start(bf16[16,24,3,384]{3,1,0,2:T(8,128)(2,1)S(1)} %copy.308), channel_id=1, source_target_pairs={{0,2},{2,0},{4,6},{6,4},{8,10},{10,8},{12,14},{14,12},{16,18},{18,... | collective-permute-start | bytes 2654216 | tf_op jit(solution)/shard_map/ppermute | solution.py:189
  88.4 2.9 collective-permute-start.7
  89.7 4.0 collective-permute-start.2
  91.4 39.2 %copy-start.14 = (bf16[256,1536]{1,0:T(8,128)(2,1)}, bf16[256,1536]{1,0:T(8,128)(2,1)S(1)}, u32[]{:S(2)}) copy-start(bf16[256,1536]{1,0:T(8,128)(2,1)S(1)} %maximum_select_fusion.5) | copy-start | bytes 2359300
  123.2 26.5 %all-to-all-start.3 = ((bf16[16,24,3,384]{3,1,2,0:T(8,128)(2,1)}), bf16[16,24,3,384]{3,1,2,0:T(8,128)(2,1)}, u32[]{:S(2)}, u32[]{:S(2)}) async-start(bf16[16,24,3,384]{3,1,2,0:T(8,128)(2,1)} %bitcast.32), calls=%async_computation.3 | async-start | bytes 1769472 | tf_op jit(solution)/shard_map/all_to_all | solution.py:188
  128.3 30.9 %collective-permute-start.3 = (bf16[16,24,1536]{2,1,0:T(8,128)(2,1)}, bf16[16,24,1536]{2,1,0:T(8,128)(2,1)}, u32[]{:S(2)}, u32[]{:S(2)}) collective-permute-start(bf16[16,24,1536]{2,1,0:T(8,128)(2,1)} %all-to-all-done.2), channel_id=1, source_target_pairs={{0,2},{2,0},{4,6},{6,4},{8,10},{10,8},{12,14},{14,12},{16,18},{18,... | collective-permute-start | bytes 3538952 | tf_op jit(solution)/shard_map/ppermute | solution.py:189
  151.8 32.8 %all-to-all-start.5 = ((bf16[16,24,1536]{2,1,0:T(8,128)(2,1)}), bf16[16,24,1536]{2,1,0:T(8,128)(2,1)S(1)}, u32[]{:S(2)}, u32[]{:S(2)}) async-start(bf16[16,24,1536]{2,1,0:T(8,128)(2,1)} %bitcast.389), calls=%async_computation.5 | async-start | bytes 2359296 | tf_op jit(solution)/shard_map/all_to_all | solution.py:188
  173.1 12.1 %collective-permute-start.4 = (f32[128,768]{1,0:T(8,128)}, f32[128,768]{1,0:T(8,128)}, u32[]{:S(2)}, u32[]{:S(2)}) collective-permute-start(f32[128,768]{1,0:T(8,128)} %constant_dynamic-slice_fusion.5), channel_id=1, source_target_pairs={{0,1},{1,0},{2,3},{3,2},{4,5},{5,4},{6,7},{7,6},{8,9},{9,8},{10,11... | collective-permute-start | bytes 1179656 | tf_op jit(solution)/shard_map/ppermute | solution.py:163
  177.9 10.4 %collective-permute-start.6 = (bf16[16,24,3,384]{3,1,0,2:T(8,128)(2,1)}, bf16[16,24,3,384]{3,1,0,2:T(8,128)(2,1)}, u32[]{:S(2)}, u32[]{:S(2)}) collective-permute-start(bf16[16,24,3,384]{3,1,0,2:T(8,128)(2,1)} %copy.307), channel_id=1, source_target_pairs={{0,2},{2,0},{4,6},{6,4},{8,10},{10,8},{12,14},{14,12},{16,18},{18,... | collective-permute-start | bytes 2654216 | tf_op jit(solution)/shard_map/ppermute | solution.py:189
  184.6 6.3 collective-permute-start.8
  187.0 10.2 %collective-permute-start.5 = (bf16[128,1536]{1,0:T(8,128)(2,1)S(1)}, bf16[128,1536]{1,0:T(8,128)(2,1)S(1)}, u32[]{:S(2)}, u32[]{:S(2)}) collective-permute-start(bf16[128,1536]{1,0:T(8,128)(2,1)S(1)} %pad_maximum_fusion.9), channel_id=1, source_target_pairs={{0,1},{1,0},{2,3},{3,2},{4,5},{5,4},{6,7},{7,6},{8,9},{9,8},{10,11... | collective-permute-start | bytes 1179656 | tf_op jit(solution)/shard_map/ppermute | solution.py:163
  225.0 87.2 %collective-permute-start.22 = (f32[16,24,384]{2,1,0:T(8,128)}, f32[16,24,384]{2,1,0:T(8,128)}, u32[]{:S(2)}, u32[]{:S(2)}) collective-permute-start(f32[16,24,384]{2,1,0:T(8,128)} %dynamic-slice_bitcast_fusion.3), channel_id=1, source_target_pairs={{0,2},{2,0},{4,6},{6,4},{8,10},{10,8},{12,14},{14,12},{16,18},{18,... | collective-permute-start | bytes 1769480 | tf_op jit(solution)/shard_map/ppermute | solution.py:201
  240.9 18.5 %collective-permute-start.11 = (f32[128,1536]{1,0:T(8,128)S(1)}, f32[128,1536]{1,0:T(8,128)S(1)}, u32[]{:S(2)}, u32[]{:S(2)}) collective-permute-start(f32[128,1536]{1,0:T(8,128)S(1)} %fusion.112), channel_id=1, source_target_pairs={{0,1},{1,0},{2,3},{3,2},{4,5},{5,4},{6,7},{7,6},{8,9},{9,8},{10,11... | collective-permute-start | bytes 2359304 | tf_op jit(solution)/shard_map/ppermute | solution.py:163
  243.5 109.9 %collective-permute-start.20 = (f32[16,24,3,384]{3,1,2,0:T(8,128)}, f32[16,24,3,384]{3,1,2,0:T(8,128)}, u32[]{:S(2)}, u32[]{:S(2)}) collective-permute-start(f32[16,24,3,384]{3,1,2,0:T(8,128)} %dynamic-slice_bitcast_fusion.2), channel_id=1, source_target_pairs={{0,2},{2,0},{4,6},{6,4},{8,10},{10,8},{12,14},{14,12},{16,18},{18,... | collective-permute-start | bytes 5308424 | tf_op jit(solution)/shard_map/ppermute | solution.py:201
  245.4 22.4 %collective-permute-start.9 = (f32[128,768]{1,0:T(8,128)S(1)}, f32[128,768]{1,0:T(8,128)S(1)}, u32[]{:S(2)}, u32[]{:S(2)}) collective-permute-start(f32[128,768]{1,0:T(8,128)S(1)} %constant_dynamic-slice_fusion.2), channel_id=1, source_target_pairs={{0,1},{1,0},{2,3},{3,2},{4,5},{5,4},{6,7},{7,6},{8,9},{9,8},{10,11... | collective-permute-start | bytes 1179656 | tf_op jit(solution)/shard_map/ppermute | solution.py:163
  246.3 21.4 %copy-start.140 = (f32[768]{0:T(1024)S(1)}, f32[768]{0:T(1024)}, u32[]{:S(2)}) copy-start(f32[768]{0:T(1024)} %get-tuple-element.172) | copy-start | bytes 9220
  246.3 21.4 %copy-start.141 = (f32[768]{0:T(1024)S(1)}, f32[768]{0:T(1024)}, u32[]{:S(2)}) copy-start(f32[768]{0:T(1024)} %get-tuple-element.179) | copy-start | bytes 9220
  269.5 5.0 collective-permute-start.12
  286.7 17.0 %collective-permute-start.13 = (f32[128,1536]{1,0:T(8,128)}, f32[128,1536]{1,0:T(8,128)}, u32[]{:S(2)}, u32[]{:S(2)}) collective-permute-start(f32[128,1536]{1,0:T(8,128)} %fusion.109), channel_id=1, source_target_pairs={{0,1},{1,0},{2,3},{3,2},{4,5},{5,4},{6,7},{7,6},{8,9},{9,8},{10,11... | collective-permute-start | bytes 2359304 | tf_op jit(solution)/shard_map/ppermute | solution.py:163
  308.9 10.2 %collective-permute-start.14 = (f32[19968]{0:T(1024)S(1)}, f32[19968]{0:T(1024)S(1)}, u32[]{:S(2)}, u32[]{:S(2)}) collective-permute-start(f32[19968]{0:T(1024)S(1)} %constant_dynamic-update-slice_fusion.4), channel_id=1, source_target_pairs={{0,2},{2,0},{4,6},{6,4},{8,10},{10,8},{12,14},{14,12},{16,18},{18,... | collective-permute-start | bytes 239624 | tf_op jit(solution)/shard_map/ppermute | solution.py:157
  314.1 32.2 %all-to-all-start.9 = ((f32[16,24,384]{2,1,0:T(8,128)}), f32[16,24,384]{2,1,0:T(8,128)}, u32[]{:S(2)}, u32[]{:S(2)}) async-start(f32[16,24,384]{2,1,0:T(8,128)} %bitcast_add_fusion.4), calls=%async_computation.9 | async-start | bytes 1179648 | tf_op jit(solution)/shard_map/all_to_all | solution.py:202
  319.2 5.2 collective-permute-start.15
  324.4 7.0 collective-permute-start.16
  331.4 4.4 collective-permute-start.17
  335.8 3.4 collective-permute-start.18
  339.9 5.6 collective-permute-start.21
  346.4 22.1 %all-to-all-start.8 = ((f32[16,24,384]{2,1,0:T(8,128)}), f32[16,24,384]{2,1,0:T(8,128)}, u32[]{:S(2)}, u32[]{:S(2)}) async-start(f32[16,24,384]{2,1,0:T(8,128)} %bitcast_add_fusion.5), calls=%async_computation.8 | async-start | bytes 1179648 | tf_op jit(solution)/shard_map/all_to_all | solution.py:202
  356.3 17.1 %copy-start.63 = (bf16[128,768]{1,0:T(8,128)(2,1)S(1)}, bf16[128,768]{1,0:T(8,128)(2,1)}, u32[]{:S(2)}) copy-start(bf16[128,768]{1,0:T(8,128)(2,1)} %copy-done.60) | copy-start | bytes 589828
  368.5 49.5 %all-to-all-start.7 = ((f32[16,24,3,384]{3,1,2,0:T(8,128)}), f32[16,24,3,384]{3,1,2,0:T(8,128)}, u32[]{:S(2)}, u32[]{:S(2)}) async-start(f32[16,24,3,384]{3,1,2,0:T(8,128)} %bitcast_add_fusion.2), calls=%async_computation.7 | async-start | bytes 3538944 | tf_op jit(solution)/shard_map/all_to_all | solution.py:202
  373.3 252.6 %reduce-scatter.5.cloned.1.call-start = ((), (), s32[]{:S(2)}) async-start(), calls=%async_computation.17 | async-start | bytes 5013504 | tf_op jit(solution)/shard_map/reduce_scatter | solution.py:142
  377.1 4.8 collective-permute-start.24
  385.3 38.3 %copy-start.3 = (f32[768,3,384]{2,0,1:T(8,128)S(1)}, f32[768,3,384]{2,0,1:T(8,128)}, u32[]{:S(2)}) copy-start(f32[768,3,384]{2,0,1:T(8,128)} %fusion.148) | copy-start | bytes 10616836
  418.0 77.4 %all-to-all-start.11 = ((f32[16,24,1536]{2,1,0:T(8,128)}), f32[16,24,1536]{2,1,0:T(8,128)}, u32[]{:S(2)}, u32[]{:S(2)}) async-start(f32[16,24,1536]{2,1,0:T(8,128)} %bitcast_add_fusion), calls=%async_computation.13 | async-start | bytes 4718592 | tf_op jit(solution)/shard_map/all_to_all | solution.py:202
  424.0 3.8 collective-permute-start.19
  495.4 55.3 %all-to-all-start.6 = ((f32[16,24,3,384]{3,1,2,0:T(8,128)}), f32[16,24,3,384]{3,1,2,0:T(8,128)S(1)}, u32[]{:S(2)}, u32[]{:S(2)}) async-start(f32[16,24,3,384]{3,1,2,0:T(8,128)} %bitcast_add_fusion.3), calls=%async_computation.6 | async-start | bytes 3538944 | tf_op jit(solution)/shard_map/all_to_all | solution.py:202
  500.1 125.8 %reduce-scatter.3.cloned.1.call-start = ((), (), s32[]{:S(2)}) async-start(), calls=%async_computation.16 | async-start | bytes 5013504 | tf_op jit(solution)/shard_map/reduce_scatter | solution.py:142
  503.4 4.9 collective-permute-start.23
  512.4 46.6 %copy-start.91 = (f32[2,384,48]{1,2,0:T(8,128)S(1)}, f32[2,384,48]{1,2,0:T(8,128)}, u32[]{:S(2)}) copy-start(f32[2,384,48]{1,2,0:T(8,128)} %param.27) | copy-start | bytes 442372
  551.9 69.3 %all-to-all-start.10 = ((f32[16,24,1536]{2,1,0:T(8,128)}), f32[16,24,1536]{2,1,0:T(8,128)S(1)}, u32[]{:S(2)}, u32[]{:S(2)}) async-start(f32[16,24,1536]{2,1,0:T(8,128)} %bitcast_add_fusion.1), calls=%async_computation.12 | async-start | bytes 4718592 | tf_op jit(solution)/shard_map/all_to_all | solution.py:202
  640.4 58.1 %all-to-all-start.12 = ((f32[16,48,768]{2,1,0:T(8,128)}), f32[16,48,768]{2,1,0:T(8,128)S(1)}, u32[]{:S(2)}, u32[]{:S(2)}) async-start(f32[16,48,768]{2,1,0:T(8,128)} %copy.259), calls=%async_computation.14 | async-start | bytes 4718592 | tf_op jit(solution)/shard_map/all_to_all | solution.py:438
  702.9 4.9 collective-permute-start.25
  709.6 28.7 %copy-start.80 = (f32[19968]{0:T(1024)S(1)}, f32[19968]{0:T(1024)}, u32[]{:S(2)}) copy-start(f32[19968]{0:T(1024)} %add.471) | copy-start | bytes 239620
  709.6 27.5 %collective-permute-start.26 = (f32[384,768]{1,0:T(8,128)S(1)}, f32[384,768]{1,0:T(8,128)S(1)}, u32[]{:S(2)}, u32[]{:S(2)}) collective-permute-start(f32[384,768]{1,0:T(8,128)S(1)} %dynamic-slice_add_fusion), channel_id=1, source_target_pairs={{0,1},{1,0},{2,3},{3,2},{4,5},{5,4},{6,7},{7,6},{8,9},{9,8},{10,11... | collective-permute-start | bytes 3538952 | tf_op jit(solution)/shard_map/ppermute | solution.py:449
  737.2 5.3 collective-permute-start.27
  811.8 32.7 %all-to-all-start.13 = ((bf16[16,48,768]{2,1,0:T(8,128)(2,1)}), bf16[16,48,768]{2,1,0:T(8,128)(2,1)S(1)}, u32[]{:S(2)}, u32[]{:S(2)}) async-start(bf16[16,48,768]{2,1,0:T(8,128)(2,1)} %bitcast.142), calls=%async_computation.15 | async-start | bytes 2359296 | tf_op jit(solution)/shard_map/all_to_all | solution.py:475
  817.4 28.2 %copy-start.95 = (f32[2,2,768]{2,1,0:T(2,128)}, f32[2,2,768]{2,1,0:T(2,128)S(1)}, u32[]{:S(2)}) copy-start(f32[2,2,768]{2,1,0:T(2,128)S(1)} %slice.420) | copy-start | bytes 36868
  818.0 27.5 %copy-start.84 = (f32[2,3072]{1,0:T(2,128)}, f32[2,3072]{1,0:T(2,128)S(1)}, u32[]{:S(2)}) copy-start(f32[2,3072]{1,0:T(2,128)S(1)} %reshape.602) | copy-start | bytes 73732
  818.1 27.5 %copy-start.85 = (f32[2,4,768]{2,1,0:T(4,128)}, f32[2,4,768]{2,1,0:T(4,128)S(1)}, u32[]{:S(2)}) copy-start(f32[2,4,768]{2,1,0:T(4,128)S(1)} %reshape.600) | copy-start | bytes 73732
  (147 other events, 723.1 us)
Sparse Core Ops, SparseCore 0:
  10.9 44.5 all-gather.4
  58.3 52.4 all-gather.6
  380.6 103.0 reduce-scatter.4
  504.5 105.3 reduce-scatter.2

commit v8 on v7

--- a/solution.py
+++ b/solution.py
@@ -216,219 +216,12 @@
     )
 
 
-def vector_step(params, gradients):
-    return params - vector_rate * gradients * lax.rsqrt(
-        jnp.mean(gradients * gradients, axis=-1, keepdims=True) + vector_eps
-    )
-
-
-def local(
-    block_input,
-    cotangent,
-    segments,
-    qkv_weight,
-    proj_weight,
-    up_weight,
-    down_weight,
-    norm_gains,
-    biases,
-    qkv_bias,
-    up_bias,
-    qkv_state,
-    proj_state,
-    up_state,
-    down_state,
-):
-    tensor_rank = lax.axis_index("tensor")
-    local_width = qkv_weight.shape[3]
-    local_hidden = up_weight.shape[2]
-    head_count = local_width // HD
-    model_width = block_input.shape[1]
-    segment_row = segments[0]
-    cosine_table, sine_table = rotary_tables(segment_row)
-    stream = block_input.astype(jnp.float32)
-    saved_layers = []
-    for layer_id in range(LAYERS):
-        layer_weights = (
-            chip_gather_rows(qkv_weight[layer_id]),
-            chip_gather_rows(proj_weight[layer_id].T),
-            dp_gather(up_weight[layer_id], 0),
-            chip_gather_rows(down_weight[layer_id].T),
-        )
-        qkv_full, proj_full, up_full, down_full = layer_weights
-        normed, inverse = normalize(stream)
-        attn_rows = (normed * norm_gains[layer_id, 0] + biases[layer_id, 0]).astype(jnp.bfloat16)
-        mlp_rows = (normed * norm_gains[layer_id, 1] + biases[layer_id, 1]).astype(jnp.bfloat16)
-        both_in = tensor_gather(jnp.concatenate([attn_rows, mlp_rows], axis=1))
-        attn_in, mlp_in = both_in[:, :model_width], both_in[:, model_width:]
-        length = attn_in.shape[0]
-        qkv_local_bias = lax.dynamic_slice_in_dim(
-            qkv_bias[layer_id], tensor_rank * local_width, local_width, 1
-        )
-        qkv_pre = (
-            jnp.einsum("ld,dcf->lcf", attn_in, qkv_full, preferred_element_type=jnp.float32)
-            + qkv_local_bias
-        )
-        shaped = qkv_pre.reshape(length, 3, head_count, HD)
-        queries = rotate(shaped[:, 0], cosine_table, sine_table).astype(jnp.bfloat16)
-        key_rows = rotate(shaped[:, 1], cosine_table, sine_table).astype(jnp.bfloat16)
-        values = shaped[:, 2].astype(jnp.bfloat16)
-        heads_out, log_sums = attend(queries, key_rows, values, segment_row)
-        heads_flat = heads_out.reshape(length, local_width)
-        up_local_bias = lax.dynamic_slice_in_dim(
-            up_bias[layer_id], tensor_rank * local_hidden, local_hidden, 0
-        )
-        up_pre = jnp.dot(mlp_in, up_full, preferred_element_type=jnp.float32) + up_local_bias
-        act_low = gelu_exact(up_pre).astype(jnp.bfloat16)
-        partial_sum = jnp.einsum(
-            "lf,df->ld", heads_flat, proj_full, preferred_element_type=jnp.float32
-        ) + jnp.einsum("lf,df->ld", act_low, down_full, preferred_element_type=jnp.float32)
-        branch = tensor_scatter(partial_sum)
-        saved_layers.append(
-            (
-                normed,
-                inverse,
-                attn_in,
-                mlp_in,
-                queries,
-                key_rows,
-                values,
-                log_sums,
-                heads_flat,
-                up_pre,
-                act_low,
-                layer_weights,
-            )
-        )
-        stream = stream + branch + biases[layer_id, 2] + biases[layer_id, 3]
-    grad_stream = cotangent.astype(jnp.float32)
-    gains_list = [None] * LAYERS
-    biases_list = [None] * LAYERS
-    qkv_bias_list = [None] * LAYERS
-    up_bias_list = [None] * LAYERS
-    weight_list = [None] * LAYERS
-    for layer_id in reversed(range(LAYERS)):
-        (
-            normed,
-            inverse,
-            attn_in,
-            mlp_in,
-            queries,
-            key_rows,
-            values,
-            log_sums,
-            heads_flat,
-            up_pre,
-            act_low,
-            layer_weights,
-        ) = saved_layers[layer_id]
-        qkv_full, proj_full, up_full, down_full = layer_weights
-        length = attn_in.shape[0]
-        out_bias_grad = jnp.sum(grad_stream, axis=0)
-        branch_grad = tensor_gather(grad_stream.astype(jnp.bfloat16))
-        down_part = jnp.einsum(
-            "lf,ld->df", act_low, branch_grad, preferred_element_type=jnp.float32
-        )
-        act_grad = jnp.einsum(
-            "ld,df->lf", branch_grad, down_full, preferred_element_type=jnp.float32
-        )
-        gelu_back = jax.vjp(gelu_exact, up_pre)[1]
-        up_pre_grad = gelu_back(act_grad)[0].astype(jnp.bfloat16)
-        up_bias_part = jnp.sum(up_pre_grad, axis=0, dtype=jnp.float32)
-        up_part = jnp.einsum("ld,lf->df", mlp_in, up_pre_grad, preferred_element_type=jnp.float32)
-        mlp_in_grad = jnp.einsum(
-            "lf,df->ld", up_pre_grad, up_full, preferred_element_type=jnp.float32
-        )
-        proj_part = jnp.einsum(
-            "lf,ld->df", heads_flat, branch_grad, preferred_element_type=jnp.float32
-        )
-        heads_grad = (
-            jnp.einsum("ld,df->lf", branch_grad, proj_full, preferred_element_type=jnp.float32)
-            .astype(jnp.bfloat16)
-            .reshape(length, head_count, HD)
-        )
-        query_grad, key_grad, value_grad = attend_back(
-            queries, key_rows, values, heads_grad, log_sums, segment_row
-        )
-        qkv_pre_grad = jnp.stack(
-            [
-                unrotate(query_grad, cosine_table, sine_table),
-                unrotate(key_grad, cosine_table, sine_table),
-                value_grad,
-            ],
-            axis=1,
-        )
-        qkv_pre_grad = qkv_pre_grad.reshape(length, 3, local_width).astype(jnp.bfloat16)
-        qkv_bias_part = jnp.sum(qkv_pre_grad, axis=0, dtype=jnp.float32)
-        qkv_part = jnp.einsum(
-            "ld,lcf->dcf", attn_in, qkv_pre_grad, preferred_element_type=jnp.float32
-        )
-        attn_in_grad = jnp.einsum(
-            "lcf,dcf->ld", qkv_pre_grad, qkv_full, preferred_element_type=jnp.float32
-        )
-        both_grad = tensor_scatter(jnp.concatenate([attn_in_grad, mlp_in_grad], axis=1))
-        attn_rows_grad, mlp_rows_grad = both_grad[:, :model_width], both_grad[:, model_width:]
-        gains_list[layer_id] = jnp.stack(
-            [jnp.sum(attn_rows_grad * normed, axis=0), jnp.sum(mlp_rows_grad * normed, axis=0)]
-        )
-        biases_list[layer_id] = jnp.stack(
-            [
-                jnp.sum(attn_rows_grad, axis=0),
-                jnp.sum(mlp_rows_grad, axis=0),
-                out_bias_grad,
-                out_bias_grad,
-            ]
-        )
-        qkv_bias_list[layer_id] = lax.dynamic_update_slice_in_dim(
-            jnp.zeros((3, model_width), jnp.float32), qkv_bias_part, tensor_rank * local_width, 1
-        )
-        up_bias_list[layer_id] = lax.dynamic_update_slice_in_dim(
-            jnp.zeros((up_bias.shape[1],), jnp.float32), up_bias_part, tensor_rank * local_hidden, 0
-        )
-        normed_grad = (
-            attn_rows_grad * norm_gains[layer_id, 0] + mlp_rows_grad * norm_gains[layer_id, 1]
-        )
-        normed_mean = jnp.mean(normed_grad, axis=-1, keepdims=True)
-        product_mean = jnp.mean(normed_grad * normed, axis=-1, keepdims=True)
-        grad_stream = grad_stream + inverse * (normed_grad - normed_mean - normed * product_mean)
-        weight_list[layer_id] = (qkv_part, proj_part, up_part, down_part)
-        if layer_id > 0:
-            weight_list[layer_id] = scatter_layer(weight_list[layer_id])
-    small_parts = (
-        jnp.stack(gains_list),
-        jnp.stack(biases_list),
-        jnp.stack(qkv_bias_list),
-        jnp.stack(up_bias_list),
-    )
-    flat = butterfly_sum(jnp.concatenate([part.reshape(-1) for part in small_parts]))
-    small_sums = []
-    offset = 0
-    for part in small_parts:
-        small_sums.append(flat[offset : offset + part.size].reshape(part.shape))
-        offset += part.size
-    gains_grad, biases_grad, qkv_bias_grad, up_bias_grad = small_sums
-    flat, first_parts = lax.optimization_barrier((flat, weight_list[0]))
-    weight_list[0] = scatter_layer(first_parts)
-    qkv_grad = jnp.stack([weight_list[layer_id][0] for layer_id in range(LAYERS)])
-    proj_grad = jnp.stack([weight_list[layer_id][1] for layer_id in range(LAYERS)])
-    up_grad = jnp.stack([weight_list[layer_id][2] for layer_id in range(LAYERS)])
-    down_grad = jnp.stack([weight_list[layer_id][3] for layer_id in range(LAYERS)])
-    qkv_state_new = momentum * qkv_state + qkv_grad
-    proj_state_new = momentum * proj_state + proj_grad
-    up_state_new = momentum * up_state + up_grad
-    down_state_new = momentum * down_state + down_grad
-    rows_local = qkv_state.shape[1]
+def orthogonal_rows(slot_mats, rows_local, keep_with=None):
     dp_count = lax.axis_size("dp")
     dp_rank = lax.axis_index("dp")
-    slot_count = 4 * LAYERS
+    slot_count = len(slot_mats)
     sub = dp_count // slot_count
-    piece_width = up_state.shape[2] // sub
-    slot_mats = []
-    for layer_id in range(LAYERS):
-        slot_mats.append(qkv_state_new[layer_id].reshape(rows_local, 3 * local_width))
-        slot_mats.append(proj_state_new[layer_id].T)
-        slot_mats.append(up_state_new[layer_id])
-        slot_mats.append(down_state_new[layer_id].T)
+    piece_width = max(mat.shape[1] for mat in slot_mats) // sub
     pieces = []
     for mat in slot_mats:
         width = mat.shape[1] // sub
@@ -437,7 +230,8 @@
     outgoing = jnp.concatenate(pieces, axis=0)
     owned = lax.all_to_all(outgoing, "dp", split_axis=0, concat_axis=0, tiled=True)
     owned = owned.reshape(dp_count * rows_local, piece_width)
-    owned, grad_stream = lax.optimization_barrier((owned, grad_stream))
+    if keep_with is not None:
+        owned, keep_with = lax.optimization_barrier((owned, keep_with))
     gram = jnp.dot(owned, owned.T, precision=ns_precision)
     bit = 1
     while bit < sub:
@@ -488,14 +282,234 @@
             .transpose(1, 0, 2)
             .reshape(rows_local, sub * width)
         )
+    return my_rows, keep_with
+
+
+def vector_step(params, gradients):
+    return params - vector_rate * gradients * lax.rsqrt(
+        jnp.mean(gradients * gradients, axis=-1, keepdims=True) + vector_eps
+    )
+
+
+def local(
+    block_input,
+    cotangent,
+    segments,
+    qkv_weight,
+    proj_weight,
+    up_weight,
+    down_weight,
+    norm_gains,
+    biases,
+    qkv_bias,
+    up_bias,
+    qkv_state,
+    proj_state,
+    up_state,
+    down_state,
+):
+    tensor_rank = lax.axis_index("tensor")
+    local_width = qkv_weight.shape[3]
+    local_hidden = up_weight.shape[2]
+    head_count = local_width // HD
+    model_width = block_input.shape[1]
+    segment_row = segments[0]
+    cosine_table, sine_table = rotary_tables(segment_row)
+    stream = block_input.astype(jnp.float32)
+    saved_layers = []
+    for layer_id in range(LAYERS):
+        layer_weights = (
+            chip_gather_rows(qkv_weight[layer_id]),
+            chip_gather_rows(proj_weight[layer_id].T),
+            dp_gather(up_weight[layer_id], 0),
+            chip_gather_rows(down_weight[layer_id].T),
+        )
+        qkv_full, proj_full, up_full, down_full = layer_weights
+        normed, inverse = normalize(stream)
+        attn_rows = (normed * norm_gains[layer_id, 0] + biases[layer_id, 0]).astype(jnp.bfloat16)
+        mlp_rows = (normed * norm_gains[layer_id, 1] + biases[layer_id, 1]).astype(jnp.bfloat16)
+        both_in = tensor_gather(jnp.concatenate([attn_rows, mlp_rows], axis=1))
+        attn_in, mlp_in = both_in[:, :model_width], both_in[:, model_width:]
+        length = attn_in.shape[0]
+        qkv_local_bias = lax.dynamic_slice_in_dim(
+            qkv_bias[layer_id], tensor_rank * local_width, local_width, 1
+        )
+        qkv_pre = (
+            jnp.einsum("ld,dcf->lcf", attn_in, qkv_full, preferred_element_type=jnp.float32)
+            + qkv_local_bias
+        )
+        shaped = qkv_pre.reshape(length, 3, head_count, HD)
+        queries = rotate(shaped[:, 0], cosine_table, sine_table).astype(jnp.bfloat16)
+        key_rows = rotate(shaped[:, 1], cosine_table, sine_table).astype(jnp.bfloat16)
+        values = shaped[:, 2].astype(jnp.bfloat16)
+        heads_out, log_sums = attend(queries, key_rows, values, segment_row)
+        heads_flat = heads_out.reshape(length, local_width)
+        up_local_bias = lax.dynamic_slice_in_dim(
+            up_bias[layer_id], tensor_rank * local_hidden, local_hidden, 0
+        )
+        up_pre = jnp.dot(mlp_in, up_full, preferred_element_type=jnp.float32) + up_local_bias
+        act_low = gelu_exact(up_pre).astype(jnp.bfloat16)
+        partial_sum = jnp.einsum(
+            "lf,df->ld", heads_flat, proj_full, preferred_element_type=jnp.float32
+        ) + jnp.einsum("lf,df->ld", act_low, down_full, preferred_element_type=jnp.float32)
+        branch = tensor_scatter(partial_sum)
+        saved_layers.append(
+            (
+                normed,
+                inverse,
+                attn_in,
+                mlp_in,
+                queries,
+                key_rows,
+                values,
+                log_sums,
+                heads_flat,
+                up_pre,
+                act_low,
+                layer_weights,
+            )
+        )
+        stream = stream + branch + biases[layer_id, 2] + biases[layer_id, 3]
+    grad_stream = cotangent.astype(jnp.float32)
+    gains_list = [None] * LAYERS
+    biases_list = [None] * LAYERS
+    qkv_bias_list = [None] * LAYERS
+    up_bias_list = [None] * LAYERS
+    weight_list = [None] * LAYERS
+    for layer_id in reversed(range(LAYERS)):
+        (
+            normed,
+            inverse,
+            attn_in,
+            mlp_in,
+            queries,
+            key_rows,
+            values,
+            log_sums,
+            heads_flat,
+            up_pre,
+            act_low,
+            layer_weights,
+        ) = saved_layers[layer_id]
+        qkv_full, proj_full, up_full, down_full = layer_weights
+        length = attn_in.shape[0]
+        out_bias_grad = jnp.sum(grad_stream, axis=0)
+        branch_grad = tensor_gather(grad_stream.astype(jnp.bfloat16))
+        down_part = jnp.einsum(
+            "lf,ld->df", act_low, branch_grad, preferred_element_type=jnp.float32
+        )
+        act_grad = jnp.einsum(
+            "ld,df->lf", branch_grad, down_full, preferred_element_type=jnp.float32
+        )
+        gelu_back = jax.vjp(gelu_exact, up_pre)[1]
+        up_pre_grad = gelu_back(act_grad)[0].astype(jnp.bfloat16)
+        up_bias_part = jnp.sum(up_pre_grad, axis=0, dtype=jnp.float32)
+        up_part = jnp.einsum("ld,lf->df", mlp_in, up_pre_grad, preferred_element_type=jnp.float32)
+        mlp_in_grad = jnp.einsum(
+            "lf,df->ld", up_pre_grad, up_full, preferred_element_type=jnp.float32
+        )
+        proj_part = jnp.einsum(
+            "lf,ld->df", heads_flat, branch_grad, preferred_element_type=jnp.float32
+        )
+        heads_grad = (
+            jnp.einsum("ld,df->lf", branch_grad, proj_full, preferred_element_type=jnp.float32)
+            .astype(jnp.bfloat16)
+            .reshape(length, head_count, HD)
+        )
+        query_grad, key_grad, value_grad = attend_back(
+            queries, key_rows, values, heads_grad, log_sums, segment_row
+        )
+        qkv_pre_grad = jnp.stack(
+            [
+                unrotate(query_grad, cosine_table, sine_table),
+                unrotate(key_grad, cosine_table, sine_table),
+                value_grad,
+            ],
+            axis=1,
+        )
+        qkv_pre_grad = qkv_pre_grad.reshape(length, 3, local_width).astype(jnp.bfloat16)
+        qkv_bias_part = jnp.sum(qkv_pre_grad, axis=0, dtype=jnp.float32)
+        qkv_part = jnp.einsum(
+            "ld,lcf->dcf", attn_in, qkv_pre_grad, preferred_element_type=jnp.float32
+        )
+        attn_in_grad = jnp.einsum(
+            "lcf,dcf->ld", qkv_pre_grad, qkv_full, preferred_element_type=jnp.float32
+        )
+        both_grad = tensor_scatter(jnp.concatenate([attn_in_grad, mlp_in_grad], axis=1))
+        attn_rows_grad, mlp_rows_grad = both_grad[:, :model_width], both_grad[:, model_width:]
+        gains_list[layer_id] = jnp.stack(
+            [jnp.sum(attn_rows_grad * normed, axis=0), jnp.sum(mlp_rows_grad * normed, axis=0)]
+        )
+        biases_list[layer_id] = jnp.stack(
+            [
+                jnp.sum(attn_rows_grad, axis=0),
+                jnp.sum(mlp_rows_grad, axis=0),
+                out_bias_grad,
+                out_bias_grad,
+            ]
+        )
+        qkv_bias_list[layer_id] = lax.dynamic_update_slice_in_dim(
+            jnp.zeros((3, model_width), jnp.float32), qkv_bias_part, tensor_rank * local_width, 1
+        )
+        up_bias_list[layer_id] = lax.dynamic_update_slice_in_dim(
+            jnp.zeros((up_bias.shape[1],), jnp.float32), up_bias_part, tensor_rank * local_hidden, 0
+        )
+        normed_grad = (
+            attn_rows_grad * norm_gains[layer_id, 0] + mlp_rows_grad * norm_gains[layer_id, 1]
+        )
+        normed_mean = jnp.mean(normed_grad, axis=-1, keepdims=True)
+        product_mean = jnp.mean(normed_grad * normed, axis=-1, keepdims=True)
+        grad_stream = grad_stream + inverse * (normed_grad - normed_mean - normed * product_mean)
+        weight_list[layer_id] = (qkv_part, proj_part, up_part, down_part)
+        if layer_id > 0:
+            weight_list[layer_id] = scatter_layer(weight_list[layer_id])
+    small_parts = (
+        jnp.stack(gains_list),
+        jnp.stack(biases_list),
+        jnp.stack(qkv_bias_list),
+        jnp.stack(up_bias_list),
+    )
+    flat = butterfly_sum(jnp.concatenate([part.reshape(-1) for part in small_parts]))
+    small_sums = []
+    offset = 0
+    for part in small_parts:
+        small_sums.append(flat[offset : offset + part.size].reshape(part.shape))
+        offset += part.size
+    gains_grad, biases_grad, qkv_bias_grad, up_bias_grad = small_sums
+    flat, first_parts = lax.optimization_barrier((flat, weight_list[0]))
+    weight_list[0] = scatter_layer(first_parts)
+    qkv_grad = jnp.stack([weight_list[layer_id][0] for layer_id in range(LAYERS)])
+    proj_grad = jnp.stack([weight_list[layer_id][1] for layer_id in range(LAYERS)])
+    up_grad = jnp.stack([weight_list[layer_id][2] for layer_id in range(LAYERS)])
+    down_grad = jnp.stack([weight_list[layer_id][3] for layer_id in range(LAYERS)])
+    qkv_states = [momentum * qkv_state[i] + weight_list[i][0] for i in range(LAYERS)]
+    proj_states = [momentum * proj_state[i] + weight_list[i][1] for i in range(LAYERS)]
+    up_states = [momentum * up_state[i] + weight_list[i][2] for i in range(LAYERS)]
+    down_states = [momentum * down_state[i] + weight_list[i][3] for i in range(LAYERS)]
+    qkv_state_new = jnp.stack(qkv_states)
+    proj_state_new = jnp.stack(proj_states)
+    up_state_new = jnp.stack(up_states)
+    down_state_new = jnp.stack(down_states)
+    rows_local = qkv_state.shape[1]
+    my_rows = [None] * LAYERS
+    for layer_id in reversed(range(LAYERS)):
+        slot_mats = [
+            qkv_states[layer_id].reshape(rows_local, 3 * local_width),
+            proj_states[layer_id].T,
+            up_states[layer_id],
+            down_states[layer_id].T,
+        ]
+        keep_with = grad_stream if layer_id == 0 else None
+        my_rows[layer_id], keep_with = orthogonal_rows(slot_mats, rows_local, keep_with)
+        if layer_id == 0:
+            grad_stream = keep_with
     muon_step = muon_rate * match_rms
     qkv_list, proj_list, up_list, down_list = ([], [], [], [])
     for layer_id in range(LAYERS):
-        base_slot = 4 * layer_id
-        qkv_ortho = my_rows[base_slot].reshape(rows_local, 3, local_width)
-        proj_ortho = my_rows[base_slot + 1].T
-        up_ortho = my_rows[base_slot + 2]
-        down_ortho = my_rows[base_slot + 3].T
+        qkv_ortho = my_rows[layer_id][0].reshape(rows_local, 3, local_width)
+        proj_ortho = my_rows[layer_id][1].T
+        up_ortho = my_rows[layer_id][2]
+        down_ortho = my_rows[layer_id][3].T
         qkv_list.append(
             qkv_weight[layer_id].astype(jnp.float32) - muon_step * math.sqrt(3 * D) * qkv_ortho
         )

time: 866 us -> 1030 us (1.19)
  matrix products: 129 us -> 202 us
  waiting for transfers between devices: 452 us -> 509 us
  other arithmetic: 73.2 us -> 92.4 us
  starting transfers between devices: 102 us -> 114 us
    dot_general x19 -> x38, matrix products: 70.5 us -> 143 us  [the longest x10 39.9 us: orthogonal_rows(): squared = jnp.dot(current_gram, current_gram, precision=ns_precision)]
    ppermute x3 -> x8, waiting for transfers between devices: 31 us -> 100 us  [the longest x4 81.1 us: orthogonal_rows(): gram = gram + lax.ppermute(gram, 'dp', swap_pairs(dp_count, bit))]
    all_to_all x2 -> x4, waiting for transfers between devices: 75.6 us -> 60.4 us  [the longest x2 47.4 us: orthogonal_rows(): lax.all_to_all(outgoing, 'dp', split_axis=0, concat_axis=0, tiled=True)]
    all_to_all x2 -> x4, starting transfers between devices: 10.4 us -> 21.1 us  [the longest x2 11.1 us: orthogonal_rows(): lax.all_to_all(current.astype(jnp.bfloat16).reshape(dp_count, rows_local,...]
  transfers between devices with their start and end apart: 46 -> 53, of which waited for: 28 -> 30; matrix products, arithmetic and copies ran while one was open for 20% -> 28% of each run, Pallas kernels for 0% -> 0%
where the time goes in v8:
time: 1030 us; the launch traced here: 1020 us
  waiting for transfers between devices  509 us (49%)
  matrix products  202 us (20%)
  starting transfers between devices  114 us (11%)
  other arithmetic  92.4 us (9%)
  local copies, waits for them, and re-layouts  80.7 us (8%)
  between operations  19 us (2%)
    all_to_all x6, waiting for transfers between devices, chip_scatter_rows(): lax.all_to_all(chip_sum, 'dp', split_axis=0, concat_axis=0, tiled=True)  200 us
    all_to_all x6, waiting for transfers between devices, chip_gather_rows(): lax.all_to_all(outgoing, 'dp', split_axis=0, concat_axis=0, tiled=True)  91 us
    ppermute x4, waiting for transfers between devices, orthogonal_rows(): gram = gram + lax.ppermute(gram, 'dp', swap_pairs(dp_count, bit))  81.1 us
    all_to_all x2, waiting for transfers between devices, orthogonal_rows(): lax.all_to_all(outgoing, 'dp', split_axis=0, concat_axis=0, tiled=True)  47.4 us
    ppermute x8, waiting for transfers between devices, tensor_swap(): return lax.ppermute(block, 'tensor', [(0, 1), (1, 0)])  40.9 us
    dot_general x10, matrix products, orthogonal_rows(): squared = jnp.dot(current_gram, current_gram, precision=ns_precision)  39.9 us
    all_to_all x6, starting transfers between devices, chip_scatter_rows(): lax.all_to_all(chip_sum, 'dp', split_axis=0, concat_axis=0, tiled=True)  31 us
    dot_general x8, matrix products, orthogonal_rows(): jnp.dot(current_gram, polynomial, precision=ns_precision)  30.8 us
  transfers between devices with their start and end apart: 53, of which 30 were waited for; matrix products, arithmetic and copies ran while one was open for 28% of the time, Pallas kernels for 0%

profile of v8, /device:TPU:11, one launch (start us, length us, event | category | flops | bytes accessed | tf_op | source)
XLA Modules:
  0.0 1016.9 jit_solution(15224126788398839533)
XLA Ops:
  10.6 6.5 all-to-all-start.1
  19.6 9.4 all-to-all-done.1
  29.7 3.9 all-to-all-start.4
  33.9 12.6 %all-to-all-done.4 = bf16[16,24,384]{2,1,0:T(8,128)(2,1)S(1)} async-done(((bf16[16,24,384]{2,1,0:T(8,128)(2,1)}), bf16[16,24,384]{2,1,0:T(8,128)(2,1)S(1)}, u32[]{:S(2)}, u32[]{:S(2)}) %all-to-all-start.4) | async-done | bytes 294944 | tf_op jit(solution)/shard_map/all_to_all | solution.py:188
  47.5 4.9 all-to-all-start
  57.1 21.6 %all-to-all-done = bf16[16,24,3,384]{3,1,2,0:T(8,128)(2,1)S(1)} async-done(((bf16[16,24,3,384]{3,1,2,0:T(8,128)(2,1)}), bf16[16,24,3,384]{3,1,2,0:T(8,128)(2,1)S(1)}, u32[]{:S(2)}, u32[]{:S(2)}) %all-to-all-start) | async-done | bytes 884768 | tf_op jit(solution)/shard_map/all_to_all | solution.py:188
  79.8 4.4 all-to-all-start.2
  93.9 27.5 %all-to-all-done.2 = bf16[16,24,1536]{2,1,0:T(8,128)(2,1)} async-done(((bf16[16,24,1536]{2,1,0:T(8,128)(2,1)}), bf16[16,24,1536]{2,1,0:T(8,128)(2,1)}, u32[]{:S(2)}, u32[]{:S(2)}) %all-to-all-start.2) | async-done | bytes 1179680 | tf_op jit(solution)/shard_map/all_to_all | solution.py:188
  122.4 5.1 all-to-all-start.3
  135.7 13.3 %all-to-all-done.3 = bf16[16,24,3,384]{3,1,2,0:T(8,128)(2,1)} async-done(((bf16[16,24,3,384]{3,1,2,0:T(8,128)(2,1)}), bf16[16,24,3,384]{3,1,2,0:T(8,128)(2,1)}, u32[]{:S(2)}, u32[]{:S(2)}) %all-to-all-start.3) | async-done | bytes 884768 | tf_op jit(solution)/shard_map/all_to_all | solution.py:188
  151.0 5.3 all-to-all-start.5
  158.7 4.3 maximum_select_fusion
  163.1 7.4 multiply_convert_fusion.3
  177.3 6.6 all-to-all-done.5
  192.3 5.0 collective-permute-done.5
  232.4 5.6 multiply_convert_fusion.2
  245.9 13.5 %collective-permute-done.11 = f32[128,1536]{1,0:T(8,128)S(1)} collective-permute-done((f32[128,1536]{1,0:T(8,128)S(1)}, f32[128,1536]{1,0:T(8,128)S(1)}, u32[]{:S(2)}, u32[]{:S(2)}) %collective-permute-start.11) | collective-permute-done | bytes 786464 | tf_op jit(solution)/shard_map/ppermute | solution.py:163
  259.9 8.0 collective-permute-done.9
  296.5 12.6 %collective-permute-done.13 = f32[128,1536]{1,0:T(8,128)} collective-permute-done((f32[128,1536]{1,0:T(8,128)S(1)}, f32[128,1536]{1,0:T(8,128)}, u32[]{:S(2)}, u32[]{:S(2)}) %collective-permute-start.13) | collective-permute-done | bytes 786464 | tf_op jit(solution)/shard_map/ppermute | solution.py:163
  318.9 5.1 all-to-all-start.11
  324.3 4.1 fusion.223
  344.7 4.0 collective-permute-start.20
  351.2 7.0 all-to-all-start.7
  361.2 12.1 %all-to-all-done.7 = f32[16,24,384]{2,1,0:T(8,128)} async-done(((f32[16,24,384]{2,1,0:T(8,128)}), f32[16,24,384]{2,1,0:T(8,128)}, u32[]{:S(2)}, u32[]{:S(2)}) %all-to-all-start.7) | async-done | bytes 589856 | tf_op jit(solution)/shard_map/all_to_all | solution.py:202
  373.3 4.8 all-to-all-start.10
  386.7 3.5 bitcast_add_fusion
  390.2 34.0 %all-to-all-done.10 = f32[16,24,3,384]{3,1,2,0:T(8,128)} async-done(((f32[16,24,3,384]{3,1,2,0:T(8,128)}), f32[16,24,3,384]{3,1,2,0:T(8,128)}, u32[]{:S(2)}, u32[]{:S(2)}) %all-to-all-start.10) | async-done | bytes 1769504 | tf_op jit(solution)/shard_map/all_to_all | solution.py:202
  424.2 5.0 all-to-all-start.12
  435.0 65.2 %all-to-all-done.12 = f32[16,24,1536]{2,1,0:T(8,128)} async-done(((f32[16,24,1536]{2,1,0:T(8,128)}), f32[16,24,1536]{2,1,0:T(8,128)}, u32[]{:S(2)}, u32[]{:S(2)}) %all-to-all-start.12) | async-done | bytes 2359328 | tf_op jit(solution)/shard_map/all_to_all | solution.py:202
  500.3 4.3 all-to-all-start.6
  508.3 4.5 collective-permute-done.21
  512.8 4.2 bitcast_add_fusion.1
  516.9 38.4 %all-to-all-done.6 = f32[16,24,3,384]{3,1,2,0:T(8,128)S(1)} async-done(((f32[16,24,3,384]{3,1,2,0:T(8,128)}), f32[16,24,3,384]{3,1,2,0:T(8,128)S(1)}, u32[]{:S(2)}, u32[]{:S(2)}) %all-to-all-start.6) | async-done | bytes 1769504 | tf_op jit(solution)/shard_map/all_to_all | solution.py:202
  556.6 4.8 all-to-all-start.8
  575.4 50.0 %all-to-all-done.8 = f32[16,24,1536]{2,1,0:T(8,128)S(1)} async-done(((f32[16,24,1536]{2,1,0:T(8,128)}), f32[16,24,1536]{2,1,0:T(8,128)S(1)}, u32[]{:S(2)}, u32[]{:S(2)}) %all-to-all-start.8) | async-done | bytes 2359328 | tf_op jit(solution)/shard_map/all_to_all | solution.py:202
  630.6 5.1 all-to-all-start.14
  638.7 24.8 %all-to-all-done.14 = f32[16,48,384]{2,1,0:T(8,128)S(1)} async-done(((f32[16,48,384]{2,1,0:T(8,128)}), f32[16,48,384]{2,1,0:T(8,128)S(1)}, u32[]{:S(2)}, u32[]{:S(2)}) %all-to-all-start.14) | async-done | bytes 1179680 | tf_op jit(solution)/shard_map/all_to_all | solution.py:231
  663.4 4.9 all-to-all-start.9
  668.4 3.5 fusion.378
  673.3 22.7 %all-to-all-done.9 = f32[16,48,384]{2,1,0:T(8,128)S(1)} async-done(((f32[16,48,384]{2,1,0:T(8,128)}), f32[16,48,384]{2,1,0:T(8,128)S(1)}, u32[]{:S(2)}, u32[]{:S(2)}) %all-to-all-start.9) | async-done | bytes 1179680 | tf_op jit(solution)/shard_map/all_to_all | solution.py:231
  695.9 3.4 fusion.372
  709.8 4.1 add.553
  715.7 39.0 %collective-permute-done.30 = f32[768,768]{1,0:T(8,128)} collective-permute-done((f32[768,768]{1,0:T(8,128)S(1)}, f32[768,768]{1,0:T(8,128)}, u32[]{:S(2)}, u32[]{:S(2)}) %collective-permute-start.30) | collective-permute-done | bytes 2359328 | tf_op jit(solution)/shard_map/ppermute | solution.py:238
  763.2 42.1 %collective-permute-done.26 = f32[768,768]{1,0:T(8,128)} collective-permute-done((f32[768,768]{1,0:T(8,128)}, f32[768,768]{1,0:T(8,128)}, u32[]{:S(2)}, u32[]{:S(2)}) %collective-permute-start.26) | collective-permute-done | bytes 2359328 | tf_op jit(solution)/shard_map/ppermute | solution.py:238
  814.7 18.8 %collective-permute-done.27 = f32[384,768]{1,0:T(8,128)S(1)} collective-permute-done((f32[384,768]{1,0:T(8,128)S(1)}, f32[384,768]{1,0:T(8,128)S(1)}, u32[]{:S(2)}, u32[]{:S(2)}) %collective-permute-start.27) | collective-permute-done | bytes 1179680 | tf_op jit(solution)/shard_map/ppermute | solution.py:243
  838.3 7.2 fusion.7
  845.5 3.4 fusion.24
  855.2 4.7 fusion.48
  859.9 5.0 fusion.52
  868.1 7.4 fusion
  875.5 4.9 fusion.30
  886.7 4.8 fusion.66
  891.5 4.6 fusion.70
  896.1 3.6 fusion.50
  909.5 3.8 fusion.44
  919.6 3.4 fusion.36
  923.0 3.5 fusion.38
  935.9 5.0 all-to-all-start.15
  940.9 5.6 fusion.68
  952.9 3.8 fusion.60
  966.5 3.5 fusion.54
  976.5 3.4 fusion.5
  983.0 6.1 all-to-all-start.13
  991.2 13.0 %all-to-all-done.13 = bf16[16,48,384]{2,1,0:T(8,128)(2,1)S(1)} async-done(((bf16[16,48,384]{2,1,0:T(8,128)(2,1)}), bf16[16,48,384]{2,1,0:T(8,128)(2,1)S(1)}, u32[]{:S(2)}, u32[]{:S(2)}) %all-to-all-start.13) | async-done | bytes 589856 | tf_op jit(solution)/shard_map/all_to_all | solution.py:269
  (806 shorter events, 304.2 us)
Async XLA Ops:
  7.2 155.9 %all-gather.5.cloned.1.call-start = ((), (), s32[]{:S(2)}) async-start(), calls=%async_computation.20 | async-start | bytes 2506752 | tf_op jit(solution)/shard_map/all_gather | solution.py:146
  10.6 18.4 %all-to-all-start.1 = ((bf16[16,24,384]{2,1,0:T(8,128)(2,1)}), bf16[16,24,384]{2,1,0:T(8,128)(2,1)S(1)}, u32[]{:S(2)}, u32[]{:S(2)}) async-start(bf16[16,24,384]{2,1,0:T(8,128)(2,1)} %bitcast.18), calls=%async_computation.1 | async-start | bytes 589824 | tf_op jit(solution)/shard_map/all_to_all | solution.py:188
  17.1 71.0 %collective-permute-start.10 = (bf16[128,768]{1,0:T(8,128)(2,1)}, bf16[128,768]{1,0:T(8,128)(2,1)S(1)}, u32[]{:S(2)}, u32[]{:S(2)}) collective-permute-start(bf16[128,768]{1,0:T(8,128)(2,1)} %param.16), channel_id=1, source_target_pairs={{0,1},{1,0},{2,3},{3,2},{4,5},{5,4},{6,7},{7,6},{8,9},{9,8},{10,11... | collective-permute-start | bytes 589832 | tf_op jit(solution)/shard_map/ppermute | solution.py:163
  19.3 34.4 %copy-start.92 = (bf16[1,48,3,384]{3,1,2,0:T(8,128)(2,1)}, bf16[1,48,3,384]{3,1,2,0:T(8,128)(2,1)S(1)}, u32[]{:S(2)}) copy-start(bf16[1,48,3,384]{3,1,2,0:T(8,128)(2,1)S(1)} %get-tuple-element.256) | copy-start | bytes 331780
  19.3 67.0 %copy-start.90 = (bf16[1,48,3,384]{3,1,2,0:T(8,128)(2,1)}, bf16[1,48,3,384]{3,1,2,0:T(8,128)(2,1)S(1)}, u32[]{:S(2)}) copy-start(bf16[1,48,3,384]{3,1,2,0:T(8,128)(2,1)S(1)} %get-tuple-element.255) | copy-start | bytes 331780
  19.3 33.7 %copy-start.144 = (f32[2,4,768]{2,1,0:T(4,128)S(1)}, f32[2,4,768]{2,1,0:T(4,128)}, u32[]{:S(2)}) copy-start(f32[2,4,768]{2,1,0:T(4,128)} %param.23) | copy-start | bytes 73732
  29.7 16.8 %all-to-all-start.4 = ((bf16[16,24,384]{2,1,0:T(8,128)(2,1)}), bf16[16,24,384]{2,1,0:T(8,128)(2,1)S(1)}, u32[]{:S(2)}, u32[]{:S(2)}) async-start(bf16[16,24,384]{2,1,0:T(8,128)(2,1)} %bitcast.45), calls=%async_computation.4 | async-start | bytes 589824 | tf_op jit(solution)/shard_map/all_to_all | solution.py:188
  47.5 31.2 %all-to-all-start = ((bf16[16,24,3,384]{3,1,2,0:T(8,128)(2,1)}), bf16[16,24,3,384]{3,1,2,0:T(8,128)(2,1)S(1)}, u32[]{:S(2)}, u32[]{:S(2)}) async-start(bf16[16,24,3,384]{3,1,2,0:T(8,128)(2,1)} %bitcast.2), calls=%async_computation | async-start | bytes 1769472 | tf_op jit(solution)/shard_map/all_to_all | solution.py:188
  52.4 180.0 %all-gather.7.cloned.1.call-start = ((), (), s32[]{:S(2)}) async-start(), calls=%async_computation.21 | async-start | bytes 2506752 | tf_op jit(solution)/shard_map/all_gather | solution.py:146
  54.7 34.6 %collective-permute-start = (bf16[128,1536]{1,0:T(8,128)(2,1)}, bf16[128,1536]{1,0:T(8,128)(2,1)}, u32[]{:S(2)}, u32[]{:S(2)}) collective-permute-start(bf16[128,1536]{1,0:T(8,128)(2,1)} %pad_maximum_fusion.11), channel_id=1, source_target_pairs={{0,1},{1,0},{2,3},{3,2},{4,5},{5,4},{6,7},{7,6},{8,9},{9,8},{10,11... | collective-permute-start | bytes 1179656 | tf_op jit(solution)/shard_map/ppermute | solution.py:163
  79.8 41.6 %all-to-all-start.2 = ((bf16[16,24,1536]{2,1,0:T(8,128)(2,1)}), bf16[16,24,1536]{2,1,0:T(8,128)(2,1)}, u32[]{:S(2)}, u32[]{:S(2)}) async-start(bf16[16,24,1536]{2,1,0:T(8,128)(2,1)} %bitcast.26), calls=%async_computation.2 | async-start | bytes 2359296 | tf_op jit(solution)/shard_map/all_to_all | solution.py:188
  85.3 42.6 %collective-permute-start.1 = (bf16[16,24,3,384]{3,1,0,2:T(8,128)(2,1)S(1)}, bf16[16,24,3,384]{3,1,0,2:T(8,128)(2,1)}, u32[]{:S(2)}, u32[]{:S(2)}) collective-permute-start(bf16[16,24,3,384]{3,1,0,2:T(8,128)(2,1)S(1)} %copy.333), channel_id=1, source_target_pairs={{0,2},{2,0},{4,6},{6,4},{8,10},{10,8},{12,14},{14,12},{16,18},{18,... | collective-permute-start | bytes 2654216 | tf_op jit(solution)/shard_map/ppermute | solution.py:189
  87.8 2.9 collective-permute-start.7
  89.1 3.9 collective-permute-start.2
  90.7 39.1 %copy-start.24 = (bf16[256,1536]{1,0:T(8,128)(2,1)}, bf16[256,1536]{1,0:T(8,128)(2,1)S(1)}, u32[]{:S(2)}) copy-start(bf16[256,1536]{1,0:T(8,128)(2,1)S(1)} %maximum_select_fusion.6) | copy-start | bytes 2359300
  122.4 26.6 %all-to-all-start.3 = ((bf16[16,24,3,384]{3,1,2,0:T(8,128)(2,1)}), bf16[16,24,3,384]{3,1,2,0:T(8,128)(2,1)}, u32[]{:S(2)}, u32[]{:S(2)}) async-start(bf16[16,24,3,384]{3,1,2,0:T(8,128)(2,1)} %bitcast.32), calls=%async_computation.3 | async-start | bytes 1769472 | tf_op jit(solution)/shard_map/all_to_all | solution.py:188
  127.5 31.2 %collective-permute-start.3 = (bf16[16,24,1536]{2,1,0:T(8,128)(2,1)}, bf16[16,24,1536]{2,1,0:T(8,128)(2,1)}, u32[]{:S(2)}, u32[]{:S(2)}) collective-permute-start(bf16[16,24,1536]{2,1,0:T(8,128)(2,1)} %all-to-all-done.2), channel_id=1, source_target_pairs={{0,2},{2,0},{4,6},{6,4},{8,10},{10,8},{12,14},{14,12},{16,18},{18,... | collective-permute-start | bytes 3538952 | tf_op jit(solution)/shard_map/ppermute | solution.py:189
  151.0 32.9 %all-to-all-start.5 = ((bf16[16,24,1536]{2,1,0:T(8,128)(2,1)}), bf16[16,24,1536]{2,1,0:T(8,128)(2,1)S(1)}, u32[]{:S(2)}, u32[]{:S(2)}) async-start(bf16[16,24,1536]{2,1,0:T(8,128)(2,1)} %bitcast.474), calls=%async_computation.5 | async-start | bytes 2359296 | tf_op jit(solution)/shard_map/all_to_all | solution.py:188
  172.5 12.8 %collective-permute-start.4 = (f32[128,768]{1,0:T(8,128)}, f32[128,768]{1,0:T(8,128)}, u32[]{:S(2)}, u32[]{:S(2)}) collective-permute-start(f32[128,768]{1,0:T(8,128)} %constant_dynamic-slice_fusion.5), channel_id=1, source_target_pairs={{0,1},{1,0},{2,3},{3,2},{4,5},{5,4},{6,7},{7,6},{8,9},{9,8},{10,11... | collective-permute-start | bytes 1179656 | tf_op jit(solution)/shard_map/ppermute | solution.py:163
  176.7 11.2 %collective-permute-start.6 = (bf16[16,24,3,384]{3,1,0,2:T(8,128)(2,1)}, bf16[16,24,3,384]{3,1,0,2:T(8,128)(2,1)}, u32[]{:S(2)}, u32[]{:S(2)}) collective-permute-start(bf16[16,24,3,384]{3,1,0,2:T(8,128)(2,1)} %copy.332), channel_id=1, source_target_pairs={{0,2},{2,0},{4,6},{6,4},{8,10},{10,8},{12,14},{14,12},{16,18},{18,... | collective-permute-start | bytes 2654216 | tf_op jit(solution)/shard_map/ppermute | solution.py:189
  183.9 6.4 collective-permute-start.8
  187.1 10.2 %collective-permute-start.5 = (bf16[128,1536]{1,0:T(8,128)(2,1)S(1)}, bf16[128,1536]{1,0:T(8,128)(2,1)S(1)}, u32[]{:S(2)}, u32[]{:S(2)}) collective-permute-start(bf16[128,1536]{1,0:T(8,128)(2,1)S(1)} %pad_maximum_fusion.12), channel_id=1, source_target_pairs={{0,1},{1,0},{2,3},{3,2},{4,5},{5,4},{6,7},{7,6},{8,9},{9,8},{10,11... | collective-permute-start | bytes 1179656 | tf_op jit(solution)/shard_map/ppermute | solution.py:163
  225.4 91.5 %collective-permute-start.23 = (f32[16,24,384]{2,1,0:T(8,128)}, f32[16,24,384]{2,1,0:T(8,128)}, u32[]{:S(2)}, u32[]{:S(2)}) collective-permute-start(f32[16,24,384]{2,1,0:T(8,128)} %dynamic-slice_bitcast_fusion.3), channel_id=1, source_target_pairs={{0,2},{2,0},{4,6},{6,4},{8,10},{10,8},{12,14},{14,12},{16,18},{18,... | collective-permute-start | bytes 1769480 | tf_op jit(solution)/shard_map/ppermute | solution.py:201
  240.9 18.5 %collective-permute-start.11 = (f32[128,1536]{1,0:T(8,128)S(1)}, f32[128,1536]{1,0:T(8,128)S(1)}, u32[]{:S(2)}, u32[]{:S(2)}) collective-permute-start(f32[128,1536]{1,0:T(8,128)S(1)} %fusion.188), channel_id=1, source_target_pairs={{0,1},{1,0},{2,3},{3,2},{4,5},{5,4},{6,7},{7,6},{8,9},{9,8},{10,11... | collective-permute-start | bytes 2359304 | tf_op jit(solution)/shard_map/ppermute | solution.py:163
  243.4 114.9 %collective-permute-start.22 = (f32[16,24,3,384]{3,1,2,0:T(8,128)}, f32[16,24,3,384]{3,1,2,0:T(8,128)}, u32[]{:S(2)}, u32[]{:S(2)}) collective-permute-start(f32[16,24,3,384]{3,1,2,0:T(8,128)} %dynamic-slice_bitcast_fusion.2), channel_id=1, source_target_pairs={{0,2},{2,0},{4,6},{6,4},{8,10},{10,8},{12,14},{14,12},{16,18},{18,... | collective-permute-start | bytes 5308424 | tf_op jit(solution)/shard_map/ppermute | solution.py:201
  244.9 22.9 %collective-permute-start.9 = (f32[128,768]{1,0:T(8,128)S(1)}, f32[128,768]{1,0:T(8,128)S(1)}, u32[]{:S(2)}, u32[]{:S(2)}) collective-permute-start(f32[128,768]{1,0:T(8,128)S(1)} %constant_dynamic-slice_fusion.2), channel_id=1, source_target_pairs={{0,1},{1,0},{2,3},{3,2},{4,5},{5,4},{6,7},{7,6},{8,9},{9,8},{10,11... | collective-permute-start | bytes 1179656 | tf_op jit(solution)/shard_map/ppermute | solution.py:163
  268.8 5.0 collective-permute-start.12
  292.2 16.9 %collective-permute-start.13 = (f32[128,1536]{1,0:T(8,128)S(1)}, f32[128,1536]{1,0:T(8,128)}, u32[]{:S(2)}, u32[]{:S(2)}) collective-permute-start(f32[128,1536]{1,0:T(8,128)S(1)} %fusion.185), channel_id=1, source_target_pairs={{0,1},{1,0},{2,3},{3,2},{4,5},{5,4},{6,7},{7,6},{8,9},{9,8},{10,11... | collective-permute-start | bytes 2359304 | tf_op jit(solution)/shard_map/ppermute | solution.py:163
  313.7 10.3 %collective-permute-start.14 = (f32[19968]{0:T(1024)S(1)}, f32[19968]{0:T(1024)S(1)}, u32[]{:S(2)}, u32[]{:S(2)}) collective-permute-start(f32[19968]{0:T(1024)S(1)} %constant_dynamic-update-slice_fusion.4), channel_id=1, source_target_pairs={{0,2},{2,0},{4,6},{6,4},{8,10},{10,8},{12,14},{14,12},{16,18},{18,... | collective-permute-start | bytes 239624 | tf_op jit(solution)/shard_map/ppermute | solution.py:157
  318.9 32.4 %all-to-all-start.11 = ((f32[16,24,384]{2,1,0:T(8,128)}), f32[16,24,384]{2,1,0:T(8,128)}, u32[]{:S(2)}, u32[]{:S(2)}) async-start(f32[16,24,384]{2,1,0:T(8,128)} %bitcast_add_fusion.4), calls=%async_computation.12 | async-start | bytes 1179648 | tf_op jit(solution)/shard_map/all_to_all | solution.py:202
  324.0 5.2 collective-permute-start.15
  329.2 7.0 collective-permute-start.16
  336.3 4.4 collective-permute-start.17
  340.7 3.4 collective-permute-start.18
  344.7 5.6 collective-permute-start.20
  351.2 22.1 %all-to-all-start.7 = ((f32[16,24,384]{2,1,0:T(8,128)}), f32[16,24,384]{2,1,0:T(8,128)}, u32[]{:S(2)}, u32[]{:S(2)}) async-start(f32[16,24,384]{2,1,0:T(8,128)} %bitcast_add_fusion.5), calls=%async_computation.7 | async-start | bytes 1179648 | tf_op jit(solution)/shard_map/all_to_all | solution.py:202
  373.3 50.9 %all-to-all-start.10 = ((f32[16,24,3,384]{3,1,2,0:T(8,128)}), f32[16,24,3,384]{3,1,2,0:T(8,128)}, u32[]{:S(2)}, u32[]{:S(2)}) async-start(f32[16,24,3,384]{3,1,2,0:T(8,128)} %bitcast_add_fusion.2), calls=%async_computation.11 | async-start | bytes 3538944 | tf_op jit(solution)/shard_map/all_to_all | solution.py:202
  378.2 249.5 %reduce-scatter.5.cloned.1.call-start = ((), (), s32[]{:S(2)}) async-start(), calls=%async_computation.19 | async-start | bytes 5013504 | tf_op jit(solution)/shard_map/reduce_scatter | solution.py:142
  381.9 4.8 collective-permute-start.24
  390.2 39.1 %copy-start.10 = (f32[768,3,384]{2,0,1:T(8,128)S(1)}, f32[768,3,384]{2,0,1:T(8,128)}, u32[]{:S(2)}) copy-start(f32[768,3,384]{2,0,1:T(8,128)} %fusion.226) | copy-start | bytes 10616836
  424.2 76.0 %all-to-all-start.12 = ((f32[16,24,1536]{2,1,0:T(8,128)}), f32[16,24,1536]{2,1,0:T(8,128)}, u32[]{:S(2)}, u32[]{:S(2)}) async-start(f32[16,24,1536]{2,1,0:T(8,128)} %bitcast_add_fusion), calls=%async_computation.14 | async-start | bytes 4718592 | tf_op jit(solution)/shard_map/all_to_all | solution.py:202
  429.7 3.8 collective-permute-start.19
  500.3 55.0 %all-to-all-start.6 = ((f32[16,24,3,384]{3,1,2,0:T(8,128)}), f32[16,24,3,384]{3,1,2,0:T(8,128)S(1)}, u32[]{:S(2)}, u32[]{:S(2)}) async-start(f32[16,24,3,384]{3,1,2,0:T(8,128)} %bitcast_add_fusion.3), calls=%async_computation.6 | async-start | bytes 3538944 | tf_op jit(solution)/shard_map/all_to_all | solution.py:202
  504.6 123.1 %reduce-scatter.3.cloned.1.call-start = ((), (), s32[]{:S(2)}) async-start(), calls=%async_computation.18 | async-start | bytes 5013504 | tf_op jit(solution)/shard_map/reduce_scatter | solution.py:142
  507.9 4.9 collective-permute-start.21
  516.9 47.3 %copy-start.139 = (f32[2,384,48]{1,2,0:T(8,128)S(1)}, f32[2,384,48]{1,2,0:T(8,128)}, u32[]{:S(2)}) copy-start(f32[2,384,48]{1,2,0:T(8,128)} %param.27) | copy-start | bytes 442372
  556.6 68.9 %all-to-all-start.8 = ((f32[16,24,1536]{2,1,0:T(8,128)}), f32[16,24,1536]{2,1,0:T(8,128)S(1)}, u32[]{:S(2)}, u32[]{:S(2)}) async-start(f32[16,24,1536]{2,1,0:T(8,128)} %bitcast_add_fusion.1), calls=%async_computation.9 | async-start | bytes 4718592 | tf_op jit(solution)/shard_map/all_to_all | solution.py:202
  570.3 55.3 %copy-start.75 = (f32[24,1536]{1,0:T(8,128)}, f32[24,1536]{1,0:T(8,128)S(1)}, u32[]{:S(2)}) copy-start(f32[24,1536]{1,0:T(8,128)S(1)} %get-tuple-element.144) | copy-start | bytes 442372
  570.3 55.3 %copy-start.77 = (f32[24,1536]{1,0:T(8,128)}, f32[24,1536]{1,0:T(8,128)S(1)}, u32[]{:S(2)}) copy-start(f32[24,1536]{1,0:T(8,128)S(1)} %get-tuple-element.145) | copy-start | bytes 442372
  570.6 65.2 %copy-start.64 = (f32[24,3,384]{2,0,1:T(8,128)}, f32[24,3,384]{2,0,1:T(8,128)S(1)}, u32[]{:S(2)}) copy-start(f32[24,3,384]{2,0,1:T(8,128)S(1)} %get-tuple-element.150) | copy-start | bytes 331780
  570.6 65.2 %copy-start.66 = (f32[24,3,384]{2,0,1:T(8,128)}, f32[24,3,384]{2,0,1:T(8,128)S(1)}, u32[]{:S(2)}) copy-start(f32[24,3,384]{2,0,1:T(8,128)S(1)} %get-tuple-element.151) | copy-start | bytes 331780
  630.6 32.8 %all-to-all-start.14 = ((f32[16,48,384]{2,1,0:T(8,128)}), f32[16,48,384]{2,1,0:T(8,128)S(1)}, u32[]{:S(2)}, u32[]{:S(2)}) async-start(f32[16,48,384]{2,1,0:T(8,128)} %copy.285), calls=%async_computation.16 | async-start | bytes 2359296 | tf_op jit(solution)/shard_map/all_to_all | solution.py:231
  663.4 32.5 %all-to-all-start.9 = ((f32[16,48,384]{2,1,0:T(8,128)}), f32[16,48,384]{2,1,0:T(8,128)S(1)}, u32[]{:S(2)}, u32[]{:S(2)}) async-start(f32[16,48,384]{2,1,0:T(8,128)} %copy.277), calls=%async_computation.10 | async-start | bytes 2359296 | tf_op jit(solution)/shard_map/all_to_all | solution.py:231
  671.9 27.6 %collective-permute-start.29 = (f32[768,768]{1,0:T(8,128)}, f32[768,768]{1,0:T(8,128)}, u32[]{:S(2)}, u32[]{:S(2)}) collective-permute-start(f32[768,768]{1,0:T(8,128)} %fusion.378), channel_id=1, source_target_pairs={{0,2},{2,0},{4,6},{6,4},{8,10},{10,8},{12,14},{14,12},{16,18},{18,... | collective-permute-start | bytes 7077896 | tf_op jit(solution)/shard_map/ppermute | solution.py:238
  699.4 10.4 %collective-permute-start.25 = (f32[768,768]{1,0:T(8,128)}, f32[768,768]{1,0:T(8,128)}, u32[]{:S(2)}, u32[]{:S(2)}) collective-permute-start(f32[768,768]{1,0:T(8,128)} %fusion.372), channel_id=1, source_target_pairs={{0,2},{2,0},{4,6},{6,4},{8,10},{10,8},{12,14},{14,12},{16,18},{18,... | collective-permute-start | bytes 7077896 | tf_op jit(solution)/shard_map/ppermute | solution.py:238
  702.2 52.6 %collective-permute-start.30 = (f32[768,768]{1,0:T(8,128)S(1)}, f32[768,768]{1,0:T(8,128)}, u32[]{:S(2)}, u32[]{:S(2)}) collective-permute-start(f32[768,768]{1,0:T(8,128)S(1)} %add.572), channel_id=1, source_target_pairs={{0,4},{2,6},{4,0},{6,2},{8,12},{10,14},{12,8},{14,10},{16,20},{18,... | collective-permute-start | bytes 7077896 | tf_op jit(solution)/shard_map/ppermute | solution.py:238
  713.9 91.4 %collective-permute-start.26 = (f32[768,768]{1,0:T(8,128)}, f32[768,768]{1,0:T(8,128)}, u32[]{:S(2)}, u32[]{:S(2)}) collective-permute-start(f32[768,768]{1,0:T(8,128)} %add.553), channel_id=1, source_target_pairs={{0,4},{2,6},{4,0},{6,2},{8,12},{10,14},{12,8},{14,10},{16,20},{18,... | collective-permute-start | bytes 7077896 | tf_op jit(solution)/shard_map/ppermute | solution.py:238
  757.1 51.2 %collective-permute-start.31 = (f32[384,768]{1,0:T(8,128)}, f32[384,768]{1,0:T(8,128)S(1)}, u32[]{:S(2)}, u32[]{:S(2)}) collective-permute-start(f32[384,768]{1,0:T(8,128)} %dynamic-slice_add_fusion), channel_id=1, source_target_pairs={{0,1},{1,0},{2,3},{3,2},{4,5},{5,4},{6,7},{7,6},{8,9},{9,8},{10,11... | collective-permute-start | bytes 3538952 | tf_op jit(solution)/shard_map/ppermute | solution.py:243
  760.3 48.1 %copy-start.132 = (f32[2,4,768]{2,1,0:T(4,128)}, f32[2,4,768]{2,1,0:T(4,128)S(1)}, u32[]{:S(2)}) copy-start(f32[2,4,768]{2,1,0:T(4,128)S(1)} %reshape.640) | copy-start | bytes 73732
  807.2 26.3 %collective-permute-start.27 = (f32[384,768]{1,0:T(8,128)S(1)}, f32[384,768]{1,0:T(8,128)S(1)}, u32[]{:S(2)}, u32[]{:S(2)}) collective-permute-start(f32[384,768]{1,0:T(8,128)S(1)} %dynamic-slice_add_fusion.1), channel_id=1, source_target_pairs={{0,1},{1,0},{2,3},{3,2},{4,5},{5,4},{6,7},{7,6},{8,9},{9,8},{10,11... | collective-permute-start | bytes 3538952 | tf_op jit(solution)/shard_map/ppermute | solution.py:243
  809.8 26.1 %collective-permute-start.32 = (f32[384,768]{1,0:T(8,128)S(1)}, f32[384,768]{1,0:T(8,128)S(1)}, u32[]{:S(2)}, u32[]{:S(2)}) collective-permute-start(f32[384,768]{1,0:T(8,128)S(1)} %add.574), channel_id=1, source_target_pairs={{0,2},{2,0},{4,6},{6,4},{8,10},{10,8},{12,14},{14,12},{16,18},{18,... | collective-permute-start | bytes 3538952 | tf_op jit(solution)/shard_map/ppermute | solution.py:244
  833.7 31.3 %collective-permute-start.28 = (f32[384,768]{1,0:T(8,128)S(1)}, f32[384,768]{1,0:T(8,128)}, u32[]{:S(2)}, u32[]{:S(2)}) collective-permute-start(f32[384,768]{1,0:T(8,128)S(1)} %add.556), channel_id=1, source_target_pairs={{0,2},{2,0},{4,6},{6,4},{8,10},{10,8},{12,14},{14,12},{16,18},{18,... | collective-permute-start | bytes 3538952 | tf_op jit(solution)/shard_map/ppermute | solution.py:244
  935.9 47.1 %all-to-all-start.15 = ((bf16[16,48,384]{2,1,0:T(8,128)(2,1)}), bf16[16,48,384]{2,1,0:T(8,128)(2,1)S(1)}, u32[]{:S(2)}, u32[]{:S(2)}) async-start(bf16[16,48,384]{2,1,0:T(8,128)(2,1)} %bitcast.478), calls=%async_computation.17 | async-start | bytes 1179648 | tf_op jit(solution)/shard_map/all_to_all | solution.py:269
  983.0 21.2 %all-to-all-start.13 = ((bf16[16,48,384]{2,1,0:T(8,128)(2,1)}), bf16[16,48,384]{2,1,0:T(8,128)(2,1)S(1)}, u32[]{:S(2)}, u32[]{:S(2)}) async-start(bf16[16,48,384]{2,1,0:T(8,128)(2,1)} %bitcast.135), calls=%async_computation.15 | async-start | bytes 1179648 | tf_op jit(solution)/shard_map/all_to_all | solution.py:269
  (200 other events, 1178.5 us)
Sparse Core Ops, SparseCore 0:
  10.9 44.4 all-gather.4
  58.2 52.2 all-gather.6
  385.5 103.5 reduce-scatter.4
  508.9 105.1 reduce-scatter.2

commit v9 on v7

--- a/solution.py
+++ b/solution.py
@@ -394,6 +394,8 @@
         weight_list[layer_id] = (qkv_part, proj_part, up_part, down_part)
         if layer_id > 0:
             weight_list[layer_id] = scatter_layer(weight_list[layer_id])
+            first_sum, grad_stream = lax.optimization_barrier((weight_list[layer_id][0], grad_stream))
+            weight_list[layer_id] = (first_sum,) + weight_list[layer_id][1:]
     small_parts = (
         jnp.stack(gains_list),
         jnp.stack(biases_list),

time: 866 us -> 804 us (0.928)
  waiting for transfers between devices: 452 us -> 343 us
  blocking collectives: 0 us -> 57.4 us
  starting transfers between devices: 102 us -> 88.3 us
    all_to_all x6, waiting for transfers between devices: 199 us -> 123 us  [chip_scatter_rows(): lax.all_to_all(chip_sum, 'dp', split_axis=0, concat_axis=0, tiled=True)]
    all_to_all x0 -> x1, blocking collectives: none -> 57.4 us  [local(): lax.all_to_all(outgoing, 'dp', split_axis=0, concat_axis=0, tiled=True)]
    all_to_all x1 -> x0, waiting for transfers between devices: 51.6 us -> none  [local(): lax.all_to_all(outgoing, 'dp', split_axis=0, concat_axis=0, tiled=True)]
    ppermute x4, waiting for transfers between devices: 3.95 us -> 36.2 us  [butterfly_sum(): flat = flat + lax.ppermute(flat, 'dp', swap_pairs(count, bit))]
    ppermute x8, waiting for transfers between devices: 39.1 us -> 26.3 us  [tensor_swap(): return lax.ppermute(block, 'tensor', [(0, 1), (1, 0)])]
    unnamed x339 -> x325, local copies, waits for them, and re-layouts: 18.9 us -> 15.1 us
  transfers between devices with their start and end apart: 46 -> 45, of which waited for: 28 -> 23; matrix products, arithmetic and copies ran while one was open for 20% -> 23% of each run, Pallas kernels for 0% -> 0%
where the time goes in v9:
time: 804 us; the launch traced here: 795 us
  waiting for transfers between devices  343 us (43%)
  matrix products  131 us (16%)
  starting transfers between devices  88.3 us (11%)
  other arithmetic  81 us (10%)
  local copies, waits for them, and re-layouts  77.1 us (10%)
  blocking collectives  57.4 us (7%)
  between operations  17.4 us (2%)
    all_to_all x6, waiting for transfers between devices, chip_scatter_rows(): lax.all_to_all(chip_sum, 'dp', split_axis=0, concat_axis=0, tiled=True)  123 us
    all_to_all x6, waiting for transfers between devices, chip_gather_rows(): lax.all_to_all(outgoing, 'dp', split_axis=0, concat_axis=0, tiled=True)  91.4 us
    all_to_all x1, blocking collectives, local(): lax.all_to_all(outgoing, 'dp', split_axis=0, concat_axis=0, tiled=True)  57.4 us
    ppermute x4, waiting for transfers between devices, butterfly_sum(): flat = flat + lax.ppermute(flat, 'dp', swap_pairs(count, bit))  36.2 us
    all_to_all x6, starting transfers between devices, chip_scatter_rows(): lax.all_to_all(chip_sum, 'dp', split_axis=0, concat_axis=0, tiled=True)  34.8 us
    all_to_all x6, starting transfers between devices, chip_gather_rows(): lax.all_to_all(outgoing, 'dp', split_axis=0, concat_axis=0, tiled=True)  29.9 us
    ppermute x1, waiting for transfers between devices, local(): mine = mine + lax.ppermute(mine, 'tensor', [(0, 1), (1, 0)])  26.4 us
    ppermute x8, waiting for transfers between devices, tensor_swap(): return lax.ppermute(block, 'tensor', [(0, 1), (1, 0)])  26.3 us
  transfers between devices with their start and end apart: 45, of which 23 were waited for; matrix products, arithmetic and copies ran while one was open for 23% of the time, Pallas kernels for 0%

profile of v9, /device:TPU:11, one launch (start us, length us, event | category | flops | bytes accessed | tf_op | source)
XLA Modules:
  0.0 795.4 jit_solution(16219346266263553668)
XLA Ops:
  10.7 6.5 all-to-all-start.1
  18.8 10.3 %all-to-all-done.1 = bf16[16,24,384]{2,1,0:T(8,128)(2,1)S(1)} async-done(((bf16[16,24,384]{2,1,0:T(8,128)(2,1)}), bf16[16,24,384]{2,1,0:T(8,128)(2,1)S(1)}, u32[]{:S(2)}, u32[]{:S(2)}) %all-to-all-start.1) | async-done | bytes 294944 | tf_op jit(solution)/shard_map/all_to_all | solution.py:188
  29.8 4.2 all-to-all-start.4
  34.2 12.9 %all-to-all-done.4 = bf16[16,24,384]{2,1,0:T(8,128)(2,1)S(1)} async-done(((bf16[16,24,384]{2,1,0:T(8,128)(2,1)}), bf16[16,24,384]{2,1,0:T(8,128)(2,1)S(1)}, u32[]{:S(2)}, u32[]{:S(2)}) %all-to-all-start.4) | async-done | bytes 294944 | tf_op jit(solution)/shard_map/all_to_all | solution.py:188
  48.1 4.9 all-to-all-start
  58.1 21.3 %all-to-all-done = bf16[16,24,3,384]{3,1,2,0:T(8,128)(2,1)S(1)} async-done(((bf16[16,24,3,384]{3,1,2,0:T(8,128)(2,1)}), bf16[16,24,3,384]{3,1,2,0:T(8,128)(2,1)S(1)}, u32[]{:S(2)}, u32[]{:S(2)}) %all-to-all-start) | async-done | bytes 884768 | tf_op jit(solution)/shard_map/all_to_all | solution.py:188
  80.6 4.3 all-to-all-start.2
  94.7 27.6 %all-to-all-done.2 = bf16[16,24,1536]{2,1,0:T(8,128)(2,1)} async-done(((bf16[16,24,1536]{2,1,0:T(8,128)(2,1)}), bf16[16,24,1536]{2,1,0:T(8,128)(2,1)}, u32[]{:S(2)}, u32[]{:S(2)}) %all-to-all-start.2) | async-done | bytes 1179680 | tf_op jit(solution)/shard_map/all_to_all | solution.py:188
  123.2 5.0 all-to-all-start.3
  136.5 13.2 %all-to-all-done.3 = bf16[16,24,3,384]{3,1,2,0:T(8,128)(2,1)} async-done(((bf16[16,24,3,384]{3,1,2,0:T(8,128)(2,1)}), bf16[16,24,3,384]{3,1,2,0:T(8,128)(2,1)}, u32[]{:S(2)}, u32[]{:S(2)}) %all-to-all-start.3) | async-done | bytes 884768 | tf_op jit(solution)/shard_map/all_to_all | solution.py:188
  151.8 5.0 all-to-all-start.5
  159.2 4.1 maximum_select_fusion
  163.3 7.5 multiply_convert_fusion.3
  178.1 6.2 all-to-all-done.5
  188.2 3.6 maximum_select_fusion.4
  193.5 3.7 collective-permute-done.5
  198.4 3.2 convolution_add_fusion.2
  225.7 5.6 multiply_convert_fusion.2
  243.7 5.4 all-to-all-start.6
  257.6 3.2 dynamic-slice_bitcast_fusion
  265.5 4.9 collective-permute-done.12
  274.1 15.6 %all-to-all-done.6 = f32[16,24,3,384]{3,1,2,0:T(8,128)} async-done(((f32[16,24,3,384]{3,1,2,0:T(8,128)}), f32[16,24,3,384]{3,1,2,0:T(8,128)}, u32[]{:S(2)}, u32[]{:S(2)}) %all-to-all-start.6) | async-done | bytes 1769504 | tf_op jit(solution)/shard_map/all_to_all | solution.py:202
  289.6 5.1 all-to-all-start.9
  298.6 4.8 collective-permute-done.13
  311.0 3.5 convert_reduce_fusion.1
  315.8 3.5 bitcast_add_fusion
  320.8 12.9 %collective-permute-done.14 = f32[128,1536]{1,0:T(8,128)} collective-permute-done((f32[128,1536]{1,0:T(8,128)S(1)}, f32[128,1536]{1,0:T(8,128)}, u32[]{:S(2)}, u32[]{:S(2)}) %collective-permute-start.14) | collective-permute-done | bytes 786464 | tf_op jit(solution)/shard_map/ppermute | solution.py:163
  335.8 7.8 all-to-all-start.11
  352.5 4.1 fusion.145
  356.8 4.6 fusion.214
  361.3 24.1 %collective-permute-done.17 = f32[19968]{0:T(1024)S(1)} collective-permute-done((f32[19968]{0:T(1024)S(1)}, f32[19968]{0:T(1024)S(1)}, u32[]{:S(2)}, u32[]{:S(2)}) %collective-permute-start.17) | collective-permute-done | bytes 79904 | tf_op jit(solution)/shard_map/ppermute | solution.py:157
  386.7 11.2 %collective-permute-done.18 = f32[19968]{0:T(1024)S(1)} collective-permute-done((f32[19968]{0:T(1024)S(1)}, f32[19968]{0:T(1024)S(1)}, u32[]{:S(2)}, u32[]{:S(2)}) %collective-permute-start.18) | collective-permute-done | bytes 79904 | tf_op jit(solution)/shard_map/ppermute | solution.py:157
  407.0 4.3 collective-permute-done.21
  412.2 7.0 all-to-all-start.8
  419.2 3.5 bitcast_add_fusion.2
  422.6 11.6 %all-to-all-done.8 = f32[16,24,384]{2,1,0:T(8,128)S(1)} async-done(((f32[16,24,384]{2,1,0:T(8,128)}), f32[16,24,384]{2,1,0:T(8,128)S(1)}, u32[]{:S(2)}, u32[]{:S(2)}) %all-to-all-start.8) | async-done | bytes 589856 | tf_op jit(solution)/shard_map/all_to_all | solution.py:202
  434.2 4.8 all-to-all-start.7
  439.1 3.2 dynamic-slice_bitcast_fusion.1
  442.7 4.5 collective-permute-done.23
  447.2 4.3 bitcast_add_fusion.1
  451.4 38.8 %all-to-all-done.7 = f32[16,24,3,384]{3,1,2,0:T(8,128)} async-done(((f32[16,24,3,384]{3,1,2,0:T(8,128)}), f32[16,24,3,384]{3,1,2,0:T(8,128)}, u32[]{:S(2)}, u32[]{:S(2)}) %all-to-all-start.7) | async-done | bytes 1769504 | tf_op jit(solution)/shard_map/all_to_all | solution.py:202
  490.2 4.6 all-to-all-start.10
  503.0 56.9 %all-to-all-done.10 = f32[16,24,1536]{2,1,0:T(8,128)} async-done(((f32[16,24,1536]{2,1,0:T(8,128)}), f32[16,24,1536]{2,1,0:T(8,128)}, u32[]{:S(2)}, u32[]{:S(2)}) %all-to-all-start.10) | async-done | bytes 2359328 | tf_op jit(solution)/shard_map/all_to_all | solution.py:202
  569.9 7.0 concatenate.136
  578.3 57.4 %all_to_all.70 = f32[16,48,768]{2,1,0:T(8,128)S(1)} all-to-all(f32[16,48,768]{2,1,0:T(8,128)S(1)} %copy.259), channel_id=1, replica_groups=mesh['dp'=16,'tensor'=2] {'dp'}, dimensions={0} | all-to-all | bytes 4718592 | tf_op jit(solution)/shard_map/all_to_all | solution.py:440
  635.8 4.4 fusion.239
  640.3 4.8 collective-permute-done.25
  647.9 26.4 %collective-permute-done.26 = f32[384,768]{1,0:T(8,128)S(1)} collective-permute-done((f32[384,768]{1,0:T(8,128)S(1)}, f32[384,768]{1,0:T(8,128)S(1)}, u32[]{:S(2)}, u32[]{:S(2)}) %collective-permute-start.26) | collective-permute-done | bytes 1179680 | tf_op jit(solution)/shard_map/ppermute | solution.py:451
  682.9 7.3 fusion
  690.2 4.9 fusion.17
  695.0 3.4 fusion.240
  701.6 3.3 fusion.35
  704.9 3.2 fusion.39
  708.1 3.6 fusion.37
  714.9 3.2 fusion.33
  718.1 3.3 fusion.29
  721.5 3.8 fusion.31
  728.4 3.2 fusion.27
  731.6 3.5 fusion.23
  735.2 3.3 fusion.25
  741.7 3.4 fusion.5
  745.0 4.3 fusion.53
  749.4 5.2 all-to-all-start.13
  758.3 24.0 %all-to-all-done.13 = bf16[16,48,768]{2,1,0:T(8,128)(2,1)S(1)} async-done(((bf16[16,48,768]{2,1,0:T(8,128)(2,1)}), bf16[16,48,768]{2,1,0:T(8,128)(2,1)S(1)}, u32[]{:S(2)}, u32[]{:S(2)}) %all-to-all-start.13) | async-done | bytes 1179680 | tf_op jit(solution)/shard_map/all_to_all | solution.py:477
  (651 shorter events, 192.0 us)
Async XLA Ops:
  7.2 156.1 %all-gather.5.cloned.1.call-start = ((), (), s32[]{:S(2)}) async-start(), calls=%async_computation.18 | async-start | bytes 2506752 | tf_op jit(solution)/shard_map/all_gather | solution.py:146
  10.7 18.4 %all-to-all-start.1 = ((bf16[16,24,384]{2,1,0:T(8,128)(2,1)}), bf16[16,24,384]{2,1,0:T(8,128)(2,1)S(1)}, u32[]{:S(2)}, u32[]{:S(2)}) async-start(bf16[16,24,384]{2,1,0:T(8,128)(2,1)} %bitcast.18), calls=%async_computation.1 | async-start | bytes 589824 | tf_op jit(solution)/shard_map/all_to_all | solution.py:188
  17.2 71.5 %collective-permute-start.10 = (bf16[128,768]{1,0:T(8,128)(2,1)S(1)}, bf16[128,768]{1,0:T(8,128)(2,1)S(1)}, u32[]{:S(2)}, u32[]{:S(2)}) collective-permute-start(bf16[128,768]{1,0:T(8,128)(2,1)S(1)} %copy-done.40), channel_id=1, source_target_pairs={{0,1},{1,0},{2,3},{3,2},{4,5},{5,4},{6,7},{7,6},{8,9},{9,8},{10,11... | collective-permute-start | bytes 589832 | tf_op jit(solution)/shard_map/ppermute | solution.py:163
  18.5 29.6 %copy-start.51 = (bf16[1,48,3,384]{3,1,2,0:T(8,128)(2,1)}, bf16[1,48,3,384]{3,1,2,0:T(8,128)(2,1)S(1)}, u32[]{:S(2)}) copy-start(bf16[1,48,3,384]{3,1,2,0:T(8,128)(2,1)S(1)} %get-tuple-element.263) | copy-start | bytes 331780
  18.5 68.5 %copy-start.49 = (bf16[1,48,3,384]{3,1,2,0:T(8,128)(2,1)}, bf16[1,48,3,384]{3,1,2,0:T(8,128)(2,1)S(1)}, u32[]{:S(2)}) copy-start(bf16[1,48,3,384]{3,1,2,0:T(8,128)(2,1)S(1)} %get-tuple-element.262) | copy-start | bytes 331780
  29.8 23.2 %copy-start.117 = (f32[2,2,768]{2,1,0:T(2,128)S(1)}, f32[2,2,768]{2,1,0:T(2,128)}, u32[]{:S(2)}) copy-start(f32[2,2,768]{2,1,0:T(2,128)} %param.22) | copy-start | bytes 36868
  29.8 23.9 %copy-start.93 = (f32[2,4,768]{2,1,0:T(4,128)S(1)}, f32[2,4,768]{2,1,0:T(4,128)}, u32[]{:S(2)}) copy-start(f32[2,4,768]{2,1,0:T(4,128)} %param.23) | copy-start | bytes 73732
  29.8 17.3 %all-to-all-start.4 = ((bf16[16,24,384]{2,1,0:T(8,128)(2,1)}), bf16[16,24,384]{2,1,0:T(8,128)(2,1)S(1)}, u32[]{:S(2)}, u32[]{:S(2)}) async-start(bf16[16,24,384]{2,1,0:T(8,128)(2,1)} %bitcast.45), calls=%async_computation.4 | async-start | bytes 589824 | tf_op jit(solution)/shard_map/all_to_all | solution.py:188
  34.0 20.5 %copy-start.145 = (f32[128]{0:T(128)}, f32[128]{0:T(128)S(1)}, u32[]{:S(2)}) copy-start(f32[128]{0:T(128)S(1)} %broadcast_multiply_fusion.5) | copy-start | bytes 1540
  34.2 21.1 %copy-start.150 = (f32[128]{0:T(128)}, f32[128]{0:T(128)S(1)}, u32[]{:S(2)}) copy-start(f32[128]{0:T(128)S(1)} %add_rsqrt_fusion.1) | copy-start | bytes 1540
  48.1 31.4 %all-to-all-start = ((bf16[16,24,3,384]{3,1,2,0:T(8,128)(2,1)}), bf16[16,24,3,384]{3,1,2,0:T(8,128)(2,1)S(1)}, u32[]{:S(2)}, u32[]{:S(2)}) async-start(bf16[16,24,3,384]{3,1,2,0:T(8,128)(2,1)} %bitcast.2), calls=%async_computation | async-start | bytes 1769472 | tf_op jit(solution)/shard_map/all_to_all | solution.py:188
  53.0 172.7 %all-gather.7.cloned.1.call-start = ((), (), s32[]{:S(2)}) async-start(), calls=%async_computation.19 | async-start | bytes 2506752 | tf_op jit(solution)/shard_map/all_gather | solution.py:146
  53.7 25.8 %copy-start.124 = (f32[768]{0:T(1024)}, f32[768]{0:T(1024)S(1)}, u32[]{:S(2)}) copy-start(f32[768]{0:T(1024)S(1)} %get-tuple-element.185) | copy-start | bytes 9220
  53.7 26.9 %copy-start.126 = (f32[768]{0:T(1024)}, f32[768]{0:T(1024)S(1)}, u32[]{:S(2)}) copy-start(f32[768]{0:T(1024)S(1)} %get-tuple-element.186) | copy-start | bytes 9220
  55.3 34.8 %collective-permute-start = (bf16[128,1536]{1,0:T(8,128)(2,1)}, bf16[128,1536]{1,0:T(8,128)(2,1)}, u32[]{:S(2)}, u32[]{:S(2)}) collective-permute-start(bf16[128,1536]{1,0:T(8,128)(2,1)} %pad_maximum_fusion.8), channel_id=1, source_target_pairs={{0,1},{1,0},{2,3},{3,2},{4,5},{5,4},{6,7},{7,6},{8,9},{9,8},{10,11... | collective-permute-start | bytes 1179656 | tf_op jit(solution)/shard_map/ppermute | solution.py:163
  80.6 41.6 %all-to-all-start.2 = ((bf16[16,24,1536]{2,1,0:T(8,128)(2,1)}), bf16[16,24,1536]{2,1,0:T(8,128)(2,1)}, u32[]{:S(2)}, u32[]{:S(2)}) async-start(bf16[16,24,1536]{2,1,0:T(8,128)(2,1)} %bitcast.26), calls=%async_computation.2 | async-start | bytes 2359296 | tf_op jit(solution)/shard_map/all_to_all | solution.py:188
  86.0 42.6 %collective-permute-start.1 = (bf16[16,24,3,384]{3,1,0,2:T(8,128)(2,1)S(1)}, bf16[16,24,3,384]{3,1,0,2:T(8,128)(2,1)}, u32[]{:S(2)}, u32[]{:S(2)}) collective-permute-start(bf16[16,24,3,384]{3,1,0,2:T(8,128)(2,1)S(1)} %copy.308), channel_id=1, source_target_pairs={{0,2},{2,0},{4,6},{6,4},{8,10},{10,8},{12,14},{14,12},{16,18},{18,... | collective-permute-start | bytes 2654216 | tf_op jit(solution)/shard_map/ppermute | solution.py:189
  88.5 2.9 collective-permute-start.7
  89.7 4.0 collective-permute-start.2
  91.4 39.1 %copy-start.9 = (bf16[256,1536]{1,0:T(8,128)(2,1)}, bf16[256,1536]{1,0:T(8,128)(2,1)S(1)}, u32[]{:S(2)}) copy-start(bf16[256,1536]{1,0:T(8,128)(2,1)S(1)} %maximum_select_fusion.5) | copy-start | bytes 2359300
  123.2 26.5 %all-to-all-start.3 = ((bf16[16,24,3,384]{3,1,2,0:T(8,128)(2,1)}), bf16[16,24,3,384]{3,1,2,0:T(8,128)(2,1)}, u32[]{:S(2)}, u32[]{:S(2)}) async-start(bf16[16,24,3,384]{3,1,2,0:T(8,128)(2,1)} %bitcast.32), calls=%async_computation.3 | async-start | bytes 1769472 | tf_op jit(solution)/shard_map/all_to_all | solution.py:188
  128.2 30.9 %collective-permute-start.3 = (bf16[16,24,1536]{2,1,0:T(8,128)(2,1)}, bf16[16,24,1536]{2,1,0:T(8,128)(2,1)}, u32[]{:S(2)}, u32[]{:S(2)}) collective-permute-start(bf16[16,24,1536]{2,1,0:T(8,128)(2,1)} %all-to-all-done.2), channel_id=1, source_target_pairs={{0,2},{2,0},{4,6},{6,4},{8,10},{10,8},{12,14},{14,12},{16,18},{18,... | collective-permute-start | bytes 3538952 | tf_op jit(solution)/shard_map/ppermute | solution.py:189
  151.8 32.6 %all-to-all-start.5 = ((bf16[16,24,1536]{2,1,0:T(8,128)(2,1)}), bf16[16,24,1536]{2,1,0:T(8,128)(2,1)S(1)}, u32[]{:S(2)}, u32[]{:S(2)}) async-start(bf16[16,24,1536]{2,1,0:T(8,128)(2,1)} %bitcast.389), calls=%async_computation.5 | async-start | bytes 2359296 | tf_op jit(solution)/shard_map/all_to_all | solution.py:188
  172.7 12.3 %collective-permute-start.4 = (f32[128,768]{1,0:T(8,128)}, f32[128,768]{1,0:T(8,128)}, u32[]{:S(2)}, u32[]{:S(2)}) collective-permute-start(f32[128,768]{1,0:T(8,128)} %constant_dynamic-slice_fusion.5), channel_id=1, source_target_pairs={{0,1},{1,0},{2,3},{3,2},{4,5},{5,4},{6,7},{7,6},{8,9},{9,8},{10,11... | collective-permute-start | bytes 1179656 | tf_op jit(solution)/shard_map/ppermute | solution.py:163
  177.5 10.7 %collective-permute-start.6 = (bf16[16,24,3,384]{3,1,0,2:T(8,128)(2,1)}, bf16[16,24,3,384]{3,1,0,2:T(8,128)(2,1)}, u32[]{:S(2)}, u32[]{:S(2)}) collective-permute-start(bf16[16,24,3,384]{3,1,0,2:T(8,128)(2,1)} %copy.307), channel_id=1, source_target_pairs={{0,2},{2,0},{4,6},{6,4},{8,10},{10,8},{12,14},{14,12},{16,18},{18,... | collective-permute-start | bytes 2654216 | tf_op jit(solution)/shard_map/ppermute | solution.py:189
  184.3 7.4 collective-permute-start.8
  186.8 10.3 %collective-permute-start.5 = (bf16[128,1536]{1,0:T(8,128)(2,1)S(1)}, bf16[128,1536]{1,0:T(8,128)(2,1)S(1)}, u32[]{:S(2)}, u32[]{:S(2)}) collective-permute-start(bf16[128,1536]{1,0:T(8,128)(2,1)S(1)} %pad_maximum_fusion.9), channel_id=1, source_target_pairs={{0,1},{1,0},{2,3},{3,2},{4,5},{5,4},{6,7},{7,6},{8,9},{9,8},{10,11... | collective-permute-start | bytes 1179656 | tf_op jit(solution)/shard_map/ppermute | solution.py:163
  221.0 42.5 %collective-permute-start.22 = (f32[16,24,384]{2,1,0:T(8,128)}, f32[16,24,384]{2,1,0:T(8,128)}, u32[]{:S(2)}, u32[]{:S(2)}) collective-permute-start(f32[16,24,384]{2,1,0:T(8,128)} %dynamic-slice_bitcast_fusion.3), channel_id=1, source_target_pairs={{0,2},{2,0},{4,6},{6,4},{8,10},{10,8},{12,14},{14,12},{16,18},{18,... | collective-permute-start | bytes 1769480 | tf_op jit(solution)/shard_map/ppermute | solution.py:201
  225.7 14.2 %collective-permute-start.11 = (f32[16,24,3,384]{3,1,2,0:T(8,128)}, f32[16,24,3,384]{3,1,2,0:T(8,128)}, u32[]{:S(2)}, u32[]{:S(2)}) collective-permute-start(f32[16,24,3,384]{3,1,2,0:T(8,128)} %dynamic-slice_bitcast_fusion.2), channel_id=1, source_target_pairs={{0,2},{2,0},{4,6},{6,4},{8,10},{10,8},{12,14},{14,12},{16,18},{18,... | collective-permute-start | bytes 5308424 | tf_op jit(solution)/shard_map/ppermute | solution.py:201
  233.5 38.6 %collective-permute-start.9 = (f32[128,768]{1,0:T(8,128)}, f32[128,768]{1,0:T(8,128)}, u32[]{:S(2)}, u32[]{:S(2)}) collective-permute-start(f32[128,768]{1,0:T(8,128)} %constant_dynamic-slice_fusion.2), channel_id=1, source_target_pairs={{0,1},{1,0},{2,3},{3,2},{4,5},{5,4},{6,7},{7,6},{8,9},{9,8},{10,11... | collective-permute-start | bytes 1179656 | tf_op jit(solution)/shard_map/ppermute | solution.py:163
  243.7 45.9 %all-to-all-start.6 = ((f32[16,24,3,384]{3,1,2,0:T(8,128)}), f32[16,24,3,384]{3,1,2,0:T(8,128)}, u32[]{:S(2)}, u32[]{:S(2)}) async-start(f32[16,24,3,384]{3,1,2,0:T(8,128)} %bitcast_add_fusion.3), calls=%async_computation.6 | async-start | bytes 3538944 | tf_op jit(solution)/shard_map/all_to_all | solution.py:202
  249.1 316.2 %reduce-scatter.5.cloned.1.call-start = ((), (), s32[]{:S(2)}) async-start(), calls=%async_computation.17 | async-start | bytes 5013504 | tf_op jit(solution)/shard_map/reduce_scatter | solution.py:142
  251.4 19.0 %collective-permute-start.12 = (f32[128,1536]{1,0:T(8,128)}, f32[128,1536]{1,0:T(8,128)}, u32[]{:S(2)}, u32[]{:S(2)}) collective-permute-start(f32[128,1536]{1,0:T(8,128)} %fusion.112), channel_id=1, source_target_pairs={{0,1},{1,0},{2,3},{3,2},{4,5},{5,4},{6,7},{7,6},{8,9},{9,8},{10,11... | collective-permute-start | bytes 2359304 | tf_op jit(solution)/shard_map/ppermute | solution.py:163
  260.8 55.0 %collective-permute-start.24 = (f32[16,24,1536]{2,1,0:T(8,128)}, f32[16,24,1536]{2,1,0:T(8,128)}, u32[]{:S(2)}, u32[]{:S(2)}) collective-permute-start(f32[16,24,1536]{2,1,0:T(8,128)} %dynamic-slice_bitcast_fusion), channel_id=1, source_target_pairs={{0,2},{2,0},{4,6},{6,4},{8,10},{10,8},{12,14},{14,12},{16,18},{18,... | collective-permute-start | bytes 7077896 | tf_op jit(solution)/shard_map/ppermute | solution.py:201
  274.0 23.0 %copy-start.13 = (f32[128,768]{1,0:T(8,128)}, f32[128,768]{1,0:T(8,128)S(1)}, u32[]{:S(2)}) copy-start(f32[128,768]{1,0:T(8,128)S(1)} %get-tuple-element.30) | copy-start | bytes 1179652
  289.6 46.2 %all-to-all-start.9 = ((f32[16,24,384]{2,1,0:T(8,128)}), f32[16,24,384]{2,1,0:T(8,128)}, u32[]{:S(2)}, u32[]{:S(2)}) async-start(f32[16,24,384]{2,1,0:T(8,128)} %bitcast_add_fusion.4), calls=%async_computation.9 | async-start | bytes 1179648 | tf_op jit(solution)/shard_map/all_to_all | solution.py:202
  297.1 6.2 collective-permute-start.13
  315.5 18.2 %collective-permute-start.14 = (f32[128,1536]{1,0:T(8,128)S(1)}, f32[128,1536]{1,0:T(8,128)}, u32[]{:S(2)}, u32[]{:S(2)}) collective-permute-start(f32[128,1536]{1,0:T(8,128)S(1)} %fusion.109), channel_id=1, source_target_pairs={{0,1},{1,0},{2,3},{3,2},{4,5},{5,4},{6,7},{7,6},{8,9},{9,8},{10,11... | collective-permute-start | bytes 2359304 | tf_op jit(solution)/shard_map/ppermute | solution.py:163
  335.8 76.4 %all-to-all-start.11 = ((f32[16,24,1536]{2,1,0:T(8,128)}), f32[16,24,1536]{2,1,0:T(8,128)S(1)}, u32[]{:S(2)}, u32[]{:S(2)}) async-start(f32[16,24,1536]{2,1,0:T(8,128)} %bitcast_add_fusion), calls=%async_computation.13 | async-start | bytes 4718592 | tf_op jit(solution)/shard_map/all_to_all | solution.py:202
  350.8 1.3 collective-permute-start.15
  352.1 4.5 collective-permute-start.16
  356.6 29.4 %copy-start.29 = (bf16[256,1,384]{2,0,1:T(8,128)(2,1)S(1)}, bf16[256,1,384]{2,0,1:T(8,128)(2,1)}, u32[]{:S(2)}) copy-start(bf16[256,1,384]{2,0,1:T(8,128)(2,1)} %copy-done.28) | copy-start | bytes 589828
  356.6 29.3 %copy-start.31 = (bf16[256,1,384]{2,0,1:T(8,128)(2,1)S(1)}, bf16[256,1,384]{2,0,1:T(8,128)(2,1)}, u32[]{:S(2)}) copy-start(bf16[256,1,384]{2,0,1:T(8,128)(2,1)} %copy.250) | copy-start | bytes 589828
  356.6 28.8 %collective-permute-start.17 = (f32[19968]{0:T(1024)S(1)}, f32[19968]{0:T(1024)S(1)}, u32[]{:S(2)}, u32[]{:S(2)}) collective-permute-start(f32[19968]{0:T(1024)S(1)} %add.471), channel_id=1, source_target_pairs={{0,8},{2,10},{4,12},{6,14},{8,0},{10,2},{12,4},{14,6},{16,24},{18,... | collective-permute-start | bytes 239624 | tf_op jit(solution)/shard_map/ppermute | solution.py:157
  385.5 13.0 %copy-start.64 = (bf16[128,768]{1,0:T(8,128)(2,1)S(1)}, bf16[128,768]{1,0:T(8,128)(2,1)}, u32[]{:S(2)}) copy-start(bf16[128,768]{1,0:T(8,128)(2,1)} %copy-done.63) | copy-start | bytes 589828
  385.5 12.9 %copy-start.85 = (bf16[6,64,256]{2,1,0:T(8,128)(2,1)S(1)}, bf16[6,64,256]{2,1,0:T(8,128)(2,1)}, u32[]{:S(2)}) copy-start(bf16[6,64,256]{2,1,0:T(8,128)(2,1)} %convolution_convert_fusion.5) | copy-start | bytes 589828
  385.5 12.4 %collective-permute-start.18 = (f32[19968]{0:T(1024)S(1)}, f32[19968]{0:T(1024)S(1)}, u32[]{:S(2)}, u32[]{:S(2)}) collective-permute-start(f32[19968]{0:T(1024)S(1)} %add.472), channel_id=1, source_target_pairs={{0,16},{2,18},{4,20},{6,22},{8,24},{10,26},{12,28},{14,30},{16,0},... | collective-permute-start | bytes 239624 | tf_op jit(solution)/shard_map/ppermute | solution.py:157
  397.9 3.4 collective-permute-start.19
  404.8 14.4 %collective-permute-start.20 = (f32[16,24,3,384]{3,1,2,0:T(8,128)}, f32[16,24,3,384]{3,1,2,0:T(8,128)}, u32[]{:S(2)}, u32[]{:S(2)}) collective-permute-start(f32[16,24,3,384]{3,1,2,0:T(8,128)} %bitcast.363), channel_id=1, source_target_pairs={{0,2},{2,0},{4,6},{6,4},{8,10},{10,8},{12,14},{14,12},{16,18},{18,... | collective-permute-start | bytes 5308424 | tf_op jit(solution)/shard_map/ppermute | solution.py:201
  406.9 4.3 collective-permute-start.21
  412.2 22.0 %all-to-all-start.8 = ((f32[16,24,384]{2,1,0:T(8,128)}), f32[16,24,384]{2,1,0:T(8,128)S(1)}, u32[]{:S(2)}, u32[]{:S(2)}) async-start(f32[16,24,384]{2,1,0:T(8,128)} %bitcast_add_fusion.5), calls=%async_computation.8 | async-start | bytes 1179648 | tf_op jit(solution)/shard_map/all_to_all | solution.py:202
  434.2 56.0 %all-to-all-start.7 = ((f32[16,24,3,384]{3,1,2,0:T(8,128)}), f32[16,24,3,384]{3,1,2,0:T(8,128)}, u32[]{:S(2)}, u32[]{:S(2)}) async-start(f32[16,24,3,384]{3,1,2,0:T(8,128)} %bitcast_add_fusion.2), calls=%async_computation.7 | async-start | bytes 3538944 | tf_op jit(solution)/shard_map/all_to_all | solution.py:202
  439.0 126.3 %reduce-scatter.3.cloned.1.call-start = ((), (), s32[]{:S(2)}) async-start(), calls=%async_computation.16 | async-start | bytes 5013504 | tf_op jit(solution)/shard_map/reduce_scatter | solution.py:142
  442.3 4.9 collective-permute-start.23
  490.2 69.6 %all-to-all-start.10 = ((f32[16,24,1536]{2,1,0:T(8,128)}), f32[16,24,1536]{2,1,0:T(8,128)}, u32[]{:S(2)}, u32[]{:S(2)}) async-start(f32[16,24,1536]{2,1,0:T(8,128)} %bitcast_add_fusion.1), calls=%async_computation.12 | async-start | bytes 4718592 | tf_op jit(solution)/shard_map/all_to_all | solution.py:202
  502.8 58.8 %copy-start.74 = (f32[2,1536,48]{1,2,0:T(8,128)S(1)}, f32[2,1536,48]{1,2,0:T(8,128)}, u32[]{:S(2)}) copy-start(f32[2,1536,48]{1,2,0:T(8,128)} %param.29) | copy-start | bytes 1769476
  640.2 4.9 collective-permute-start.25
  646.8 28.7 %copy-start.78 = (f32[19968]{0:T(1024)S(1)}, f32[19968]{0:T(1024)}, u32[]{:S(2)}) copy-start(f32[19968]{0:T(1024)} %add.474) | copy-start | bytes 239620
  646.9 27.5 %collective-permute-start.26 = (f32[384,768]{1,0:T(8,128)S(1)}, f32[384,768]{1,0:T(8,128)S(1)}, u32[]{:S(2)}, u32[]{:S(2)}) collective-permute-start(f32[384,768]{1,0:T(8,128)S(1)} %dynamic-slice_add_fusion), channel_id=1, source_target_pairs={{0,1},{1,0},{2,3},{3,2},{4,5},{5,4},{6,7},{7,6},{8,9},{9,8},{10,11... | collective-permute-start | bytes 3538952 | tf_op jit(solution)/shard_map/ppermute | solution.py:451
  674.5 5.3 collective-permute-start.27
  749.4 32.9 %all-to-all-start.13 = ((bf16[16,48,768]{2,1,0:T(8,128)(2,1)}), bf16[16,48,768]{2,1,0:T(8,128)(2,1)S(1)}, u32[]{:S(2)}, u32[]{:S(2)}) async-start(bf16[16,48,768]{2,1,0:T(8,128)(2,1)} %bitcast.142), calls=%async_computation.15 | async-start | bytes 2359296 | tf_op jit(solution)/shard_map/all_to_all | solution.py:477
  755.2 28.2 %copy-start.92 = (f32[2,2,768]{2,1,0:T(2,128)}, f32[2,2,768]{2,1,0:T(2,128)S(1)}, u32[]{:S(2)}) copy-start(f32[2,2,768]{2,1,0:T(2,128)S(1)} %slice.420) | copy-start | bytes 36868
  755.9 27.5 %copy-start.82 = (f32[2,3072]{1,0:T(2,128)}, f32[2,3072]{1,0:T(2,128)S(1)}, u32[]{:S(2)}) copy-start(f32[2,3072]{1,0:T(2,128)S(1)} %reshape.602) | copy-start | bytes 73732
  755.9 27.5 %copy-start.83 = (f32[2,4,768]{2,1,0:T(4,128)}, f32[2,4,768]{2,1,0:T(4,128)S(1)}, u32[]{:S(2)}) copy-start(f32[2,4,768]{2,1,0:T(4,128)S(1)} %reshape.600) | copy-start | bytes 73732
  (139 other events, 590.6 us)
Sparse Core Ops, SparseCore 0:
  10.9 44.5 all-gather.4
  58.3 52.5 all-gather.6
  261.7 82.9 reduce-scatter.4
  443.4 105.5 reduce-scatter.2

commit v10 on v9

--- a/solution.py
+++ b/solution.py
@@ -251,7 +251,7 @@
     for layer_id in range(LAYERS):
         layer_weights = (
             chip_gather_rows(qkv_weight[layer_id]),
-            chip_gather_rows(proj_weight[layer_id].T),
+            dp_gather(proj_weight[layer_id].T, 0),
             dp_gather(up_weight[layer_id], 0),
             chip_gather_rows(down_weight[layer_id].T),
         )

time: 804 us -> 809 us (level)
  blocking collectives: 57.4 us -> 125 us
  waiting for transfers between devices: 343 us -> 291 us
    all_gather x0 -> x2, blocking collectives: none -> 67.1 us  [dp_gather(): return lax.all_gather(block, 'dp', axis=axis, tiled=True)]
    all_to_all x6 -> x4, waiting for transfers between devices: 91.4 us -> 41.7 us  [chip_gather_rows(): lax.all_to_all(outgoing, 'dp', split_axis=0, concat_axis=0, tiled=True)]
    all_to_all x6 -> x4, starting transfers between devices: 29.9 us -> 24.7 us  [chip_gather_rows(): lax.all_to_all(outgoing, 'dp', split_axis=0, concat_axis=0, tiled=True)]
  transfers between devices with their start and end apart: 45 -> 41, of which waited for: 23 -> 20; matrix products, arithmetic and copies ran while one was open for 23% -> 22% of each run, Pallas kernels for 0% -> 0%
where the time goes in v10:
time: 809 us; the launch traced here: 800 us
  waiting for transfers between devices  291 us (36%)
  matrix products  131 us (16%)
  blocking collectives  125 us (15%)
  starting transfers between devices  82.8 us (10%)
  other arithmetic  77.7 us (10%)
  local copies, waits for them, and re-layouts  75.8 us (9%)
  between operations  17.5 us (2%)
    all_to_all x6, waiting for transfers between devices, chip_scatter_rows(): lax.all_to_all(chip_sum, 'dp', split_axis=0, concat_axis=0, tiled=True)  123 us
    all_gather x2, blocking collectives, dp_gather(): return lax.all_gather(block, 'dp', axis=axis, tiled=True)  67.1 us
    all_to_all x1, blocking collectives, local(): lax.all_to_all(outgoing, 'dp', split_axis=0, concat_axis=0, tiled=True)  57.6 us
    all_to_all x4, waiting for transfers between devices, chip_gather_rows(): lax.all_to_all(outgoing, 'dp', split_axis=0, concat_axis=0, tiled=True)  41.7 us
    ppermute x4, waiting for transfers between devices, butterfly_sum(): flat = flat + lax.ppermute(flat, 'dp', swap_pairs(count, bit))  36.2 us
    all_to_all x6, starting transfers between devices, chip_scatter_rows(): lax.all_to_all(chip_sum, 'dp', split_axis=0, concat_axis=0, tiled=True)  35.6 us
    ppermute x1, waiting for transfers between devices, local(): mine = mine + lax.ppermute(mine, 'tensor', [(0, 1), (1, 0)])  26.3 us
    all_to_all x4, starting transfers between devices, chip_gather_rows(): lax.all_to_all(outgoing, 'dp', split_axis=0, concat_axis=0, tiled=True)  24.7 us
  transfers between devices with their start and end apart: 41, of which 20 were waited for; matrix products, arithmetic and copies ran while one was open for 22% of the time, Pallas kernels for 0%

profile of v10, /device:TPU:11, one launch (start us, length us, event | category | flops | bytes accessed | tf_op | source)
XLA Modules:
  0.0 800.1 jit_solution(13410960594077224745)
XLA Ops:
  12.5 6.9 all-to-all-start
  23.8 21.7 %all-to-all-done = bf16[16,24,3,384]{3,1,2,0:T(8,128)(2,1)S(1)} async-done(((bf16[16,24,3,384]{3,1,2,0:T(8,128)(2,1)}), bf16[16,24,3,384]{3,1,2,0:T(8,128)(2,1)S(1)}, u32[]{:S(2)}, u32[]{:S(2)}) %all-to-all-start) | async-done | bytes 884768 | tf_op jit(solution)/shard_map/all_to_all | solution.py:188
  46.6 4.9 all-to-all-start.1
  51.7 45.8 %all_gather.14 = bf16[768,384]{1,0:T(8,128)(2,1)} all-gather(bf16[48,384]{1,0:T(8,128)(2,1)S(1)} %get-tuple-element.273), channel_id=1, replica_groups=mesh['dp'=16,'tensor'=2] {'dp'}, dimensions={0}, use_global_device_ids=true | all-gather | bytes 626688 | tf_op jit(solution)/shard_map/all_gather | solution.py:146
  97.4 21.3 %all_gather.12 = bf16[768,384]{1,0:T(8,128)(2,1)} all-gather(bf16[48,384]{1,0:T(8,128)(2,1)S(1)} %get-tuple-element.274), channel_id=1, replica_groups=mesh['dp'=16,'tensor'=2] {'dp'}, dimensions={0}, use_global_device_ids=true | all-gather | bytes 626688 | tf_op jit(solution)/shard_map/all_gather | solution.py:146
  124.8 7.8 all-to-all-start.2
  141.0 13.1 %all-to-all-done.2 = bf16[16,24,3,384]{3,1,2,0:T(8,128)(2,1)} async-done(((bf16[16,24,3,384]{3,1,2,0:T(8,128)(2,1)}), bf16[16,24,3,384]{3,1,2,0:T(8,128)(2,1)}, u32[]{:S(2)}, u32[]{:S(2)}) %all-to-all-start.2) | async-done | bytes 884768 | tf_op jit(solution)/shard_map/all_to_all | solution.py:188
  156.2 5.0 all-to-all-start.3
  163.6 4.3 maximum_select_fusion
  167.9 7.5 multiply_convert_fusion.3
  181.9 6.9 all-to-all-done.3
  192.5 3.5 maximum_select_fusion.4
  197.7 4.6 collective-permute-done.4
  203.4 3.2 convolution_add_fusion.2
  230.8 5.6 multiply_convert_fusion.2
  247.9 5.4 all-to-all-start.4
  262.6 3.2 dynamic-slice_bitcast_fusion
  270.4 4.1 collective-permute-done.10
  278.2 15.6 %all-to-all-done.4 = f32[16,24,3,384]{3,1,2,0:T(8,128)} async-done(((f32[16,24,3,384]{3,1,2,0:T(8,128)}), f32[16,24,3,384]{3,1,2,0:T(8,128)}, u32[]{:S(2)}, u32[]{:S(2)}) %all-to-all-start.4) | async-done | bytes 1769504 | tf_op jit(solution)/shard_map/all_to_all | solution.py:202
  293.8 5.1 all-to-all-start.7
  303.6 3.9 collective-permute-done.11
  315.1 3.5 convert_reduce_fusion.1
  320.9 3.5 bitcast_add_fusion
  325.8 12.0 %collective-permute-done.12 = f32[128,1536]{1,0:T(8,128)} collective-permute-done((f32[128,1536]{1,0:T(8,128)S(1)}, f32[128,1536]{1,0:T(8,128)}, u32[]{:S(2)}, u32[]{:S(2)}) %collective-permute-start.12) | collective-permute-done | bytes 786464 | tf_op jit(solution)/shard_map/ppermute | solution.py:163
  340.0 7.9 all-to-all-start.9
  356.7 4.1 fusion.145
  361.0 4.5 fusion.214
  365.5 24.0 %collective-permute-done.15 = f32[19968]{0:T(1024)S(1)} collective-permute-done((f32[19968]{0:T(1024)S(1)}, f32[19968]{0:T(1024)S(1)}, u32[]{:S(2)}, u32[]{:S(2)}) %collective-permute-start.15) | collective-permute-done | bytes 79904 | tf_op jit(solution)/shard_map/ppermute | solution.py:157
  390.9 11.2 %collective-permute-done.16 = f32[19968]{0:T(1024)S(1)} collective-permute-done((f32[19968]{0:T(1024)S(1)}, f32[19968]{0:T(1024)S(1)}, u32[]{:S(2)}, u32[]{:S(2)}) %collective-permute-start.16) | collective-permute-done | bytes 79904 | tf_op jit(solution)/shard_map/ppermute | solution.py:157
  411.2 4.3 collective-permute-done.19
  416.4 7.0 all-to-all-start.6
  423.4 3.5 bitcast_add_fusion.2
  426.8 11.6 %all-to-all-done.6 = f32[16,24,384]{2,1,0:T(8,128)S(1)} async-done(((f32[16,24,384]{2,1,0:T(8,128)}), f32[16,24,384]{2,1,0:T(8,128)S(1)}, u32[]{:S(2)}, u32[]{:S(2)}) %all-to-all-start.6) | async-done | bytes 589856 | tf_op jit(solution)/shard_map/all_to_all | solution.py:202
  438.4 4.8 all-to-all-start.5
  443.3 3.2 dynamic-slice_bitcast_fusion.1
  446.9 4.5 collective-permute-done.21
  451.4 4.1 bitcast_add_fusion.1
  455.5 37.7 %all-to-all-done.5 = f32[16,24,3,384]{3,1,2,0:T(8,128)} async-done(((f32[16,24,3,384]{3,1,2,0:T(8,128)}), f32[16,24,3,384]{3,1,2,0:T(8,128)}, u32[]{:S(2)}, u32[]{:S(2)}) %all-to-all-start.5) | async-done | bytes 1769504 | tf_op jit(solution)/shard_map/all_to_all | solution.py:202
  493.2 5.4 all-to-all-start.8
  506.8 57.8 %all-to-all-done.8 = f32[16,24,1536]{2,1,0:T(8,128)} async-done(((f32[16,24,1536]{2,1,0:T(8,128)}), f32[16,24,1536]{2,1,0:T(8,128)}, u32[]{:S(2)}, u32[]{:S(2)}) %all-to-all-start.8) | async-done | bytes 2359328 | tf_op jit(solution)/shard_map/all_to_all | solution.py:202
  574.6 7.0 concatenate.136
  583.0 57.6 %all_to_all.60 = f32[16,48,768]{2,1,0:T(8,128)S(1)} all-to-all(f32[16,48,768]{2,1,0:T(8,128)S(1)} %copy.259), channel_id=1, replica_groups=mesh['dp'=16,'tensor'=2] {'dp'}, dimensions={0} | all-to-all | bytes 4718592 | tf_op jit(solution)/shard_map/all_to_all | solution.py:440
  640.6 4.4 fusion.238
  645.1 4.8 collective-permute-done.23
  652.8 26.3 %collective-permute-done.24 = f32[384,768]{1,0:T(8,128)S(1)} collective-permute-done((f32[384,768]{1,0:T(8,128)S(1)}, f32[384,768]{1,0:T(8,128)S(1)}, u32[]{:S(2)}, u32[]{:S(2)}) %collective-permute-start.24) | collective-permute-done | bytes 1179680 | tf_op jit(solution)/shard_map/ppermute | solution.py:451
  687.7 7.2 fusion
  694.9 4.9 fusion.17
  699.8 3.4 fusion.239
  703.2 3.1 fusion.240
  706.3 3.4 fusion.35
  709.7 3.2 fusion.39
  712.9 3.6 fusion.37
  716.5 3.1 fusion.241
  719.6 3.2 fusion.33
  722.9 3.3 fusion.29
  726.2 3.8 fusion.31
  733.2 3.2 fusion.27
  736.4 3.5 fusion.23
  739.9 3.3 fusion.25
  743.3 3.1 fusion.243
  746.5 3.4 fusion.5
  749.8 4.3 fusion.53
  754.2 5.2 all-to-all-start.11
  763.1 24.0 %all-to-all-done.11 = bf16[16,48,768]{2,1,0:T(8,128)(2,1)S(1)} async-done(((bf16[16,48,768]{2,1,0:T(8,128)(2,1)}), bf16[16,48,768]{2,1,0:T(8,128)(2,1)S(1)}, u32[]{:S(2)}, u32[]{:S(2)}) %all-to-all-start.11) | async-done | bytes 1179680 | tf_op jit(solution)/shard_map/all_to_all | solution.py:477
  (633 shorter events, 176.3 us)
Async XLA Ops:
  7.2 160.7 %all-gather.5.cloned.1.call-start = ((), (), s32[]{:S(2)}) async-start(), calls=%async_computation.16 | async-start | bytes 2506752 | tf_op jit(solution)/shard_map/all_gather | solution.py:146
  9.0 11.1 %copy-start.93 = (f32[2,4,768]{2,1,0:T(4,128)S(1)}, f32[2,4,768]{2,1,0:T(4,128)}, u32[]{:S(2)}) copy-start(f32[2,4,768]{2,1,0:T(4,128)} %param.23) | copy-start | bytes 73732
  9.0 112.3 %collective-permute-start.8 = (bf16[128,768]{1,0:T(8,128)(2,1)}, bf16[128,768]{1,0:T(8,128)(2,1)S(1)}, u32[]{:S(2)}, u32[]{:S(2)}) collective-permute-start(bf16[128,768]{1,0:T(8,128)(2,1)} %param.16), channel_id=1, source_target_pairs={{0,1},{1,0},{2,3},{3,2},{4,5},{5,4},{6,7},{7,6},{8,9},{9,8},{10,11... | collective-permute-start | bytes 589832 | tf_op jit(solution)/shard_map/ppermute | solution.py:163
  11.3 108.5 %copy-start.49 = (bf16[1,48,3,384]{3,1,2,0:T(8,128)(2,1)}, bf16[1,48,3,384]{3,1,2,0:T(8,128)(2,1)S(1)}, u32[]{:S(2)}) copy-start(bf16[1,48,3,384]{3,1,2,0:T(8,128)(2,1)S(1)} %get-tuple-element.262) | copy-start | bytes 331780
  12.4 10.6 %copy-start.80 = (bf16[2,384,48]{1,2,0:T(8,128)(2,1)S(1)}, bf16[2,384,48]{1,2,0:T(8,128)(2,1)}, u32[]{:S(2)}) copy-start(bf16[2,384,48]{1,2,0:T(8,128)(2,1)} %param.19) | copy-start | bytes 221188
  12.4 10.6 %copy-start.46 = (bf16[2,1536,48]{1,2,0:T(8,128)(2,1)S(1)}, bf16[2,1536,48]{1,2,0:T(8,128)(2,1)}, u32[]{:S(2)}) copy-start(bf16[2,1536,48]{1,2,0:T(8,128)(2,1)} %param.21) | copy-start | bytes 884740
  12.5 33.0 %all-to-all-start = ((bf16[16,24,3,384]{3,1,2,0:T(8,128)(2,1)}), bf16[16,24,3,384]{3,1,2,0:T(8,128)(2,1)S(1)}, u32[]{:S(2)}, u32[]{:S(2)}) async-start(bf16[16,24,3,384]{3,1,2,0:T(8,128)(2,1)} %bitcast.2), calls=%async_computation | async-start | bytes 1769472 | tf_op jit(solution)/shard_map/all_to_all | solution.py:188
  19.4 211.4 %all-gather.7.cloned.1.call-start = ((), (), s32[]{:S(2)}) async-start(), calls=%async_computation.17 | async-start | bytes 2506752 | tf_op jit(solution)/shard_map/all_gather | solution.py:146
  21.3 101.0 %collective-permute-start = (bf16[128,1536]{1,0:T(8,128)(2,1)S(1)}, bf16[128,1536]{1,0:T(8,128)(2,1)}, u32[]{:S(2)}, u32[]{:S(2)}) collective-permute-start(bf16[128,1536]{1,0:T(8,128)(2,1)S(1)} %pad_maximum_fusion.8), channel_id=1, source_target_pairs={{0,1},{1,0},{2,3},{3,2},{4,5},{5,4},{6,7},{7,6},{8,9},{9,8},{10,11... | collective-permute-start | bytes 1179656 | tf_op jit(solution)/shard_map/ppermute | solution.py:163
  46.6 72.1 %copy-start.95 = (f32[2,3072]{1,0:T(2,128)S(1)}, f32[2,3072]{1,0:T(2,128)}, u32[]{:S(2)}) copy-start(f32[2,3072]{1,0:T(2,128)} %param.25) | copy-start | bytes 73732
  46.6 77.0 %all-to-all-start.1 = ((bf16[16,24,1536]{2,1,0:T(8,128)(2,1)}), bf16[16,24,1536]{2,1,0:T(8,128)(2,1)}, u32[]{:S(2)}, u32[]{:S(2)}) async-start(bf16[16,24,1536]{2,1,0:T(8,128)(2,1)} %bitcast.21), calls=%async_computation.1 | async-start | bytes 2359296 | tf_op jit(solution)/shard_map/all_to_all | solution.py:188
  51.7 69.7 %copy-start.40 = (bf16[128,768]{1,0:T(8,128)(2,1)S(1)}, bf16[128,768]{1,0:T(8,128)(2,1)}, u32[]{:S(2)}) copy-start(bf16[128,768]{1,0:T(8,128)(2,1)} %param.16) | copy-start | bytes 589828
  118.9 14.1 %collective-permute-start.1 = (bf16[16,24,3,384]{3,1,0,2:T(8,128)(2,1)S(1)}, bf16[16,24,3,384]{3,1,0,2:T(8,128)(2,1)}, u32[]{:S(2)}, u32[]{:S(2)}) collective-permute-start(bf16[16,24,3,384]{3,1,0,2:T(8,128)(2,1)S(1)} %copy.308), channel_id=1, source_target_pairs={{0,2},{2,0},{4,6},{6,4},{8,10},{10,8},{12,14},{14,12},{16,18},{18,... | collective-permute-start | bytes 2654216 | tf_op jit(solution)/shard_map/ppermute | solution.py:189
  123.6 11.4 %copy-start.9 = (bf16[256,1536]{1,0:T(8,128)(2,1)}, bf16[256,1536]{1,0:T(8,128)(2,1)S(1)}, u32[]{:S(2)}) copy-start(bf16[256,1536]{1,0:T(8,128)(2,1)S(1)} %maximum_select_fusion.5) | copy-start | bytes 2359300
  124.8 29.3 %all-to-all-start.2 = ((bf16[16,24,3,384]{3,1,2,0:T(8,128)(2,1)}), bf16[16,24,3,384]{3,1,2,0:T(8,128)(2,1)}, u32[]{:S(2)}, u32[]{:S(2)}) async-start(bf16[16,24,3,384]{3,1,2,0:T(8,128)(2,1)} %bitcast.27), calls=%async_computation.2 | async-start | bytes 1769472 | tf_op jit(solution)/shard_map/all_to_all | solution.py:188
  132.6 31.0 %collective-permute-start.2 = (bf16[16,24,1536]{2,1,0:T(8,128)(2,1)}, bf16[16,24,1536]{2,1,0:T(8,128)(2,1)}, u32[]{:S(2)}, u32[]{:S(2)}) collective-permute-start(bf16[16,24,1536]{2,1,0:T(8,128)(2,1)} %all-to-all-done.1), channel_id=1, source_target_pairs={{0,2},{2,0},{4,6},{6,4},{8,10},{10,8},{12,14},{14,12},{16,18},{18,... | collective-permute-start | bytes 3538952 | tf_op jit(solution)/shard_map/ppermute | solution.py:189
  156.2 32.6 %all-to-all-start.3 = ((bf16[16,24,1536]{2,1,0:T(8,128)(2,1)}), bf16[16,24,1536]{2,1,0:T(8,128)(2,1)S(1)}, u32[]{:S(2)}, u32[]{:S(2)}) async-start(bf16[16,24,1536]{2,1,0:T(8,128)(2,1)} %bitcast.379), calls=%async_computation.3 | async-start | bytes 2359296 | tf_op jit(solution)/shard_map/all_to_all | solution.py:188
  177.4 12.8 %collective-permute-start.3 = (f32[128,768]{1,0:T(8,128)}, f32[128,768]{1,0:T(8,128)}, u32[]{:S(2)}, u32[]{:S(2)}) collective-permute-start(f32[128,768]{1,0:T(8,128)} %constant_dynamic-slice_fusion.5), channel_id=1, source_target_pairs={{0,1},{1,0},{2,3},{3,2},{4,5},{5,4},{6,7},{7,6},{8,9},{9,8},{10,11... | collective-permute-start | bytes 1179656 | tf_op jit(solution)/shard_map/ppermute | solution.py:163
  179.0 12.7 %copy-start.127 = (f32[768]{0:T(1024)S(1)}, f32[768]{0:T(1024)}, u32[]{:S(2)}) copy-start(f32[768]{0:T(1024)} %get-tuple-element.184) | copy-start | bytes 9220
  179.0 12.7 %copy-start.129 = (f32[768]{0:T(1024)S(1)}, f32[768]{0:T(1024)}, u32[]{:S(2)}) copy-start(f32[768]{0:T(1024)} %get-tuple-element.187) | copy-start | bytes 9220
  179.0 12.7 %copy-start.138 = (f32[768]{0:T(1024)S(1)}, f32[768]{0:T(1024)}, u32[]{:S(2)}) copy-start(f32[768]{0:T(1024)} %get-tuple-element.177) | copy-start | bytes 9220
  179.0 12.8 %copy-start.139 = (f32[768]{0:T(1024)S(1)}, f32[768]{0:T(1024)}, u32[]{:S(2)}) copy-start(f32[768]{0:T(1024)} %get-tuple-element.178) | copy-start | bytes 9220
  181.2 11.2 %collective-permute-start.5 = (bf16[16,24,3,384]{3,1,0,2:T(8,128)(2,1)}, bf16[16,24,3,384]{3,1,0,2:T(8,128)(2,1)}, u32[]{:S(2)}, u32[]{:S(2)}) collective-permute-start(bf16[16,24,3,384]{3,1,0,2:T(8,128)(2,1)} %copy.307), channel_id=1, source_target_pairs={{0,2},{2,0},{4,6},{6,4},{8,10},{10,8},{12,14},{14,12},{16,18},{18,... | collective-permute-start | bytes 2654216 | tf_op jit(solution)/shard_map/ppermute | solution.py:189
  188.8 7.2 collective-permute-start.6
  192.0 10.3 %collective-permute-start.4 = (bf16[128,1536]{1,0:T(8,128)(2,1)S(1)}, bf16[128,1536]{1,0:T(8,128)(2,1)S(1)}, u32[]{:S(2)}, u32[]{:S(2)}) collective-permute-start(bf16[128,1536]{1,0:T(8,128)(2,1)S(1)} %pad_maximum_fusion.9), channel_id=1, source_target_pairs={{0,1},{1,0},{2,3},{3,2},{4,5},{5,4},{6,7},{7,6},{8,9},{9,8},{10,11... | collective-permute-start | bytes 1179656 | tf_op jit(solution)/shard_map/ppermute | solution.py:163
  226.0 42.4 %collective-permute-start.20 = (f32[16,24,384]{2,1,0:T(8,128)}, f32[16,24,384]{2,1,0:T(8,128)}, u32[]{:S(2)}, u32[]{:S(2)}) collective-permute-start(f32[16,24,384]{2,1,0:T(8,128)} %dynamic-slice_bitcast_fusion.3), channel_id=1, source_target_pairs={{0,2},{2,0},{4,6},{6,4},{8,10},{10,8},{12,14},{14,12},{16,18},{18,... | collective-permute-start | bytes 1769480 | tf_op jit(solution)/shard_map/ppermute | solution.py:201
  230.7 13.3 %collective-permute-start.9 = (f32[16,24,3,384]{3,1,2,0:T(8,128)}, f32[16,24,3,384]{3,1,2,0:T(8,128)}, u32[]{:S(2)}, u32[]{:S(2)}) collective-permute-start(f32[16,24,3,384]{3,1,2,0:T(8,128)} %dynamic-slice_bitcast_fusion.2), channel_id=1, source_target_pairs={{0,2},{2,0},{4,6},{6,4},{8,10},{10,8},{12,14},{14,12},{16,18},{18,... | collective-permute-start | bytes 5308424 | tf_op jit(solution)/shard_map/ppermute | solution.py:201
  238.5 37.7 %collective-permute-start.7 = (f32[128,768]{1,0:T(8,128)}, f32[128,768]{1,0:T(8,128)}, u32[]{:S(2)}, u32[]{:S(2)}) collective-permute-start(f32[128,768]{1,0:T(8,128)} %constant_dynamic-slice_fusion.2), channel_id=1, source_target_pairs={{0,1},{1,0},{2,3},{3,2},{4,5},{5,4},{6,7},{7,6},{8,9},{9,8},{10,11... | collective-permute-start | bytes 1179656 | tf_op jit(solution)/shard_map/ppermute | solution.py:163
  247.9 45.9 %all-to-all-start.4 = ((f32[16,24,3,384]{3,1,2,0:T(8,128)}), f32[16,24,3,384]{3,1,2,0:T(8,128)}, u32[]{:S(2)}, u32[]{:S(2)}) async-start(f32[16,24,3,384]{3,1,2,0:T(8,128)} %bitcast_add_fusion.3), calls=%async_computation.4 | async-start | bytes 3538944 | tf_op jit(solution)/shard_map/all_to_all | solution.py:202
  253.3 316.7 %reduce-scatter.5.cloned.1.call-start = ((), (), s32[]{:S(2)}) async-start(), calls=%async_computation.15 | async-start | bytes 5013504 | tf_op jit(solution)/shard_map/reduce_scatter | solution.py:142
  255.5 19.0 %collective-permute-start.10 = (f32[128,1536]{1,0:T(8,128)}, f32[128,1536]{1,0:T(8,128)}, u32[]{:S(2)}, u32[]{:S(2)}) collective-permute-start(f32[128,1536]{1,0:T(8,128)} %fusion.112), channel_id=1, source_target_pairs={{0,1},{1,0},{2,3},{3,2},{4,5},{5,4},{6,7},{7,6},{8,9},{9,8},{10,11... | collective-permute-start | bytes 2359304 | tf_op jit(solution)/shard_map/ppermute | solution.py:163
  265.8 55.1 %collective-permute-start.22 = (f32[16,24,1536]{2,1,0:T(8,128)}, f32[16,24,1536]{2,1,0:T(8,128)}, u32[]{:S(2)}, u32[]{:S(2)}) collective-permute-start(f32[16,24,1536]{2,1,0:T(8,128)} %dynamic-slice_bitcast_fusion), channel_id=1, source_target_pairs={{0,2},{2,0},{4,6},{6,4},{8,10},{10,8},{12,14},{14,12},{16,18},{18,... | collective-permute-start | bytes 7077896 | tf_op jit(solution)/shard_map/ppermute | solution.py:201
  278.2 23.0 %copy-start.13 = (f32[128,768]{1,0:T(8,128)}, f32[128,768]{1,0:T(8,128)S(1)}, u32[]{:S(2)}) copy-start(f32[128,768]{1,0:T(8,128)S(1)} %get-tuple-element.30) | copy-start | bytes 1179652
  293.8 46.2 %all-to-all-start.7 = ((f32[16,24,384]{2,1,0:T(8,128)}), f32[16,24,384]{2,1,0:T(8,128)}, u32[]{:S(2)}, u32[]{:S(2)}) async-start(f32[16,24,384]{2,1,0:T(8,128)} %bitcast_add_fusion.4), calls=%async_computation.7 | async-start | bytes 1179648 | tf_op jit(solution)/shard_map/all_to_all | solution.py:202
  301.3 6.2 collective-permute-start.11
  311.8 13.2 %copy-start.28 = (bf16[256,1,384]{2,0,1:T(8,128)(2,1)}, bf16[256,1,384]{2,0,1:T(8,128)(2,1)S(1)}, u32[]{:S(2)}) copy-start(bf16[256,1,384]{2,0,1:T(8,128)(2,1)S(1)} %copy.249) | copy-start | bytes 589828
  319.7 18.1 %collective-permute-start.12 = (f32[128,1536]{1,0:T(8,128)S(1)}, f32[128,1536]{1,0:T(8,128)}, u32[]{:S(2)}, u32[]{:S(2)}) collective-permute-start(f32[128,1536]{1,0:T(8,128)S(1)} %fusion.109), channel_id=1, source_target_pairs={{0,1},{1,0},{2,3},{3,2},{4,5},{5,4},{6,7},{7,6},{8,9},{9,8},{10,11... | collective-permute-start | bytes 2359304 | tf_op jit(solution)/shard_map/ppermute | solution.py:163
  340.0 76.4 %all-to-all-start.9 = ((f32[16,24,1536]{2,1,0:T(8,128)}), f32[16,24,1536]{2,1,0:T(8,128)S(1)}, u32[]{:S(2)}, u32[]{:S(2)}) async-start(f32[16,24,1536]{2,1,0:T(8,128)} %bitcast_add_fusion), calls=%async_computation.11 | async-start | bytes 4718592 | tf_op jit(solution)/shard_map/all_to_all | solution.py:202
  355.0 1.3 collective-permute-start.13
  356.3 4.5 collective-permute-start.14
  360.8 29.4 %copy-start.29 = (bf16[256,1,384]{2,0,1:T(8,128)(2,1)S(1)}, bf16[256,1,384]{2,0,1:T(8,128)(2,1)}, u32[]{:S(2)}) copy-start(bf16[256,1,384]{2,0,1:T(8,128)(2,1)} %copy-done.28) | copy-start | bytes 589828
  360.8 29.4 %copy-start.31 = (bf16[256,1,384]{2,0,1:T(8,128)(2,1)S(1)}, bf16[256,1,384]{2,0,1:T(8,128)(2,1)}, u32[]{:S(2)}) copy-start(bf16[256,1,384]{2,0,1:T(8,128)(2,1)} %copy.250) | copy-start | bytes 589828
  360.8 28.7 %collective-permute-start.15 = (f32[19968]{0:T(1024)S(1)}, f32[19968]{0:T(1024)S(1)}, u32[]{:S(2)}, u32[]{:S(2)}) collective-permute-start(f32[19968]{0:T(1024)S(1)} %add.469), channel_id=1, source_target_pairs={{0,8},{2,10},{4,12},{6,14},{8,0},{10,2},{12,4},{14,6},{16,24},{18,... | collective-permute-start | bytes 239624 | tf_op jit(solution)/shard_map/ppermute | solution.py:157
  389.6 13.8 %copy-start.64 = (bf16[128,768]{1,0:T(8,128)(2,1)S(1)}, bf16[128,768]{1,0:T(8,128)(2,1)}, u32[]{:S(2)}) copy-start(bf16[128,768]{1,0:T(8,128)(2,1)} %copy-done.63) | copy-start | bytes 589828
  389.6 13.8 %copy-start.85 = (bf16[6,64,256]{2,1,0:T(8,128)(2,1)S(1)}, bf16[6,64,256]{2,1,0:T(8,128)(2,1)}, u32[]{:S(2)}) copy-start(bf16[6,64,256]{2,1,0:T(8,128)(2,1)} %convolution_convert_fusion.5) | copy-start | bytes 589828
  389.6 13.8 %copy-start.87 = (bf16[128,768]{1,0:T(8,128)(2,1)S(1)}, bf16[128,768]{1,0:T(8,128)(2,1)}, u32[]{:S(2)}) copy-start(bf16[128,768]{1,0:T(8,128)(2,1)} %copy-done.86) | copy-start | bytes 589828
  389.6 12.5 %collective-permute-start.16 = (f32[19968]{0:T(1024)S(1)}, f32[19968]{0:T(1024)S(1)}, u32[]{:S(2)}, u32[]{:S(2)}) collective-permute-start(f32[19968]{0:T(1024)S(1)} %add.470), channel_id=1, source_target_pairs={{0,16},{2,18},{4,20},{6,22},{8,24},{10,26},{12,28},{14,30},{16,0},... | collective-permute-start | bytes 239624 | tf_op jit(solution)/shard_map/ppermute | solution.py:157
  402.1 3.4 collective-permute-start.17
  409.0 14.4 %collective-permute-start.18 = (f32[16,24,3,384]{3,1,2,0:T(8,128)}, f32[16,24,3,384]{3,1,2,0:T(8,128)}, u32[]{:S(2)}, u32[]{:S(2)}) collective-permute-start(f32[16,24,3,384]{3,1,2,0:T(8,128)} %bitcast.353), channel_id=1, source_target_pairs={{0,2},{2,0},{4,6},{6,4},{8,10},{10,8},{12,14},{14,12},{16,18},{18,... | collective-permute-start | bytes 5308424 | tf_op jit(solution)/shard_map/ppermute | solution.py:201
  411.1 4.3 collective-permute-start.19
  416.4 22.0 %all-to-all-start.6 = ((f32[16,24,384]{2,1,0:T(8,128)}), f32[16,24,384]{2,1,0:T(8,128)S(1)}, u32[]{:S(2)}, u32[]{:S(2)}) async-start(f32[16,24,384]{2,1,0:T(8,128)} %bitcast_add_fusion.5), calls=%async_computation.6 | async-start | bytes 1179648 | tf_op jit(solution)/shard_map/all_to_all | solution.py:202
  438.4 54.8 %all-to-all-start.5 = ((f32[16,24,3,384]{3,1,2,0:T(8,128)}), f32[16,24,3,384]{3,1,2,0:T(8,128)}, u32[]{:S(2)}, u32[]{:S(2)}) async-start(f32[16,24,3,384]{3,1,2,0:T(8,128)} %bitcast_add_fusion.2), calls=%async_computation.5 | async-start | bytes 3538944 | tf_op jit(solution)/shard_map/all_to_all | solution.py:202
  443.2 126.8 %reduce-scatter.3.cloned.1.call-start = ((), (), s32[]{:S(2)}) async-start(), calls=%async_computation.14 | async-start | bytes 5013504 | tf_op jit(solution)/shard_map/reduce_scatter | solution.py:142
  446.5 4.9 collective-permute-start.21
  493.2 71.3 %all-to-all-start.8 = ((f32[16,24,1536]{2,1,0:T(8,128)}), f32[16,24,1536]{2,1,0:T(8,128)}, u32[]{:S(2)}, u32[]{:S(2)}) async-start(f32[16,24,1536]{2,1,0:T(8,128)} %bitcast_add_fusion.1), calls=%async_computation.10 | async-start | bytes 4718592 | tf_op jit(solution)/shard_map/all_to_all | solution.py:202
  506.7 59.7 %copy-start.74 = (f32[2,1536,48]{1,2,0:T(8,128)S(1)}, f32[2,1536,48]{1,2,0:T(8,128)}, u32[]{:S(2)}) copy-start(f32[2,1536,48]{1,2,0:T(8,128)} %param.29) | copy-start | bytes 1769476
  645.0 4.9 collective-permute-start.23
  651.7 28.7 %copy-start.78 = (f32[19968]{0:T(1024)S(1)}, f32[19968]{0:T(1024)}, u32[]{:S(2)}) copy-start(f32[19968]{0:T(1024)} %add.472) | copy-start | bytes 239620
  651.7 27.5 %collective-permute-start.24 = (f32[384,768]{1,0:T(8,128)S(1)}, f32[384,768]{1,0:T(8,128)S(1)}, u32[]{:S(2)}, u32[]{:S(2)}) collective-permute-start(f32[384,768]{1,0:T(8,128)S(1)} %dynamic-slice_add_fusion), channel_id=1, source_target_pairs={{0,1},{1,0},{2,3},{3,2},{4,5},{5,4},{6,7},{7,6},{8,9},{9,8},{10,11... | collective-permute-start | bytes 3538952 | tf_op jit(solution)/shard_map/ppermute | solution.py:451
  679.3 5.3 collective-permute-start.25
  754.2 32.9 %all-to-all-start.11 = ((bf16[16,48,768]{2,1,0:T(8,128)(2,1)}), bf16[16,48,768]{2,1,0:T(8,128)(2,1)S(1)}, u32[]{:S(2)}, u32[]{:S(2)}) async-start(bf16[16,48,768]{2,1,0:T(8,128)(2,1)} %bitcast.132), calls=%async_computation.13 | async-start | bytes 2359296 | tf_op jit(solution)/shard_map/all_to_all | solution.py:477
  760.0 28.2 %copy-start.92 = (f32[2,2,768]{2,1,0:T(2,128)}, f32[2,2,768]{2,1,0:T(2,128)S(1)}, u32[]{:S(2)}) copy-start(f32[2,2,768]{2,1,0:T(2,128)S(1)} %slice.420) | copy-start | bytes 36868
  760.7 27.5 %copy-start.82 = (f32[2,3072]{1,0:T(2,128)}, f32[2,3072]{1,0:T(2,128)S(1)}, u32[]{:S(2)}) copy-start(f32[2,3072]{1,0:T(2,128)S(1)} %reshape.564) | copy-start | bytes 73732
  760.7 27.5 %copy-start.83 = (f32[2,4,768]{2,1,0:T(4,128)}, f32[2,4,768]{2,1,0:T(4,128)S(1)}, u32[]{:S(2)}) copy-start(f32[2,4,768]{2,1,0:T(4,128)S(1)} %reshape.562) | copy-start | bytes 73732
  (131 other events, 460.7 us)
Sparse Core Ops, SparseCore 0:
  10.9 53.4 all-gather.4
  67.2 48.0 all-gather.6
  266.6 82.3 reduce-scatter.4
  447.6 105.9 reduce-scatter.2

commit v11 on v9

--- a/solution.py
+++ b/solution.py
@@ -409,8 +409,8 @@
         small_sums.append(flat[offset : offset + part.size].reshape(part.shape))
         offset += part.size
     gains_grad, biases_grad, qkv_bias_grad, up_bias_grad = small_sums
-    flat, first_parts = lax.optimization_barrier((flat, weight_list[0]))
-    weight_list[0] = scatter_layer(first_parts)
+    flat, first_down = lax.optimization_barrier((flat, weight_list[0][3]))
+    weight_list[0] = scatter_layer(weight_list[0][:3] + (first_down,))
     qkv_grad = jnp.stack([weight_list[layer_id][0] for layer_id in range(LAYERS)])
     proj_grad = jnp.stack([weight_list[layer_id][1] for layer_id in range(LAYERS)])
     up_grad = jnp.stack([weight_list[layer_id][2] for layer_id in range(LAYERS)])

time: 804 us -> 796 us (0.990)
  waiting for transfers between devices: 343 us -> 316 us
  local copies, waits for them, and re-layouts: 77.1 us -> 92.9 us
    ppermute x4, waiting for transfers between devices: 36.2 us -> 8.15 us  [butterfly_sum(): flat = flat + lax.ppermute(flat, 'dp', swap_pairs(count, bit))]
    ppermute x8, waiting for transfers between devices: 26.3 us -> 15 us  [tensor_swap(): return lax.ppermute(block, 'tensor', [(0, 1), (1, 0)])]
    reduce_scatter x2, waiting for transfers between devices: 0.01 us -> 9.64 us  [dp_scatter(): lax.psum_scatter(partial, 'dp', scatter_dimension=dimension, tiled=True)]
    unnamed x325 -> x361, local copies, waits for them, and re-layouts: 15.1 us -> 24.1 us
    all_to_all x6, waiting for transfers between devices: 123 us -> 132 us  [chip_scatter_rows(): lax.all_to_all(chip_sum, 'dp', split_axis=0, concat_axis=0, tiled=True)]
  transfers between devices with their start and end apart: 45 -> 45, of which waited for: 23 -> 22; matrix products, arithmetic and copies ran while one was open for 23% -> 25% of each run, Pallas kernels for 0% -> 0%
where the time goes in v11:
time: 796 us; the launch traced here: 786 us
  waiting for transfers between devices  316 us (40%)
  matrix products  127 us (16%)
  local copies, waits for them, and re-layouts  92.9 us (12%)
  starting transfers between devices  90.2 us (11%)
  other arithmetic  86 us (11%)
  blocking collectives  56.9 us (7%)
  between operations  17.5 us (2%)
    all_to_all x6, waiting for transfers between devices, chip_scatter_rows(): lax.all_to_all(chip_sum, 'dp', split_axis=0, concat_axis=0, tiled=True)  132 us
    all_to_all x6, waiting for transfers between devices, chip_gather_rows(): lax.all_to_all(outgoing, 'dp', split_axis=0, concat_axis=0, tiled=True)  91.6 us
    all_to_all x1, blocking collectives, local(): lax.all_to_all(outgoing, 'dp', split_axis=0, concat_axis=0, tiled=True)  56.9 us
    all_to_all x6, starting transfers between devices, chip_scatter_rows(): lax.all_to_all(chip_sum, 'dp', split_axis=0, concat_axis=0, tiled=True)  31.4 us
    all_to_all x6, starting transfers between devices, chip_gather_rows(): lax.all_to_all(outgoing, 'dp', split_axis=0, concat_axis=0, tiled=True)  30.4 us
    ppermute x1, waiting for transfers between devices, local(): mine = mine + lax.ppermute(mine, 'tensor', [(0, 1), (1, 0)])  26.2 us
    unnamed x361, local copies, waits for them, and re-layouts  24.1 us
    all_to_all x1, waiting for transfers between devices, local(): lax.all_to_all(current.astype(jnp.bfloat16).reshape(dp_count, rows_local,...  24 us
  transfers between devices with their start and end apart: 45, of which 22 were waited for; matrix products, arithmetic and copies ran while one was open for 25% of the time, Pallas kernels for 0%

profile of v11, /device:TPU:11, one launch (start us, length us, event | category | flops | bytes accessed | tf_op | source)
XLA Modules:
  0.0 786.2 jit_solution(4689305172025663289)
XLA Ops:
  12.0 6.8 all-to-all-start.1
  20.4 11.6 %all-to-all-done.1 = bf16[16,24,384]{2,1,0:T(8,128)(2,1)S(1)} async-done(((bf16[16,24,384]{2,1,0:T(8,128)(2,1)}), bf16[16,24,384]{2,1,0:T(8,128)(2,1)S(1)}, u32[]{:S(2)}, u32[]{:S(2)}) %all-to-all-start.1) | async-done | bytes 294944 | tf_op jit(solution)/shard_map/all_to_all | solution.py:188
  32.7 4.0 all-to-all-start.4
  36.9 14.3 %all-to-all-done.4 = bf16[16,24,384]{2,1,0:T(8,128)(2,1)S(1)} async-done(((bf16[16,24,384]{2,1,0:T(8,128)(2,1)}), bf16[16,24,384]{2,1,0:T(8,128)(2,1)S(1)}, u32[]{:S(2)}, u32[]{:S(2)}) %all-to-all-start.4) | async-done | bytes 294944 | tf_op jit(solution)/shard_map/all_to_all | solution.py:188
  52.2 4.7 all-to-all-start
  60.2 22.8 %all-to-all-done = bf16[16,24,3,384]{3,1,2,0:T(8,128)(2,1)S(1)} async-done(((bf16[16,24,3,384]{3,1,2,0:T(8,128)(2,1)}), bf16[16,24,3,384]{3,1,2,0:T(8,128)(2,1)S(1)}, u32[]{:S(2)}, u32[]{:S(2)}) %all-to-all-start) | async-done | bytes 884768 | tf_op jit(solution)/shard_map/all_to_all | solution.py:188
  84.1 4.8 all-to-all-start.2
  100.8 22.8 %all-to-all-done.2 = bf16[16,24,1536]{2,1,0:T(8,128)(2,1)} async-done(((bf16[16,24,1536]{2,1,0:T(8,128)(2,1)}), bf16[16,24,1536]{2,1,0:T(8,128)(2,1)}, u32[]{:S(2)}, u32[]{:S(2)}) %all-to-all-start.2) | async-done | bytes 1179680 | tf_op jit(solution)/shard_map/all_to_all | solution.py:188
  124.7 5.1 all-to-all-start.3
  137.3 13.8 %all-to-all-done.3 = bf16[16,24,3,384]{3,1,2,0:T(8,128)(2,1)} async-done(((bf16[16,24,3,384]{3,1,2,0:T(8,128)(2,1)}), bf16[16,24,3,384]{3,1,2,0:T(8,128)(2,1)}, u32[]{:S(2)}, u32[]{:S(2)}) %all-to-all-start.3) | async-done | bytes 884768 | tf_op jit(solution)/shard_map/all_to_all | solution.py:188
  152.3 5.0 all-to-all-start.5
  159.7 4.1 maximum_select_fusion
  163.9 7.4 multiply_convert_fusion.3
  178.7 6.2 all-to-all-done.5
  188.9 3.5 maximum_select_fusion.4
  194.1 3.6 collective-permute-done.5
  198.9 3.2 convolution_add_fusion.2
  227.6 5.6 multiply_convert_fusion.2
  241.7 3.0 bitcast_add_fusion.3
  244.7 5.4 all-to-all-start.6
  250.2 4.6 fusion.220
  257.8 3.2 dynamic-slice_bitcast_fusion
  270.4 20.2 %all-to-all-done.6 = f32[16,24,3,384]{3,1,2,0:T(8,128)} async-done(((f32[16,24,3,384]{3,1,2,0:T(8,128)}), f32[16,24,3,384]{3,1,2,0:T(8,128)}, u32[]{:S(2)}, u32[]{:S(2)}) %all-to-all-start.6) | async-done | bytes 1769504 | tf_op jit(solution)/shard_map/all_to_all | solution.py:202
  290.6 5.0 all-to-all-start.9
  299.1 4.1 bitcast_add_fusion
  315.1 3.4 convert_reduce_fusion.1
  318.5 5.9 all-to-all-done.9
  325.3 4.4 all-to-all-start.11
  343.3 10.4 %collective-permute-done.17 = f32[128,1536]{1,0:T(8,128)} collective-permute-done((f32[128,1536]{1,0:T(8,128)}, f32[128,1536]{1,0:T(8,128)}, u32[]{:S(2)}, u32[]{:S(2)}) %collective-permute-start.17) | collective-permute-done | bytes 786464 | tf_op jit(solution)/shard_map/ppermute | solution.py:163
  364.8 27.5 %all-to-all-done.11 = f32[16,24,1536]{2,1,0:T(8,128)} async-done(((f32[16,24,1536]{2,1,0:T(8,128)}), f32[16,24,1536]{2,1,0:T(8,128)}, u32[]{:S(2)}, u32[]{:S(2)}) %all-to-all-start.11) | async-done | bytes 2359328 | tf_op jit(solution)/shard_map/all_to_all | solution.py:202
  392.3 4.7 all-to-all-start.8
  402.6 4.1 collective-permute-done.19
  414.4 4.3 fusion.148
  424.5 7.0 all-to-all-start.7
  434.5 5.0 collective-permute-done.23
  441.4 49.4 %all-to-all-done.7 = f32[16,24,3,384]{3,1,2,0:T(8,128)S(1)} async-done(((f32[16,24,3,384]{3,1,2,0:T(8,128)}), f32[16,24,3,384]{3,1,2,0:T(8,128)S(1)}, u32[]{:S(2)}, u32[]{:S(2)}) %all-to-all-start.7) | async-done | bytes 1769504 | tf_op jit(solution)/shard_map/all_to_all | solution.py:202
  492.0 4.8 all-to-all-start.10
  510.9 9.6 %reduce-scatter.3.cloned.1.call-done = f32[48,1536]{1,0:T(8,128)} async-done(((f32[768,1536]{1,0:T(8,128)}), f32[48,1536]{1,0:T(8,128)}) %reduce-scatter.3.cloned.1.call-update) | async-done | bytes 294928 | tf_op jit(solution)/shard_map/reduce_scatter | solution.py:142
  528.1 28.6 %all-to-all-done.10 = f32[16,24,1536]{2,1,0:T(8,128)S(1)} async-done(((f32[16,24,1536]{2,1,0:T(8,128)}), f32[16,24,1536]{2,1,0:T(8,128)S(1)}, u32[]{:S(2)}, u32[]{:S(2)}) %all-to-all-start.10) | async-done | bytes 2359328 | tf_op jit(solution)/shard_map/all_to_all | solution.py:202
  561.3 7.1 concatenate.136
  569.8 56.9 %all_to_all.70 = f32[16,48,768]{2,1,0:T(8,128)S(1)} all-to-all(f32[16,48,768]{2,1,0:T(8,128)S(1)} %copy.267), channel_id=1, replica_groups=mesh['dp'=16,'tensor'=2] {'dp'}, dimensions={0} | all-to-all | bytes 4718592 | tf_op jit(solution)/shard_map/all_to_all | solution.py:440
  626.7 4.4 fusion.243
  631.2 4.8 collective-permute-done.25
  639.5 26.2 %collective-permute-done.26 = f32[384,768]{1,0:T(8,128)S(1)} collective-permute-done((f32[384,768]{1,0:T(8,128)S(1)}, f32[384,768]{1,0:T(8,128)S(1)}, u32[]{:S(2)}, u32[]{:S(2)}) %collective-permute-start.26) | collective-permute-done | bytes 1179680 | tf_op jit(solution)/shard_map/ppermute | solution.py:451
  674.0 7.1 fusion
  681.1 4.8 fusion.17
  685.9 3.4 fusion.244
  689.3 3.1 fusion.245
  692.4 3.4 fusion.35
  695.8 3.2 fusion.39
  699.0 3.6 fusion.37
  702.6 3.1 fusion.246
  705.8 3.2 fusion.33
  709.0 3.3 fusion.29
  712.3 3.8 fusion.31
  716.1 3.1 fusion.247
  719.3 3.2 fusion.27
  722.5 3.5 fusion.23
  726.0 3.3 fusion.25
  729.4 3.1 fusion.248
  732.6 3.4 fusion.5
  735.9 4.3 fusion.53
  740.3 5.2 all-to-all-start.13
  749.2 24.0 %all-to-all-done.13 = bf16[16,48,768]{2,1,0:T(8,128)(2,1)S(1)} async-done(((bf16[16,48,768]{2,1,0:T(8,128)(2,1)}), bf16[16,48,768]{2,1,0:T(8,128)(2,1)S(1)}, u32[]{:S(2)}, u32[]{:S(2)}) %all-to-all-start.13) | async-done | bytes 1179680 | tf_op jit(solution)/shard_map/all_to_all | solution.py:477
  (689 shorter events, 209.8 us)
Async XLA Ops:
  7.2 156.6 %all-gather.5.cloned.1.call-start = ((), (), s32[]{:S(2)}) async-start(), calls=%async_computation.18 | async-start | bytes 2506752 | tf_op jit(solution)/shard_map/all_gather | solution.py:146
  9.2 83.8 %collective-permute-start.10 = (bf16[128,768]{1,0:T(8,128)(2,1)}, bf16[128,768]{1,0:T(8,128)(2,1)S(1)}, u32[]{:S(2)}, u32[]{:S(2)}) collective-permute-start(bf16[128,768]{1,0:T(8,128)(2,1)} %param.16), channel_id=1, source_target_pairs={{0,1},{1,0},{2,3},{3,2},{4,5},{5,4},{6,7},{7,6},{8,9},{9,8},{10,11... | collective-permute-start | bytes 589832 | tf_op jit(solution)/shard_map/ppermute | solution.py:163
  12.0 20.0 %all-to-all-start.1 = ((bf16[16,24,384]{2,1,0:T(8,128)(2,1)}), bf16[16,24,384]{2,1,0:T(8,128)(2,1)S(1)}, u32[]{:S(2)}, u32[]{:S(2)}) async-start(bf16[16,24,384]{2,1,0:T(8,128)(2,1)} %bitcast.18), calls=%async_computation.1 | async-start | bytes 589824 | tf_op jit(solution)/shard_map/all_to_all | solution.py:188
  18.8 33.4 %copy-start.67 = (bf16[1,48,3,384]{3,1,2,0:T(8,128)(2,1)}, bf16[1,48,3,384]{3,1,2,0:T(8,128)(2,1)S(1)}, u32[]{:S(2)}) copy-start(bf16[1,48,3,384]{3,1,2,0:T(8,128)(2,1)S(1)} %get-tuple-element.255) | copy-start | bytes 331780
  18.8 72.1 %copy-start.65 = (bf16[1,48,3,384]{3,1,2,0:T(8,128)(2,1)}, bf16[1,48,3,384]{3,1,2,0:T(8,128)(2,1)S(1)}, u32[]{:S(2)}) copy-start(bf16[1,48,3,384]{3,1,2,0:T(8,128)(2,1)S(1)} %get-tuple-element.254) | copy-start | bytes 331780
  19.6 37.4 %copy-start.139 = (f32[768]{0:T(1024)}, f32[768]{0:T(1024)S(1)}, u32[]{:S(2)}) copy-start(f32[768]{0:T(1024)S(1)} %get-tuple-element.179) | copy-start | bytes 9220
  19.6 37.4 %copy-start.141 = (f32[768]{0:T(1024)}, f32[768]{0:T(1024)S(1)}, u32[]{:S(2)}) copy-start(f32[768]{0:T(1024)S(1)} %get-tuple-element.180) | copy-start | bytes 9220
  32.7 18.5 %all-to-all-start.4 = ((bf16[16,24,384]{2,1,0:T(8,128)(2,1)}), bf16[16,24,384]{2,1,0:T(8,128)(2,1)S(1)}, u32[]{:S(2)}, u32[]{:S(2)}) async-start(bf16[16,24,384]{2,1,0:T(8,128)(2,1)} %bitcast.45), calls=%async_computation.4 | async-start | bytes 589824 | tf_op jit(solution)/shard_map/all_to_all | solution.py:188
  36.7 20.5 %copy-start.161 = (f32[128]{0:T(128)}, f32[128]{0:T(128)S(1)}, u32[]{:S(2)}) copy-start(f32[128]{0:T(128)S(1)} %broadcast_multiply_fusion.5) | copy-start | bytes 1540
  36.9 21.1 %copy-start.168 = (f32[128]{0:T(128)}, f32[128]{0:T(128)S(1)}, u32[]{:S(2)}) copy-start(f32[128]{0:T(128)S(1)} %add_rsqrt_fusion.1) | copy-start | bytes 1540
  52.2 30.8 %all-to-all-start = ((bf16[16,24,3,384]{3,1,2,0:T(8,128)(2,1)}), bf16[16,24,3,384]{3,1,2,0:T(8,128)(2,1)S(1)}, u32[]{:S(2)}, u32[]{:S(2)}) async-start(bf16[16,24,3,384]{3,1,2,0:T(8,128)(2,1)} %bitcast.2), calls=%async_computation | async-start | bytes 1769472 | tf_op jit(solution)/shard_map/all_to_all | solution.py:188
  56.9 170.7 %all-gather.7.cloned.1.call-start = ((), (), s32[]{:S(2)}) async-start(), calls=%async_computation.19 | async-start | bytes 2506752 | tf_op jit(solution)/shard_map/all_gather | solution.py:146
  58.0 36.1 %collective-permute-start = (bf16[128,1536]{1,0:T(8,128)(2,1)}, bf16[128,1536]{1,0:T(8,128)(2,1)}, u32[]{:S(2)}, u32[]{:S(2)}) collective-permute-start(bf16[128,1536]{1,0:T(8,128)(2,1)} %pad_maximum_fusion.8), channel_id=1, source_target_pairs={{0,1},{1,0},{2,3},{3,2},{4,5},{5,4},{6,7},{7,6},{8,9},{9,8},{10,11... | collective-permute-start | bytes 1179656 | tf_op jit(solution)/shard_map/ppermute | solution.py:163
  84.1 39.5 %all-to-all-start.2 = ((bf16[16,24,1536]{2,1,0:T(8,128)(2,1)}), bf16[16,24,1536]{2,1,0:T(8,128)(2,1)}, u32[]{:S(2)}, u32[]{:S(2)}) async-start(bf16[16,24,1536]{2,1,0:T(8,128)(2,1)} %bitcast.26), calls=%async_computation.2 | async-start | bytes 2359296 | tf_op jit(solution)/shard_map/all_to_all | solution.py:188
  89.3 40.8 %collective-permute-start.1 = (bf16[16,24,3,384]{3,1,0,2:T(8,128)(2,1)S(1)}, bf16[16,24,3,384]{3,1,0,2:T(8,128)(2,1)}, u32[]{:S(2)}, u32[]{:S(2)}) collective-permute-start(bf16[16,24,3,384]{3,1,0,2:T(8,128)(2,1)S(1)} %copy.315), channel_id=1, source_target_pairs={{0,2},{2,0},{4,6},{6,4},{8,10},{10,8},{12,14},{14,12},{16,18},{18,... | collective-permute-start | bytes 2654216 | tf_op jit(solution)/shard_map/ppermute | solution.py:189
  93.9 2.9 collective-permute-start.7
  95.4 36.7 %copy-start.12 = (bf16[256,1536]{1,0:T(8,128)(2,1)}, bf16[256,1536]{1,0:T(8,128)(2,1)S(1)}, u32[]{:S(2)}) copy-start(bf16[256,1536]{1,0:T(8,128)(2,1)S(1)} %maximum_select_fusion.5) | copy-start | bytes 2359300
  95.4 3.4 collective-permute-start.2
  95.9 27.8 %copy-start.95 = (bf16[2,24,3,384]{3,1,2,0:T(8,128)(2,1)S(1)}, bf16[2,24,3,384]{3,1,2,0:T(8,128)(2,1)}, u32[]{:S(2)}) copy-start(bf16[2,24,3,384]{3,1,2,0:T(8,128)(2,1)} %copy.240) | copy-start | bytes 331780
  124.7 26.5 %all-to-all-start.3 = ((bf16[16,24,3,384]{3,1,2,0:T(8,128)(2,1)}), bf16[16,24,3,384]{3,1,2,0:T(8,128)(2,1)}, u32[]{:S(2)}, u32[]{:S(2)}) async-start(bf16[16,24,3,384]{3,1,2,0:T(8,128)(2,1)} %bitcast.32), calls=%async_computation.3 | async-start | bytes 1769472 | tf_op jit(solution)/shard_map/all_to_all | solution.py:188
  129.7 30.0 %collective-permute-start.3 = (bf16[16,24,1536]{2,1,0:T(8,128)(2,1)}, bf16[16,24,1536]{2,1,0:T(8,128)(2,1)}, u32[]{:S(2)}, u32[]{:S(2)}) collective-permute-start(bf16[16,24,1536]{2,1,0:T(8,128)(2,1)} %all-to-all-done.2), channel_id=1, source_target_pairs={{0,2},{2,0},{4,6},{6,4},{8,10},{10,8},{12,14},{14,12},{16,18},{18,... | collective-permute-start | bytes 3538952 | tf_op jit(solution)/shard_map/ppermute | solution.py:189
  136.9 14.2 %copy-start.94 = (bf16[1,1536,48]{1,2,0:T(8,128)(2,1)S(1)}, bf16[1,1536,48]{1,2,0:T(8,128)(2,1)}, u32[]{:S(2)}) copy-start(bf16[1,1536,48]{1,2,0:T(8,128)(2,1)} %get-tuple-element.250) | copy-start | bytes 442372
  137.3 20.0 %copy-start.73 = (bf16[6,64,256]{2,1,0:T(8,128)(2,1)}, bf16[6,64,256]{2,1,0:T(8,128)(2,1)S(1)}, u32[]{:S(2)}) copy-start(bf16[6,64,256]{2,1,0:T(8,128)(2,1)S(1)} %convolution_convert_fusion.5) | copy-start | bytes 589828
  152.3 32.6 %all-to-all-start.5 = ((bf16[16,24,1536]{2,1,0:T(8,128)(2,1)}), bf16[16,24,1536]{2,1,0:T(8,128)(2,1)S(1)}, u32[]{:S(2)}, u32[]{:S(2)}) async-start(bf16[16,24,1536]{2,1,0:T(8,128)(2,1)} %bitcast.401), calls=%async_computation.5 | async-start | bytes 2359296 | tf_op jit(solution)/shard_map/all_to_all | solution.py:188
  173.2 12.5 %collective-permute-start.4 = (f32[128,768]{1,0:T(8,128)}, f32[128,768]{1,0:T(8,128)}, u32[]{:S(2)}, u32[]{:S(2)}) collective-permute-start(f32[128,768]{1,0:T(8,128)} %constant_dynamic-slice_fusion.3), channel_id=1, source_target_pairs={{0,1},{1,0},{2,3},{3,2},{4,5},{5,4},{6,7},{7,6},{8,9},{9,8},{10,11... | collective-permute-start | bytes 1179656 | tf_op jit(solution)/shard_map/ppermute | solution.py:163
  178.0 10.9 %collective-permute-start.6 = (bf16[16,24,3,384]{3,1,0,2:T(8,128)(2,1)}, bf16[16,24,3,384]{3,1,0,2:T(8,128)(2,1)}, u32[]{:S(2)}, u32[]{:S(2)}) collective-permute-start(bf16[16,24,3,384]{3,1,0,2:T(8,128)(2,1)} %copy.314), channel_id=1, source_target_pairs={{0,2},{2,0},{4,6},{6,4},{8,10},{10,8},{12,14},{14,12},{16,18},{18,... | collective-permute-start | bytes 2654216 | tf_op jit(solution)/shard_map/ppermute | solution.py:189
  184.9 7.5 collective-permute-start.8
  187.4 10.3 %collective-permute-start.5 = (bf16[128,1536]{1,0:T(8,128)(2,1)S(1)}, bf16[128,1536]{1,0:T(8,128)(2,1)S(1)}, u32[]{:S(2)}, u32[]{:S(2)}) collective-permute-start(bf16[128,1536]{1,0:T(8,128)(2,1)S(1)} %pad_maximum_fusion.9), channel_id=1, source_target_pairs={{0,1},{1,0},{2,3},{3,2},{4,5},{5,4},{6,7},{7,6},{8,9},{9,8},{10,11... | collective-permute-start | bytes 1179656 | tf_op jit(solution)/shard_map/ppermute | solution.py:163
  221.5 41.9 %collective-permute-start.16 = (f32[16,24,384]{2,1,0:T(8,128)}, f32[16,24,384]{2,1,0:T(8,128)}, u32[]{:S(2)}, u32[]{:S(2)}) collective-permute-start(f32[16,24,384]{2,1,0:T(8,128)} %dynamic-slice_bitcast_fusion.4), channel_id=1, source_target_pairs={{0,2},{2,0},{4,6},{6,4},{8,10},{10,8},{12,14},{14,12},{16,18},{18,... | collective-permute-start | bytes 1769480 | tf_op jit(solution)/shard_map/ppermute | solution.py:201
  226.3 14.9 %collective-permute-start.11 = (f32[16,24,3,384]{3,1,2,0:T(8,128)}, f32[16,24,3,384]{3,1,2,0:T(8,128)}, u32[]{:S(2)}, u32[]{:S(2)}) collective-permute-start(f32[16,24,3,384]{3,1,2,0:T(8,128)} %dynamic-slice_bitcast_fusion.3), channel_id=1, source_target_pairs={{0,2},{2,0},{4,6},{6,4},{8,10},{10,8},{12,14},{14,12},{16,18},{18,... | collective-permute-start | bytes 5308424 | tf_op jit(solution)/shard_map/ppermute | solution.py:201
  234.9 32.2 %collective-permute-start.9 = (f32[128,768]{1,0:T(8,128)}, f32[128,768]{1,0:T(8,128)}, u32[]{:S(2)}, u32[]{:S(2)}) collective-permute-start(f32[128,768]{1,0:T(8,128)} %constant_dynamic-slice_fusion), channel_id=1, source_target_pairs={{0,1},{1,0},{2,3},{3,2},{4,5},{5,4},{6,7},{7,6},{8,9},{9,8},{10,11... | collective-permute-start | bytes 1179656 | tf_op jit(solution)/shard_map/ppermute | solution.py:163
  241.0 24.4 %collective-permute-start.12 = (f32[128,1536]{1,0:T(8,128)}, f32[128,1536]{1,0:T(8,128)}, u32[]{:S(2)}, u32[]{:S(2)}) collective-permute-start(f32[128,1536]{1,0:T(8,128)} %fusion.112), channel_id=1, source_target_pairs={{0,1},{1,0},{2,3},{3,2},{4,5},{5,4},{6,7},{7,6},{8,9},{9,8},{10,11... | collective-permute-start | bytes 2359304 | tf_op jit(solution)/shard_map/ppermute | solution.py:163
  244.7 45.9 %all-to-all-start.6 = ((f32[16,24,3,384]{3,1,2,0:T(8,128)}), f32[16,24,3,384]{3,1,2,0:T(8,128)}, u32[]{:S(2)}, u32[]{:S(2)}) async-start(f32[16,24,3,384]{3,1,2,0:T(8,128)} %bitcast_add_fusion.3), calls=%async_computation.6 | async-start | bytes 3538944 | tf_op jit(solution)/shard_map/all_to_all | solution.py:202
  250.1 260.8 %reduce-scatter.5.cloned.1.call-start = ((), (), s32[]{:S(2)}) async-start(), calls=%async_computation.17 | async-start | bytes 5013504 | tf_op jit(solution)/shard_map/reduce_scatter | solution.py:142
  261.0 38.1 %collective-permute-start.24 = (f32[16,24,1536]{2,1,0:T(8,128)}, f32[16,24,1536]{2,1,0:T(8,128)}, u32[]{:S(2)}, u32[]{:S(2)}) collective-permute-start(f32[16,24,1536]{2,1,0:T(8,128)} %dynamic-slice_bitcast_fusion), channel_id=1, source_target_pairs={{0,2},{2,0},{4,6},{6,4},{8,10},{10,8},{12,14},{14,12},{16,18},{18,... | collective-permute-start | bytes 7077896 | tf_op jit(solution)/shard_map/ppermute | solution.py:201
  269.1 28.8 %copy-start.15 = (f32[128,768]{1,0:T(8,128)}, f32[128,768]{1,0:T(8,128)S(1)}, u32[]{:S(2)}) copy-start(f32[128,768]{1,0:T(8,128)S(1)} %get-tuple-element.27) | copy-start | bytes 1179652
  290.6 33.9 %all-to-all-start.9 = ((f32[16,24,384]{2,1,0:T(8,128)}), f32[16,24,384]{2,1,0:T(8,128)S(1)}, u32[]{:S(2)}, u32[]{:S(2)}) async-start(f32[16,24,384]{2,1,0:T(8,128)} %bitcast_add_fusion.4), calls=%async_computation.9 | async-start | bytes 1179648 | tf_op jit(solution)/shard_map/all_to_all | solution.py:202
  298.0 17.1 %copy-start.55 = (bf16[128,768]{1,0:T(8,128)(2,1)}, bf16[128,768]{1,0:T(8,128)(2,1)S(1)}, u32[]{:S(2)}) copy-start(bf16[128,768]{1,0:T(8,128)(2,1)S(1)} %convert_element_type.190) | copy-start | bytes 589828
  298.0 6.2 collective-permute-start.13
  312.6 28.7 %collective-permute-start.15 = (f32[16,24,384]{2,1,0:T(8,128)}, f32[16,24,384]{2,1,0:T(8,128)}, u32[]{:S(2)}, u32[]{:S(2)}) collective-permute-start(f32[16,24,384]{2,1,0:T(8,128)} %dynamic-slice_bitcast_fusion.5), channel_id=1, source_target_pairs={{0,2},{2,0},{4,6},{6,4},{8,10},{10,8},{12,14},{14,12},{16,18},{18,... | collective-permute-start | bytes 1769480 | tf_op jit(solution)/shard_map/ppermute | solution.py:201
  325.3 67.0 %all-to-all-start.11 = ((f32[16,24,1536]{2,1,0:T(8,128)}), f32[16,24,1536]{2,1,0:T(8,128)}, u32[]{:S(2)}, u32[]{:S(2)}) async-start(f32[16,24,1536]{2,1,0:T(8,128)} %bitcast_add_fusion), calls=%async_computation.13 | async-start | bytes 4718592 | tf_op jit(solution)/shard_map/all_to_all | solution.py:202
  334.6 19.0 %collective-permute-start.17 = (f32[128,1536]{1,0:T(8,128)}, f32[128,1536]{1,0:T(8,128)}, u32[]{:S(2)}, u32[]{:S(2)}) collective-permute-start(f32[128,1536]{1,0:T(8,128)} %fusion.109), channel_id=1, source_target_pairs={{0,1},{1,0},{2,3},{3,2},{4,5},{5,4},{6,7},{7,6},{8,9},{9,8},{10,11... | collective-permute-start | bytes 2359304 | tf_op jit(solution)/shard_map/ppermute | solution.py:163
  340.6 13.0 %copy-start.30 = (f32[256,768]{1,0:T(8,128)S(1)}, f32[256,768]{1,0:T(8,128)}, u32[]{:S(2)}) copy-start(f32[256,768]{1,0:T(8,128)} %copy-done.29) | copy-start | bytes 2359300
  340.6 13.0 %copy-start.32 = (f32[256,768]{1,0:T(8,128)S(1)}, f32[256,768]{1,0:T(8,128)}, u32[]{:S(2)}) copy-start(f32[256,768]{1,0:T(8,128)} %copy-done.31) | copy-start | bytes 2359300
  340.6 81.0 %collective-permute-start.14 = (f32[16,24,3,384]{3,1,2,0:T(8,128)}, f32[16,24,3,384]{3,1,2,0:T(8,128)}, u32[]{:S(2)}, u32[]{:S(2)}) collective-permute-start(f32[16,24,3,384]{3,1,2,0:T(8,128)} %dynamic-slice_bitcast_fusion.2), channel_id=1, source_target_pairs={{0,2},{2,0},{4,6},{6,4},{8,10},{10,8},{12,14},{14,12},{16,18},{18,... | collective-permute-start | bytes 5308424 | tf_op jit(solution)/shard_map/ppermute | solution.py:201
  392.3 32.2 %all-to-all-start.8 = ((f32[16,24,384]{2,1,0:T(8,128)}), f32[16,24,384]{2,1,0:T(8,128)}, u32[]{:S(2)}, u32[]{:S(2)}) async-start(f32[16,24,384]{2,1,0:T(8,128)} %bitcast_add_fusion.5), calls=%async_computation.8 | async-start | bytes 1179648 | tf_op jit(solution)/shard_map/all_to_all | solution.py:202
  397.0 123.5 %reduce-scatter.3.cloned.1.call-start = ((), (), s32[]{:S(2)}) async-start(), calls=%async_computation.16 | async-start | bytes 5013504 | tf_op jit(solution)/shard_map/reduce_scatter | solution.py:142
  399.8 1.5 collective-permute-start.18
  402.2 4.4 collective-permute-start.19
  406.7 4.4 collective-permute-start.20
  411.8 6.9 collective-permute-start.21
  420.3 12.0 %collective-permute-start.22 = (f32[19968]{0:T(1024)}, f32[19968]{0:T(1024)}, u32[]{:S(2)}, u32[]{:S(2)}) collective-permute-start(f32[19968]{0:T(1024)} %add.479), channel_id=1, source_target_pairs={{0,1},{1,0},{2,3},{3,2},{4,5},{5,4},{6,7},{7,6},{8,9},{9,8},{10,11... | collective-permute-start | bytes 239624 | tf_op jit(solution)/shard_map/ppermute | solution.py:159
  424.5 66.3 %all-to-all-start.7 = ((f32[16,24,3,384]{3,1,2,0:T(8,128)}), f32[16,24,3,384]{3,1,2,0:T(8,128)S(1)}, u32[]{:S(2)}, u32[]{:S(2)}) async-start(f32[16,24,3,384]{3,1,2,0:T(8,128)} %bitcast_add_fusion.2), calls=%async_computation.7 | async-start | bytes 3538944 | tf_op jit(solution)/shard_map/all_to_all | solution.py:202
  434.1 5.5 collective-permute-start.23
  441.4 55.4 %copy-start.37 = (f32[16,24,384]{2,1,0:T(8,128)S(1)}, f32[16,24,384]{2,1,0:T(8,128)}, u32[]{:S(2)}) copy-start(f32[16,24,384]{2,1,0:T(8,128)} %copy-done.36) | copy-start | bytes 1769476
  492.0 64.6 %all-to-all-start.10 = ((f32[16,24,1536]{2,1,0:T(8,128)}), f32[16,24,1536]{2,1,0:T(8,128)S(1)}, u32[]{:S(2)}, u32[]{:S(2)}) async-start(f32[16,24,1536]{2,1,0:T(8,128)} %bitcast_add_fusion.1), calls=%async_computation.12 | async-start | bytes 4718592 | tf_op jit(solution)/shard_map/all_to_all | solution.py:202
  631.1 4.9 collective-permute-start.25
  637.7 28.9 %copy-start.97 = (f32[19968]{0:T(1024)S(1)}, f32[19968]{0:T(1024)}, u32[]{:S(2)}) copy-start(f32[19968]{0:T(1024)} %add.480) | copy-start | bytes 239620
  637.7 28.0 %collective-permute-start.26 = (f32[384,768]{1,0:T(8,128)S(1)}, f32[384,768]{1,0:T(8,128)S(1)}, u32[]{:S(2)}, u32[]{:S(2)}) collective-permute-start(f32[384,768]{1,0:T(8,128)S(1)} %dynamic-slice_add_fusion), channel_id=1, source_target_pairs={{0,1},{1,0},{2,3},{3,2},{4,5},{5,4},{6,7},{7,6},{8,9},{9,8},{10,11... | collective-permute-start | bytes 3538952 | tf_op jit(solution)/shard_map/ppermute | solution.py:451
  665.8 5.1 collective-permute-start.27
  740.3 32.9 %all-to-all-start.13 = ((bf16[16,48,768]{2,1,0:T(8,128)(2,1)}), bf16[16,48,768]{2,1,0:T(8,128)(2,1)S(1)}, u32[]{:S(2)}, u32[]{:S(2)}) async-start(bf16[16,48,768]{2,1,0:T(8,128)(2,1)} %bitcast.148), calls=%async_computation.15 | async-start | bytes 2359296 | tf_op jit(solution)/shard_map/all_to_all | solution.py:477
  746.1 28.2 %copy-start.108 = (f32[2,2,768]{2,1,0:T(2,128)}, f32[2,2,768]{2,1,0:T(2,128)S(1)}, u32[]{:S(2)}) copy-start(f32[2,2,768]{2,1,0:T(2,128)S(1)} %slice.420) | copy-start | bytes 36868
  746.8 27.5 %copy-start.101 = (f32[2,3072]{1,0:T(2,128)}, f32[2,3072]{1,0:T(2,128)S(1)}, u32[]{:S(2)}) copy-start(f32[2,3072]{1,0:T(2,128)S(1)} %reshape.598) | copy-start | bytes 73732
  746.8 27.5 %copy-start.102 = (f32[2,4,768]{2,1,0:T(4,128)}, f32[2,4,768]{2,1,0:T(4,128)S(1)}, u32[]{:S(2)}) copy-start(f32[2,4,768]{2,1,0:T(4,128)S(1)} %reshape.596) | copy-start | bytes 73732
  (157 other events, 601.0 us)
Sparse Core Ops, SparseCore 0:
  10.9 46.6 all-gather.4
  60.6 51.4 all-gather.6
  261.6 99.7 reduce-scatter.4
  418.8 101.6 reduce-scatter.2

commit v12 on v11

--- a/solution.py
+++ b/solution.py
@@ -250,7 +250,9 @@
     saved_layers = []
     for layer_id in range(LAYERS):
         layer_weights = (
-            chip_gather_rows(qkv_weight[layer_id]),
+            dp_gather(qkv_weight[layer_id], 0)
+            if layer_id == LAYERS - 1
+            else chip_gather_rows(qkv_weight[layer_id]),
             chip_gather_rows(proj_weight[layer_id].T),
             dp_gather(up_weight[layer_id], 0),
             chip_gather_rows(down_weight[layer_id].T),

time: 796 us -> 779 us (0.979)
    all_to_all x6 -> x5, waiting for transfers between devices: 91.6 us -> 85.7 us  [chip_gather_rows(): lax.all_to_all(outgoing, 'dp', split_axis=0, concat_axis=0, tiled=True)]
    all_to_all x6 -> x5, starting transfers between devices: 30.4 us -> 25.7 us  [chip_gather_rows(): lax.all_to_all(outgoing, 'dp', split_axis=0, concat_axis=0, tiled=True)]
    unnamed x361 -> x346, local copies, waits for them, and re-layouts: 24.1 us -> 23.7 us
  transfers between devices with their start and end apart: 45 -> 44, of which waited for: 22 -> 21; matrix products, arithmetic and copies ran while one was open for 25% -> 24% of each run, Pallas kernels for 0% -> 0%
where the time goes in v12:
time: 779 us; the launch traced here: 768 us
  waiting for transfers between devices  312 us (40%)
  matrix products  126 us (16%)
  local copies, waits for them, and re-layouts  88.9 us (11%)
  starting transfers between devices  85.5 us (11%)
  other arithmetic  81.2 us (10%)
  blocking collectives  56.9 us (7%)
  between operations  17.5 us (2%)
    all_to_all x6, waiting for transfers between devices, chip_scatter_rows(): lax.all_to_all(chip_sum, 'dp', split_axis=0, concat_axis=0, tiled=True)  132 us
    all_to_all x5, waiting for transfers between devices, chip_gather_rows(): lax.all_to_all(outgoing, 'dp', split_axis=0, concat_axis=0, tiled=True)  85.7 us
    all_to_all x1, blocking collectives, local(): lax.all_to_all(outgoing, 'dp', split_axis=0, concat_axis=0, tiled=True)  56.9 us
    all_to_all x6, starting transfers between devices, chip_scatter_rows(): lax.all_to_all(chip_sum, 'dp', split_axis=0, concat_axis=0, tiled=True)  31.1 us
    ppermute x1, waiting for transfers between devices, local(): mine = mine + lax.ppermute(mine, 'tensor', [(0, 1), (1, 0)])  26.1 us
    all_to_all x5, starting transfers between devices, chip_gather_rows(): lax.all_to_all(outgoing, 'dp', split_axis=0, concat_axis=0, tiled=True)  25.7 us
    all_to_all x1, waiting for transfers between devices, local(): lax.all_to_all(current.astype(jnp.bfloat16).reshape(dp_count, rows_local,...  24 us
    unnamed x346, local copies, waits for them, and re-layouts  23.7 us
  transfers between devices with their start and end apart: 44, of which 21 were waited for; matrix products, arithmetic and copies ran while one was open for 24% of the time, Pallas kernels for 0%

profile of v12, /device:TPU:11, one launch (start us, length us, event | category | flops | bytes accessed | tf_op | source)
XLA Modules:
  0.0 767.6 jit_solution(10223029563262225550)
XLA Ops:
  12.4 6.5 all-to-all-start.1
  20.2 11.8 %all-to-all-done.1 = bf16[16,24,384]{2,1,0:T(8,128)(2,1)S(1)} async-done(((bf16[16,24,384]{2,1,0:T(8,128)(2,1)}), bf16[16,24,384]{2,1,0:T(8,128)(2,1)S(1)}, u32[]{:S(2)}, u32[]{:S(2)}) %all-to-all-start.1) | async-done | bytes 294944 | tf_op jit(solution)/shard_map/all_to_all | solution.py:188
  32.7 4.8 all-to-all-start.3
  38.5 13.9 %all-to-all-done.3 = bf16[16,24,384]{2,1,0:T(8,128)(2,1)} async-done(((bf16[16,24,384]{2,1,0:T(8,128)(2,1)}), bf16[16,24,384]{2,1,0:T(8,128)(2,1)}, u32[]{:S(2)}, u32[]{:S(2)}) %all-to-all-start.3) | async-done | bytes 294944 | tf_op jit(solution)/shard_map/all_to_all | solution.py:188
  53.4 4.9 all-to-all-start
  61.8 21.3 %all-to-all-done = bf16[16,24,3,384]{3,1,2,0:T(8,128)(2,1)S(1)} async-done(((bf16[16,24,3,384]{3,1,2,0:T(8,128)(2,1)}), bf16[16,24,3,384]{3,1,2,0:T(8,128)(2,1)S(1)}, u32[]{:S(2)}, u32[]{:S(2)}) %all-to-all-start) | async-done | bytes 884768 | tf_op jit(solution)/shard_map/all_to_all | solution.py:188
  84.3 4.7 all-to-all-start.2
  96.5 26.5 %all-to-all-done.2 = bf16[16,24,1536]{2,1,0:T(8,128)(2,1)} async-done(((bf16[16,24,1536]{2,1,0:T(8,128)(2,1)}), bf16[16,24,1536]{2,1,0:T(8,128)(2,1)}, u32[]{:S(2)}, u32[]{:S(2)}) %all-to-all-start.2) | async-done | bytes 1179680 | tf_op jit(solution)/shard_map/all_to_all | solution.py:188
  124.1 4.9 all-to-all-start.4
  137.6 4.3 maximum_select_fusion
  141.9 7.1 multiply_convert_fusion.3
  156.8 12.3 %all-to-all-done.4 = bf16[16,24,1536]{2,1,0:T(8,128)(2,1)} async-done(((bf16[16,24,1536]{2,1,0:T(8,128)(2,1)}), bf16[16,24,1536]{2,1,0:T(8,128)(2,1)}, u32[]{:S(2)}, u32[]{:S(2)}) %all-to-all-start.4) | async-done | bytes 1179680 | tf_op jit(solution)/shard_map/all_to_all | solution.py:188
  173.1 3.5 maximum_select_fusion.1
  176.7 5.1 collective-permute-done.5
  182.0 3.5 fusion.60
  208.9 6.0 multiply_convert_fusion.2
  223.3 3.0 bitcast_add_fusion.3
  226.3 5.2 all-to-all-start.5
  231.6 4.6 fusion.230
  236.2 3.0 fusion.154
  239.2 3.2 dynamic-slice_bitcast_fusion
  251.8 20.2 %all-to-all-done.5 = f32[16,24,3,384]{3,1,2,0:T(8,128)} async-done(((f32[16,24,3,384]{3,1,2,0:T(8,128)}), f32[16,24,3,384]{3,1,2,0:T(8,128)}, u32[]{:S(2)}, u32[]{:S(2)}) %all-to-all-start.5) | async-done | bytes 1769504 | tf_op jit(solution)/shard_map/all_to_all | solution.py:202
  272.0 4.8 all-to-all-start.8
  280.2 4.1 bitcast_add_fusion
  296.2 3.5 convert_reduce_fusion.1
  299.7 6.1 all-to-all-done.8
  306.6 4.7 all-to-all-start.10
  324.8 10.4 %collective-permute-done.16 = f32[128,1536]{1,0:T(8,128)} collective-permute-done((f32[128,1536]{1,0:T(8,128)}, f32[128,1536]{1,0:T(8,128)}, u32[]{:S(2)}, u32[]{:S(2)}) %collective-permute-start.16) | collective-permute-done | bytes 786464 | tf_op jit(solution)/shard_map/ppermute | solution.py:163
  346.3 27.5 %all-to-all-done.10 = f32[16,24,1536]{2,1,0:T(8,128)} async-done(((f32[16,24,1536]{2,1,0:T(8,128)}), f32[16,24,1536]{2,1,0:T(8,128)}, u32[]{:S(2)}, u32[]{:S(2)}) %all-to-all-start.10) | async-done | bytes 2359328 | tf_op jit(solution)/shard_map/all_to_all | solution.py:202
  373.8 4.7 all-to-all-start.7
  384.0 4.1 collective-permute-done.18
  389.6 2.9 collective-permute-done.19
  395.8 4.3 fusion.158
  405.8 7.0 all-to-all-start.6
  415.9 5.0 collective-permute-done.22
  422.7 49.4 %all-to-all-done.6 = f32[16,24,3,384]{3,1,2,0:T(8,128)S(1)} async-done(((f32[16,24,3,384]{3,1,2,0:T(8,128)}), f32[16,24,3,384]{3,1,2,0:T(8,128)S(1)}, u32[]{:S(2)}, u32[]{:S(2)}) %all-to-all-start.6) | async-done | bytes 1769504 | tf_op jit(solution)/shard_map/all_to_all | solution.py:202
  473.4 4.8 all-to-all-start.9
  492.3 9.7 %reduce-scatter.3.cloned.1.call-done = f32[48,1536]{1,0:T(8,128)} async-done(((f32[768,1536]{1,0:T(8,128)}), f32[48,1536]{1,0:T(8,128)}) %reduce-scatter.3.cloned.1.call-update) | async-done | bytes 294928 | tf_op jit(solution)/shard_map/reduce_scatter | solution.py:142
  509.5 28.6 %all-to-all-done.9 = f32[16,24,1536]{2,1,0:T(8,128)S(1)} async-done(((f32[16,24,1536]{2,1,0:T(8,128)}), f32[16,24,1536]{2,1,0:T(8,128)S(1)}, u32[]{:S(2)}, u32[]{:S(2)}) %all-to-all-start.9) | async-done | bytes 2359328 | tf_op jit(solution)/shard_map/all_to_all | solution.py:202
  542.8 7.1 concatenate.136
  551.3 56.9 %all_to_all.65 = f32[16,48,768]{2,1,0:T(8,128)S(1)} all-to-all(f32[16,48,768]{2,1,0:T(8,128)S(1)} %copy.251), channel_id=1, replica_groups=mesh['dp'=16,'tensor'=2] {'dp'}, dimensions={0} | all-to-all | bytes 4718592 | tf_op jit(solution)/shard_map/all_to_all | solution.py:442
  608.2 4.4 fusion.253
  612.7 4.8 collective-permute-done.24
  621.0 26.1 %collective-permute-done.25 = f32[384,768]{1,0:T(8,128)S(1)} collective-permute-done((f32[384,768]{1,0:T(8,128)S(1)}, f32[384,768]{1,0:T(8,128)S(1)}, u32[]{:S(2)}, u32[]{:S(2)}) %collective-permute-start.25) | collective-permute-done | bytes 1179680 | tf_op jit(solution)/shard_map/ppermute | solution.py:453
  655.4 7.2 fusion
  662.7 4.8 fusion.17
  667.5 3.4 fusion.254
  670.9 3.1 fusion.255
  674.0 3.4 fusion.35
  677.4 3.2 fusion.39
  680.6 3.6 fusion.37
  684.2 3.1 fusion.256
  687.4 3.2 fusion.33
  690.6 3.4 fusion.29
  694.0 3.8 fusion.31
  697.7 3.1 fusion.257
  700.9 3.2 fusion.27
  704.1 3.5 fusion.23
  707.7 3.4 fusion.25
  711.0 3.1 fusion.258
  714.2 3.4 fusion.5
  717.5 4.3 fusion.57
  721.9 5.2 all-to-all-start.12
  730.8 24.0 %all-to-all-done.12 = bf16[16,48,768]{2,1,0:T(8,128)(2,1)S(1)} async-done(((bf16[16,48,768]{2,1,0:T(8,128)(2,1)}), bf16[16,48,768]{2,1,0:T(8,128)(2,1)S(1)}, u32[]{:S(2)}, u32[]{:S(2)}) %all-to-all-start.12) | async-done | bytes 1179680 | tf_op jit(solution)/shard_map/all_to_all | solution.py:479
  (668 shorter events, 193.6 us)
Async XLA Ops:
  7.2 30.3 %copy-start.105 = (f32[2,4,768]{2,1,0:T(4,128)S(1)}, f32[2,4,768]{2,1,0:T(4,128)}, u32[]{:S(2)}) copy-start(f32[2,4,768]{2,1,0:T(4,128)} %param.23) | copy-start | bytes 73732
  7.2 31.0 %copy-start.6 = (bf16[128,768]{1,0:T(8,128)(2,1)S(1)}, bf16[128,768]{1,0:T(8,128)(2,1)}, u32[]{:S(2)}) copy-start(bf16[128,768]{1,0:T(8,128)(2,1)} %param.15) | copy-start | bytes 589828
  7.2 134.7 %all-gather.7.cloned.1.call-start = ((), (), s32[]{:S(2)}) async-start(), calls=%async_computation.17 | async-start | bytes 2506752 | tf_op jit(solution)/shard_map/all_gather | solution.py:146
  9.1 172.8 %all-gather.9.cloned.1.call-start = ((), (), s32[]{:S(2)}) async-start(), calls=%async_computation.18 | async-start | bytes 1880064 | tf_op jit(solution)/shard_map/all_gather | solution.py:146
  12.4 19.6 %all-to-all-start.1 = ((bf16[16,24,384]{2,1,0:T(8,128)(2,1)}), bf16[16,24,384]{2,1,0:T(8,128)(2,1)S(1)}, u32[]{:S(2)}, u32[]{:S(2)}) async-start(bf16[16,24,384]{2,1,0:T(8,128)(2,1)} %bitcast.18), calls=%async_computation.1 | async-start | bytes 589824 | tf_op jit(solution)/shard_map/all_to_all | solution.py:188
  18.9 73.8 %collective-permute-start.9 = (bf16[128,768]{1,0:T(8,128)(2,1)S(1)}, bf16[128,768]{1,0:T(8,128)(2,1)S(1)}, u32[]{:S(2)}, u32[]{:S(2)}) collective-permute-start(bf16[128,768]{1,0:T(8,128)(2,1)S(1)} %copy-done.54), channel_id=1, source_target_pairs={{0,1},{1,0},{2,3},{3,2},{4,5},{5,4},{6,7},{7,6},{8,9},{9,8},{10,11... | collective-permute-start | bytes 589832 | tf_op jit(solution)/shard_map/ppermute | solution.py:163
  32.7 25.6 %copy-start.129 = (f32[2,2,768]{2,1,0:T(2,128)S(1)}, f32[2,2,768]{2,1,0:T(2,128)}, u32[]{:S(2)}) copy-start(f32[2,2,768]{2,1,0:T(2,128)} %param.22) | copy-start | bytes 36868
  32.7 19.6 %all-to-all-start.3 = ((bf16[16,24,384]{2,1,0:T(8,128)(2,1)}), bf16[16,24,384]{2,1,0:T(8,128)(2,1)}, u32[]{:S(2)}, u32[]{:S(2)}) async-start(bf16[16,24,384]{2,1,0:T(8,128)(2,1)} %bitcast.41), calls=%async_computation.3 | async-start | bytes 589824 | tf_op jit(solution)/shard_map/all_to_all | solution.py:188
  38.3 20.8 %copy-start.155 = (f32[128]{0:T(128)}, f32[128]{0:T(128)S(1)}, u32[]{:S(2)}) copy-start(f32[128]{0:T(128)S(1)} %broadcast_multiply_fusion.5) | copy-start | bytes 1540
  53.4 29.8 %all-to-all-start = ((bf16[16,24,3,384]{3,1,2,0:T(8,128)(2,1)}), bf16[16,24,3,384]{3,1,2,0:T(8,128)(2,1)S(1)}, u32[]{:S(2)}, u32[]{:S(2)}) async-start(bf16[16,24,3,384]{3,1,2,0:T(8,128)(2,1)} %bitcast.2), calls=%async_computation | async-start | bytes 1769472 | tf_op jit(solution)/shard_map/all_to_all | solution.py:188
  58.2 150.7 %all-gather.11.cloned.1.call-start = ((), (), s32[]{:S(2)}) async-start(), calls=%async_computation.19 | async-start | bytes 2506752 | tf_op jit(solution)/shard_map/all_gather | solution.py:146
  59.9 33.8 %collective-permute-start = (bf16[128,1536]{1,0:T(8,128)(2,1)}, bf16[128,1536]{1,0:T(8,128)(2,1)}, u32[]{:S(2)}, u32[]{:S(2)}) collective-permute-start(bf16[128,1536]{1,0:T(8,128)(2,1)} %pad_maximum_fusion.8), channel_id=1, source_target_pairs={{0,1},{1,0},{2,3},{3,2},{4,5},{5,4},{6,7},{7,6},{8,9},{9,8},{10,11... | collective-permute-start | bytes 1179656 | tf_op jit(solution)/shard_map/ppermute | solution.py:163
  84.3 38.6 %all-to-all-start.2 = ((bf16[16,24,1536]{2,1,0:T(8,128)(2,1)}), bf16[16,24,1536]{2,1,0:T(8,128)(2,1)}, u32[]{:S(2)}, u32[]{:S(2)}) async-start(bf16[16,24,1536]{2,1,0:T(8,128)(2,1)} %bitcast.26), calls=%async_computation.2 | async-start | bytes 2359296 | tf_op jit(solution)/shard_map/all_to_all | solution.py:188
  90.1 39.3 %collective-permute-start.1 = (bf16[16,24,3,384]{3,1,0,2:T(8,128)(2,1)S(1)}, bf16[16,24,3,384]{3,1,0,2:T(8,128)(2,1)}, u32[]{:S(2)}, u32[]{:S(2)}) collective-permute-start(bf16[16,24,3,384]{3,1,0,2:T(8,128)(2,1)S(1)} %copy.295), channel_id=1, source_target_pairs={{0,2},{2,0},{4,6},{6,4},{8,10},{10,8},{12,14},{14,12},{16,18},{18,... | collective-permute-start | bytes 2654216 | tf_op jit(solution)/shard_map/ppermute | solution.py:189
  92.5 3.0 collective-permute-start.2
  95.0 36.2 %copy-start.12 = (bf16[256,1536]{1,0:T(8,128)(2,1)}, bf16[256,1536]{1,0:T(8,128)(2,1)S(1)}, u32[]{:S(2)}) copy-start(bf16[256,1536]{1,0:T(8,128)(2,1)S(1)} %maximum_select_fusion.4) | copy-start | bytes 2359300
  95.0 58.3 %collective-permute-start.6 = (bf16[16,24,384]{2,1,0:T(8,128)(2,1)}, bf16[16,24,384]{2,1,0:T(8,128)(2,1)}, u32[]{:S(2)}, u32[]{:S(2)}) collective-permute-start(bf16[16,24,384]{2,1,0:T(8,128)(2,1)} %all-to-all-done.3), channel_id=1, source_target_pairs={{0,2},{2,0},{4,6},{6,4},{8,10},{10,8},{12,14},{14,12},{16,18},{18,... | collective-permute-start | bytes 884744 | tf_op jit(solution)/shard_map/ppermute | solution.py:189
  124.1 45.0 %all-to-all-start.4 = ((bf16[16,24,1536]{2,1,0:T(8,128)(2,1)}), bf16[16,24,1536]{2,1,0:T(8,128)(2,1)}, u32[]{:S(2)}, u32[]{:S(2)}) async-start(bf16[16,24,1536]{2,1,0:T(8,128)(2,1)} %bitcast.49), calls=%async_computation.4 | async-start | bytes 2359296 | tf_op jit(solution)/shard_map/all_to_all | solution.py:188
  129.0 8.6 %collective-permute-start.3 = (bf16[16,24,1536]{2,1,0:T(8,128)(2,1)}, bf16[16,24,1536]{2,1,0:T(8,128)(2,1)}, u32[]{:S(2)}, u32[]{:S(2)}) collective-permute-start(bf16[16,24,1536]{2,1,0:T(8,128)(2,1)} %all-to-all-done.2), channel_id=1, source_target_pairs={{0,2},{2,0},{4,6},{6,4},{8,10},{10,8},{12,14},{14,12},{16,18},{18,... | collective-permute-start | bytes 3538952 | tf_op jit(solution)/shard_map/ppermute | solution.py:189
  151.0 18.4 %collective-permute-start.4 = (f32[128,768]{1,0:T(8,128)}, f32[128,768]{1,0:T(8,128)}, u32[]{:S(2)}, u32[]{:S(2)}) collective-permute-start(f32[128,768]{1,0:T(8,128)} %constant_dynamic-slice_fusion.3), channel_id=1, source_target_pairs={{0,1},{1,0},{2,3},{3,2},{4,5},{5,4},{6,7},{7,6},{8,9},{9,8},{10,11... | collective-permute-start | bytes 1179656 | tf_op jit(solution)/shard_map/ppermute | solution.py:163
  153.3 16.2 %copy-start.26 = (f32[256,768]{1,0:T(8,128)S(1)}, f32[256,768]{1,0:T(8,128)}, u32[]{:S(2)}) copy-start(f32[256,768]{1,0:T(8,128)} %copy-done.25) | copy-start | bytes 2359300
  155.9 15.0 %copy-start.139 = (f32[768]{0:T(1024)S(1)}, f32[768]{0:T(1024)}, u32[]{:S(2)}) copy-start(f32[768]{0:T(1024)} %get-tuple-element.178) | copy-start | bytes 9220
  155.9 15.0 %copy-start.141 = (f32[768]{0:T(1024)S(1)}, f32[768]{0:T(1024)}, u32[]{:S(2)}) copy-start(f32[768]{0:T(1024)} %get-tuple-element.181) | copy-start | bytes 9220
  155.9 15.0 %copy-start.152 = (f32[768]{0:T(1024)S(1)}, f32[768]{0:T(1024)}, u32[]{:S(2)}) copy-start(f32[768]{0:T(1024)} %get-tuple-element.171) | copy-start | bytes 9220
  156.0 15.0 %copy-start.153 = (f32[768]{0:T(1024)S(1)}, f32[768]{0:T(1024)}, u32[]{:S(2)}) copy-start(f32[768]{0:T(1024)} %get-tuple-element.172) | copy-start | bytes 9220
  156.8 15.7 %copy-start.144 = (f32[6,256]{1,0:T(8,128)S(1)}, f32[6,256]{1,0:T(8,128)}, u32[]{:S(2)}) copy-start(f32[6,256]{1,0:T(8,128)} %copy-done.143) | copy-start | bytes 18436
  156.8 15.7 %copy-start.146 = (f32[6,256]{1,0:T(8,128)S(1)}, f32[6,256]{1,0:T(8,128)}, u32[]{:S(2)}) copy-start(f32[6,256]{1,0:T(8,128)} %copy-done.145) | copy-start | bytes 18436
  169.1 4.1 collective-permute-start.7
  171.1 10.6 %collective-permute-start.5 = (bf16[128,1536]{1,0:T(8,128)(2,1)S(1)}, bf16[128,1536]{1,0:T(8,128)(2,1)S(1)}, u32[]{:S(2)}, u32[]{:S(2)}) collective-permute-start(bf16[128,1536]{1,0:T(8,128)(2,1)S(1)} %pad_maximum_fusion.9), channel_id=1, source_target_pairs={{0,1},{1,0},{2,3},{3,2},{4,5},{5,4},{6,7},{7,6},{8,9},{9,8},{10,11... | collective-permute-start | bytes 1179656 | tf_op jit(solution)/shard_map/ppermute | solution.py:163
  203.6 41.2 %collective-permute-start.15 = (f32[16,24,384]{2,1,0:T(8,128)}, f32[16,24,384]{2,1,0:T(8,128)}, u32[]{:S(2)}, u32[]{:S(2)}) collective-permute-start(f32[16,24,384]{2,1,0:T(8,128)} %dynamic-slice_bitcast_fusion.4), channel_id=1, source_target_pairs={{0,2},{2,0},{4,6},{6,4},{8,10},{10,8},{12,14},{14,12},{16,18},{18,... | collective-permute-start | bytes 1769480 | tf_op jit(solution)/shard_map/ppermute | solution.py:201
  207.6 15.2 %collective-permute-start.10 = (f32[16,24,3,384]{3,1,2,0:T(8,128)}, f32[16,24,3,384]{3,1,2,0:T(8,128)}, u32[]{:S(2)}, u32[]{:S(2)}) collective-permute-start(f32[16,24,3,384]{3,1,2,0:T(8,128)} %dynamic-slice_bitcast_fusion.3), channel_id=1, source_target_pairs={{0,2},{2,0},{4,6},{6,4},{8,10},{10,8},{12,14},{14,12},{16,18},{18,... | collective-permute-start | bytes 5308424 | tf_op jit(solution)/shard_map/ppermute | solution.py:201
  216.6 31.9 %collective-permute-start.8 = (f32[128,768]{1,0:T(8,128)}, f32[128,768]{1,0:T(8,128)}, u32[]{:S(2)}, u32[]{:S(2)}) collective-permute-start(f32[128,768]{1,0:T(8,128)} %constant_dynamic-slice_fusion), channel_id=1, source_target_pairs={{0,1},{1,0},{2,3},{3,2},{4,5},{5,4},{6,7},{7,6},{8,9},{9,8},{10,11... | collective-permute-start | bytes 1179656 | tf_op jit(solution)/shard_map/ppermute | solution.py:163
  222.7 24.1 %collective-permute-start.11 = (f32[128,1536]{1,0:T(8,128)}, f32[128,1536]{1,0:T(8,128)}, u32[]{:S(2)}, u32[]{:S(2)}) collective-permute-start(f32[128,1536]{1,0:T(8,128)} %fusion.122), channel_id=1, source_target_pairs={{0,1},{1,0},{2,3},{3,2},{4,5},{5,4},{6,7},{7,6},{8,9},{9,8},{10,11... | collective-permute-start | bytes 2359304 | tf_op jit(solution)/shard_map/ppermute | solution.py:163
  226.3 45.7 %all-to-all-start.5 = ((f32[16,24,3,384]{3,1,2,0:T(8,128)}), f32[16,24,3,384]{3,1,2,0:T(8,128)}, u32[]{:S(2)}, u32[]{:S(2)}) async-start(f32[16,24,3,384]{3,1,2,0:T(8,128)} %bitcast_add_fusion.3), calls=%async_computation.5 | async-start | bytes 3538944 | tf_op jit(solution)/shard_map/all_to_all | solution.py:202
  231.5 260.7 %reduce-scatter.5.cloned.1.call-start = ((), (), s32[]{:S(2)}) async-start(), calls=%async_computation.16 | async-start | bytes 5013504 | tf_op jit(solution)/shard_map/reduce_scatter | solution.py:142
  242.4 37.7 %collective-permute-start.23 = (f32[16,24,1536]{2,1,0:T(8,128)}, f32[16,24,1536]{2,1,0:T(8,128)}, u32[]{:S(2)}, u32[]{:S(2)}) collective-permute-start(f32[16,24,1536]{2,1,0:T(8,128)} %dynamic-slice_bitcast_fusion), channel_id=1, source_target_pairs={{0,2},{2,0},{4,6},{6,4},{8,10},{10,8},{12,14},{14,12},{16,18},{18,... | collective-permute-start | bytes 7077896 | tf_op jit(solution)/shard_map/ppermute | solution.py:201
  250.5 28.6 %copy-start.16 = (f32[128,768]{1,0:T(8,128)}, f32[128,768]{1,0:T(8,128)S(1)}, u32[]{:S(2)}) copy-start(f32[128,768]{1,0:T(8,128)S(1)} %get-tuple-element.27) | copy-start | bytes 1179652
  272.0 33.8 %all-to-all-start.8 = ((f32[16,24,384]{2,1,0:T(8,128)}), f32[16,24,384]{2,1,0:T(8,128)S(1)}, u32[]{:S(2)}, u32[]{:S(2)}) async-start(f32[16,24,384]{2,1,0:T(8,128)} %bitcast_add_fusion.4), calls=%async_computation.8 | async-start | bytes 1179648 | tf_op jit(solution)/shard_map/all_to_all | solution.py:202
  279.1 17.1 %copy-start.57 = (bf16[128,768]{1,0:T(8,128)(2,1)}, bf16[128,768]{1,0:T(8,128)(2,1)S(1)}, u32[]{:S(2)}) copy-start(bf16[128,768]{1,0:T(8,128)(2,1)S(1)} %convert_element_type.190) | copy-start | bytes 589828
  279.1 6.2 collective-permute-start.12
  293.7 29.1 %collective-permute-start.14 = (f32[16,24,384]{2,1,0:T(8,128)}, f32[16,24,384]{2,1,0:T(8,128)}, u32[]{:S(2)}, u32[]{:S(2)}) collective-permute-start(f32[16,24,384]{2,1,0:T(8,128)} %dynamic-slice_bitcast_fusion.5), channel_id=1, source_target_pairs={{0,2},{2,0},{4,6},{6,4},{8,10},{10,8},{12,14},{14,12},{16,18},{18,... | collective-permute-start | bytes 1769480 | tf_op jit(solution)/shard_map/ppermute | solution.py:201
  306.6 67.1 %all-to-all-start.10 = ((f32[16,24,1536]{2,1,0:T(8,128)}), f32[16,24,1536]{2,1,0:T(8,128)}, u32[]{:S(2)}, u32[]{:S(2)}) async-start(f32[16,24,1536]{2,1,0:T(8,128)} %bitcast_add_fusion), calls=%async_computation.12 | async-start | bytes 4718592 | tf_op jit(solution)/shard_map/all_to_all | solution.py:202
  316.2 19.0 %collective-permute-start.16 = (f32[128,1536]{1,0:T(8,128)}, f32[128,1536]{1,0:T(8,128)}, u32[]{:S(2)}, u32[]{:S(2)}) collective-permute-start(f32[128,1536]{1,0:T(8,128)} %fusion.119), channel_id=1, source_target_pairs={{0,1},{1,0},{2,3},{3,2},{4,5},{5,4},{6,7},{7,6},{8,9},{9,8},{10,11... | collective-permute-start | bytes 2359304 | tf_op jit(solution)/shard_map/ppermute | solution.py:163
  322.2 13.0 %copy-start.34 = (f32[256,768]{1,0:T(8,128)S(1)}, f32[256,768]{1,0:T(8,128)}, u32[]{:S(2)}) copy-start(f32[256,768]{1,0:T(8,128)} %copy-done.33) | copy-start | bytes 2359300
  322.2 80.8 %collective-permute-start.13 = (f32[16,24,3,384]{3,1,2,0:T(8,128)}, f32[16,24,3,384]{3,1,2,0:T(8,128)}, u32[]{:S(2)}, u32[]{:S(2)}) collective-permute-start(f32[16,24,3,384]{3,1,2,0:T(8,128)} %dynamic-slice_bitcast_fusion.2), channel_id=1, source_target_pairs={{0,2},{2,0},{4,6},{6,4},{8,10},{10,8},{12,14},{14,12},{16,18},{18,... | collective-permute-start | bytes 5308424 | tf_op jit(solution)/shard_map/ppermute | solution.py:201
  373.8 32.1 %all-to-all-start.7 = ((f32[16,24,384]{2,1,0:T(8,128)}), f32[16,24,384]{2,1,0:T(8,128)}, u32[]{:S(2)}, u32[]{:S(2)}) async-start(f32[16,24,384]{2,1,0:T(8,128)} %bitcast_add_fusion.5), calls=%async_computation.7 | async-start | bytes 1179648 | tf_op jit(solution)/shard_map/all_to_all | solution.py:202
  378.5 123.5 %reduce-scatter.3.cloned.1.call-start = ((), (), s32[]{:S(2)}) async-start(), calls=%async_computation.15 | async-start | bytes 5013504 | tf_op jit(solution)/shard_map/reduce_scatter | solution.py:142
  381.2 1.5 collective-permute-start.17
  383.7 4.4 collective-permute-start.18
  388.1 4.4 collective-permute-start.19
  393.2 6.9 collective-permute-start.20
  401.7 12.0 %collective-permute-start.21 = (f32[19968]{0:T(1024)}, f32[19968]{0:T(1024)}, u32[]{:S(2)}, u32[]{:S(2)}) collective-permute-start(f32[19968]{0:T(1024)} %add.478), channel_id=1, source_target_pairs={{0,1},{1,0},{2,3},{3,2},{4,5},{5,4},{6,7},{7,6},{8,9},{9,8},{10,11... | collective-permute-start | bytes 239624 | tf_op jit(solution)/shard_map/ppermute | solution.py:159
  405.8 66.3 %all-to-all-start.6 = ((f32[16,24,3,384]{3,1,2,0:T(8,128)}), f32[16,24,3,384]{3,1,2,0:T(8,128)S(1)}, u32[]{:S(2)}, u32[]{:S(2)}) async-start(f32[16,24,3,384]{3,1,2,0:T(8,128)} %bitcast_add_fusion.2), calls=%async_computation.6 | async-start | bytes 3538944 | tf_op jit(solution)/shard_map/all_to_all | solution.py:202
  415.4 5.4 collective-permute-start.22
  422.7 55.4 %copy-start.40 = (f32[16,24,384]{2,1,0:T(8,128)S(1)}, f32[16,24,384]{2,1,0:T(8,128)}, u32[]{:S(2)}) copy-start(f32[16,24,384]{2,1,0:T(8,128)} %copy-done.39) | copy-start | bytes 1769476
  473.4 64.8 %all-to-all-start.9 = ((f32[16,24,1536]{2,1,0:T(8,128)}), f32[16,24,1536]{2,1,0:T(8,128)S(1)}, u32[]{:S(2)}, u32[]{:S(2)}) async-start(f32[16,24,1536]{2,1,0:T(8,128)} %bitcast_add_fusion.1), calls=%async_computation.11 | async-start | bytes 4718592 | tf_op jit(solution)/shard_map/all_to_all | solution.py:202
  612.6 4.9 collective-permute-start.24
  619.2 28.9 %copy-start.94 = (f32[19968]{0:T(1024)S(1)}, f32[19968]{0:T(1024)}, u32[]{:S(2)}) copy-start(f32[19968]{0:T(1024)} %add.479) | copy-start | bytes 239620
  619.2 27.9 %collective-permute-start.25 = (f32[384,768]{1,0:T(8,128)S(1)}, f32[384,768]{1,0:T(8,128)S(1)}, u32[]{:S(2)}, u32[]{:S(2)}) collective-permute-start(f32[384,768]{1,0:T(8,128)S(1)} %dynamic-slice_add_fusion), channel_id=1, source_target_pairs={{0,1},{1,0},{2,3},{3,2},{4,5},{5,4},{6,7},{7,6},{8,9},{9,8},{10,11... | collective-permute-start | bytes 3538952 | tf_op jit(solution)/shard_map/ppermute | solution.py:453
  647.2 5.1 collective-permute-start.26
  721.9 32.9 %all-to-all-start.12 = ((bf16[16,48,768]{2,1,0:T(8,128)(2,1)}), bf16[16,48,768]{2,1,0:T(8,128)(2,1)S(1)}, u32[]{:S(2)}, u32[]{:S(2)}) async-start(bf16[16,48,768]{2,1,0:T(8,128)(2,1)} %bitcast.144), calls=%async_computation.14 | async-start | bytes 2359296 | tf_op jit(solution)/shard_map/all_to_all | solution.py:479
  727.7 28.2 %copy-start.104 = (f32[2,2,768]{2,1,0:T(2,128)}, f32[2,2,768]{2,1,0:T(2,128)S(1)}, u32[]{:S(2)}) copy-start(f32[2,2,768]{2,1,0:T(2,128)S(1)} %slice.420) | copy-start | bytes 36868
  728.4 27.5 %copy-start.97 = (f32[2,3072]{1,0:T(2,128)}, f32[2,3072]{1,0:T(2,128)S(1)}, u32[]{:S(2)}) copy-start(f32[2,3072]{1,0:T(2,128)S(1)} %reshape.589) | copy-start | bytes 73732
  728.4 27.5 %copy-start.98 = (f32[2,4,768]{2,1,0:T(4,128)}, f32[2,4,768]{2,1,0:T(4,128)S(1)}, u32[]{:S(2)}) copy-start(f32[2,4,768]{2,1,0:T(4,128)S(1)} %reshape.587) | copy-start | bytes 73732
  (150 other events, 514.9 us)
Sparse Core Ops, SparseCore 0:
  10.9 47.7 all-gather.6
  61.5 48.9 all-gather.8
  113.4 54.8 all-gather.10
  243.0 99.5 reduce-scatter.4
  400.2 101.6 reduce-scatter.2

commit v13 on v12

--- a/solution.py
+++ b/solution.py
@@ -206,11 +206,11 @@
     return jnp.concatenate([even, odd], axis=0)
 
 
-def scatter_layer(parts):
+def scatter_layer(parts, proj_whole=False):
     qkv_part, proj_part, up_part, down_part = parts
     return (
         chip_scatter_rows(qkv_part),
-        chip_scatter_rows(proj_part).T,
+        (dp_scatter(proj_part, 0) if proj_whole else chip_scatter_rows(proj_part)).T,
         dp_scatter(up_part, 0),
         chip_scatter_rows(down_part).T,
     )
@@ -395,7 +395,7 @@
         grad_stream = grad_stream + inverse * (normed_grad - normed_mean - normed * product_mean)
         weight_list[layer_id] = (qkv_part, proj_part, up_part, down_part)
         if layer_id > 0:
-            weight_list[layer_id] = scatter_layer(weight_list[layer_id])
+            weight_list[layer_id] = scatter_layer(weight_list[layer_id], proj_whole=True)
             first_sum, grad_stream = lax.optimization_barrier((weight_list[layer_id][0], grad_stream))
             weight_list[layer_id] = (first_sum,) + weight_list[layer_id][1:]
     small_parts = (

time: 779 us -> 774 us (level)
  blocking collectives: 56.9 us -> 76.7 us
  waiting for transfers between devices: 312 us -> 293 us
  starting transfers between devices: 85.5 us -> 71.2 us
    all_to_all x5 -> x4, waiting for transfers between devices: 85.7 us -> 65.3 us  [chip_gather_rows(): lax.all_to_all(outgoing, 'dp', split_axis=0, concat_axis=0, tiled=True)]
    all_to_all x0 -> x1, blocking collectives: none -> 19.1 us  [chip_gather_rows(): lax.all_to_all(outgoing, 'dp', split_axis=0, concat_axis=0, tiled=True)]
    all_to_all x5 -> x4, starting transfers between devices: 25.7 us -> 18 us  [chip_gather_rows(): lax.all_to_all(outgoing, 'dp', split_axis=0, concat_axis=0, tiled=True)]
    all_to_all x6 -> x5, starting transfers between devices: 31.1 us -> 26.9 us  [chip_scatter_rows(): lax.all_to_all(chip_sum, 'dp', split_axis=0, concat_axis=0, tiled=True)]
    unnamed x346 -> x312, local copies, waits for them, and re-layouts: 23.7 us -> 26.7 us
    add x6 -> x5, other arithmetic: 15.8 us -> 13.8 us  [chip_scatter_rows(): chip_sum = keep + lax.ppermute(send, 'dp', swap_pairs(count, 1))]
    all_to_all x6 -> x5, waiting for transfers between devices: 132 us -> 133 us  [chip_scatter_rows(): lax.all_to_all(chip_sum, 'dp', split_axis=0, concat_axis=0, tiled=True)]
  transfers between devices with their start and end apart: 44 -> 42, of which waited for: 21 -> 19; matrix products, arithmetic and copies ran while one was open for 24% -> 25% of each run, Pallas kernels for 0% -> 0%
where the time goes in v13:
time: 774 us; the launch traced here: 764 us
  waiting for transfers between devices  293 us (38%)
  matrix products  131 us (17%)
  local copies, waits for them, and re-layouts  93.7 us (12%)
  other arithmetic  81.1 us (10%)
  blocking collectives  76.7 us (10%)
  starting transfers between devices  71.2 us (9%)
  between operations  17.5 us (2%)
    all_to_all x5, waiting for transfers between devices, chip_scatter_rows(): lax.all_to_all(chip_sum, 'dp', split_axis=0, concat_axis=0, tiled=True)  133 us
    all_to_all x4, waiting for transfers between devices, chip_gather_rows(): lax.all_to_all(outgoing, 'dp', split_axis=0, concat_axis=0, tiled=True)  65.3 us
    all_to_all x1, blocking collectives, local(): lax.all_to_all(outgoing, 'dp', split_axis=0, concat_axis=0, tiled=True)  57.6 us
    all_to_all x5, starting transfers between devices, chip_scatter_rows(): lax.all_to_all(chip_sum, 'dp', split_axis=0, concat_axis=0, tiled=True)  26.9 us
    unnamed x312, local copies, waits for them, and re-layouts  26.7 us
    ppermute x1, waiting for transfers between devices, local(): mine = mine + lax.ppermute(mine, 'tensor', [(0, 1), (1, 0)])  26.4 us
    all_to_all x1, waiting for transfers between devices, local(): lax.all_to_all(current.astype(jnp.bfloat16).reshape(dp_count, rows_local,...  24 us
    ppermute x8, waiting for transfers between devices, tensor_swap(): return lax.ppermute(block, 'tensor', [(0, 1), (1, 0)])  22.5 us
  transfers between devices with their start and end apart: 42, of which 19 were waited for; matrix products, arithmetic and copies ran while one was open for 25% of the time, Pallas kernels for 0%

profile of v13, /device:TPU:11, one launch (start us, length us, event | category | flops | bytes accessed | tf_op | source)
XLA Modules:
  0.0 764.3 jit_solution(18000668906948003532)
XLA Ops:
  11.6 19.1 %all_to_all.60 = bf16[16,24,384]{2,1,0:T(8,128)(2,1)S(1)} all-to-all(bf16[16,24,384]{2,1,0:T(8,128)(2,1)S(1)} %bitcast.409), channel_id=1, replica_groups=mesh['dp'=16,'tensor'=2] {'dp'}, dimensions={0} | all-to-all | bytes 589824 | tf_op jit(solution)/shard_map/all_to_all | solution.py:188
  31.4 4.4 all-to-all-start.3
  38.0 11.7 %all-to-all-done.3 = bf16[16,24,384]{2,1,0:T(8,128)(2,1)} async-done(((bf16[16,24,384]{2,1,0:T(8,128)(2,1)}), bf16[16,24,384]{2,1,0:T(8,128)(2,1)}, u32[]{:S(2)}, u32[]{:S(2)}) %all-to-all-start.3) | async-done | bytes 294944 | tf_op jit(solution)/shard_map/all_to_all | solution.py:188
  50.8 4.4 all-to-all-start
  59.7 20.6 %all-to-all-done = bf16[16,24,3,384]{3,1,2,0:T(8,128)(2,1)S(1)} async-done(((bf16[16,24,3,384]{3,1,2,0:T(8,128)(2,1)}), bf16[16,24,3,384]{3,1,2,0:T(8,128)(2,1)S(1)}, u32[]{:S(2)}, u32[]{:S(2)}) %all-to-all-start) | async-done | bytes 884768 | tf_op jit(solution)/shard_map/all_to_all | solution.py:188
  81.6 4.3 all-to-all-start.2
  98.5 21.5 %all-to-all-done.2 = bf16[16,24,1536]{2,1,0:T(8,128)(2,1)} async-done(((bf16[16,24,1536]{2,1,0:T(8,128)(2,1)}), bf16[16,24,1536]{2,1,0:T(8,128)(2,1)}, u32[]{:S(2)}, u32[]{:S(2)}) %all-to-all-start.2) | async-done | bytes 1179680 | tf_op jit(solution)/shard_map/all_to_all | solution.py:188
  122.1 4.9 all-to-all-start.4
  134.4 4.3 maximum_select_fusion
  138.7 7.6 multiply_convert_fusion.3
  155.2 11.4 %all-to-all-done.4 = bf16[16,24,1536]{2,1,0:T(8,128)(2,1)} async-done(((bf16[16,24,1536]{2,1,0:T(8,128)(2,1)}), bf16[16,24,1536]{2,1,0:T(8,128)(2,1)}, u32[]{:S(2)}, u32[]{:S(2)}) %all-to-all-start.4) | async-done | bytes 1179680 | tf_op jit(solution)/shard_map/all_to_all | solution.py:188
  170.9 3.4 maximum_select_fusion.1
  174.4 5.3 collective-permute-done.5
  180.8 3.2 fusion.60
  205.6 2.7 fusion.231
  208.4 5.7 multiply_convert_fusion.2
  217.4 3.1 convert_reduce_fusion
  225.7 3.0 bitcast_add_fusion.3
  228.7 4.9 all-to-all-start.5
  241.6 3.0 fusion.154
  248.0 6.7 collective-permute-done.11
  259.6 21.7 %all-to-all-done.5 = f32[16,24,3,384]{3,1,2,0:T(8,128)} async-done(((f32[16,24,3,384]{3,1,2,0:T(8,128)}), f32[16,24,3,384]{3,1,2,0:T(8,128)}, u32[]{:S(2)}, u32[]{:S(2)}) %all-to-all-start.5) | async-done | bytes 1769504 | tf_op jit(solution)/shard_map/all_to_all | solution.py:202
  284.0 4.2 bitcast_add_fusion
  288.2 5.5 all-to-all-start.9
  303.6 3.6 convert_reduce_fusion.1
  320.5 10.5 %collective-permute-done.15 = f32[128,1536]{1,0:T(8,128)} collective-permute-done((f32[128,1536]{1,0:T(8,128)}, f32[128,1536]{1,0:T(8,128)}, u32[]{:S(2)}, u32[]{:S(2)}) %collective-permute-start.15) | collective-permute-done | bytes 786464 | tf_op jit(solution)/shard_map/ppermute | solution.py:163
  342.2 26.8 %all-to-all-done.9 = f32[16,24,1536]{2,1,0:T(8,128)} async-done(((f32[16,24,1536]{2,1,0:T(8,128)}), f32[16,24,1536]{2,1,0:T(8,128)}, u32[]{:S(2)}, u32[]{:S(2)}) %all-to-all-start.9) | async-done | bytes 2359328 | tf_op jit(solution)/shard_map/all_to_all | solution.py:202
  369.0 4.6 all-to-all-start.7
  379.1 5.5 collective-permute-done.17
  385.2 3.1 collective-permute-done.18
  389.0 3.1 collective-permute-start.19
  392.1 4.2 fusion.158
  398.8 2.9 bitcast_add_fusion.2
  401.8 6.6 all-to-all-start.6
  411.4 5.1 collective-permute-done.21
  418.3 49.4 %all-to-all-done.6 = f32[16,24,3,384]{3,1,2,0:T(8,128)S(1)} async-done(((f32[16,24,3,384]{3,1,2,0:T(8,128)}), f32[16,24,3,384]{3,1,2,0:T(8,128)S(1)}, u32[]{:S(2)}, u32[]{:S(2)}) %all-to-all-start.6) | async-done | bytes 1769504 | tf_op jit(solution)/shard_map/all_to_all | solution.py:202
  468.9 5.3 all-to-all-start.8
  498.9 34.7 %all-to-all-done.8 = f32[16,24,1536]{2,1,0:T(8,128)S(1)} async-done(((f32[16,24,1536]{2,1,0:T(8,128)}), f32[16,24,1536]{2,1,0:T(8,128)S(1)}, u32[]{:S(2)}, u32[]{:S(2)}) %all-to-all-start.8) | async-done | bytes 2359328 | tf_op jit(solution)/shard_map/all_to_all | solution.py:202
  538.3 7.1 concatenate.132
  546.7 57.6 %all_to_all.61 = f32[16,48,768]{2,1,0:T(8,128)S(1)} all-to-all(f32[16,48,768]{2,1,0:T(8,128)S(1)} %copy.239), channel_id=1, replica_groups=mesh['dp'=16,'tensor'=2] {'dp'}, dimensions={0} | all-to-all | bytes 4718592 | tf_op jit(solution)/shard_map/all_to_all | solution.py:442
  604.3 4.4 fusion.252
  608.8 4.8 collective-permute-done.23
  616.4 26.4 %collective-permute-done.24 = f32[384,768]{1,0:T(8,128)S(1)} collective-permute-done((f32[384,768]{1,0:T(8,128)S(1)}, f32[384,768]{1,0:T(8,128)S(1)}, u32[]{:S(2)}, u32[]{:S(2)}) %collective-permute-start.24) | collective-permute-done | bytes 1179680 | tf_op jit(solution)/shard_map/ppermute | solution.py:453
  648.3 2.5 select_reduce_fusion
  651.4 7.5 fusion
  659.0 5.0 fusion.17
  663.9 3.4 fusion.253
  667.3 3.1 fusion.254
  670.4 3.4 fusion.35
  673.8 3.2 fusion.39
  677.0 3.6 fusion.37
  680.6 3.1 fusion.255
  683.8 3.2 fusion.33
  687.0 3.3 fusion.29
  690.4 3.8 fusion.31
  694.1 3.1 fusion.256
  697.3 3.2 fusion.27
  700.5 3.5 fusion.23
  704.1 3.3 fusion.25
  707.4 3.1 fusion.257
  710.6 3.4 fusion.5
  713.9 4.3 fusion.57
  718.3 5.2 all-to-all-start.11
  727.2 24.0 %all-to-all-done.11 = bf16[16,48,768]{2,1,0:T(8,128)(2,1)S(1)} async-done(((bf16[16,48,768]{2,1,0:T(8,128)(2,1)}), bf16[16,48,768]{2,1,0:T(8,128)(2,1)S(1)}, u32[]{:S(2)}, u32[]{:S(2)}) %all-to-all-start.11) | async-done | bytes 1179680 | tf_op jit(solution)/shard_map/all_to_all | solution.py:479
  (626 shorter events, 196.1 us)
Async XLA Ops:
  7.2 30.0 %copy-start.89 = (f32[2,4,768]{2,1,0:T(4,128)S(1)}, f32[2,4,768]{2,1,0:T(4,128)}, u32[]{:S(2)}) copy-start(f32[2,4,768]{2,1,0:T(4,128)} %param.23) | copy-start | bytes 73732
  7.2 30.7 %copy-start.7 = (bf16[128,768]{1,0:T(8,128)(2,1)S(1)}, bf16[128,768]{1,0:T(8,128)(2,1)}, u32[]{:S(2)}) copy-start(bf16[128,768]{1,0:T(8,128)(2,1)} %param.15) | copy-start | bytes 589828
  7.2 131.4 %all-gather.7.cloned.1.call-start = ((), (), s32[]{:S(2)}) async-start(), calls=%async_computation.18 | async-start | bytes 2506752 | tf_op jit(solution)/shard_map/all_gather | solution.py:146
  9.0 171.8 %all-gather.9.cloned.1.call-start = ((), (), s32[]{:S(2)}) async-start(), calls=%async_computation.19 | async-start | bytes 1880064 | tf_op jit(solution)/shard_map/all_gather | solution.py:146
  31.4 18.3 %all-to-all-start.3 = ((bf16[16,24,384]{2,1,0:T(8,128)(2,1)}), bf16[16,24,384]{2,1,0:T(8,128)(2,1)}, u32[]{:S(2)}, u32[]{:S(2)}) async-start(bf16[16,24,384]{2,1,0:T(8,128)(2,1)} %bitcast.41), calls=%async_computation.3 | async-start | bytes 589824 | tf_op jit(solution)/shard_map/all_to_all | solution.py:188
  35.9 19.3 %copy-start.113 = (f32[2,2,768]{2,1,0:T(2,128)S(1)}, f32[2,2,768]{2,1,0:T(2,128)}, u32[]{:S(2)}) copy-start(f32[2,2,768]{2,1,0:T(2,128)} %param.22) | copy-start | bytes 36868
  35.9 116.1 %collective-permute-start.9 = (bf16[128,768]{1,0:T(8,128)(2,1)}, bf16[128,768]{1,0:T(8,128)(2,1)}, u32[]{:S(2)}, u32[]{:S(2)}) collective-permute-start(bf16[128,768]{1,0:T(8,128)(2,1)} %param.16), channel_id=1, source_target_pairs={{0,1},{1,0},{2,3},{3,2},{4,5},{5,4},{6,7},{7,6},{8,9},{9,8},{10,11... | collective-permute-start | bytes 589832 | tf_op jit(solution)/shard_map/ppermute | solution.py:163
  38.0 18.3 %copy-start.137 = (f32[128]{0:T(128)}, f32[128]{0:T(128)S(1)}, u32[]{:S(2)}) copy-start(f32[128]{0:T(128)S(1)} %broadcast_multiply_fusion.5) | copy-start | bytes 1540
  50.8 29.6 %all-to-all-start = ((bf16[16,24,3,384]{3,1,2,0:T(8,128)(2,1)}), bf16[16,24,3,384]{3,1,2,0:T(8,128)(2,1)S(1)}, u32[]{:S(2)}, u32[]{:S(2)}) async-start(bf16[16,24,3,384]{3,1,2,0:T(8,128)(2,1)} %bitcast.2), calls=%async_computation | async-start | bytes 1769472 | tf_op jit(solution)/shard_map/all_to_all | solution.py:188
  55.1 153.2 %all-gather.11.cloned.1.call-start = ((), (), s32[]{:S(2)}) async-start(), calls=%async_computation.20 | async-start | bytes 2506752 | tf_op jit(solution)/shard_map/all_gather | solution.py:146
  57.0 37.7 %collective-permute-start = (bf16[128,1536]{1,0:T(8,128)(2,1)}, bf16[128,1536]{1,0:T(8,128)(2,1)}, u32[]{:S(2)}, u32[]{:S(2)}) collective-permute-start(bf16[128,1536]{1,0:T(8,128)(2,1)} %pad_maximum_fusion.8), channel_id=1, source_target_pairs={{0,1},{1,0},{2,3},{3,2},{4,5},{5,4},{6,7},{7,6},{8,9},{9,8},{10,11... | collective-permute-start | bytes 1179656 | tf_op jit(solution)/shard_map/ppermute | solution.py:163
  81.6 38.4 %all-to-all-start.2 = ((bf16[16,24,1536]{2,1,0:T(8,128)(2,1)}), bf16[16,24,1536]{2,1,0:T(8,128)(2,1)}, u32[]{:S(2)}, u32[]{:S(2)}) async-start(bf16[16,24,1536]{2,1,0:T(8,128)(2,1)} %bitcast.26), calls=%async_computation.2 | async-start | bytes 2359296 | tf_op jit(solution)/shard_map/all_to_all | solution.py:188
  87.3 40.2 %collective-permute-start.1 = (bf16[16,24,3,384]{3,1,0,2:T(8,128)(2,1)S(1)}, bf16[16,24,3,384]{3,1,0,2:T(8,128)(2,1)S(1)}, u32[]{:S(2)}, u32[]{:S(2)}) collective-permute-start(bf16[16,24,3,384]{3,1,0,2:T(8,128)(2,1)S(1)} %copy.281), channel_id=1, source_target_pairs={{0,2},{2,0},{4,6},{6,4},{8,10},{10,8},{12,14},{14,12},{16,18},{18,... | collective-permute-start | bytes 2654216 | tf_op jit(solution)/shard_map/ppermute | solution.py:189
  90.1 6.4 collective-permute-start.2
  96.0 32.0 %copy-start.13 = (bf16[256,1536]{1,0:T(8,128)(2,1)}, bf16[256,1536]{1,0:T(8,128)(2,1)S(1)}, u32[]{:S(2)}) copy-start(bf16[256,1536]{1,0:T(8,128)(2,1)S(1)} %maximum_select_fusion.4) | copy-start | bytes 2359300
  96.0 54.5 %collective-permute-start.6 = (bf16[16,24,384]{2,1,0:T(8,128)(2,1)}, bf16[16,24,384]{2,1,0:T(8,128)(2,1)}, u32[]{:S(2)}, u32[]{:S(2)}) collective-permute-start(bf16[16,24,384]{2,1,0:T(8,128)(2,1)} %all-to-all-done.3), channel_id=1, source_target_pairs={{0,2},{2,0},{4,6},{6,4},{8,10},{10,8},{12,14},{14,12},{16,18},{18,... | collective-permute-start | bytes 884744 | tf_op jit(solution)/shard_map/ppermute | solution.py:189
  122.1 44.5 %all-to-all-start.4 = ((bf16[16,24,1536]{2,1,0:T(8,128)(2,1)}), bf16[16,24,1536]{2,1,0:T(8,128)(2,1)}, u32[]{:S(2)}, u32[]{:S(2)}) async-start(bf16[16,24,1536]{2,1,0:T(8,128)(2,1)} %bitcast.49), calls=%async_computation.4 | async-start | bytes 2359296 | tf_op jit(solution)/shard_map/all_to_all | solution.py:188
  127.0 350.3 %reduce-scatter.4.cloned.1.call-start = ((), (), s32[]{:S(2)}) async-start(), calls=%async_computation.15 | async-start | bytes 1253376 | tf_op jit(solution)/shard_map/reduce_scatter | solution.py:142
  127.1 7.3 collective-permute-start.3
  148.2 18.7 %collective-permute-start.4 = (f32[128,768]{1,0:T(8,128)}, f32[128,768]{1,0:T(8,128)S(1)}, u32[]{:S(2)}, u32[]{:S(2)}) collective-permute-start(f32[128,768]{1,0:T(8,128)} %constant_dynamic-slice_fusion.3), channel_id=1, source_target_pairs={{0,1},{1,0},{2,3},{3,2},{4,5},{5,4},{6,7},{7,6},{8,9},{9,8},{10,11... | collective-permute-start | bytes 1179656 | tf_op jit(solution)/shard_map/ppermute | solution.py:163
  150.5 16.5 %copy-start.25 = (f32[256,768]{1,0:T(8,128)S(1)}, f32[256,768]{1,0:T(8,128)}, u32[]{:S(2)}) copy-start(f32[256,768]{1,0:T(8,128)} %copy-done.24) | copy-start | bytes 2359300
  155.2 15.1 %copy-start.126 = (f32[6,256]{1,0:T(8,128)S(1)}, f32[6,256]{1,0:T(8,128)}, u32[]{:S(2)}) copy-start(f32[6,256]{1,0:T(8,128)} %copy-done.125) | copy-start | bytes 18436
  155.2 15.1 %copy-start.128 = (f32[6,256]{1,0:T(8,128)S(1)}, f32[6,256]{1,0:T(8,128)}, u32[]{:S(2)}) copy-start(f32[6,256]{1,0:T(8,128)} %copy-done.127) | copy-start | bytes 18436
  166.6 4.4 collective-permute-start.7
  169.0 10.6 %collective-permute-start.5 = (bf16[128,1536]{1,0:T(8,128)(2,1)S(1)}, bf16[128,1536]{1,0:T(8,128)(2,1)S(1)}, u32[]{:S(2)}, u32[]{:S(2)}) collective-permute-start(bf16[128,1536]{1,0:T(8,128)(2,1)S(1)} %pad_maximum_fusion.9), channel_id=1, source_target_pairs={{0,1},{1,0},{2,3},{3,2},{4,5},{5,4},{6,7},{7,6},{8,9},{9,8},{10,11... | collective-permute-start | bytes 1179656 | tf_op jit(solution)/shard_map/ppermute | solution.py:163
  202.6 22.4 %collective-permute-start.10 = (f32[16,24,3,384]{3,1,2,0:T(8,128)}, f32[16,24,3,384]{3,1,2,0:T(8,128)}, u32[]{:S(2)}, u32[]{:S(2)}) collective-permute-start(f32[16,24,3,384]{3,1,2,0:T(8,128)} %dynamic-slice_bitcast_fusion.3), channel_id=1, source_target_pairs={{0,2},{2,0},{4,6},{6,4},{8,10},{10,8},{12,14},{14,12},{16,18},{18,... | collective-permute-start | bytes 5308424 | tf_op jit(solution)/shard_map/ppermute | solution.py:201
  216.1 40.2 %collective-permute-start.8 = (f32[128,768]{1,0:T(8,128)}, f32[128,768]{1,0:T(8,128)}, u32[]{:S(2)}, u32[]{:S(2)}) collective-permute-start(f32[128,768]{1,0:T(8,128)} %constant_dynamic-slice_fusion), channel_id=1, source_target_pairs={{0,1},{1,0},{2,3},{3,2},{4,5},{5,4},{6,7},{7,6},{8,9},{9,8},{10,11... | collective-permute-start | bytes 1179656 | tf_op jit(solution)/shard_map/ppermute | solution.py:163
  228.7 52.6 %all-to-all-start.5 = ((f32[16,24,3,384]{3,1,2,0:T(8,128)}), f32[16,24,3,384]{3,1,2,0:T(8,128)}, u32[]{:S(2)}, u32[]{:S(2)}) async-start(f32[16,24,3,384]{3,1,2,0:T(8,128)} %bitcast_add_fusion.3), calls=%async_computation.5 | async-start | bytes 3538944 | tf_op jit(solution)/shard_map/all_to_all | solution.py:202
  233.6 255.6 %reduce-scatter.8.cloned.1.call-start = ((), (), s32[]{:S(2)}) async-start(), calls=%async_computation.17 | async-start | bytes 5013504 | tf_op jit(solution)/shard_map/reduce_scatter | solution.py:142
  235.7 19.0 %collective-permute-start.11 = (f32[128,1536]{1,0:T(8,128)}, f32[128,1536]{1,0:T(8,128)}, u32[]{:S(2)}, u32[]{:S(2)}) collective-permute-start(f32[128,1536]{1,0:T(8,128)} %fusion.122), channel_id=1, source_target_pairs={{0,1},{1,0},{2,3},{3,2},{4,5},{5,4},{6,7},{7,6},{8,9},{9,8},{10,11... | collective-permute-start | bytes 2359304 | tf_op jit(solution)/shard_map/ppermute | solution.py:163
  241.0 43.1 %collective-permute-start.22 = (f32[16,24,1536]{2,1,0:T(8,128)}, f32[16,24,1536]{2,1,0:T(8,128)}, u32[]{:S(2)}, u32[]{:S(2)}) collective-permute-start(f32[16,24,1536]{2,1,0:T(8,128)} %dynamic-slice_bitcast_fusion), channel_id=1, source_target_pairs={{0,2},{2,0},{4,6},{6,4},{8,10},{10,8},{12,14},{14,12},{16,18},{18,... | collective-permute-start | bytes 7077896 | tf_op jit(solution)/shard_map/ppermute | solution.py:201
  258.3 29.9 %copy-start.17 = (f32[128,768]{1,0:T(8,128)}, f32[128,768]{1,0:T(8,128)S(1)}, u32[]{:S(2)}) copy-start(f32[128,768]{1,0:T(8,128)S(1)} %get-tuple-element.27) | copy-start | bytes 1179652
  283.6 19.7 %copy-start.48 = (bf16[128,768]{1,0:T(8,128)(2,1)}, bf16[128,768]{1,0:T(8,128)(2,1)S(1)}, u32[]{:S(2)}) copy-start(bf16[128,768]{1,0:T(8,128)(2,1)S(1)} %convert_element_type.190) | copy-start | bytes 589828
  283.6 10.1 %collective-permute-start.12 = (bf16[128,768]{1,0:T(8,128)(2,1)S(1)}, bf16[128,768]{1,0:T(8,128)(2,1)S(1)}, u32[]{:S(2)}, u32[]{:S(2)}) collective-permute-start(bf16[128,768]{1,0:T(8,128)(2,1)S(1)} %convert_element_type.190), channel_id=1, source_target_pairs={{0,1},{1,0},{2,3},{3,2},{4,5},{5,4},{6,7},{7,6},{8,9},{9,8},{10,11... | collective-permute-start | bytes 589832 | tf_op jit(solution)/shard_map/ppermute | solution.py:163
  288.2 80.8 %all-to-all-start.9 = ((f32[16,24,1536]{2,1,0:T(8,128)}), f32[16,24,1536]{2,1,0:T(8,128)}, u32[]{:S(2)}, u32[]{:S(2)}) async-start(f32[16,24,1536]{2,1,0:T(8,128)} %bitcast_add_fusion), calls=%async_computation.12 | async-start | bytes 4718592 | tf_op jit(solution)/shard_map/all_to_all | solution.py:202
  302.5 16.0 %collective-permute-start.14 = (f32[16,24,384]{2,1,0:T(8,128)}, f32[16,24,384]{2,1,0:T(8,128)}, u32[]{:S(2)}, u32[]{:S(2)}) collective-permute-start(f32[16,24,384]{2,1,0:T(8,128)} %dynamic-slice_bitcast_fusion.4), channel_id=1, source_target_pairs={{0,2},{2,0},{4,6},{6,4},{8,10},{10,8},{12,14},{14,12},{16,18},{18,... | collective-permute-start | bytes 1769480 | tf_op jit(solution)/shard_map/ppermute | solution.py:201
  311.9 19.1 %collective-permute-start.15 = (f32[128,1536]{1,0:T(8,128)}, f32[128,1536]{1,0:T(8,128)}, u32[]{:S(2)}, u32[]{:S(2)}) collective-permute-start(f32[128,1536]{1,0:T(8,128)} %fusion.119), channel_id=1, source_target_pairs={{0,1},{1,0},{2,3},{3,2},{4,5},{5,4},{6,7},{7,6},{8,9},{9,8},{10,11... | collective-permute-start | bytes 2359304 | tf_op jit(solution)/shard_map/ppermute | solution.py:163
  317.8 13.2 %copy-start.29 = (f32[256,768]{1,0:T(8,128)S(1)}, f32[256,768]{1,0:T(8,128)}, u32[]{:S(2)}) copy-start(f32[256,768]{1,0:T(8,128)} %copy-done.28) | copy-start | bytes 2359300
  317.8 13.2 %copy-start.31 = (f32[256,768]{1,0:T(8,128)S(1)}, f32[256,768]{1,0:T(8,128)}, u32[]{:S(2)}) copy-start(f32[256,768]{1,0:T(8,128)} %copy-done.30) | copy-start | bytes 2359300
  317.8 81.0 %collective-permute-start.13 = (f32[16,24,3,384]{3,1,2,0:T(8,128)}, f32[16,24,3,384]{3,1,2,0:T(8,128)}, u32[]{:S(2)}, u32[]{:S(2)}) collective-permute-start(f32[16,24,3,384]{3,1,2,0:T(8,128)} %dynamic-slice_bitcast_fusion.2), channel_id=1, source_target_pairs={{0,2},{2,0},{4,6},{6,4},{8,10},{10,8},{12,14},{14,12},{16,18},{18,... | collective-permute-start | bytes 5308424 | tf_op jit(solution)/shard_map/ppermute | solution.py:201
  320.5 11.8 %copy-start.8 = (bf16[128,768]{1,0:T(8,128)(2,1)S(1)}, bf16[128,768]{1,0:T(8,128)(2,1)}, u32[]{:S(2)}) copy-start(bf16[128,768]{1,0:T(8,128)(2,1)} %param.15) | copy-start | bytes 589828
  320.5 11.8 %copy-start.120 = (f32[768]{0:T(1024)S(1)}, f32[768]{0:T(1024)}, u32[]{:S(2)}) copy-start(f32[768]{0:T(1024)} %copy-done.119) | copy-start | bytes 9220
  320.5 11.8 %copy-start.122 = (f32[768]{0:T(1024)S(1)}, f32[768]{0:T(1024)}, u32[]{:S(2)}) copy-start(f32[768]{0:T(1024)} %copy-done.121) | copy-start | bytes 9220
  320.5 11.8 %copy-start.138 = (f32[128]{0:T(128)S(1)}, f32[128]{0:T(128)}, u32[]{:S(2)}) copy-start(f32[128]{0:T(128)} %copy-done.137) | copy-start | bytes 1540
  320.5 11.8 %copy-start.145 = (f32[128]{0:T(128)S(1)}, f32[128]{0:T(128)}, u32[]{:S(2)}) copy-start(f32[128]{0:T(128)} %copy-done.144) | copy-start | bytes 1540
  320.5 12.7 %copy-start.18 = (f32[128,768]{1,0:T(8,128)S(1)}, f32[128,768]{1,0:T(8,128)}, u32[]{:S(2)}) copy-start(f32[128,768]{1,0:T(8,128)} %copy-done.17) | copy-start | bytes 1179652
  369.0 32.8 %all-to-all-start.7 = ((f32[16,24,384]{2,1,0:T(8,128)}), f32[16,24,384]{2,1,0:T(8,128)}, u32[]{:S(2)}, u32[]{:S(2)}) async-start(f32[16,24,384]{2,1,0:T(8,128)} %bitcast_add_fusion.4), calls=%async_computation.7 | async-start | bytes 1179648 | tf_op jit(solution)/shard_map/all_to_all | solution.py:202
  373.6 117.7 %reduce-scatter.6.cloned.1.call-start = ((), (), s32[]{:S(2)}) async-start(), calls=%async_computation.16 | async-start | bytes 5013504 | tf_op jit(solution)/shard_map/reduce_scatter | solution.py:142
  376.4 1.5 collective-permute-start.16
  378.8 5.8 collective-permute-start.17
  384.6 3.8 collective-permute-start.18
  389.0 7.4 collective-permute-start.19
  398.0 11.2 %collective-permute-start.20 = (f32[19968]{0:T(1024)}, f32[19968]{0:T(1024)}, u32[]{:S(2)}, u32[]{:S(2)}) collective-permute-start(f32[19968]{0:T(1024)} %add.473), channel_id=1, source_target_pairs={{0,1},{1,0},{2,3},{3,2},{4,5},{5,4},{6,7},{7,6},{8,9},{9,8},{10,11... | collective-permute-start | bytes 239624 | tf_op jit(solution)/shard_map/ppermute | solution.py:159
  401.8 65.9 %all-to-all-start.6 = ((f32[16,24,3,384]{3,1,2,0:T(8,128)}), f32[16,24,3,384]{3,1,2,0:T(8,128)S(1)}, u32[]{:S(2)}, u32[]{:S(2)}) async-start(f32[16,24,3,384]{3,1,2,0:T(8,128)} %bitcast_add_fusion.2), calls=%async_computation.6 | async-start | bytes 3538944 | tf_op jit(solution)/shard_map/all_to_all | solution.py:202
  410.9 5.6 collective-permute-start.21
  468.9 64.7 %all-to-all-start.8 = ((f32[16,24,1536]{2,1,0:T(8,128)}), f32[16,24,1536]{2,1,0:T(8,128)S(1)}, u32[]{:S(2)}, u32[]{:S(2)}) async-start(f32[16,24,1536]{2,1,0:T(8,128)} %bitcast_add_fusion.1), calls=%async_computation.11 | async-start | bytes 4718592 | tf_op jit(solution)/shard_map/all_to_all | solution.py:202
  608.7 4.9 collective-permute-start.23
  615.3 28.7 %copy-start.76 = (f32[19968]{0:T(1024)S(1)}, f32[19968]{0:T(1024)}, u32[]{:S(2)}) copy-start(f32[19968]{0:T(1024)} %add.474) | copy-start | bytes 239620
  615.4 27.5 %collective-permute-start.24 = (f32[384,768]{1,0:T(8,128)S(1)}, f32[384,768]{1,0:T(8,128)S(1)}, u32[]{:S(2)}, u32[]{:S(2)}) collective-permute-start(f32[384,768]{1,0:T(8,128)S(1)} %dynamic-slice_add_fusion), channel_id=1, source_target_pairs={{0,1},{1,0},{2,3},{3,2},{4,5},{5,4},{6,7},{7,6},{8,9},{9,8},{10,11... | collective-permute-start | bytes 3538952 | tf_op jit(solution)/shard_map/ppermute | solution.py:453
  643.0 5.3 collective-permute-start.25
  718.3 32.9 %all-to-all-start.11 = ((bf16[16,48,768]{2,1,0:T(8,128)(2,1)}), bf16[16,48,768]{2,1,0:T(8,128)(2,1)S(1)}, u32[]{:S(2)}, u32[]{:S(2)}) async-start(bf16[16,48,768]{2,1,0:T(8,128)(2,1)} %bitcast.138), calls=%async_computation.14 | async-start | bytes 2359296 | tf_op jit(solution)/shard_map/all_to_all | solution.py:479
  724.1 28.2 %copy-start.88 = (f32[2,2,768]{2,1,0:T(2,128)}, f32[2,2,768]{2,1,0:T(2,128)S(1)}, u32[]{:S(2)}) copy-start(f32[2,2,768]{2,1,0:T(2,128)S(1)} %slice.412) | copy-start | bytes 36868
  724.7 27.5 %copy-start.79 = (f32[2,3072]{1,0:T(2,128)}, f32[2,3072]{1,0:T(2,128)S(1)}, u32[]{:S(2)}) copy-start(f32[2,3072]{1,0:T(2,128)S(1)} %reshape.583) | copy-start | bytes 73732
  724.8 27.5 %copy-start.80 = (f32[2,4,768]{2,1,0:T(4,128)}, f32[2,4,768]{2,1,0:T(4,128)S(1)}, u32[]{:S(2)}) copy-start(f32[2,4,768]{2,1,0:T(4,128)S(1)} %reshape.581) | copy-start | bytes 73732
  (131 other events, 432.7 us)
Sparse Core Ops, SparseCore 0:
  10.9 45.8 all-gather.6
  59.6 48.0 all-gather.8
  110.6 54.3 all-gather.10
  208.4 67.5 reduce-scatter.3
  279.7 96.5 reduce-scatter.7
  396.5 94.7 reduce-scatter.5

commit v14 on v13

--- a/solution.py
+++ b/solution.py
@@ -447,15 +447,23 @@
     while bit < sub:
         gram = gram + lax.ppermute(gram, "dp", swap_pairs(dp_count, bit))
         bit *= 2
-    core_half = dp_rank % 2
-    half_rows = gram.shape[0] // 2
-    mine = lax.dynamic_slice_in_dim(gram, core_half * half_rows, half_rows, 0)
+    first_core = dp_rank % 2 == 0
+    half = gram.shape[0] // 2
+    quarter = half // 2
+    upper_part = gram[:half, : half + quarter]
+    lower_part = jnp.concatenate([gram[:half, half + quarter :], gram[half:, half:]], axis=1)
+    mine = jnp.where(first_core, upper_part, lower_part)
     mine = mine + lax.ppermute(mine, "tensor", [(0, 1), (1, 0)])
     other = lax.ppermute(mine, "dp", swap_pairs(dp_count, 1))
-    gram = jnp.where(
-        core_half == 0,
-        jnp.concatenate([mine, other], axis=0),
-        jnp.concatenate([other, mine], axis=0),
+    upper_sum = jnp.where(first_core, mine, other)
+    lower_sum = jnp.where(first_core, other, mine)
+    corner = jnp.concatenate([upper_sum[:, half:], lower_sum[:, :quarter]], axis=1)
+    gram = jnp.concatenate(
+        [
+            jnp.concatenate([upper_sum[:, :half], corner], axis=1),
+            jnp.concatenate([corner.T, lower_sum[:, quarter:]], axis=1),
+        ],
+        axis=0,
     )
     norm_sq = jnp.trace(gram)
     scale = 1.0 / (jnp.sqrt(norm_sq) + frobenius_eps)

time: 774 us -> 784 us (1.013)
  matrix products: 131 us -> 142 us
    dot_general x0 -> x4, local copies, waits for them, and re-layouts: none -> 9.45 us  [local(): jnp.dot(polynomial, jnp.dot(current_gram, polynomial, precision=ns_precis...]
    unnamed x312 -> x354, local copies, waits for them, and re-layouts: 26.7 us -> 27.6 us
  transfers between devices with their start and end apart: 42 -> 42, of which waited for: 19 -> 20; matrix products, arithmetic and copies ran while one was open for 25% -> 23% of each run, Pallas kernels for 0% -> 0%
where the time goes in v14:
time: 784 us; the launch traced here: 775 us
  waiting for transfers between devices  294 us (38%)
  matrix products  142 us (18%)
  local copies, waits for them, and re-layouts  95.4 us (12%)
  blocking collectives  76.6 us (10%)
  other arithmetic  74.9 us (10%)
  starting transfers between devices  73.9 us (9%)
  between operations  18.1 us (2%)
    all_to_all x5, waiting for transfers between devices, chip_scatter_rows(): lax.all_to_all(chip_sum, 'dp', split_axis=0, concat_axis=0, tiled=True)  131 us
    all_to_all x4, waiting for transfers between devices, chip_gather_rows(): lax.all_to_all(outgoing, 'dp', split_axis=0, concat_axis=0, tiled=True)  70.8 us
    all_to_all x1, blocking collectives, local(): lax.all_to_all(outgoing, 'dp', split_axis=0, concat_axis=0, tiled=True)  57.5 us
    unnamed x354, local copies, waits for them, and re-layouts  27.6 us
    all_to_all x5, starting transfers between devices, chip_scatter_rows(): lax.all_to_all(chip_sum, 'dp', split_axis=0, concat_axis=0, tiled=True)  27.2 us
    dot_general x5, matrix products, local(): squared = jnp.dot(current_gram, current_gram, precision=ns_precision)  25.1 us
    all_to_all x1, waiting for transfers between devices, local(): lax.all_to_all(current.astype(jnp.bfloat16).reshape(dp_count, rows_local,...  24 us
    ppermute x8, waiting for transfers between devices, tensor_swap(): return lax.ppermute(block, 'tensor', [(0, 1), (1, 0)])  22.3 us
  transfers between devices with their start and end apart: 42, of which 20 were waited for; matrix products, arithmetic and copies ran while one was open for 23% of the time, Pallas kernels for 0%

profile of v14, /device:TPU:11, one launch (start us, length us, event | category | flops | bytes accessed | tf_op | source)
XLA Modules:
  0.0 775.0 jit_solution(9067659841324623583)
XLA Ops:
  11.6 19.1 %all_to_all.60 = bf16[16,24,384]{2,1,0:T(8,128)(2,1)S(1)} all-to-all(bf16[16,24,384]{2,1,0:T(8,128)(2,1)S(1)} %bitcast.420), channel_id=1, replica_groups=mesh['dp'=16,'tensor'=2] {'dp'}, dimensions={0} | all-to-all | bytes 589824 | tf_op jit(solution)/shard_map/all_to_all | solution.py:188
  31.4 4.4 all-to-all-start.3
  38.0 11.7 %all-to-all-done.3 = bf16[16,24,384]{2,1,0:T(8,128)(2,1)} async-done(((bf16[16,24,384]{2,1,0:T(8,128)(2,1)}), bf16[16,24,384]{2,1,0:T(8,128)(2,1)}, u32[]{:S(2)}, u32[]{:S(2)}) %all-to-all-start.3) | async-done | bytes 294944 | tf_op jit(solution)/shard_map/all_to_all | solution.py:188
  50.7 4.5 all-to-all-start
  59.1 21.3 %all-to-all-done = bf16[16,24,3,384]{3,1,2,0:T(8,128)(2,1)S(1)} async-done(((bf16[16,24,3,384]{3,1,2,0:T(8,128)(2,1)}), bf16[16,24,3,384]{3,1,2,0:T(8,128)(2,1)S(1)}, u32[]{:S(2)}, u32[]{:S(2)}) %all-to-all-start) | async-done | bytes 884768 | tf_op jit(solution)/shard_map/all_to_all | solution.py:188
  81.6 4.3 all-to-all-start.2
  92.2 27.9 %all-to-all-done.2 = bf16[16,24,1536]{2,1,0:T(8,128)(2,1)} async-done(((bf16[16,24,1536]{2,1,0:T(8,128)(2,1)}), bf16[16,24,1536]{2,1,0:T(8,128)(2,1)}, u32[]{:S(2)}, u32[]{:S(2)}) %all-to-all-start.2) | async-done | bytes 1179680 | tf_op jit(solution)/shard_map/all_to_all | solution.py:188
  121.3 4.9 all-to-all-start.4
  136.3 4.2 maximum_select_fusion
  140.6 7.1 multiply_convert_fusion.3
  156.3 9.9 %all-to-all-done.4 = bf16[16,24,1536]{2,1,0:T(8,128)(2,1)} async-done(((bf16[16,24,1536]{2,1,0:T(8,128)(2,1)}), bf16[16,24,1536]{2,1,0:T(8,128)(2,1)}, u32[]{:S(2)}, u32[]{:S(2)}) %all-to-all-start.4) | async-done | bytes 1179680 | tf_op jit(solution)/shard_map/all_to_all | solution.py:188
  171.5 3.4 maximum_select_fusion.1
  175.0 5.1 collective-permute-done.5
  181.2 3.2 fusion.42
  208.7 5.9 multiply_convert_fusion.2
  218.1 2.9 convert_reduce_fusion
  226.2 3.0 bitcast_add_fusion.3
  229.2 4.7 all-to-all-start.5
  241.9 3.0 fusion.100
  248.2 7.0 collective-permute-done.11
  260.8 20.9 %all-to-all-done.5 = f32[16,24,3,384]{3,1,2,0:T(8,128)} async-done(((f32[16,24,3,384]{3,1,2,0:T(8,128)}), f32[16,24,3,384]{3,1,2,0:T(8,128)}, u32[]{:S(2)}, u32[]{:S(2)}) %all-to-all-start.5) | async-done | bytes 1769504 | tf_op jit(solution)/shard_map/all_to_all | solution.py:202
  284.4 4.2 bitcast_add_fusion
  288.5 5.2 all-to-all-start.9
  304.4 2.8 convert_reduce_fusion.1
  320.4 10.2 %collective-permute-done.15 = f32[128,1536]{1,0:T(8,128)} collective-permute-done((f32[128,1536]{1,0:T(8,128)}, f32[128,1536]{1,0:T(8,128)}, u32[]{:S(2)}, u32[]{:S(2)}) %collective-permute-start.15) | collective-permute-done | bytes 786464 | tf_op jit(solution)/shard_map/ppermute | solution.py:163
  341.7 24.3 %all-to-all-done.9 = f32[16,24,1536]{2,1,0:T(8,128)} async-done(((f32[16,24,1536]{2,1,0:T(8,128)}), f32[16,24,1536]{2,1,0:T(8,128)}, u32[]{:S(2)}, u32[]{:S(2)}) %all-to-all-start.9) | async-done | bytes 2359328 | tf_op jit(solution)/shard_map/all_to_all | solution.py:202
  366.0 5.5 all-to-all-start.7
  377.1 5.2 collective-permute-done.17
  382.5 3.6 collective-permute-done.18
  386.7 4.3 collective-permute-start.19
  391.0 4.3 fusion.104
  398.8 2.9 bitcast_add_fusion.2
  401.7 6.5 all-to-all-start.6
  411.3 5.1 collective-permute-done.21
  418.3 49.3 %all-to-all-done.6 = f32[16,24,3,384]{3,1,2,0:T(8,128)S(1)} async-done(((f32[16,24,3,384]{3,1,2,0:T(8,128)}), f32[16,24,3,384]{3,1,2,0:T(8,128)S(1)}, u32[]{:S(2)}, u32[]{:S(2)}) %all-to-all-start.6) | async-done | bytes 1769504 | tf_op jit(solution)/shard_map/all_to_all | solution.py:202
  468.8 5.3 all-to-all-start.8
  486.3 3.6 reduce-scatter.6.cloned.1.call-done
  496.6 36.8 %all-to-all-done.8 = f32[16,24,1536]{2,1,0:T(8,128)S(1)} async-done(((f32[16,24,1536]{2,1,0:T(8,128)}), f32[16,24,1536]{2,1,0:T(8,128)S(1)}, u32[]{:S(2)}, u32[]{:S(2)}) %all-to-all-start.8) | async-done | bytes 2359328 | tf_op jit(solution)/shard_map/all_to_all | solution.py:202
  537.4 6.9 concatenate.143
  545.7 57.5 %all_to_all.61 = f32[16,48,768]{2,1,0:T(8,128)S(1)} all-to-all(f32[16,48,768]{2,1,0:T(8,128)S(1)} %copy.287), channel_id=1, replica_groups=mesh['dp'=16,'tensor'=2] {'dp'}, dimensions={0} | all-to-all | bytes 4718592 | tf_op jit(solution)/shard_map/all_to_all | solution.py:442
  603.2 3.1 fusion.162
  606.4 4.4 collective-permute-done.23
  612.2 20.3 %collective-permute-done.24 = f32[384,576]{0,1:T(8,128)S(1)} collective-permute-done((f32[384,576]{0,1:T(8,128)S(1)}, f32[384,576]{0,1:T(8,128)S(1)}, u32[]{:S(2)}, u32[]{:S(2)}) %collective-permute-start.24) | collective-permute-done | bytes 884768 | tf_op jit(solution)/shard_map/ppermute | solution.py:456
  637.7 3.5 fusion
  641.2 6.0 fusion.17
  647.3 3.5 fusion.163
  652.8 5.6 fusion.1
  658.4 7.3 fusion.171
  665.7 3.6 fusion.164
  669.3 3.5 fusion.165
  674.8 5.4 fusion.2
  680.2 3.1 fusion.166
  683.4 3.5 fusion.167
  689.1 5.4 fusion.3
  694.5 3.1 fusion.168
  697.7 3.7 fusion.169
  702.8 5.1 fusion.170
  707.9 3.2 copy.296
  711.1 5.4 fusion.172
  716.5 3.7 fusion.173
  720.3 3.8 fusion.5
  724.1 4.3 fusion.39
  728.4 5.5 all-to-all-start.11
  737.7 24.0 %all-to-all-done.11 = bf16[16,48,768]{2,1,0:T(8,128)(2,1)S(1)} async-done(((bf16[16,48,768]{2,1,0:T(8,128)(2,1)}), bf16[16,48,768]{2,1,0:T(8,128)(2,1)S(1)}, u32[]{:S(2)}, u32[]{:S(2)}) %all-to-all-start.11) | async-done | bytes 1179680 | tf_op jit(solution)/shard_map/all_to_all | solution.py:487
  (682 shorter events, 194.9 us)
Async XLA Ops:
  7.2 28.7 %copy-start.70 = (bf16[128,768]{1,0:T(8,128)(2,1)S(1)}, bf16[128,768]{1,0:T(8,128)(2,1)}, u32[]{:S(2)}) copy-start(bf16[128,768]{1,0:T(8,128)(2,1)} %param.16) | copy-start | bytes 589828
  7.2 133.4 %all-gather.7.cloned.1.call-start = ((), (), s32[]{:S(2)}) async-start(), calls=%async_computation.18 | async-start | bytes 2506752 | tf_op jit(solution)/shard_map/all_gather | solution.py:146
  9.0 28.2 %copy-start.106 = (f32[2,4,768]{2,1,0:T(4,128)S(1)}, f32[2,4,768]{2,1,0:T(4,128)}, u32[]{:S(2)}) copy-start(f32[2,4,768]{2,1,0:T(4,128)} %param.23) | copy-start | bytes 73732
  9.0 28.9 %copy-start.18 = (bf16[128,768]{1,0:T(8,128)(2,1)S(1)}, bf16[128,768]{1,0:T(8,128)(2,1)}, u32[]{:S(2)}) copy-start(bf16[128,768]{1,0:T(8,128)(2,1)} %param.15) | copy-start | bytes 589828
  9.0 172.2 %all-gather.9.cloned.1.call-start = ((), (), s32[]{:S(2)}) async-start(), calls=%async_computation.19 | async-start | bytes 1880064 | tf_op jit(solution)/shard_map/all_gather | solution.py:146
  31.4 18.2 %all-to-all-start.3 = ((bf16[16,24,384]{2,1,0:T(8,128)(2,1)}), bf16[16,24,384]{2,1,0:T(8,128)(2,1)}, u32[]{:S(2)}, u32[]{:S(2)}) async-start(bf16[16,24,384]{2,1,0:T(8,128)(2,1)} %bitcast.41), calls=%async_computation.3 | async-start | bytes 589824 | tf_op jit(solution)/shard_map/all_to_all | solution.py:188
  35.9 117.4 %collective-permute-start.9 = (bf16[128,768]{1,0:T(8,128)(2,1)S(1)}, bf16[128,768]{1,0:T(8,128)(2,1)}, u32[]{:S(2)}, u32[]{:S(2)}) collective-permute-start(bf16[128,768]{1,0:T(8,128)(2,1)S(1)} %copy-done.70), channel_id=1, source_target_pairs={{0,1},{1,0},{2,3},{3,2},{4,5},{5,4},{6,7},{7,6},{8,9},{9,8},{10,11... | collective-permute-start | bytes 589832 | tf_op jit(solution)/shard_map/ppermute | solution.py:163
  37.2 18.0 %copy-start.130 = (f32[2,2,768]{2,1,0:T(2,128)S(1)}, f32[2,2,768]{2,1,0:T(2,128)}, u32[]{:S(2)}) copy-start(f32[2,2,768]{2,1,0:T(2,128)} %param.22) | copy-start | bytes 36868
  38.0 18.2 %copy-start.160 = (f32[128]{0:T(128)}, f32[128]{0:T(128)S(1)}, u32[]{:S(2)}) copy-start(f32[128]{0:T(128)S(1)} %broadcast_multiply_fusion.5) | copy-start | bytes 1540
  50.7 29.7 %all-to-all-start = ((bf16[16,24,3,384]{3,1,2,0:T(8,128)(2,1)}), bf16[16,24,3,384]{3,1,2,0:T(8,128)(2,1)S(1)}, u32[]{:S(2)}, u32[]{:S(2)}) async-start(bf16[16,24,3,384]{3,1,2,0:T(8,128)(2,1)} %bitcast.2), calls=%async_computation | async-start | bytes 1769472 | tf_op jit(solution)/shard_map/all_to_all | solution.py:188
  55.2 153.5 %all-gather.11.cloned.1.call-start = ((), (), s32[]{:S(2)}) async-start(), calls=%async_computation.20 | async-start | bytes 2506752 | tf_op jit(solution)/shard_map/all_gather | solution.py:146
  56.0 25.6 %copy-start.165 = (f32[128]{0:T(128)}, f32[128]{0:T(128)S(1)}, u32[]{:S(2)}) copy-start(f32[128]{0:T(128)S(1)} %add_rsqrt_fusion.1) | copy-start | bytes 1540
  57.0 32.4 %collective-permute-start = (bf16[128,1536]{1,0:T(8,128)(2,1)}, bf16[128,1536]{1,0:T(8,128)(2,1)}, u32[]{:S(2)}, u32[]{:S(2)}) collective-permute-start(bf16[128,1536]{1,0:T(8,128)(2,1)} %pad_maximum_fusion.8), channel_id=1, source_target_pairs={{0,1},{1,0},{2,3},{3,2},{4,5},{5,4},{6,7},{7,6},{8,9},{9,8},{10,11... | collective-permute-start | bytes 1179656 | tf_op jit(solution)/shard_map/ppermute | solution.py:163
  81.6 38.5 %all-to-all-start.2 = ((bf16[16,24,1536]{2,1,0:T(8,128)(2,1)}), bf16[16,24,1536]{2,1,0:T(8,128)(2,1)}, u32[]{:S(2)}, u32[]{:S(2)}) async-start(bf16[16,24,1536]{2,1,0:T(8,128)(2,1)} %bitcast.26), calls=%async_computation.2 | async-start | bytes 2359296 | tf_op jit(solution)/shard_map/all_to_all | solution.py:188
  86.1 40.5 %collective-permute-start.1 = (bf16[16,24,3,384]{3,1,0,2:T(8,128)(2,1)S(1)}, bf16[16,24,3,384]{3,1,0,2:T(8,128)(2,1)}, u32[]{:S(2)}, u32[]{:S(2)}) collective-permute-start(bf16[16,24,3,384]{3,1,0,2:T(8,128)(2,1)S(1)} %copy.344), channel_id=1, source_target_pairs={{0,2},{2,0},{4,6},{6,4},{8,10},{10,8},{12,14},{14,12},{16,18},{18,... | collective-permute-start | bytes 2654216 | tf_op jit(solution)/shard_map/ppermute | solution.py:189
  87.5 3.8 collective-permute-start.2
  90.8 37.7 %copy-start.24 = (bf16[256,1536]{1,0:T(8,128)(2,1)}, bf16[256,1536]{1,0:T(8,128)(2,1)S(1)}, u32[]{:S(2)}) copy-start(bf16[256,1536]{1,0:T(8,128)(2,1)S(1)} %maximum_select_fusion.3) | copy-start | bytes 2359300
  90.8 61.1 %collective-permute-start.6 = (bf16[16,24,384]{2,1,0:T(8,128)(2,1)}, bf16[16,24,384]{2,1,0:T(8,128)(2,1)}, u32[]{:S(2)}, u32[]{:S(2)}) collective-permute-start(bf16[16,24,384]{2,1,0:T(8,128)(2,1)} %all-to-all-done.3), channel_id=1, source_target_pairs={{0,2},{2,0},{4,6},{6,4},{8,10},{10,8},{12,14},{14,12},{16,18},{18,... | collective-permute-start | bytes 884744 | tf_op jit(solution)/shard_map/ppermute | solution.py:189
  121.3 45.0 %all-to-all-start.4 = ((bf16[16,24,1536]{2,1,0:T(8,128)(2,1)}), bf16[16,24,1536]{2,1,0:T(8,128)(2,1)}, u32[]{:S(2)}, u32[]{:S(2)}) async-start(bf16[16,24,1536]{2,1,0:T(8,128)(2,1)} %bitcast.49), calls=%async_computation.4 | async-start | bytes 2359296 | tf_op jit(solution)/shard_map/all_to_all | solution.py:188
  126.2 351.6 %reduce-scatter.4.cloned.1.call-start = ((), (), s32[]{:S(2)}) async-start(), calls=%async_computation.15 | async-start | bytes 1253376 | tf_op jit(solution)/shard_map/reduce_scatter | solution.py:142
  126.2 10.1 %collective-permute-start.3 = (bf16[16,24,1536]{2,1,0:T(8,128)(2,1)}, bf16[16,24,1536]{2,1,0:T(8,128)(2,1)}, u32[]{:S(2)}, u32[]{:S(2)}) collective-permute-start(bf16[16,24,1536]{2,1,0:T(8,128)(2,1)} %all-to-all-done.2), channel_id=1, source_target_pairs={{0,2},{2,0},{4,6},{6,4},{8,10},{10,8},{12,14},{14,12},{16,18},{18,... | collective-permute-start | bytes 3538952 | tf_op jit(solution)/shard_map/ppermute | solution.py:189
  149.6 17.0 %collective-permute-start.4 = (f32[128,768]{1,0:T(8,128)}, f32[128,768]{1,0:T(8,128)S(1)}, u32[]{:S(2)}, u32[]{:S(2)}) collective-permute-start(f32[128,768]{1,0:T(8,128)} %constant_dynamic-slice_fusion.3), channel_id=1, source_target_pairs={{0,1},{1,0},{2,3},{3,2},{4,5},{5,4},{6,7},{7,6},{8,9},{9,8},{10,11... | collective-permute-start | bytes 1179656 | tf_op jit(solution)/shard_map/ppermute | solution.py:163
  153.3 14.1 %copy-start.35 = (f32[256,768]{1,0:T(8,128)S(1)}, f32[256,768]{1,0:T(8,128)}, u32[]{:S(2)}) copy-start(f32[256,768]{1,0:T(8,128)} %copy-done.34) | copy-start | bytes 2359300
  153.3 14.1 %copy-start.157 = (f32[768]{0:T(1024)S(1)}, f32[768]{0:T(1024)}, u32[]{:S(2)}) copy-start(f32[768]{0:T(1024)} %get-tuple-element.171) | copy-start | bytes 9220
  153.3 14.1 %copy-start.158 = (f32[768]{0:T(1024)S(1)}, f32[768]{0:T(1024)}, u32[]{:S(2)}) copy-start(f32[768]{0:T(1024)} %get-tuple-element.172) | copy-start | bytes 9220
  155.5 13.4 %copy-start.140 = (f32[768]{0:T(1024)S(1)}, f32[768]{0:T(1024)}, u32[]{:S(2)}) copy-start(f32[768]{0:T(1024)} %get-tuple-element.176) | copy-start | bytes 9220
  155.5 13.4 %copy-start.142 = (f32[768]{0:T(1024)S(1)}, f32[768]{0:T(1024)}, u32[]{:S(2)}) copy-start(f32[768]{0:T(1024)} %get-tuple-element.179) | copy-start | bytes 9220
  155.5 13.4 %copy-start.155 = (f32[768]{0:T(1024)S(1)}, f32[768]{0:T(1024)}, u32[]{:S(2)}) copy-start(f32[768]{0:T(1024)} %get-tuple-element.169) | copy-start | bytes 9220
  155.5 13.4 %copy-start.156 = (f32[768]{0:T(1024)S(1)}, f32[768]{0:T(1024)}, u32[]{:S(2)}) copy-start(f32[768]{0:T(1024)} %get-tuple-element.170) | copy-start | bytes 9220
  166.3 5.3 collective-permute-start.7
  169.4 10.6 %collective-permute-start.5 = (bf16[128,1536]{1,0:T(8,128)(2,1)S(1)}, bf16[128,1536]{1,0:T(8,128)(2,1)S(1)}, u32[]{:S(2)}, u32[]{:S(2)}) collective-permute-start(bf16[128,1536]{1,0:T(8,128)(2,1)S(1)} %pad_maximum_fusion.9), channel_id=1, source_target_pairs={{0,1},{1,0},{2,3},{3,2},{4,5},{5,4},{6,7},{7,6},{8,9},{9,8},{10,11... | collective-permute-start | bytes 1179656 | tf_op jit(solution)/shard_map/ppermute | solution.py:163
  203.1 22.4 %collective-permute-start.10 = (f32[16,24,3,384]{3,1,2,0:T(8,128)}, f32[16,24,3,384]{3,1,2,0:T(8,128)}, u32[]{:S(2)}, u32[]{:S(2)}) collective-permute-start(f32[16,24,3,384]{3,1,2,0:T(8,128)} %dynamic-slice_bitcast_fusion.3), channel_id=1, source_target_pairs={{0,2},{2,0},{4,6},{6,4},{8,10},{10,8},{12,14},{14,12},{16,18},{18,... | collective-permute-start | bytes 5308424 | tf_op jit(solution)/shard_map/ppermute | solution.py:201
  216.7 40.1 %collective-permute-start.8 = (f32[128,768]{1,0:T(8,128)}, f32[128,768]{1,0:T(8,128)}, u32[]{:S(2)}, u32[]{:S(2)}) collective-permute-start(f32[128,768]{1,0:T(8,128)} %constant_dynamic-slice_fusion), channel_id=1, source_target_pairs={{0,1},{1,0},{2,3},{3,2},{4,5},{5,4},{6,7},{7,6},{8,9},{9,8},{10,11... | collective-permute-start | bytes 1179656 | tf_op jit(solution)/shard_map/ppermute | solution.py:163
  229.2 52.5 %all-to-all-start.5 = ((f32[16,24,3,384]{3,1,2,0:T(8,128)}), f32[16,24,3,384]{3,1,2,0:T(8,128)}, u32[]{:S(2)}, u32[]{:S(2)}) async-start(f32[16,24,3,384]{3,1,2,0:T(8,128)} %bitcast_add_fusion.3), calls=%async_computation.5 | async-start | bytes 3538944 | tf_op jit(solution)/shard_map/all_to_all | solution.py:202
  233.9 252.4 %reduce-scatter.8.cloned.1.call-start = ((), (), s32[]{:S(2)}) async-start(), calls=%async_computation.17 | async-start | bytes 5013504 | tf_op jit(solution)/shard_map/reduce_scatter | solution.py:142
  236.1 19.0 %collective-permute-start.11 = (f32[128,1536]{1,0:T(8,128)}, f32[128,1536]{1,0:T(8,128)}, u32[]{:S(2)}, u32[]{:S(2)}) collective-permute-start(f32[128,1536]{1,0:T(8,128)} %fusion.68), channel_id=1, source_target_pairs={{0,1},{1,0},{2,3},{3,2},{4,5},{5,4},{6,7},{7,6},{8,9},{9,8},{10,11... | collective-permute-start | bytes 2359304 | tf_op jit(solution)/shard_map/ppermute | solution.py:163
  241.2 43.2 %collective-permute-start.22 = (f32[16,24,1536]{2,1,0:T(8,128)}, f32[16,24,1536]{2,1,0:T(8,128)}, u32[]{:S(2)}, u32[]{:S(2)}) collective-permute-start(f32[16,24,1536]{2,1,0:T(8,128)} %dynamic-slice_bitcast_fusion), channel_id=1, source_target_pairs={{0,2},{2,0},{4,6},{6,4},{8,10},{10,8},{12,14},{14,12},{16,18},{18,... | collective-permute-start | bytes 7077896 | tf_op jit(solution)/shard_map/ppermute | solution.py:201
  259.5 29.1 %copy-start.28 = (f32[128,768]{1,0:T(8,128)}, f32[128,768]{1,0:T(8,128)S(1)}, u32[]{:S(2)}) copy-start(f32[128,768]{1,0:T(8,128)S(1)} %get-tuple-element.27) | copy-start | bytes 1179652
  283.9 20.1 %copy-start.58 = (bf16[128,768]{1,0:T(8,128)(2,1)}, bf16[128,768]{1,0:T(8,128)(2,1)S(1)}, u32[]{:S(2)}) copy-start(bf16[128,768]{1,0:T(8,128)(2,1)S(1)} %convert_element_type.190) | copy-start | bytes 589828
  284.0 9.8 %collective-permute-start.12 = (bf16[128,768]{1,0:T(8,128)(2,1)S(1)}, bf16[128,768]{1,0:T(8,128)(2,1)S(1)}, u32[]{:S(2)}, u32[]{:S(2)}) collective-permute-start(bf16[128,768]{1,0:T(8,128)(2,1)S(1)} %convert_element_type.190), channel_id=1, source_target_pairs={{0,1},{1,0},{2,3},{3,2},{4,5},{5,4},{6,7},{7,6},{8,9},{9,8},{10,11... | collective-permute-start | bytes 589832 | tf_op jit(solution)/shard_map/ppermute | solution.py:163
  288.5 77.5 %all-to-all-start.9 = ((f32[16,24,1536]{2,1,0:T(8,128)}), f32[16,24,1536]{2,1,0:T(8,128)}, u32[]{:S(2)}, u32[]{:S(2)}) async-start(f32[16,24,1536]{2,1,0:T(8,128)} %bitcast_add_fusion), calls=%async_computation.12 | async-start | bytes 4718592 | tf_op jit(solution)/shard_map/all_to_all | solution.py:202
  302.6 15.9 %collective-permute-start.14 = (f32[16,24,384]{2,1,0:T(8,128)}, f32[16,24,384]{2,1,0:T(8,128)}, u32[]{:S(2)}, u32[]{:S(2)}) collective-permute-start(f32[16,24,384]{2,1,0:T(8,128)} %dynamic-slice_bitcast_fusion.4), channel_id=1, source_target_pairs={{0,2},{2,0},{4,6},{6,4},{8,10},{10,8},{12,14},{14,12},{16,18},{18,... | collective-permute-start | bytes 1769480 | tf_op jit(solution)/shard_map/ppermute | solution.py:201
  311.6 19.0 %collective-permute-start.15 = (f32[128,1536]{1,0:T(8,128)}, f32[128,1536]{1,0:T(8,128)}, u32[]{:S(2)}, u32[]{:S(2)}) collective-permute-start(f32[128,1536]{1,0:T(8,128)} %fusion.65), channel_id=1, source_target_pairs={{0,1},{1,0},{2,3},{3,2},{4,5},{5,4},{6,7},{7,6},{8,9},{9,8},{10,11... | collective-permute-start | bytes 2359304 | tf_op jit(solution)/shard_map/ppermute | solution.py:163
  317.8 81.0 %collective-permute-start.13 = (f32[16,24,3,384]{3,1,2,0:T(8,128)}, f32[16,24,3,384]{3,1,2,0:T(8,128)}, u32[]{:S(2)}, u32[]{:S(2)}) collective-permute-start(f32[16,24,3,384]{3,1,2,0:T(8,128)} %dynamic-slice_bitcast_fusion.2), channel_id=1, source_target_pairs={{0,2},{2,0},{4,6},{6,4},{8,10},{10,8},{12,14},{14,12},{16,18},{18,... | collective-permute-start | bytes 5308424 | tf_op jit(solution)/shard_map/ppermute | solution.py:201
  366.0 35.7 %all-to-all-start.7 = ((f32[16,24,384]{2,1,0:T(8,128)}), f32[16,24,384]{2,1,0:T(8,128)}, u32[]{:S(2)}, u32[]{:S(2)}) async-start(f32[16,24,384]{2,1,0:T(8,128)} %bitcast_add_fusion.4), calls=%async_computation.7 | async-start | bytes 1179648 | tf_op jit(solution)/shard_map/all_to_all | solution.py:202
  371.5 118.3 %reduce-scatter.6.cloned.1.call-start = ((), (), s32[]{:S(2)}) async-start(), calls=%async_computation.16 | async-start | bytes 5013504 | tf_op jit(solution)/shard_map/reduce_scatter | solution.py:142
  374.3 1.5 collective-permute-start.16
  376.7 5.6 collective-permute-start.17
  382.3 3.8 collective-permute-start.18
  386.7 8.7 %collective-permute-start.19 = (f32[19968]{0:T(1024)}, f32[19968]{0:T(1024)}, u32[]{:S(2)}, u32[]{:S(2)}) collective-permute-start(f32[19968]{0:T(1024)} %add.469), channel_id=1, source_target_pairs={{0,16},{2,18},{4,20},{6,22},{8,24},{10,26},{12,28},{14,30},{16,0},... | collective-permute-start | bytes 239624 | tf_op jit(solution)/shard_map/ppermute | solution.py:157
  396.9 12.2 %collective-permute-start.20 = (f32[19968]{0:T(1024)}, f32[19968]{0:T(1024)}, u32[]{:S(2)}, u32[]{:S(2)}) collective-permute-start(f32[19968]{0:T(1024)} %add.470), channel_id=1, source_target_pairs={{0,1},{1,0},{2,3},{3,2},{4,5},{5,4},{6,7},{7,6},{8,9},{9,8},{10,11... | collective-permute-start | bytes 239624 | tf_op jit(solution)/shard_map/ppermute | solution.py:159
  401.7 65.9 %all-to-all-start.6 = ((f32[16,24,3,384]{3,1,2,0:T(8,128)}), f32[16,24,3,384]{3,1,2,0:T(8,128)S(1)}, u32[]{:S(2)}, u32[]{:S(2)}) async-start(f32[16,24,3,384]{3,1,2,0:T(8,128)} %bitcast_add_fusion.2), calls=%async_computation.6 | async-start | bytes 3538944 | tf_op jit(solution)/shard_map/all_to_all | solution.py:202
  410.8 5.6 collective-permute-start.21
  468.8 64.6 %all-to-all-start.8 = ((f32[16,24,1536]{2,1,0:T(8,128)}), f32[16,24,1536]{2,1,0:T(8,128)S(1)}, u32[]{:S(2)}, u32[]{:S(2)}) async-start(f32[16,24,1536]{2,1,0:T(8,128)} %bitcast_add_fusion.1), calls=%async_computation.11 | async-start | bytes 4718592 | tf_op jit(solution)/shard_map/all_to_all | solution.py:202
  492.0 41.6 %copy-start.46 = (f32[2,48,1536]{2,1,0:T(8,128)}, f32[2,48,1536]{2,1,0:T(8,128)S(1)}, u32[]{:S(2)}) copy-start(f32[2,48,1536]{2,1,0:T(8,128)S(1)} %get-tuple-element.183) | copy-start | bytes 1769476
  606.3 4.6 collective-permute-start.23
  611.4 22.3 %slice-start = ((f32[19968]{0:T(1024)}), f32[4608]{0:T(1024)S(1)}, s32[]{:S(2)}) async-start(f32[19968]{0:T(1024)} %add.471), calls=%async_computation.21 | async-start | bytes 40960 | tf_op jit(solution)/shard_map/slice | solution.py:411
  611.4 22.4 %copy-start.127 = (f32[2,3,768]{2,0,1:T(2,128)S(1)}, f32[2,3,768]{2,0,1:T(2,128)}, u32[]{:S(2)}) copy-start(f32[2,3,768]{2,0,1:T(2,128)} %param.24) | copy-start | bytes 55300
  611.4 21.1 %collective-permute-start.24 = (f32[384,576]{0,1:T(8,128)S(1)}, f32[384,576]{0,1:T(8,128)S(1)}, u32[]{:S(2)}, u32[]{:S(2)}) collective-permute-start(f32[384,576]{0,1:T(8,128)S(1)} %slice_select_fusion), channel_id=1, source_target_pairs={{0,1},{1,0},{2,3},{3,2},{4,5},{5,4},{6,7},{7,6},{8,9},{9,8},{10,11... | collective-permute-start | bytes 2654216 | tf_op jit(solution)/shard_map/ppermute | solution.py:456
  632.6 3.1 collective-permute-start.25
  728.4 33.3 %all-to-all-start.11 = ((bf16[16,48,768]{2,1,0:T(8,128)(2,1)}), bf16[16,48,768]{2,1,0:T(8,128)(2,1)S(1)}, u32[]{:S(2)}, u32[]{:S(2)}) async-start(bf16[16,48,768]{2,1,0:T(8,128)(2,1)} %bitcast.139), calls=%async_computation.14 | async-start | bytes 2359296 | tf_op jit(solution)/shard_map/all_to_all | solution.py:487
  734.5 28.1 %copy-start.105 = (f32[2,2,768]{2,1,0:T(2,128)}, f32[2,2,768]{2,1,0:T(2,128)S(1)}, u32[]{:S(2)}) copy-start(f32[2,2,768]{2,1,0:T(2,128)S(1)} %slice.432) | copy-start | bytes 36868
  735.2 27.6 %copy-start.96 = (f32[2,3072]{1,0:T(2,128)}, f32[2,3072]{1,0:T(2,128)S(1)}, u32[]{:S(2)}) copy-start(f32[2,3072]{1,0:T(2,128)S(1)} %reshape.583) | copy-start | bytes 73732
  735.2 27.5 %copy-start.97 = (f32[2,4,768]{2,1,0:T(4,128)}, f32[2,4,768]{2,1,0:T(4,128)S(1)}, u32[]{:S(2)}) copy-start(f32[2,4,768]{2,1,0:T(4,128)S(1)} %reshape.581) | copy-start | bytes 73732
  (153 other events, 518.1 us)
Sparse Core Ops, SparseCore 0:
  10.9 45.8 all-gather.6
  59.7 48.8 all-gather.8
  111.4 54.0 all-gather.10
  208.8 71.8 reduce-scatter.3
  284.3 93.6 reduce-scatter.7
  395.5 94.3 reduce-scatter.5

commit v15 on v13

--- a/solution.py
+++ b/solution.py
@@ -249,13 +249,17 @@
     stream = block_input.astype(jnp.float32)
     saved_layers = []
     for layer_id in range(LAYERS):
+        down_full = chip_gather_rows(down_weight[layer_id].T)
+        proj_block = proj_weight[layer_id].T
+        if layer_id == LAYERS - 1:
+            proj_block, down_full = lax.optimization_barrier((proj_block, down_full))
         layer_weights = (
             dp_gather(qkv_weight[layer_id], 0)
             if layer_id == LAYERS - 1
             else chip_gather_rows(qkv_weight[layer_id]),
-            chip_gather_rows(proj_weight[layer_id].T),
+            chip_gather_rows(proj_block),
             dp_gather(up_weight[layer_id], 0),
-            chip_gather_rows(down_weight[layer_id].T),
+            down_full,
         )
         qkv_full, proj_full, up_full, down_full = layer_weights
         normed, inverse = normalize(stream)

time: 774 us -> 795 us (1.027)
  waiting for transfers between devices: 293 us -> 322 us
  blocking collectives: 76.7 us -> 57.6 us
  starting transfers between devices: 71.2 us -> 81.7 us
    all_to_all x4 -> x5, waiting for transfers between devices: 65.3 us -> 91.6 us  [chip_gather_rows(): lax.all_to_all(outgoing, 'dp', split_axis=0, concat_axis=0, tiled=True)]
    all_to_all x1 -> x0, blocking collectives: 19.1 us -> none  [chip_gather_rows(): lax.all_to_all(outgoing, 'dp', split_axis=0, concat_axis=0, tiled=True)]
    all_to_all x4 -> x5, starting transfers between devices: 18 us -> 24.7 us  [chip_gather_rows(): lax.all_to_all(outgoing, 'dp', split_axis=0, concat_axis=0, tiled=True)]
    unnamed x312 -> x322, local copies, waits for them, and re-layouts: 26.7 us -> 26.4 us
  transfers between devices with their start and end apart: 42 -> 43, of which waited for: 19 -> 21; matrix products, arithmetic and copies ran while one was open for 25% -> 24% of each run, Pallas kernels for 0% -> 0%
where the time goes in v15:
time: 795 us; the launch traced here: 783 us
  waiting for transfers between devices  322 us (41%)
  matrix products  131 us (16%)
  local copies, waits for them, and re-layouts  90.5 us (11%)
  other arithmetic  82.4 us (10%)
  starting transfers between devices  81.7 us (10%)
  blocking collectives  57.6 us (7%)
  between operations  17.6 us (2%)
    all_to_all x5, waiting for transfers between devices, chip_scatter_rows(): lax.all_to_all(chip_sum, 'dp', split_axis=0, concat_axis=0, tiled=True)  130 us
    all_to_all x5, waiting for transfers between devices, chip_gather_rows(): lax.all_to_all(outgoing, 'dp', split_axis=0, concat_axis=0, tiled=True)  91.6 us
    all_to_all x1, blocking collectives, local(): lax.all_to_all(outgoing, 'dp', split_axis=0, concat_axis=0, tiled=True)  57.6 us
    all_to_all x5, starting transfers between devices, chip_scatter_rows(): lax.all_to_all(chip_sum, 'dp', split_axis=0, concat_axis=0, tiled=True)  28.5 us
    ppermute x8, waiting for transfers between devices, tensor_swap(): return lax.ppermute(block, 'tensor', [(0, 1), (1, 0)])  28 us
    unnamed x322, local copies, waits for them, and re-layouts  26.4 us
    ppermute x1, waiting for transfers between devices, local(): mine = mine + lax.ppermute(mine, 'tensor', [(0, 1), (1, 0)])  26.2 us
    all_to_all x5, starting transfers between devices, chip_gather_rows(): lax.all_to_all(outgoing, 'dp', split_axis=0, concat_axis=0, tiled=True)  24.7 us
  transfers between devices with their start and end apart: 43, of which 21 were waited for; matrix products, arithmetic and copies ran while one was open for 24% of the time, Pallas kernels for 0%

profile of v15, /device:TPU:11, one launch (start us, length us, event | category | flops | bytes accessed | tf_op | source)
XLA Modules:
  0.0 783.0 jit_solution(15202198073247777830)
XLA Ops:
  11.2 6.5 all-to-all-start.1
  18.4 12.1 %all-to-all-done.1 = bf16[16,24,384]{2,1,0:T(8,128)(2,1)S(1)} async-done(((bf16[16,24,384]{2,1,0:T(8,128)(2,1)}), bf16[16,24,384]{2,1,0:T(8,128)(2,1)S(1)}, u32[]{:S(2)}, u32[]{:S(2)}) %all-to-all-start.1) | async-done | bytes 294944 | tf_op jit(solution)/shard_map/all_to_all | solution.py:188
  31.5 3.9 all-to-all-start
  35.5 30.8 %all-to-all-done = bf16[16,24,3,384]{3,1,2,0:T(8,128)(2,1)S(1)} async-done(((bf16[16,24,3,384]{3,1,2,0:T(8,128)(2,1)}), bf16[16,24,3,384]{3,1,2,0:T(8,128)(2,1)S(1)}, u32[]{:S(2)}, u32[]{:S(2)}) %all-to-all-start) | async-done | bytes 884768 | tf_op jit(solution)/shard_map/all_to_all | solution.py:188
  67.4 4.9 all-to-all-start.3
  76.4 27.3 %all-to-all-done.3 = bf16[16,24,1536]{2,1,0:T(8,128)(2,1)} async-done(((bf16[16,24,1536]{2,1,0:T(8,128)(2,1)}), bf16[16,24,1536]{2,1,0:T(8,128)(2,1)}, u32[]{:S(2)}, u32[]{:S(2)}) %all-to-all-start.3) | async-done | bytes 1179680 | tf_op jit(solution)/shard_map/all_to_all | solution.py:188
  104.9 4.8 all-to-all-start.2
  121.0 21.4 %all-to-all-done.2 = bf16[16,24,1536]{2,1,0:T(8,128)(2,1)} async-done(((bf16[16,24,1536]{2,1,0:T(8,128)(2,1)}), bf16[16,24,1536]{2,1,0:T(8,128)(2,1)}, u32[]{:S(2)}, u32[]{:S(2)}) %all-to-all-start.2) | async-done | bytes 1179680 | tf_op jit(solution)/shard_map/all_to_all | solution.py:188
  149.7 4.3 maximum_select_fusion.1
  154.7 4.5 all-to-all-start.4
  159.3 4.2 maximum_select_fusion
  163.6 7.0 multiply_convert_fusion.3
  176.8 6.2 collective-permute-done.4
  190.1 4.3 collective-permute-done.5
  196.7 3.2 fusion.60
  223.2 2.7 fusion.231
  225.9 5.9 multiply_convert_fusion.2
  235.7 3.1 convert_reduce_fusion
  244.0 3.0 bitcast_add_fusion.3
  247.0 5.9 all-to-all-start.5
  261.0 3.0 fusion.154
  267.3 6.8 collective-permute-done.11
  279.2 21.4 %all-to-all-done.5 = f32[16,24,3,384]{3,1,2,0:T(8,128)} async-done(((f32[16,24,3,384]{3,1,2,0:T(8,128)}), f32[16,24,3,384]{3,1,2,0:T(8,128)}, u32[]{:S(2)}, u32[]{:S(2)}) %all-to-all-start.5) | async-done | bytes 1769504 | tf_op jit(solution)/shard_map/all_to_all | solution.py:202
  303.2 4.2 bitcast_add_fusion
  307.4 5.5 all-to-all-start.9
  322.8 3.6 convert_reduce_fusion.1
  340.1 10.3 %collective-permute-done.15 = f32[128,1536]{1,0:T(8,128)} collective-permute-done((f32[128,1536]{1,0:T(8,128)}, f32[128,1536]{1,0:T(8,128)}, u32[]{:S(2)}, u32[]{:S(2)}) %collective-permute-start.15) | collective-permute-done | bytes 786464 | tf_op jit(solution)/shard_map/ppermute | solution.py:163
  361.5 25.0 %all-to-all-done.9 = f32[16,24,1536]{2,1,0:T(8,128)} async-done(((f32[16,24,1536]{2,1,0:T(8,128)}), f32[16,24,1536]{2,1,0:T(8,128)}, u32[]{:S(2)}, u32[]{:S(2)}) %all-to-all-start.9) | async-done | bytes 2359328 | tf_op jit(solution)/shard_map/all_to_all | solution.py:202
  386.5 5.8 all-to-all-start.7
  397.8 4.6 collective-permute-done.17
  402.9 4.0 collective-permute-done.18
  407.6 3.3 collective-permute-start.19
  410.8 4.3 fusion.158
  418.4 2.9 bitcast_add_fusion.2
  421.4 6.6 all-to-all-start.6
  431.0 5.1 collective-permute-done.21
  437.9 49.4 %all-to-all-done.6 = f32[16,24,3,384]{3,1,2,0:T(8,128)S(1)} async-done(((f32[16,24,3,384]{3,1,2,0:T(8,128)}), f32[16,24,3,384]{3,1,2,0:T(8,128)S(1)}, u32[]{:S(2)}, u32[]{:S(2)}) %all-to-all-start.6) | async-done | bytes 1769504 | tf_op jit(solution)/shard_map/all_to_all | solution.py:202
  488.5 4.8 all-to-all-start.8
  518.0 34.7 %all-to-all-done.8 = f32[16,24,1536]{2,1,0:T(8,128)S(1)} async-done(((f32[16,24,1536]{2,1,0:T(8,128)}), f32[16,24,1536]{2,1,0:T(8,128)S(1)}, u32[]{:S(2)}, u32[]{:S(2)}) %all-to-all-start.8) | async-done | bytes 2359328 | tf_op jit(solution)/shard_map/all_to_all | solution.py:202
  557.4 7.1 concatenate.132
  565.8 57.6 %all_to_all.60 = f32[16,48,768]{2,1,0:T(8,128)S(1)} all-to-all(f32[16,48,768]{2,1,0:T(8,128)S(1)} %copy.239), channel_id=1, replica_groups=mesh['dp'=16,'tensor'=2] {'dp'}, dimensions={0} | all-to-all | bytes 4718592 | tf_op jit(solution)/shard_map/all_to_all | solution.py:446
  623.4 4.4 fusion.251
  627.9 4.8 collective-permute-done.23
  635.7 26.2 %collective-permute-done.24 = f32[384,768]{1,0:T(8,128)S(1)} collective-permute-done((f32[384,768]{1,0:T(8,128)S(1)}, f32[384,768]{1,0:T(8,128)S(1)}, u32[]{:S(2)}, u32[]{:S(2)}) %collective-permute-start.24) | collective-permute-done | bytes 1179680 | tf_op jit(solution)/shard_map/ppermute | solution.py:457
  670.5 7.3 fusion
  677.7 4.9 fusion.17
  682.6 3.4 fusion.252
  686.0 3.1 fusion.253
  689.1 3.3 fusion.35
  692.5 3.2 fusion.39
  695.7 3.6 fusion.37
  699.3 3.1 fusion.254
  702.5 3.2 fusion.33
  705.7 3.3 fusion.29
  709.1 3.8 fusion.31
  712.8 3.1 fusion.255
  716.0 3.2 fusion.27
  719.2 3.5 fusion.23
  722.8 3.4 fusion.25
  726.1 3.1 fusion.256
  729.3 3.4 fusion.5
  732.6 4.3 fusion.57
  737.0 5.2 all-to-all-start.11
  745.9 24.0 %all-to-all-done.11 = bf16[16,48,768]{2,1,0:T(8,128)(2,1)S(1)} async-done(((bf16[16,48,768]{2,1,0:T(8,128)(2,1)}), bf16[16,48,768]{2,1,0:T(8,128)(2,1)S(1)}, u32[]{:S(2)}, u32[]{:S(2)}) %all-to-all-start.11) | async-done | bytes 1179680 | tf_op jit(solution)/shard_map/all_to_all | solution.py:483
  (637 shorter events, 198.6 us)
Async XLA Ops:
  7.2 156.3 %all-gather.7.cloned.1.call-start = ((), (), s32[]{:S(2)}) async-start(), calls=%async_computation.18 | async-start | bytes 2506752 | tf_op jit(solution)/shard_map/all_gather | solution.py:146
  11.2 19.3 %all-to-all-start.1 = ((bf16[16,24,384]{2,1,0:T(8,128)(2,1)}), bf16[16,24,384]{2,1,0:T(8,128)(2,1)S(1)}, u32[]{:S(2)}, u32[]{:S(2)}) async-start(bf16[16,24,384]{2,1,0:T(8,128)(2,1)} %bitcast.18), calls=%async_computation.1 | async-start | bytes 589824 | tf_op jit(solution)/shard_map/all_to_all | solution.py:188
  17.7 17.7 %copy-start.47 = (bf16[2,1536,48]{1,2,0:T(8,128)(2,1)S(1)}, bf16[2,1536,48]{1,2,0:T(8,128)(2,1)}, u32[]{:S(2)}) copy-start(bf16[2,1536,48]{1,2,0:T(8,128)(2,1)} %param.21) | copy-start | bytes 884740
  31.5 34.8 %all-to-all-start = ((bf16[16,24,3,384]{3,1,2,0:T(8,128)(2,1)}), bf16[16,24,3,384]{3,1,2,0:T(8,128)(2,1)S(1)}, u32[]{:S(2)}, u32[]{:S(2)}) async-start(bf16[16,24,3,384]{3,1,2,0:T(8,128)(2,1)} %bitcast.2), calls=%async_computation | async-start | bytes 1769472 | tf_op jit(solution)/shard_map/all_to_all | solution.py:188
  67.4 36.3 %all-to-all-start.3 = ((bf16[16,24,1536]{2,1,0:T(8,128)(2,1)}), bf16[16,24,1536]{2,1,0:T(8,128)(2,1)}, u32[]{:S(2)}, u32[]{:S(2)}) async-start(bf16[16,24,1536]{2,1,0:T(8,128)(2,1)} %bitcast.43), calls=%async_computation.3 | async-start | bytes 2359296 | tf_op jit(solution)/shard_map/all_to_all | solution.py:188
  72.3 124.4 %all-gather.9.cloned.1.call-start = ((), (), s32[]{:S(2)}) async-start(), calls=%async_computation.19 | async-start | bytes 1880064 | tf_op jit(solution)/shard_map/all_gather | solution.py:146
  73.0 30.7 %copy-start.119 = (f32[768]{0:T(1024)}, f32[768]{0:T(1024)S(1)}, u32[]{:S(2)}) copy-start(f32[768]{0:T(1024)S(1)} %get-tuple-element.181) | copy-start | bytes 9220
  73.0 30.7 %copy-start.121 = (f32[768]{0:T(1024)}, f32[768]{0:T(1024)S(1)}, u32[]{:S(2)}) copy-start(f32[768]{0:T(1024)S(1)} %get-tuple-element.182) | copy-start | bytes 9220
  73.8 30.0 %copy-start.141 = (f32[128]{0:T(128)}, f32[128]{0:T(128)S(1)}, u32[]{:S(2)}) copy-start(f32[128]{0:T(128)S(1)} %broadcast_multiply_fusion.5) | copy-start | bytes 1540
  74.0 29.7 %copy-start.148 = (f32[128]{0:T(128)}, f32[128]{0:T(128)S(1)}, u32[]{:S(2)}) copy-start(f32[128]{0:T(128)S(1)} %add_rsqrt_fusion.1) | copy-start | bytes 1540
  75.0 42.0 %collective-permute-start = (bf16[128,1536]{1,0:T(8,128)(2,1)}, bf16[128,1536]{1,0:T(8,128)(2,1)}, u32[]{:S(2)}, u32[]{:S(2)}) collective-permute-start(bf16[128,1536]{1,0:T(8,128)(2,1)} %pad_maximum_fusion.8), channel_id=1, source_target_pairs={{0,1},{1,0},{2,3},{3,2},{4,5},{5,4},{6,7},{7,6},{8,9},{9,8},{10,11... | collective-permute-start | bytes 1179656 | tf_op jit(solution)/shard_map/ppermute | solution.py:163
  104.9 37.5 %all-to-all-start.2 = ((bf16[16,24,1536]{2,1,0:T(8,128)(2,1)}), bf16[16,24,1536]{2,1,0:T(8,128)(2,1)}, u32[]{:S(2)}, u32[]{:S(2)}) async-start(bf16[16,24,1536]{2,1,0:T(8,128)(2,1)} %bitcast.26), calls=%async_computation.2 | async-start | bytes 2359296 | tf_op jit(solution)/shard_map/all_to_all | solution.py:188
  112.2 30.6 %collective-permute-start.1 = (bf16[16,24,3,384]{3,1,0,2:T(8,128)(2,1)S(1)}, bf16[16,24,3,384]{3,1,0,2:T(8,128)(2,1)S(1)}, u32[]{:S(2)}, u32[]{:S(2)}) collective-permute-start(bf16[16,24,3,384]{3,1,0,2:T(8,128)(2,1)S(1)} %copy.281), channel_id=1, source_target_pairs={{0,2},{2,0},{4,6},{6,4},{8,10},{10,8},{12,14},{14,12},{16,18},{18,... | collective-permute-start | bytes 2654216 | tf_op jit(solution)/shard_map/ppermute | solution.py:189
  114.3 4.1 collective-permute-start.2
  118.3 24.9 %copy-start.12 = (bf16[256,1536]{1,0:T(8,128)(2,1)}, bf16[256,1536]{1,0:T(8,128)(2,1)S(1)}, u32[]{:S(2)}) copy-start(bf16[256,1536]{1,0:T(8,128)(2,1)S(1)} %maximum_select_fusion.4) | copy-start | bytes 2359300
  120.6 29.0 %collective-permute-start.6 = (bf16[16,24,1536]{2,1,0:T(8,128)(2,1)}, bf16[16,24,1536]{2,1,0:T(8,128)(2,1)}, u32[]{:S(2)}, u32[]{:S(2)}) collective-permute-start(bf16[16,24,1536]{2,1,0:T(8,128)(2,1)} %all-to-all-done.3), channel_id=1, source_target_pairs={{0,2},{2,0},{4,6},{6,4},{8,10},{10,8},{12,14},{14,12},{16,18},{18,... | collective-permute-start | bytes 3538952 | tf_op jit(solution)/shard_map/ppermute | solution.py:189
  142.4 16.9 %collective-permute-start.3 = (bf16[16,24,1536]{2,1,0:T(8,128)(2,1)}, bf16[16,24,1536]{2,1,0:T(8,128)(2,1)}, u32[]{:S(2)}, u32[]{:S(2)}) collective-permute-start(bf16[16,24,1536]{2,1,0:T(8,128)(2,1)} %all-to-all-done.2), channel_id=1, source_target_pairs={{0,2},{2,0},{4,6},{6,4},{8,10},{10,8},{12,14},{14,12},{16,18},{18,... | collective-permute-start | bytes 3538952 | tf_op jit(solution)/shard_map/ppermute | solution.py:189
  154.7 21.1 %all-to-all-start.4 = ((bf16[16,24,384]{2,1,0:T(8,128)(2,1)}), bf16[16,24,384]{2,1,0:T(8,128)(2,1)S(1)}, u32[]{:S(2)}, u32[]{:S(2)}) async-start(bf16[16,24,384]{2,1,0:T(8,128)(2,1)} %bitcast.48), calls=%async_computation.4 | async-start | bytes 589824 | tf_op jit(solution)/shard_map/all_to_all | solution.py:188
  159.2 66.7 %all-gather.11.cloned.1.call-start = ((), (), s32[]{:S(2)}) async-start(), calls=%async_computation.20 | async-start | bytes 2506752 | tf_op jit(solution)/shard_map/all_gather | solution.py:146
  171.4 11.6 %copy-start.138 = (f32[768]{0:T(1024)S(1)}, f32[768]{0:T(1024)}, u32[]{:S(2)}) copy-start(f32[768]{0:T(1024)} %get-tuple-element.175) | copy-start | bytes 9220
  171.4 11.6 %copy-start.139 = (f32[768]{0:T(1024)S(1)}, f32[768]{0:T(1024)}, u32[]{:S(2)}) copy-start(f32[768]{0:T(1024)} %get-tuple-element.176) | copy-start | bytes 9220
  172.4 10.6 %collective-permute-start.4 = (f32[128,768]{1,0:T(8,128)}, f32[128,768]{1,0:T(8,128)}, u32[]{:S(2)}, u32[]{:S(2)}) collective-permute-start(f32[128,768]{1,0:T(8,128)} %constant_dynamic-slice_fusion.3), channel_id=1, source_target_pairs={{0,1},{1,0},{2,3},{3,2},{4,5},{5,4},{6,7},{7,6},{8,9},{9,8},{10,11... | collective-permute-start | bytes 1179656 | tf_op jit(solution)/shard_map/ppermute | solution.py:163
  173.7 13.6 %collective-permute-start.9 = (bf16[128,768]{1,0:T(8,128)(2,1)}, bf16[128,768]{1,0:T(8,128)(2,1)}, u32[]{:S(2)}, u32[]{:S(2)}) collective-permute-start(bf16[128,768]{1,0:T(8,128)(2,1)} %param.16), channel_id=1, source_target_pairs={{0,1},{1,0},{2,3},{3,2},{4,5},{5,4},{6,7},{7,6},{8,9},{9,8},{10,11... | collective-permute-start | bytes 589832 | tf_op jit(solution)/shard_map/ppermute | solution.py:163
  173.9 322.3 %reduce-scatter.4.cloned.1.call-start = ((), (), s32[]{:S(2)}) async-start(), calls=%async_computation.15 | async-start | bytes 1253376 | tf_op jit(solution)/shard_map/reduce_scatter | solution.py:142
  175.9 10.9 %collective-permute-start.7 = (bf16[16,24,384]{2,1,0:T(8,128)(2,1)S(1)}, bf16[16,24,384]{2,1,0:T(8,128)(2,1)S(1)}, u32[]{:S(2)}, u32[]{:S(2)}) collective-permute-start(bf16[16,24,384]{2,1,0:T(8,128)(2,1)S(1)} %all-to-all-done.4), channel_id=1, source_target_pairs={{0,2},{2,0},{4,6},{6,4},{8,10},{10,8},{12,14},{14,12},{16,18},{18,... | collective-permute-start | bytes 884744 | tf_op jit(solution)/shard_map/ppermute | solution.py:189
  184.8 9.6 %collective-permute-start.5 = (bf16[128,1536]{1,0:T(8,128)(2,1)S(1)}, bf16[128,1536]{1,0:T(8,128)(2,1)}, u32[]{:S(2)}, u32[]{:S(2)}) collective-permute-start(bf16[128,1536]{1,0:T(8,128)(2,1)S(1)} %pad_maximum_fusion.9), channel_id=1, source_target_pairs={{0,1},{1,0},{2,3},{3,2},{4,5},{5,4},{6,7},{7,6},{8,9},{9,8},{10,11... | collective-permute-start | bytes 1179656 | tf_op jit(solution)/shard_map/ppermute | solution.py:163
  218.6 24.7 %collective-permute-start.10 = (f32[16,24,3,384]{3,1,2,0:T(8,128)}, f32[16,24,3,384]{3,1,2,0:T(8,128)}, u32[]{:S(2)}, u32[]{:S(2)}) collective-permute-start(f32[16,24,3,384]{3,1,2,0:T(8,128)} %dynamic-slice_bitcast_fusion.3), channel_id=1, source_target_pairs={{0,2},{2,0},{4,6},{6,4},{8,10},{10,8},{12,14},{14,12},{16,18},{18,... | collective-permute-start | bytes 5308424 | tf_op jit(solution)/shard_map/ppermute | solution.py:201
  234.5 41.4 %collective-permute-start.8 = (f32[128,768]{1,0:T(8,128)}, f32[128,768]{1,0:T(8,128)}, u32[]{:S(2)}, u32[]{:S(2)}) collective-permute-start(f32[128,768]{1,0:T(8,128)} %constant_dynamic-slice_fusion), channel_id=1, source_target_pairs={{0,1},{1,0},{2,3},{3,2},{4,5},{5,4},{6,7},{7,6},{8,9},{9,8},{10,11... | collective-permute-start | bytes 1179656 | tf_op jit(solution)/shard_map/ppermute | solution.py:163
  247.0 53.6 %all-to-all-start.5 = ((f32[16,24,3,384]{3,1,2,0:T(8,128)}), f32[16,24,3,384]{3,1,2,0:T(8,128)}, u32[]{:S(2)}, u32[]{:S(2)}) async-start(f32[16,24,3,384]{3,1,2,0:T(8,128)} %bitcast_add_fusion.3), calls=%async_computation.5 | async-start | bytes 3538944 | tf_op jit(solution)/shard_map/all_to_all | solution.py:202
  252.9 255.3 %reduce-scatter.8.cloned.1.call-start = ((), (), s32[]{:S(2)}) async-start(), calls=%async_computation.17 | async-start | bytes 5013504 | tf_op jit(solution)/shard_map/reduce_scatter | solution.py:142
  255.2 19.0 %collective-permute-start.11 = (f32[128,1536]{1,0:T(8,128)}, f32[128,1536]{1,0:T(8,128)}, u32[]{:S(2)}, u32[]{:S(2)}) collective-permute-start(f32[128,1536]{1,0:T(8,128)} %fusion.122), channel_id=1, source_target_pairs={{0,1},{1,0},{2,3},{3,2},{4,5},{5,4},{6,7},{7,6},{8,9},{9,8},{10,11... | collective-permute-start | bytes 2359304 | tf_op jit(solution)/shard_map/ppermute | solution.py:163
  260.4 42.9 %collective-permute-start.22 = (f32[16,24,1536]{2,1,0:T(8,128)}, f32[16,24,1536]{2,1,0:T(8,128)}, u32[]{:S(2)}, u32[]{:S(2)}) collective-permute-start(f32[16,24,1536]{2,1,0:T(8,128)} %dynamic-slice_bitcast_fusion), channel_id=1, source_target_pairs={{0,2},{2,0},{4,6},{6,4},{8,10},{10,8},{12,14},{14,12},{16,18},{18,... | collective-permute-start | bytes 7077896 | tf_op jit(solution)/shard_map/ppermute | solution.py:201
  277.9 29.5 %copy-start.16 = (f32[128,768]{1,0:T(8,128)}, f32[128,768]{1,0:T(8,128)S(1)}, u32[]{:S(2)}) copy-start(f32[128,768]{1,0:T(8,128)S(1)} %get-tuple-element.31) | copy-start | bytes 1179652
  302.9 19.7 %copy-start.44 = (bf16[128,768]{1,0:T(8,128)(2,1)}, bf16[128,768]{1,0:T(8,128)(2,1)S(1)}, u32[]{:S(2)}) copy-start(bf16[128,768]{1,0:T(8,128)(2,1)S(1)} %convert_element_type.190) | copy-start | bytes 589828
  302.9 10.1 %collective-permute-start.12 = (bf16[128,768]{1,0:T(8,128)(2,1)S(1)}, bf16[128,768]{1,0:T(8,128)(2,1)S(1)}, u32[]{:S(2)}, u32[]{:S(2)}) collective-permute-start(bf16[128,768]{1,0:T(8,128)(2,1)S(1)} %convert_element_type.190), channel_id=1, source_target_pairs={{0,1},{1,0},{2,3},{3,2},{4,5},{5,4},{6,7},{7,6},{8,9},{9,8},{10,11... | collective-permute-start | bytes 589832 | tf_op jit(solution)/shard_map/ppermute | solution.py:163
  307.4 79.1 %all-to-all-start.9 = ((f32[16,24,1536]{2,1,0:T(8,128)}), f32[16,24,1536]{2,1,0:T(8,128)}, u32[]{:S(2)}, u32[]{:S(2)}) async-start(f32[16,24,1536]{2,1,0:T(8,128)} %bitcast_add_fusion), calls=%async_computation.12 | async-start | bytes 4718592 | tf_op jit(solution)/shard_map/all_to_all | solution.py:202
  321.7 16.4 %collective-permute-start.14 = (f32[16,24,384]{2,1,0:T(8,128)}, f32[16,24,384]{2,1,0:T(8,128)}, u32[]{:S(2)}, u32[]{:S(2)}) collective-permute-start(f32[16,24,384]{2,1,0:T(8,128)} %dynamic-slice_bitcast_fusion.4), channel_id=1, source_target_pairs={{0,2},{2,0},{4,6},{6,4},{8,10},{10,8},{12,14},{14,12},{16,18},{18,... | collective-permute-start | bytes 1769480 | tf_op jit(solution)/shard_map/ppermute | solution.py:201
  331.2 19.2 %collective-permute-start.15 = (f32[128,1536]{1,0:T(8,128)}, f32[128,1536]{1,0:T(8,128)}, u32[]{:S(2)}, u32[]{:S(2)}) collective-permute-start(f32[128,1536]{1,0:T(8,128)} %fusion.119), channel_id=1, source_target_pairs={{0,1},{1,0},{2,3},{3,2},{4,5},{5,4},{6,7},{7,6},{8,9},{9,8},{10,11... | collective-permute-start | bytes 2359304 | tf_op jit(solution)/shard_map/ppermute | solution.py:163
  337.4 13.0 %copy-start.24 = (f32[256,768]{1,0:T(8,128)S(1)}, f32[256,768]{1,0:T(8,128)}, u32[]{:S(2)}) copy-start(f32[256,768]{1,0:T(8,128)} %copy-done.23) | copy-start | bytes 2359300
  337.4 13.0 %copy-start.26 = (f32[256,768]{1,0:T(8,128)S(1)}, f32[256,768]{1,0:T(8,128)}, u32[]{:S(2)}) copy-start(f32[256,768]{1,0:T(8,128)} %copy-done.25) | copy-start | bytes 2359300
  337.4 81.0 %collective-permute-start.13 = (f32[16,24,3,384]{3,1,2,0:T(8,128)}, f32[16,24,3,384]{3,1,2,0:T(8,128)}, u32[]{:S(2)}, u32[]{:S(2)}) collective-permute-start(f32[16,24,3,384]{3,1,2,0:T(8,128)} %dynamic-slice_bitcast_fusion.2), channel_id=1, source_target_pairs={{0,2},{2,0},{4,6},{6,4},{8,10},{10,8},{12,14},{14,12},{16,18},{18,... | collective-permute-start | bytes 5308424 | tf_op jit(solution)/shard_map/ppermute | solution.py:201
  340.1 11.6 %copy-start.120 = (f32[768]{0:T(1024)S(1)}, f32[768]{0:T(1024)}, u32[]{:S(2)}) copy-start(f32[768]{0:T(1024)} %copy-done.119) | copy-start | bytes 9220
  340.1 11.6 %copy-start.122 = (f32[768]{0:T(1024)S(1)}, f32[768]{0:T(1024)}, u32[]{:S(2)}) copy-start(f32[768]{0:T(1024)} %copy-done.121) | copy-start | bytes 9220
  340.1 11.6 %copy-start.142 = (f32[128]{0:T(128)S(1)}, f32[128]{0:T(128)}, u32[]{:S(2)}) copy-start(f32[128]{0:T(128)} %copy-done.141) | copy-start | bytes 1540
  340.1 11.6 %copy-start.149 = (f32[128]{0:T(128)S(1)}, f32[128]{0:T(128)}, u32[]{:S(2)}) copy-start(f32[128]{0:T(128)} %copy-done.148) | copy-start | bytes 1540
  340.1 12.5 %copy-start.17 = (f32[128,768]{1,0:T(8,128)S(1)}, f32[128,768]{1,0:T(8,128)}, u32[]{:S(2)}) copy-start(f32[128,768]{1,0:T(8,128)} %copy-done.16) | copy-start | bytes 1179652
  386.5 34.8 %all-to-all-start.7 = ((f32[16,24,384]{2,1,0:T(8,128)}), f32[16,24,384]{2,1,0:T(8,128)}, u32[]{:S(2)}, u32[]{:S(2)}) async-start(f32[16,24,384]{2,1,0:T(8,128)} %bitcast_add_fusion.4), calls=%async_computation.7 | async-start | bytes 1179648 | tf_op jit(solution)/shard_map/all_to_all | solution.py:202
  392.3 118.2 %reduce-scatter.6.cloned.1.call-start = ((), (), s32[]{:S(2)}) async-start(), calls=%async_computation.16 | async-start | bytes 5013504 | tf_op jit(solution)/shard_map/reduce_scatter | solution.py:142
  395.1 1.5 collective-permute-start.16
  397.5 4.9 collective-permute-start.17
  402.5 4.5 collective-permute-start.18
  407.6 7.6 collective-permute-start.19
  416.7 12.1 %collective-permute-start.20 = (f32[19968]{0:T(1024)}, f32[19968]{0:T(1024)}, u32[]{:S(2)}, u32[]{:S(2)}) collective-permute-start(f32[19968]{0:T(1024)} %add.473), channel_id=1, source_target_pairs={{0,1},{1,0},{2,3},{3,2},{4,5},{5,4},{6,7},{7,6},{8,9},{9,8},{10,11... | collective-permute-start | bytes 239624 | tf_op jit(solution)/shard_map/ppermute | solution.py:159
  421.4 65.9 %all-to-all-start.6 = ((f32[16,24,3,384]{3,1,2,0:T(8,128)}), f32[16,24,3,384]{3,1,2,0:T(8,128)S(1)}, u32[]{:S(2)}, u32[]{:S(2)}) async-start(f32[16,24,3,384]{3,1,2,0:T(8,128)} %bitcast_add_fusion.2), calls=%async_computation.6 | async-start | bytes 3538944 | tf_op jit(solution)/shard_map/all_to_all | solution.py:202
  430.5 5.6 collective-permute-start.21
  488.5 64.2 %all-to-all-start.8 = ((f32[16,24,1536]{2,1,0:T(8,128)}), f32[16,24,1536]{2,1,0:T(8,128)S(1)}, u32[]{:S(2)}, u32[]{:S(2)}) async-start(f32[16,24,1536]{2,1,0:T(8,128)} %bitcast_add_fusion.1), calls=%async_computation.11 | async-start | bytes 4718592 | tf_op jit(solution)/shard_map/all_to_all | solution.py:202
  627.8 4.9 collective-permute-start.23
  634.4 28.7 %copy-start.75 = (f32[19968]{0:T(1024)S(1)}, f32[19968]{0:T(1024)}, u32[]{:S(2)}) copy-start(f32[19968]{0:T(1024)} %add.474) | copy-start | bytes 239620
  634.4 27.5 %collective-permute-start.24 = (f32[384,768]{1,0:T(8,128)S(1)}, f32[384,768]{1,0:T(8,128)S(1)}, u32[]{:S(2)}, u32[]{:S(2)}) collective-permute-start(f32[384,768]{1,0:T(8,128)S(1)} %dynamic-slice_add_fusion), channel_id=1, source_target_pairs={{0,1},{1,0},{2,3},{3,2},{4,5},{5,4},{6,7},{7,6},{8,9},{9,8},{10,11... | collective-permute-start | bytes 3538952 | tf_op jit(solution)/shard_map/ppermute | solution.py:457
  662.0 5.3 collective-permute-start.25
  737.0 32.9 %all-to-all-start.11 = ((bf16[16,48,768]{2,1,0:T(8,128)(2,1)}), bf16[16,48,768]{2,1,0:T(8,128)(2,1)S(1)}, u32[]{:S(2)}, u32[]{:S(2)}) async-start(bf16[16,48,768]{2,1,0:T(8,128)(2,1)} %bitcast.138), calls=%async_computation.14 | async-start | bytes 2359296 | tf_op jit(solution)/shard_map/all_to_all | solution.py:483
  742.8 28.2 %copy-start.88 = (f32[2,2,768]{2,1,0:T(2,128)}, f32[2,2,768]{2,1,0:T(2,128)S(1)}, u32[]{:S(2)}) copy-start(f32[2,2,768]{2,1,0:T(2,128)S(1)} %slice.412) | copy-start | bytes 36868
  743.5 27.5 %copy-start.78 = (f32[2,3072]{1,0:T(2,128)}, f32[2,3072]{1,0:T(2,128)S(1)}, u32[]{:S(2)}) copy-start(f32[2,3072]{1,0:T(2,128)S(1)} %reshape.583) | copy-start | bytes 73732
  743.5 27.5 %copy-start.79 = (f32[2,4,768]{2,1,0:T(4,128)}, f32[2,4,768]{2,1,0:T(4,128)S(1)}, u32[]{:S(2)}) copy-start(f32[2,4,768]{2,1,0:T(4,128)S(1)} %reshape.581) | copy-start | bytes 73732
  (137 other events, 490.5 us)
Sparse Core Ops, SparseCore 0:
  10.9 51.8 all-gather.6
  76.4 53.1 all-gather.8
  174.1 42.0 all-gather.10
  226.0 69.7 reduce-scatter.3
  299.5 96.2 reduce-scatter.7
  415.2 95.1 reduce-scatter.5

commit v16 on v13

--- a/solution.py
+++ b/solution.py
@@ -412,7 +412,7 @@
         offset += part.size
     gains_grad, biases_grad, qkv_bias_grad, up_bias_grad = small_sums
     flat, first_down = lax.optimization_barrier((flat, weight_list[0][3]))
-    weight_list[0] = scatter_layer(weight_list[0][:3] + (first_down,))
+    weight_list[0] = scatter_layer(weight_list[0][:3] + (first_down,), proj_whole=True)
     qkv_grad = jnp.stack([weight_list[layer_id][0] for layer_id in range(LAYERS)])
     proj_grad = jnp.stack([weight_list[layer_id][1] for layer_id in range(LAYERS)])
     up_grad = jnp.stack([weight_list[layer_id][2] for layer_id in range(LAYERS)])

time: 774 us -> 802 us (1.036)
  waiting for transfers between devices: 293 us -> 331 us
  blocking collectives: 76.7 us -> 59.6 us
    reduce_scatter x3 -> x4, waiting for transfers between devices: 2.13 us -> 96.3 us  [dp_scatter(): lax.psum_scatter(partial, 'dp', scatter_dimension=dimension, tiled=True)]
    all_to_all x5 -> x4, waiting for transfers between devices: 133 us -> 57.9 us  [chip_scatter_rows(): lax.all_to_all(chip_sum, 'dp', split_axis=0, concat_axis=0, tiled=True)]
    all_to_all x1 -> x0, blocking collectives: 19.1 us -> none  [chip_gather_rows(): lax.all_to_all(outgoing, 'dp', split_axis=0, concat_axis=0, tiled=True)]
    ppermute x8, waiting for transfers between devices: 22.5 us -> 36.1 us  [tensor_swap(): return lax.ppermute(block, 'tensor', [(0, 1), (1, 0)])]
    all_to_all x4 -> x5, starting transfers between devices: 18 us -> 26.2 us  [chip_gather_rows(): lax.all_to_all(outgoing, 'dp', split_axis=0, concat_axis=0, tiled=True)]
    all_to_all x4 -> x5, waiting for transfers between devices: 65.3 us -> 73.2 us  [chip_gather_rows(): lax.all_to_all(outgoing, 'dp', split_axis=0, concat_axis=0, tiled=True)]
    unnamed x312 -> x300, local copies, waits for them, and re-layouts: 26.7 us -> 22.3 us
    all_to_all x5 -> x4, starting transfers between devices: 26.9 us -> 25.5 us  [chip_scatter_rows(): lax.all_to_all(chip_sum, 'dp', split_axis=0, concat_axis=0, tiled=True)]
  transfers between devices with their start and end apart: 42 -> 42, of which waited for: 19 -> 22; matrix products, arithmetic and copies ran while one was open for 25% -> 24% of each run, Pallas kernels for 0% -> 0%
where the time goes in v16:
time: 802 us; the launch traced here: 790 us
  waiting for transfers between devices  331 us (41%)
  matrix products  139 us (17%)
  local copies, waits for them, and re-layouts  87.1 us (11%)
  starting transfers between devices  78.9 us (10%)
  other arithmetic  77.5 us (10%)
  blocking collectives  59.6 us (7%)
  between operations  17.5 us (2%)
    reduce_scatter x4, waiting for transfers between devices, dp_scatter(): lax.psum_scatter(partial, 'dp', scatter_dimension=dimension, tiled=True)  96.3 us
    all_to_all x5, waiting for transfers between devices, chip_gather_rows(): lax.all_to_all(outgoing, 'dp', split_axis=0, concat_axis=0, tiled=True)  73.2 us
    all_to_all x1, blocking collectives, local(): lax.all_to_all(outgoing, 'dp', split_axis=0, concat_axis=0, tiled=True)  59.6 us
    all_to_all x4, waiting for transfers between devices, chip_scatter_rows(): lax.all_to_all(chip_sum, 'dp', split_axis=0, concat_axis=0, tiled=True)  57.9 us
    ppermute x8, waiting for transfers between devices, tensor_swap(): return lax.ppermute(block, 'tensor', [(0, 1), (1, 0)])  36.1 us
    all_to_all x5, starting transfers between devices, chip_gather_rows(): lax.all_to_all(outgoing, 'dp', split_axis=0, concat_axis=0, tiled=True)  26.2 us
    ppermute x1, waiting for transfers between devices, local(): mine = mine + lax.ppermute(mine, 'tensor', [(0, 1), (1, 0)])  26.2 us
    all_to_all x4, starting transfers between devices, chip_scatter_rows(): lax.all_to_all(chip_sum, 'dp', split_axis=0, concat_axis=0, tiled=True)  25.5 us
  transfers between devices with their start and end apart: 42, of which 22 were waited for; matrix products, arithmetic and copies ran while one was open for 24% of the time, Pallas kernels for 0%

profile of v16, /device:TPU:11, one launch (start us, length us, event | category | flops | bytes accessed | tf_op | source)
XLA Modules:
  0.0 790.4 jit_solution(16586029721545296906)
XLA Ops:
  10.6 6.5 all-to-all-start.1
  18.0 10.9 %all-to-all-done.1 = bf16[16,24,384]{2,1,0:T(8,128)(2,1)S(1)} async-done(((bf16[16,24,384]{2,1,0:T(8,128)(2,1)}), bf16[16,24,384]{2,1,0:T(8,128)(2,1)S(1)}, u32[]{:S(2)}, u32[]{:S(2)}) %all-to-all-start.1) | async-done | bytes 294944 | tf_op jit(solution)/shard_map/all_to_all | solution.py:188
  30.0 4.3 all-to-all-start
  38.4 26.8 %all-to-all-done = bf16[16,24,3,384]{3,1,2,0:T(8,128)(2,1)S(1)} async-done(((bf16[16,24,3,384]{3,1,2,0:T(8,128)(2,1)}), bf16[16,24,3,384]{3,1,2,0:T(8,128)(2,1)S(1)}, u32[]{:S(2)}, u32[]{:S(2)}) %all-to-all-start) | async-done | bytes 884768 | tf_op jit(solution)/shard_map/all_to_all | solution.py:188
  66.3 4.8 all-to-all-start.2
  77.0 25.5 %all-to-all-done.2 = bf16[16,24,1536]{2,1,0:T(8,128)(2,1)} async-done(((bf16[16,24,1536]{2,1,0:T(8,128)(2,1)}), bf16[16,24,1536]{2,1,0:T(8,128)(2,1)}, u32[]{:S(2)}, u32[]{:S(2)}) %all-to-all-start.2) | async-done | bytes 1179680 | tf_op jit(solution)/shard_map/all_to_all | solution.py:188
  103.2 4.7 all-to-all-start.3
  117.9 4.2 maximum_select_fusion
  122.1 7.0 multiply_convert_fusion.3
  132.0 5.9 all-to-all-start.4
  141.5 8.1 %collective-permute-done.4 = f32[128,768]{1,0:T(8,128)S(1)} collective-permute-done((f32[128,768]{1,0:T(8,128)}, f32[128,768]{1,0:T(8,128)S(1)}, u32[]{:S(2)}, u32[]{:S(2)}) %collective-permute-start.4) | collective-permute-done | bytes 393248 | tf_op jit(solution)/shard_map/ppermute | solution.py:163
  160.5 10.0 %all-to-all-done.4 = bf16[16,24,1536]{2,1,0:T(8,128)(2,1)} async-done(((bf16[16,24,1536]{2,1,0:T(8,128)(2,1)}), bf16[16,24,1536]{2,1,0:T(8,128)(2,1)}, u32[]{:S(2)}, u32[]{:S(2)}) %all-to-all-start.4) | async-done | bytes 1179680 | tf_op jit(solution)/shard_map/all_to_all | solution.py:188
  172.8 3.2 fusion.60
  201.3 4.3 maximum_select_fusion.1
  205.6 6.6 multiply_convert_fusion.2
  212.2 3.8 convert_reduce_fusion
  216.1 3.0 bitcast_add_fusion.3
  219.0 4.8 all-to-all-start.5
  224.0 2.9 fusion.7
  239.4 8.6 %collective-permute-done.11 = f32[128,1536]{1,0:T(8,128)} collective-permute-done((f32[128,1536]{1,0:T(8,128)}, f32[128,1536]{1,0:T(8,128)}, u32[]{:S(2)}, u32[]{:S(2)}) %collective-permute-start.11) | collective-permute-done | bytes 786464 | tf_op jit(solution)/shard_map/ppermute | solution.py:163
  250.2 6.1 collective-permute-done.8
  257.8 8.4 %all-to-all-done.5 = f32[16,24,3,384]{3,1,2,0:T(8,128)} async-done(((f32[16,24,3,384]{3,1,2,0:T(8,128)}), f32[16,24,3,384]{3,1,2,0:T(8,128)}, u32[]{:S(2)}, u32[]{:S(2)}) %all-to-all-start.5) | async-done | bytes 1769504 | tf_op jit(solution)/shard_map/all_to_all | solution.py:202
  270.0 4.0 fusion.230
  276.0 3.3 dynamic-slice_bitcast_fusion
  281.0 3.0 fusion.154
  286.6 4.2 bitcast_add_fusion
  290.8 5.0 all-to-all-start.8
  302.4 3.4 convert_reduce_fusion.1
  316.8 12.8 %collective-permute-done.14 = f32[128,1536]{1,0:T(8,128)} collective-permute-done((f32[128,1536]{1,0:T(8,128)}, f32[128,1536]{1,0:T(8,128)}, u32[]{:S(2)}, u32[]{:S(2)}) %collective-permute-start.14) | collective-permute-done | bytes 786464 | tf_op jit(solution)/shard_map/ppermute | solution.py:163
  343.6 3.4 collective-permute-done.16
  347.0 3.4 collective-permute-start.17
  353.9 4.2 fusion.158
  361.3 2.9 bitcast_add_fusion.2
  364.2 10.4 %all-to-all-start.6 = ((f32[16,24,3,384]{3,1,2,0:T(8,128)}), f32[16,24,3,384]{3,1,2,0:T(8,128)S(1)}, u32[]{:S(2)}, u32[]{:S(2)}) async-start(f32[16,24,3,384]{3,1,2,0:T(8,128)} %bitcast_add_fusion.2), calls=%async_computation.6 | async-start | bytes 3538944 | tf_op jit(solution)/shard_map/all_to_all | solution.py:202
  377.6 5.0 collective-permute-done.20
  384.4 49.5 %all-to-all-done.6 = f32[16,24,3,384]{3,1,2,0:T(8,128)S(1)} async-done(((f32[16,24,3,384]{3,1,2,0:T(8,128)}), f32[16,24,3,384]{3,1,2,0:T(8,128)S(1)}, u32[]{:S(2)}, u32[]{:S(2)}) %all-to-all-start.6) | async-done | bytes 1769504 | tf_op jit(solution)/shard_map/all_to_all | solution.py:202
  435.1 5.3 all-to-all-start.7
  454.3 8.0 %reduce-scatter.11.cloned.1.call-done = f32[48,1536]{1,0:T(8,128)} async-done(((f32[768,1536]{1,0:T(8,128)}), f32[48,1536]{1,0:T(8,128)}) %reduce-scatter.11.cloned.1.call-update) | async-done | bytes 294928 | tf_op jit(solution)/shard_map/reduce_scatter | solution.py:142
  462.2 88.3 %reduce-scatter.9.cloned.1.call-done = f32[48,1536]{1,0:T(8,128)} async-done(((f32[768,1536]{1,0:T(8,128)}), f32[48,1536]{1,0:T(8,128)}) %reduce-scatter.9.cloned.1.call-update) | async-done | bytes 294928 | tf_op jit(solution)/shard_map/reduce_scatter | solution.py:142
  562.8 7.1 concatenate.128
  571.2 59.6 %all_to_all.55 = f32[16,48,768]{2,1,0:T(8,128)S(1)} all-to-all(f32[16,48,768]{2,1,0:T(8,128)S(1)} %copy.227), channel_id=1, replica_groups=mesh['dp'=16,'tensor'=2] {'dp'}, dimensions={0} | all-to-all | bytes 4718592 | tf_op jit(solution)/shard_map/all_to_all | solution.py:442
  630.8 4.4 fusion.251
  635.3 4.8 collective-permute-done.22
  643.1 26.2 %collective-permute-done.23 = f32[384,768]{1,0:T(8,128)S(1)} collective-permute-done((f32[384,768]{1,0:T(8,128)S(1)}, f32[384,768]{1,0:T(8,128)S(1)}, u32[]{:S(2)}, u32[]{:S(2)}) %collective-permute-start.23) | collective-permute-done | bytes 1179680 | tf_op jit(solution)/shard_map/ppermute | solution.py:453
  677.9 7.2 fusion
  685.1 4.9 fusion.17
  690.0 3.4 fusion.252
  693.3 3.1 fusion.253
  696.5 3.3 fusion.35
  699.9 3.2 fusion.39
  703.1 3.6 fusion.37
  706.7 3.1 fusion.254
  709.8 3.2 fusion.33
  713.1 3.3 fusion.29
  716.4 3.8 fusion.31
  720.2 3.1 fusion.255
  723.3 3.2 fusion.27
  726.6 3.5 fusion.23
  730.1 3.3 fusion.25
  733.5 3.1 fusion.256
  736.6 3.4 fusion.5
  740.0 4.3 fusion.57
  744.3 5.2 all-to-all-start.10
  753.3 24.0 %all-to-all-done.10 = bf16[16,48,768]{2,1,0:T(8,128)(2,1)S(1)} async-done(((bf16[16,48,768]{2,1,0:T(8,128)(2,1)}), bf16[16,48,768]{2,1,0:T(8,128)(2,1)S(1)}, u32[]{:S(2)}, u32[]{:S(2)}) %all-to-all-start.10) | async-done | bytes 1179680 | tf_op jit(solution)/shard_map/all_to_all | solution.py:479
  (608 shorter events, 189.1 us)
Async XLA Ops:
  7.2 114.9 %all-gather.7.cloned.1.call-start = ((), (), s32[]{:S(2)}) async-start(), calls=%async_computation.19 | async-start | bytes 2506752 | tf_op jit(solution)/shard_map/all_gather | solution.py:146
  10.6 18.3 %all-to-all-start.1 = ((bf16[16,24,384]{2,1,0:T(8,128)(2,1)}), bf16[16,24,384]{2,1,0:T(8,128)(2,1)S(1)}, u32[]{:S(2)}, u32[]{:S(2)}) async-start(bf16[16,24,384]{2,1,0:T(8,128)(2,1)} %bitcast.18), calls=%async_computation.1 | async-start | bytes 589824 | tf_op jit(solution)/shard_map/all_to_all | solution.py:188
  17.2 17.2 %copy-start.105 = (f32[2,2,768]{2,1,0:T(2,128)S(1)}, f32[2,2,768]{2,1,0:T(2,128)}, u32[]{:S(2)}) copy-start(f32[2,2,768]{2,1,0:T(2,128)} %param.22) | copy-start | bytes 36868
  17.2 17.8 %copy-start.87 = (f32[2,4,768]{2,1,0:T(4,128)S(1)}, f32[2,4,768]{2,1,0:T(4,128)}, u32[]{:S(2)}) copy-start(f32[2,4,768]{2,1,0:T(4,128)} %param.23) | copy-start | bytes 73732
  18.0 18.1 %copy-start.134 = (f32[128]{0:T(128)}, f32[128]{0:T(128)S(1)}, u32[]{:S(2)}) copy-start(f32[128]{0:T(128)S(1)} %broadcast_multiply_fusion.5) | copy-start | bytes 1540
  30.0 35.2 %all-to-all-start = ((bf16[16,24,3,384]{3,1,2,0:T(8,128)(2,1)}), bf16[16,24,3,384]{3,1,2,0:T(8,128)(2,1)S(1)}, u32[]{:S(2)}, u32[]{:S(2)}) async-start(bf16[16,24,3,384]{3,1,2,0:T(8,128)(2,1)} %bitcast.2), calls=%async_computation | async-start | bytes 1769472 | tf_op jit(solution)/shard_map/all_to_all | solution.py:188
  34.3 137.6 %all-gather.9.cloned.1.call-start = ((), (), s32[]{:S(2)}) async-start(), calls=%async_computation.20 | async-start | bytes 1880064 | tf_op jit(solution)/shard_map/all_gather | solution.py:146
  36.9 37.7 %collective-permute-start = (bf16[128,1536]{1,0:T(8,128)(2,1)}, bf16[128,1536]{1,0:T(8,128)(2,1)}, u32[]{:S(2)}, u32[]{:S(2)}) collective-permute-start(bf16[128,1536]{1,0:T(8,128)(2,1)} %pad_maximum_fusion.8), channel_id=1, source_target_pairs={{0,1},{1,0},{2,3},{3,2},{4,5},{5,4},{6,7},{7,6},{8,9},{9,8},{10,11... | collective-permute-start | bytes 1179656 | tf_op jit(solution)/shard_map/ppermute | solution.py:163
  66.3 36.1 %all-to-all-start.2 = ((bf16[16,24,1536]{2,1,0:T(8,128)(2,1)}), bf16[16,24,1536]{2,1,0:T(8,128)(2,1)}, u32[]{:S(2)}, u32[]{:S(2)}) async-start(bf16[16,24,1536]{2,1,0:T(8,128)(2,1)} %bitcast.26), calls=%async_computation.2 | async-start | bytes 2359296 | tf_op jit(solution)/shard_map/all_to_all | solution.py:188
  73.1 35.3 %collective-permute-start.1 = (bf16[16,24,3,384]{3,1,0,2:T(8,128)(2,1)S(1)}, bf16[16,24,3,384]{3,1,0,2:T(8,128)(2,1)}, u32[]{:S(2)}, u32[]{:S(2)}) collective-permute-start(bf16[16,24,3,384]{3,1,0,2:T(8,128)(2,1)S(1)} %copy.267), channel_id=1, source_target_pairs={{0,2},{2,0},{4,6},{6,4},{8,10},{10,8},{12,14},{14,12},{16,18},{18,... | collective-permute-start | bytes 2654216 | tf_op jit(solution)/shard_map/ppermute | solution.py:189
  73.7 41.3 %copy-start.103 = (pred[256,256]{0,1:T(8,128)(4,1)}, pred[256,256]{0,1:T(8,128)(4,1)S(1)}, u32[]{:S(2)}) copy-start(pred[256,256]{0,1:T(8,128)(4,1)S(1)} %fusion.164) | copy-start | bytes 196612
  73.8 2.2 collective-permute-start.2
  75.9 34.3 %copy-start.11 = (bf16[256,1536]{1,0:T(8,128)(2,1)}, bf16[256,1536]{1,0:T(8,128)(2,1)S(1)}, u32[]{:S(2)}) copy-start(bf16[256,1536]{1,0:T(8,128)(2,1)S(1)} %maximum_select_fusion.4) | copy-start | bytes 2359300
  103.2 27.6 %all-to-all-start.3 = ((bf16[16,24,384]{2,1,0:T(8,128)(2,1)}), bf16[16,24,384]{2,1,0:T(8,128)(2,1)}, u32[]{:S(2)}, u32[]{:S(2)}) async-start(bf16[16,24,384]{2,1,0:T(8,128)(2,1)} %bitcast.41), calls=%async_computation.3 | async-start | bytes 589824 | tf_op jit(solution)/shard_map/all_to_all | solution.py:188
  107.9 9.9 %collective-permute-start.3 = (bf16[16,24,1536]{2,1,0:T(8,128)(2,1)}, bf16[16,24,1536]{2,1,0:T(8,128)(2,1)}, u32[]{:S(2)}, u32[]{:S(2)}) collective-permute-start(bf16[16,24,1536]{2,1,0:T(8,128)(2,1)} %all-to-all-done.2), channel_id=1, source_target_pairs={{0,2},{2,0},{4,6},{6,4},{8,10},{10,8},{12,14},{14,12},{16,18},{18,... | collective-permute-start | bytes 3538952 | tf_op jit(solution)/shard_map/ppermute | solution.py:189
  132.0 18.4 %copy-start.126 = (f32[768]{0:T(1024)S(1)}, f32[768]{0:T(1024)}, u32[]{:S(2)}) copy-start(f32[768]{0:T(1024)} %get-tuple-element.169) | copy-start | bytes 9220
  132.0 18.4 %copy-start.127 = (f32[768]{0:T(1024)S(1)}, f32[768]{0:T(1024)}, u32[]{:S(2)}) copy-start(f32[768]{0:T(1024)} %get-tuple-element.170) | copy-start | bytes 9220
  132.0 38.5 %all-to-all-start.4 = ((bf16[16,24,1536]{2,1,0:T(8,128)(2,1)}), bf16[16,24,1536]{2,1,0:T(8,128)(2,1)}, u32[]{:S(2)}, u32[]{:S(2)}) async-start(bf16[16,24,1536]{2,1,0:T(8,128)(2,1)} %bitcast.49), calls=%async_computation.4 | async-start | bytes 2359296 | tf_op jit(solution)/shard_map/all_to_all | solution.py:188
  137.9 67.7 %all-gather.11.cloned.1.call-start = ((), (), s32[]{:S(2)}) async-start(), calls=%async_computation.21 | async-start | bytes 2506752 | tf_op jit(solution)/shard_map/all_gather | solution.py:146
  139.0 10.6 %collective-permute-start.4 = (f32[128,768]{1,0:T(8,128)}, f32[128,768]{1,0:T(8,128)S(1)}, u32[]{:S(2)}, u32[]{:S(2)}) collective-permute-start(f32[128,768]{1,0:T(8,128)} %constant_dynamic-slice_fusion.3), channel_id=1, source_target_pairs={{0,1},{1,0},{2,3},{3,2},{4,5},{5,4},{6,7},{7,6},{8,9},{9,8},{10,11... | collective-permute-start | bytes 1179656 | tf_op jit(solution)/shard_map/ppermute | solution.py:163
  140.3 17.8 %collective-permute-start.9 = (bf16[128,768]{1,0:T(8,128)(2,1)S(1)}, bf16[128,768]{1,0:T(8,128)(2,1)}, u32[]{:S(2)}, u32[]{:S(2)}) collective-permute-start(bf16[128,768]{1,0:T(8,128)(2,1)S(1)} %copy-done.57), channel_id=1, source_target_pairs={{0,1},{1,0},{2,3},{3,2},{4,5},{5,4},{6,7},{7,6},{8,9},{9,8},{10,11... | collective-permute-start | bytes 589832 | tf_op jit(solution)/shard_map/ppermute | solution.py:163
  140.5 16.2 %collective-permute-start.6 = (bf16[16,24,384]{2,1,0:T(8,128)(2,1)}, bf16[16,24,384]{2,1,0:T(8,128)(2,1)}, u32[]{:S(2)}, u32[]{:S(2)}) collective-permute-start(bf16[16,24,384]{2,1,0:T(8,128)(2,1)} %all-to-all-done.3), channel_id=1, source_target_pairs={{0,2},{2,0},{4,6},{6,4},{8,10},{10,8},{12,14},{14,12},{16,18},{18,... | collective-permute-start | bytes 884744 | tf_op jit(solution)/shard_map/ppermute | solution.py:189
  153.4 17.2 %collective-permute-start.5 = (bf16[128,1536]{1,0:T(8,128)(2,1)}, bf16[128,1536]{1,0:T(8,128)(2,1)}, u32[]{:S(2)}, u32[]{:S(2)}) collective-permute-start(bf16[128,1536]{1,0:T(8,128)(2,1)} %pad_maximum_fusion.9), channel_id=1, source_target_pairs={{0,1},{1,0},{2,3},{3,2},{4,5},{5,4},{6,7},{7,6},{8,9},{9,8},{10,11... | collective-permute-start | bytes 1179656 | tf_op jit(solution)/shard_map/ppermute | solution.py:163
  170.5 30.8 %collective-permute-start.7 = (bf16[16,24,1536]{2,1,0:T(8,128)(2,1)}, bf16[16,24,1536]{2,1,0:T(8,128)(2,1)}, u32[]{:S(2)}, u32[]{:S(2)}) collective-permute-start(bf16[16,24,1536]{2,1,0:T(8,128)(2,1)} %all-to-all-done.4), channel_id=1, source_target_pairs={{0,2},{2,0},{4,6},{6,4},{8,10},{10,8},{12,14},{14,12},{16,18},{18,... | collective-permute-start | bytes 3538952 | tf_op jit(solution)/shard_map/ppermute | solution.py:189
  200.9 15.1 %collective-permute-start.10 = (f32[16,24,3,384]{3,1,2,0:T(8,128)}, f32[16,24,3,384]{3,1,2,0:T(8,128)}, u32[]{:S(2)}, u32[]{:S(2)}) collective-permute-start(f32[16,24,3,384]{3,1,2,0:T(8,128)} %dynamic-slice_bitcast_fusion.3), channel_id=1, source_target_pairs={{0,2},{2,0},{4,6},{6,4},{8,10},{10,8},{12,14},{14,12},{16,18},{18,... | collective-permute-start | bytes 5308424 | tf_op jit(solution)/shard_map/ppermute | solution.py:201
  219.0 47.1 %all-to-all-start.5 = ((f32[16,24,3,384]{3,1,2,0:T(8,128)}), f32[16,24,3,384]{3,1,2,0:T(8,128)}, u32[]{:S(2)}, u32[]{:S(2)}) async-start(f32[16,24,3,384]{3,1,2,0:T(8,128)} %bitcast_add_fusion.3), calls=%async_computation.5 | async-start | bytes 3538944 | tf_op jit(solution)/shard_map/all_to_all | solution.py:202
  223.9 218.4 %reduce-scatter.7.cloned.1.call-start = ((), (), s32[]{:S(2)}) async-start(), calls=%async_computation.16 | async-start | bytes 1253376 | tf_op jit(solution)/shard_map/reduce_scatter | solution.py:142
  228.8 19.1 %collective-permute-start.11 = (f32[128,1536]{1,0:T(8,128)}, f32[128,1536]{1,0:T(8,128)}, u32[]{:S(2)}, u32[]{:S(2)}) collective-permute-start(f32[128,1536]{1,0:T(8,128)} %fusion.122), channel_id=1, source_target_pairs={{0,1},{1,0},{2,3},{3,2},{4,5},{5,4},{6,7},{7,6},{8,9},{9,8},{10,11... | collective-permute-start | bytes 2359304 | tf_op jit(solution)/shard_map/ppermute | solution.py:163
  234.7 207.6 %reduce-scatter.5.cloned.1.call-start = ((), (), s32[]{:S(2)}) async-start(), calls=%async_computation.15 | async-start | bytes 1253376 | tf_op jit(solution)/shard_map/reduce_scatter | solution.py:142
  239.1 17.2 %copy-start.60 = (bf16[128,768]{1,0:T(8,128)(2,1)S(1)}, bf16[128,768]{1,0:T(8,128)(2,1)}, u32[]{:S(2)}) copy-start(bf16[128,768]{1,0:T(8,128)(2,1)} %param.16) | copy-start | bytes 589828
  239.1 17.2 %copy-start.124 = (f32[768]{0:T(1024)S(1)}, f32[768]{0:T(1024)}, u32[]{:S(2)}) copy-start(f32[768]{0:T(1024)} %get-tuple-element.166) | copy-start | bytes 9220
  239.1 17.2 %copy-start.125 = (f32[768]{0:T(1024)S(1)}, f32[768]{0:T(1024)}, u32[]{:S(2)}) copy-start(f32[768]{0:T(1024)} %get-tuple-element.173) | copy-start | bytes 9220
  239.1 17.2 %collective-permute-start.8 = (f32[128,768]{1,0:T(8,128)S(1)}, f32[128,768]{1,0:T(8,128)S(1)}, u32[]{:S(2)}, u32[]{:S(2)}) collective-permute-start(f32[128,768]{1,0:T(8,128)S(1)} %constant_dynamic-slice_fusion), channel_id=1, source_target_pairs={{0,1},{1,0},{2,3},{3,2},{4,5},{5,4},{6,7},{7,6},{8,9},{9,8},{10,11... | collective-permute-start | bytes 1179656 | tf_op jit(solution)/shard_map/ppermute | solution.py:163
  257.8 16.2 %copy-start.17 = (f32[128,768]{1,0:T(8,128)}, f32[128,768]{1,0:T(8,128)S(1)}, u32[]{:S(2)}) copy-start(f32[128,768]{1,0:T(8,128)S(1)} %get-tuple-element.27) | copy-start | bytes 1179652
  268.5 6.1 collective-permute-start.12
  276.0 186.3 %reduce-scatter.11.cloned.1.call-start = ((), (), s32[]{:S(2)}) async-start(), calls=%async_computation.18 | async-start | bytes 5013504 | tf_op jit(solution)/shard_map/reduce_scatter | solution.py:142
  279.3 7.3 collective-permute-start.21
  290.8 73.3 %all-to-all-start.8 = ((f32[16,24,1536]{2,1,0:T(8,128)}), f32[16,24,1536]{2,1,0:T(8,128)}, u32[]{:S(2)}, u32[]{:S(2)}) async-start(f32[16,24,1536]{2,1,0:T(8,128)} %bitcast_add_fusion), calls=%async_computation.12 | async-start | bytes 4718592 | tf_op jit(solution)/shard_map/all_to_all | solution.py:202
  295.9 254.7 %reduce-scatter.9.cloned.1.call-start = ((), (), s32[]{:S(2)}) async-start(), calls=%async_computation.17 | async-start | bytes 5013504 | tf_op jit(solution)/shard_map/reduce_scatter | solution.py:142
  310.6 19.0 %collective-permute-start.14 = (f32[128,1536]{1,0:T(8,128)}, f32[128,1536]{1,0:T(8,128)}, u32[]{:S(2)}, u32[]{:S(2)}) collective-permute-start(f32[128,1536]{1,0:T(8,128)} %fusion.119), channel_id=1, source_target_pairs={{0,1},{1,0},{2,3},{3,2},{4,5},{5,4},{6,7},{7,6},{8,9},{9,8},{10,11... | collective-permute-start | bytes 2359304 | tf_op jit(solution)/shard_map/ppermute | solution.py:163
  314.6 15.0 %copy-start.23 = (f32[256,768]{1,0:T(8,128)S(1)}, f32[256,768]{1,0:T(8,128)}, u32[]{:S(2)}) copy-start(f32[256,768]{1,0:T(8,128)} %copy-done.22) | copy-start | bytes 2359300
  314.6 15.0 %copy-start.29 = (f32[256,768]{1,0:T(8,128)S(1)}, f32[256,768]{1,0:T(8,128)}, u32[]{:S(2)}) copy-start(f32[256,768]{1,0:T(8,128)} %copy-done.28) | copy-start | bytes 2359300
  316.1 14.8 %copy-start.112 = (f32[768]{0:T(1024)S(1)}, f32[768]{0:T(1024)}, u32[]{:S(2)}) copy-start(f32[768]{0:T(1024)} %copy-done.111) | copy-start | bytes 9220
  316.1 14.8 %copy-start.114 = (f32[768]{0:T(1024)S(1)}, f32[768]{0:T(1024)}, u32[]{:S(2)}) copy-start(f32[768]{0:T(1024)} %copy-done.113) | copy-start | bytes 9220
  316.1 14.9 %copy-start.135 = (f32[128]{0:T(128)S(1)}, f32[128]{0:T(128)}, u32[]{:S(2)}) copy-start(f32[128]{0:T(128)} %copy-done.134) | copy-start | bytes 1540
  316.1 14.9 %copy-start.141 = (f32[128]{0:T(128)S(1)}, f32[128]{0:T(128)}, u32[]{:S(2)}) copy-start(f32[128]{0:T(128)} %copy-done.140) | copy-start | bytes 1540
  316.1 15.7 %copy-start.18 = (f32[128,768]{1,0:T(8,128)S(1)}, f32[128,768]{1,0:T(8,128)}, u32[]{:S(2)}) copy-start(f32[128,768]{1,0:T(8,128)} %copy-done.17) | copy-start | bytes 1179652
  316.1 45.2 %collective-permute-start.13 = (f32[16,24,3,384]{3,1,2,0:T(8,128)}, f32[16,24,3,384]{3,1,2,0:T(8,128)}, u32[]{:S(2)}, u32[]{:S(2)}) collective-permute-start(f32[16,24,3,384]{3,1,2,0:T(8,128)} %dynamic-slice_bitcast_fusion.2), channel_id=1, source_target_pairs={{0,2},{2,0},{4,6},{6,4},{8,10},{10,8},{12,14},{14,12},{16,18},{18,... | collective-permute-start | bytes 5308424 | tf_op jit(solution)/shard_map/ppermute | solution.py:201
  341.0 2.2 collective-permute-start.15
  343.2 3.7 collective-permute-start.16
  347.0 5.8 collective-permute-start.17
  353.4 5.0 collective-permute-start.18
  360.1 15.3 %collective-permute-start.19 = (f32[19968]{0:T(1024)}, f32[19968]{0:T(1024)}, u32[]{:S(2)}, u32[]{:S(2)}) collective-permute-start(f32[19968]{0:T(1024)} %add.467), channel_id=1, source_target_pairs={{0,1},{1,0},{2,3},{3,2},{4,5},{5,4},{6,7},{7,6},{8,9},{9,8},{10,11... | collective-permute-start | bytes 239624 | tf_op jit(solution)/shard_map/ppermute | solution.py:159
  364.2 69.7 %all-to-all-start.6 = ((f32[16,24,3,384]{3,1,2,0:T(8,128)}), f32[16,24,3,384]{3,1,2,0:T(8,128)S(1)}, u32[]{:S(2)}, u32[]{:S(2)}) async-start(f32[16,24,3,384]{3,1,2,0:T(8,128)} %bitcast_add_fusion.2), calls=%async_computation.6 | async-start | bytes 3538944 | tf_op jit(solution)/shard_map/all_to_all | solution.py:202
  377.2 5.5 collective-permute-start.20
  435.1 123.0 %all-to-all-start.7 = ((f32[16,24,1536]{2,1,0:T(8,128)}), f32[16,24,1536]{2,1,0:T(8,128)S(1)}, u32[]{:S(2)}, u32[]{:S(2)}) async-start(f32[16,24,1536]{2,1,0:T(8,128)} %bitcast_add_fusion.1), calls=%async_computation.11 | async-start | bytes 4718592 | tf_op jit(solution)/shard_map/all_to_all | solution.py:202
  635.2 4.9 collective-permute-start.22
  641.8 28.7 %copy-start.74 = (f32[19968]{0:T(1024)S(1)}, f32[19968]{0:T(1024)}, u32[]{:S(2)}) copy-start(f32[19968]{0:T(1024)} %add.468) | copy-start | bytes 239620
  641.9 27.5 %collective-permute-start.23 = (f32[384,768]{1,0:T(8,128)S(1)}, f32[384,768]{1,0:T(8,128)S(1)}, u32[]{:S(2)}, u32[]{:S(2)}) collective-permute-start(f32[384,768]{1,0:T(8,128)S(1)} %dynamic-slice_add_fusion), channel_id=1, source_target_pairs={{0,1},{1,0},{2,3},{3,2},{4,5},{5,4},{6,7},{7,6},{8,9},{9,8},{10,11... | collective-permute-start | bytes 3538952 | tf_op jit(solution)/shard_map/ppermute | solution.py:453
  669.5 5.3 collective-permute-start.24
  744.3 32.9 %all-to-all-start.10 = ((bf16[16,48,768]{2,1,0:T(8,128)(2,1)}), bf16[16,48,768]{2,1,0:T(8,128)(2,1)S(1)}, u32[]{:S(2)}, u32[]{:S(2)}) async-start(bf16[16,48,768]{2,1,0:T(8,128)(2,1)} %bitcast.132), calls=%async_computation.14 | async-start | bytes 2359296 | tf_op jit(solution)/shard_map/all_to_all | solution.py:479
  750.2 28.2 %copy-start.86 = (f32[2,2,768]{2,1,0:T(2,128)}, f32[2,2,768]{2,1,0:T(2,128)S(1)}, u32[]{:S(2)}) copy-start(f32[2,2,768]{2,1,0:T(2,128)S(1)} %slice.404) | copy-start | bytes 36868
  750.8 27.5 %copy-start.77 = (f32[2,3072]{1,0:T(2,128)}, f32[2,3072]{1,0:T(2,128)S(1)}, u32[]{:S(2)}) copy-start(f32[2,3072]{1,0:T(2,128)S(1)} %reshape.577) | copy-start | bytes 73732
  750.9 27.5 %copy-start.78 = (f32[2,4,768]{2,1,0:T(4,128)}, f32[2,4,768]{2,1,0:T(4,128)S(1)}, u32[]{:S(2)}) copy-start(f32[2,4,768]{2,1,0:T(4,128)S(1)} %reshape.575) | copy-start | bytes 73732
  (125 other events, 485.1 us)
Sparse Core Ops, SparseCore 0:
  10.9 51.3 all-gather.6
  65.1 51.9 all-gather.8
  141.5 47.9 all-gather.10
  234.8 56.3 reduce-scatter.6
  294.7 67.8 reduce-scatter.4
  366.3 95.8 reduce-scatter.10
  466.1 84.4 reduce-scatter.8
